TPU v7x, 512 devices: a whole 4x4x16 slice. The times are simulated.
512 devices in a mesh: front: 4 (over y), row: 4 (over x), col: 32 (over z, core).
Axes of the slice: x: 4, y: 4, z: 16, core: 2. Of those that a mesh axis runs over, the one named last changes fastest.
Arguments:
- inverse_factor: bfloat16 [4, 1024, 1024], P('front', ('row', 'col')), as said below
- panel: bfloat16 [4, 8192, 1024], P('front', 'row', 'col'), may hold values from -1.1953125 to 1.1953125
- trailing: float32 [4, 8192, 8192], P('front', 'row', 'col'), may hold values from -6 to 6
- extend_map: int32 [4, 512], P('front'), may hold values from 0 to 511, as said below
Outputs:
- parent_update: float32 [4, 4096, 8192], P('front', 'row', 'col')
Inputs may be any that keep to these rules, and one draw needn't show every extreme that they name: Each inverse_factor[f] is upper triangular with positive diagonal. Each row of extend_map is a permutation of 0 to 511, and extend_map[f, q] % (128) == q % 128.
All inputs are finite; a program needn't handle non-finite values.
Results may differ from a plain program's by a relative error of at most 0.0034.
Values may be sent and summed in bfloat16 or wider, within the bound.
No kernel may reach another device: no remote copies, remote signals or barrier semaphores. Data moves between devices by JAX's collectives and lax.ppermute only.
A program may use at most 64 MiB of HBM per device.

v0:
```python
import jax
import jax.numpy as jnp
from jax import lax
from jax.sharding import PartitionSpec as P


def from_partner(value, axis, distance):
    mask = 2**distance
    pairs = [(source, source ^ mask) for source in range(lax.axis_size(axis))]
    return lax.ppermute(value, axis, pairs)


def solve_rows(inverse, rows):
    lower = jnp.dot(rows, inverse, preferred_element_type=jnp.float32)
    return lower.astype(jnp.bfloat16)


def outer_rows(left, right):
    return lax.dot_general(
        left, right, (((1,), (1,)), ((), ())), preferred_element_type=jnp.float32
    )


def local(inverse_factor, panel, trailing, extend_map):
    nrow = lax.axis_size("row")
    ncol = lax.axis_size("col")
    group = nrow * ncol
    whole_inverse = lax.all_gather(inverse_factor, ("row", "col"), axis=1, tiled=True)[0]
    local_panel = panel[0]
    local_trailing = trailing[0]
    rows_here = local_trailing.shape[0]
    cols_here = local_trailing.shape[1]
    share = rows_here // ncol
    col_index = lax.axis_index("col")
    row_index = lax.axis_index("row")
    columns = lax.all_gather(local_panel, "col", axis=1, tiled=True)
    solved = solve_rows(whole_inverse, columns)
    piece = lax.dynamic_slice_in_dim(solved, col_index * share, share, 0)
    col_side = lax.all_gather(piece, "row", axis=0, tiled=True)
    schur = local_trailing - outer_rows(solved, col_side)
    block_map = extend_map[0]
    nblocks = block_map.shape[0]
    per_class = nblocks // group
    width = rows_here // (ncol * per_class)
    slots_row = jnp.arange(ncol * per_class, dtype=jnp.int32)
    class_row = slots_row // per_class
    depth_row = slots_row % per_class
    source_row = (depth_row * ncol + class_row) * nrow + row_index
    target_row = class_row * per_class + block_map[source_row] // group
    gather_row = jnp.argsort(target_row)
    slots_col = jnp.arange(nrow * per_class, dtype=jnp.int32)
    class_col = slots_col // per_class
    depth_col = slots_col % per_class
    source_col = (depth_col * ncol + col_index) * nrow + class_col
    target_col = class_col * per_class + block_map[source_col] // group
    gather_col = jnp.argsort(target_col)
    moved = schur.reshape(ncol * per_class, width, cols_here)[gather_row].reshape(
        rows_here, cols_here
    )
    moved = moved.reshape(rows_here, nrow * per_class, width)[:, gather_col].reshape(
        rows_here, cols_here
    )
    member = lax.axis_index("front") % 2
    half = rows_here // 2
    keep = lax.dynamic_slice_in_dim(moved, member * half, half, 0)
    outgoing = lax.dynamic_slice_in_dim(moved, (1 - member) * half, half, 0)
    incoming = from_partner(outgoing, "front", 0)
    return (keep + incoming)[None]


def solution(mesh):
    return jax.shard_map(
        local,
        mesh=mesh,
        in_specs=(
            P("front", ("row", "col"), None),
            P("front", "row", "col"),
            P("front", "row", "col"),
            P("front", None),
        ),
        out_specs=P("front", "row", "col"),
        check_vma=False,
    )
```

profile of v0, /device:TPU:24, one launch (start us, length us, event | category | flops | bytes accessed | tf_op | source)
XLA Modules:
  0.0 311.3 jit_solution(13778032182474074151)
XLA Ops:
  6.5 0.0 copy-start
  6.5 0.0 all-gather.4.cloned.1.call-start
  6.5 0.7 all-gather.4.cloned.1.call-update
  7.3 0.0 all-gather.6.cloned.1.call-start
  7.3 0.7 all-gather.6.cloned.1.call-update
  8.1 0.0 copy-done
  8.1 1.3 gather_fusion
  9.4 0.7 gather_fusion.2
  10.1 2.5 sort.34
  12.6 1.2 sort.35
  13.9 140.6 %all-gather.4.cloned.1.call-done = bf16[1,1024,1024]{2,1,0:T(8,128)(2,1)} async-done(((bf16[1,8,1024]{2,1,0:T(8,128)(2,1)}), bf16[1,1024,1024]{2,1,0:T(8,128)(2,1)}) %all-gather.4.cloned.1.call-update) | async-done | bytes 2097168 | tf_op jit(solution)/shard_map/all_gather | solution.py:28
  154.5 72.2 %all-gather.6.cloned.1.call-done = bf16[1,2048,1024]{1,2,0:T(8,128)(2,1)} async-done(((bf16[1,2048,32]{1,2,0:T(8,128)(2,1)}), bf16[1,2048,1024]{1,2,0:T(8,128)(2,1)}) %all-gather.6.cloned.1.call-update) | async-done | bytes 4194320 | tf_op jit(solution)/shard_map/all_gather | solution.py:36
  226.7 7.4 %fusion.2 = bf16[2048,1024]{1,0:T(8,128)(2,1)S(1)} fusion(bf16[1,2048,1024]{1,2,0:T(8,128)(2,1)} %all-gather.6.cloned.1.call-done, bf16[1,1024,1024]{2,1,0:T(8,128)(2,1)} %all-gather.4.cloned.1.call-done), kind=kOutput, calls=%fused_computation.6 | convolution fusion | flops 4297064448 | bytes 10485760 | tf_op jit(solution)/shard_map/dot_general | solution.py:14
  234.2 13.0 %all_gather.11 = bf16[256,1024]{1,0:T(8,128)(2,1)S(1)} all-gather(bf16[64,1024]{1,0:T(8,128)(2,1)S(1)} %constant_dynamic-slice_fusion.1), channel_id=1, replica_groups=mesh['front'=4,'row'=4,'col'=32] {'row'}, dimensions={0}, use_global_device_ids=true | all-gather | bytes 655360 | tf_op jit(solution)/shard_map/all_gather | solution.py:39
  247.3 3.0 convolution_subtract_fusion
  250.2 2.1 gather_fusion.1
  252.4 10.5 %reshape_reshape.3 = f32[2048,16,16]{2,1,0:T(8,128)} reshape(f32[128,16,256]{2,1,0:T(8,128)} %gather_fusion.1) | data formatting | bytes 4194304 | tf_op jit(solution)/shard_map/reshape;reshape | solution.py:60
  262.9 10.9 %copy.5 = f32[2048,16,16]{0,2,1:T(8,128)} copy(f32[2048,16,16]{2,1,0:T(8,128)} %reshape_reshape.3) | data formatting | bytes 4194304 | tf_op jit(solution)/shard_map/reshape;reshape | solution.py:60
  273.8 2.3 gather_fusion.3
  276.0 0.1 constant_dynamic-slice_fusion
  276.2 3.1 collective-permute-start
  279.2 22.5 %collective-permute-done = f32[1024,256]{0,1:T(8,128)} collective-permute-done((f32[1024,256]{0,1:T(8,128)S(1)}, f32[1024,256]{0,1:T(8,128)}, u32[]{:S(2)}, u32[]{:S(2)}) %collective-permute-start) | collective-permute-done | bytes 1048608 | tf_op jit(solution)/shard_map/ppermute | solution.py:10
  301.7 1.4 add_bitcast_fusion
  303.2 1.3 copy.6
  (13 shorter events, 0.1 us)
Async XLA Ops:
  6.5 1.5 copy-start
  6.5 148.0 %all-gather.4.cloned.1.call-start = ((), (), s32[]{:S(2)}) async-start(), calls=%async_computation | async-start | bytes 2113536 | tf_op jit(solution)/shard_map/all_gather | solution.py:28
  7.3 219.5 %all-gather.6.cloned.1.call-start = ((), (), s32[]{:S(2)}) async-start(), calls=%async_computation.1 | async-start | bytes 4325376 | tf_op jit(solution)/shard_map/all_gather | solution.py:36
  276.2 25.6 %collective-permute-start = (f32[1024,256]{0,1:T(8,128)S(1)}, f32[1024,256]{0,1:T(8,128)}, u32[]{:S(2)}, u32[]{:S(2)}) collective-permute-start(f32[1024,256]{0,1:T(8,128)S(1)} %constant_dynamic-slice_fusion), channel_id=1, source_target_pairs={{0,128},{128,0},{256,384},{384,256},{1,129},{129,1},{257,385},{385... | collective-permute-start | bytes 3145736 | tf_op jit(solution)/shard_map/ppermute | solution.py:10
Sparse Core Ops, SparseCore 0:
  10.5 143.9 all-gather.3
  156.6 70.0 all-gather.5
where the time goes:
time: 312 us; the launch traced here: 311 us
  waiting for transfers between devices  237 us (76%)
  local copies, waits for them, and re-layouts  29.2 us (9%)
  between operations  13.6 us (4%)
  blocking collectives  13 us (4%)
  matrix products  10.4 us (3%)
  other arithmetic  5.29 us (2%)
    all_gather x1, waiting for transfers between devices, local(): lax.all_gather(inverse_factor, ('row', 'col'), axis=1, tiled=True)[0]  141 us
    all_gather x1, waiting for transfers between devices, local(): columns = lax.all_gather(local_panel, 'col', axis=1, tiled=True)  72.2 us
    ppermute x1, waiting for transfers between devices, from_partner(): return lax.ppermute(value, axis, pairs)  22.5 us
    another operation x2, local copies, waits for them, and re-layouts, local(): moved.reshape(rows_here, nrow * per_class, width)[:, gather_col]  21.4 us
    all_gather x1, blocking collectives, local(): col_side = lax.all_gather(piece, 'row', axis=0, tiled=True)  13 us
    dot_general x1, matrix products, solve_rows(): lower = jnp.dot(rows, inverse, preferred_element_type=jnp.float32)  7.43 us
  transfers between devices with their start and end apart: 3, of which 3 were waited for; matrix products, arithmetic and copies ran while one was open for 2% of the time, Pallas kernels for 0%

commit v1 on v0

v1 whole, which is shorter than its diff:
```python
import jax
import jax.numpy as jnp
from jax import lax
from jax.sharding import Mesh
from jax.sharding import PartitionSpec as P


def from_partner(value, axis, distance):
    mask = 2**distance
    pairs = [(source, source ^ mask) for source in range(lax.axis_size(axis))]
    return lax.ppermute(value, axis, pairs)


def outer_rows(left, right):
    return lax.dot_general(
        left, right, (((1,), (1,)), ((), ())), preferred_element_type=jnp.float32
    )


def local(inverse_factor, panel, trailing, extend_map):
    nrow = lax.axis_size("row")
    nz = lax.axis_size("z")
    ncore = lax.axis_size("core")
    ncol = nz * ncore
    group = nrow * ncol
    row_index = lax.axis_index("row")
    col_index = lax.axis_index("z") * ncore + lax.axis_index("core")

    inverse = lax.all_gather(inverse_factor[0], "core", axis=0, tiled=True)
    inverse = lax.all_gather(inverse, "z", axis=0, tiled=True)
    inverse = lax.all_gather(inverse, "row", axis=0, tiled=True)
    order = inverse.shape[0]
    chunk = order // ncol
    inverse = (
        inverse.reshape(nz, ncore, chunk, order)
        .transpose(1, 0, 2, 3)
        .reshape(order, order)
    )

    columns = lax.all_gather(panel[0], "z", axis=1, tiled=True)
    columns = lax.all_gather(columns, "core", axis=1, tiled=True)
    solved = jnp.dot(columns, inverse, preferred_element_type=jnp.float32).astype(
        jnp.bfloat16
    )

    local_trailing = trailing[0]
    rows_here = local_trailing.shape[0]
    cols_here = local_trailing.shape[1]
    share = rows_here // ncol
    piece = lax.dynamic_slice_in_dim(solved, col_index * share, share, 0)
    col_side = lax.all_gather(piece, "row", axis=0, tiled=True)

    block_map = extend_map[0]
    nblocks = block_map.shape[0]
    per_class = nblocks // group
    width = rows_here // (ncol * per_class)
    slots_row = jnp.arange(ncol * per_class, dtype=jnp.int32)
    class_row = slots_row // per_class
    depth_row = slots_row % per_class
    source_row = (depth_row * ncol + class_row) * nrow + row_index
    target_row = class_row * per_class + block_map[source_row] // group
    gather_row = jnp.argsort(target_row)
    slots_col = jnp.arange(nrow * per_class, dtype=jnp.int32)
    class_col = slots_col // per_class
    depth_col = slots_col % per_class
    source_col = (depth_col * ncol + col_index) * nrow + class_col
    target_col = class_col * per_class + block_map[source_col] // group
    gather_col = jnp.argsort(target_col)

    col_side = col_side.reshape(nrow * per_class, width, order)[gather_col].reshape(
        cols_here, order
    )
    lane = jnp.arange(cols_here, dtype=jnp.int32)
    picked = gather_col[lane // width] * width + lane % width
    select_cols = (lane[:, None] == picked[None, :]).astype(jnp.float32)

    member = lax.axis_index("front") % 2
    half = rows_here // 2
    half_blocks = half // width

    def half_update(which):
        rows = lax.dynamic_slice_in_dim(local_trailing, which * half, half, 0)
        low = lax.dynamic_slice_in_dim(solved, which * half, half, 0)
        moved_cols = jnp.dot(
            rows,
            select_cols,
            precision=lax.Precision.HIGHEST,
            preferred_element_type=jnp.float32,
        )
        schur = moved_cols - outer_rows(low, col_side)
        blocks = (
            lax.dynamic_slice_in_dim(gather_row, which * half_blocks, half_blocks, 0)
            - which * half_blocks
        )
        return schur.reshape(half_blocks, width, cols_here)[blocks].reshape(
            half, cols_here
        )

    outgoing = half_update(1 - member)
    incoming = from_partner(outgoing, "front", 0)
    keep = half_update(member)
    return (keep + incoming)[None]


def solution(mesh):
    devices = mesh.devices
    shape = devices.shape
    fine = Mesh(
        devices.reshape(shape[0], shape[1], shape[2] // 2, 2),
        ("front", "row", "z", "core"),
    )
    cols = ("z", "core")
    return jax.shard_map(
        local,
        mesh=fine,
        in_specs=(
            P("front", ("row",) + cols, None),
            P("front", "row", cols),
            P("front", "row", cols),
            P("front", None),
        ),
        out_specs=P("front", "row", cols),
        check_vma=False,
    )
```

time: 312 us -> 214 us (0.69)
  waiting for transfers between devices: 237 us -> 97.2 us
  blocking collectives: 13 us -> 57.5 us
  local copies, waits for them, and re-layouts: 29.2 us -> 11.2 us
  other arithmetic: 5.29 us -> 16.1 us
  matrix products: 10.4 us -> 15.4 us
    all_gather x2 -> x3, waiting for transfers between devices: 213 us -> 79.7 us  [the longest x1 35.5 us: local(): columns = lax.all_gather(panel[0], 'z', axis=1, tiled=True)]
    all_gather x0 -> x2, blocking collectives: none -> 44.4 us  [the longest x1 42.4 us: local(): inverse = lax.all_gather(inverse, 'z', axis=0, tiled=True)]
    another operation x2 -> x0, local copies, waits for them, and re-layouts: 21.4 us -> none  [local(): moved.reshape(rows_here, nrow * per_class, width)[:, gather_col]]
    add x0 -> x2, other arithmetic: none -> 7.87 us  [the longest x1 5.58 us: local(): picked = gather_col[lane // width] * width + lane % width]
    ppermute x1, waiting for transfers between devices: 22.5 us -> 16.8 us  [from_partner(): return lax.ppermute(value, axis, pairs)]
    gather x2 -> x9, other arithmetic: 0.01 us -> 4.33 us  [the longest x6 4.31 us: local(): picked = gather_col[lane // width] * width + lane % width]
    transpose x0 -> x1, local copies, waits for them, and re-layouts: none -> 3.26 us  [local(): inverse = inverse.reshape(nz, ncore, chunk, order).transpose(1, 0, 2, 3)....]
    dot_general x1 -> x3, matrix products: 7.43 us -> 10.7 us  [the longest x1 7.43 us: local(): jnp.dot(columns, inverse, preferred_element_type=jnp.float32)]
  transfers between devices with their start and end apart: 3 -> 4, of which waited for: 3 -> 4; matrix products, arithmetic and copies ran while one was open for 2% -> 12% of each run, Pallas kernels for 0% -> 0%
where the time goes in v1:
time: 214 us
  waiting for transfers between devices  97.2 us (45%)
  blocking collectives  57.5 us (27%)
  other arithmetic  16.1 us (8%)
  matrix products  15.4 us (7%)
  between operations  13.3 us (6%)
  local copies, waits for them, and re-layouts  11.2 us (5%)
  starting transfers between devices  2.81 us (1%)
    all_gather x1, blocking collectives, local(): inverse = lax.all_gather(inverse, 'z', axis=0, tiled=True)  42.4 us
    all_gather x1, waiting for transfers between devices, local(): columns = lax.all_gather(panel[0], 'z', axis=1, tiled=True)  35.5 us
    all_gather x1, waiting for transfers between devices, local(): columns = lax.all_gather(columns, 'core', axis=1, tiled=True)  23.1 us
    all_gather x1, waiting for transfers between devices, local(): inverse = lax.all_gather(inverse, 'row', axis=0, tiled=True)  21.1 us
    ppermute x1, waiting for transfers between devices, from_partner(): return lax.ppermute(value, axis, pairs)  16.8 us
    all_gather x1, blocking collectives, local(): col_side = lax.all_gather(piece, 'row', axis=0, tiled=True)  13.1 us
    dot_general x1, matrix products, local(): jnp.dot(columns, inverse, preferred_element_type=jnp.float32)  7.43 us
    add x1, other arithmetic, local(): picked = gather_col[lane // width] * width + lane % width  5.58 us
  transfers between devices with their start and end apart: 4, of which 4 were waited for; matrix products, arithmetic and copies ran while one was open for 12% of the time, Pallas kernels for 0%

profile of v1, /device:TPU:24, one launch (start us, length us, event | category | flops | bytes accessed | tf_op | source)
XLA Modules:
  0.0 213.5 jit_solution(8595470988300910653)
XLA Ops:
  6.5 0.7 all-gather.9.cloned.1.call-update
  7.3 2.0 all-gather.2
  9.3 42.4 %all-gather.3 = bf16[1,256,1024]{2,1,0:T(8,128)(2,1)} all-gather(bf16[1,16,1024]{2,1,0:T(8,128)(2,1)S(1)} %all-gather.2), channel_id=5, replica_groups=mesh['front'=4,'row'=4,'z'=16,'core'=2] {'z'}, dimensions={1}, use_global_device_ids=true | all-gather | bytes 557056 | tf_op jit(solution)/shard_map/all_gather | solution.py:30
  51.8 35.5 %all-gather.9.cloned.1.call-done = bf16[1,2048,512]{1,2,0:T(8,128)(2,1)} async-done(((bf16[1,2048,32]{1,2,0:T(8,128)(2,1)}), bf16[1,2048,512]{1,2,0:T(8,128)(2,1)}) %all-gather.9.cloned.1.call-update) | async-done | bytes 2097168 | tf_op jit(solution)/shard_map/all_gather | solution.py:40
  88.0 1.3 gather_fusion.2
  89.3 1.2 sort.34
  90.6 2.5 %sort.35 = (s32[128]{0:T(128)}, s32[128]{0:T(128)S(1)}) sort(s32[128]{0:T(128)S(1)} %fusion.28, s32[128]{0:T(128)S(1)} %iota.41), dimensions={0}, to_apply=%region_1.2 | sort | flops 896 | bytes 2048 | tf_op jit(solution)/shard_map/jit(argsort)/sort | solution.py:62
  93.4 0.7 fusion.34
  94.1 4.2 %compare_select_fusion.1 = s32[256,1]{0,1:T(1,128)S(1)} fusion(s32[]{:T(128)} %bitcast.12, s32[]{:T(128)} %bitcast.13, s32[]{:T(128)} %bitcast.14, s32[]{:T(128)} %bitcast.15, s32[]{:T(128)} %bitcast.16, s32[]{:T(128)} %bitcast.18, s32[]{:T(128)} %bitcast.17), kind=kLoop, calls=%fused_computation.37 | loop fusion | flops 5888 | bytes 1052 | tf_op jit(solution)/shard_map/gather | solution.py:74
  98.3 5.6 %fusion.19 = s32[256]{0:T(256)S(1)} fusion(pred[256]{0:T(512)(128)(4,1)S(1)} %get-tuple-element.27, pred[256]{0:T(512)(128)(4,1)S(1)} %get-tuple-element.28, pred[256]{0:T(512)(128)(4,1)S(1)} %get-tuple-element.29, pred[256]{0:T(512)(128)(4,1)S(1)} %get-tuple-element.30, pred[256]{0:T(512)(128)(4,1)S(1)} %get-tuple-element.31, ...), kind=kLoop, calls=%fused_computation.72 | loop fusion | flops 4352 | bytes 4388 | tf_op jit(solution)/shard_map/add | solution.py:74
  103.9 21.1 %all-gather.13.cloned.1.call-done = bf16[1,1024,1024]{2,1,0:T(8,128)(2,1)} async-done(((bf16[1,256,1024]{2,1,0:T(8,128)(2,1)}), bf16[1,1024,1024]{2,1,0:T(8,128)(2,1)}) %all-gather.13.cloned.1.call-update) | async-done | bytes 2097168 | tf_op jit(solution)/shard_map/all_gather | solution.py:31
  125.0 3.3 %copy.5 = bf16[2,16,32,1024]{3,2,1,0:T(8,128)(2,1)} copy(bf16[2,16,32,1024]{3,2,0,1:T(8,128)(2,1)} %bitcast.54) | data formatting | bytes 4194304 | tf_op jit(solution)/shard_map/transpose | solution.py:36
  128.2 23.1 %all-gather.11.cloned.1.call-done = bf16[1,2048,1024]{1,2,0:T(8,128)(2,1)} async-done(((bf16[1,2048,512]{1,2,0:T(8,128)(2,1)}), bf16[1,2048,1024]{1,2,0:T(8,128)(2,1)}) %all-gather.11.cloned.1.call-update) | async-done | bytes 4194320 | tf_op jit(solution)/shard_map/all_gather | solution.py:41
  151.3 7.4 %fusion.2 = bf16[2048,1024]{1,0:T(8,128)(2,1)S(1)} fusion(bf16[1024,1024]{1,0:T(8,128)(2,1)} %bitcast.55, bf16[1,2048,1024]{1,2,0:T(8,128)(2,1)} %all-gather.11.cloned.1.call-done), kind=kOutput, calls=%fused_computation.7 | convolution fusion | flops 4297064448 | bytes 10485760 | tf_op jit(solution)/shard_map/dot_general | solution.py:42
  158.8 13.1 %all_gather.23 = bf16[256,1024]{1,0:T(8,128)(2,1)S(1)} all-gather(bf16[64,1024]{1,0:T(8,128)(2,1)S(1)} %constant_dynamic-slice_fusion), channel_id=1, replica_groups=mesh['front'=4,'row'=4,'z'=16,'core'=2] {'row'}, dimensions={0}, use_global_device_ids=true | all-gather | bytes 655360 | tf_op jit(solution)/shard_map/all_gather | solution.py:51
  172.5 2.3 %fusion.5 = f32[1024,256]{1,0:T(8,128)S(1)} fusion(bf16[256,1024]{1,0:T(8,128)(2,1)S(1)} %bitcast.50, bf16[2048,1024]{1,0:T(8,128)(2,1)} %copy-done.2, s32[]{:T(128)S(6)} %select_n.164), kind=kOutput, calls=%fused_computation.8 | convolution fusion | flops 536870912 | bytes 3670020 | tf_op jit(solution)/shard_map/dot_general | solution.py:15
  174.9 1.6 convolution_subtract_fusion
  176.5 2.8 %gather_fusion.4 = f32[64,16,256]{2,1,0:T(8,128)} fusion(f32[64,16,256]{2,1,0:T(8,128)} %bitcast.53, s32[1024]{0:T(1024)S(1)} %pad_clamp_fusion), kind=kCustom, calls=%fused_computation.4 | custom fusion | bytes 2097408 | tf_op jit(solution)/shard_map/gather | solution.py:95
  179.3 2.7 %collective-permute-start = (f32[1024,256]{1,0:T(8,128)}, f32[1024,256]{1,0:T(8,128)}, u32[]{:S(2)}, u32[]{:S(2)}) collective-permute-start(f32[1024,256]{1,0:T(8,128)} %bitcast.57), channel_id=1, source_target_pairs={{0,128},{128,0},{256,384},{384,256},{1,129},{129,1},{257,385},{385... | collective-permute-start | bytes 3145736 | tf_op jit(solution)/shard_map/ppermute | solution.py:11
  182.1 2.3 %fusion.7 = f32[1024,256]{1,0:T(8,128)S(1)} fusion(bf16[256,1024]{1,0:T(8,128)(2,1)S(1)} %bitcast.51, bf16[2048,1024]{1,0:T(8,128)(2,1)} %copy-done.2, s32[]{:T(128)S(6)} %select_n.146), kind=kOutput, calls=%fused_computation.10 | convolution fusion | flops 536870912 | bytes 3670020 | tf_op jit(solution)/shard_map/dot_general | solution.py:15
  184.4 1.6 convolution_subtract_fusion.1
  186.1 1.8 gather_fusion.3
  187.9 16.8 %collective-permute-done = f32[1024,256]{1,0:T(8,128)} collective-permute-done((f32[1024,256]{1,0:T(8,128)}, f32[1024,256]{1,0:T(8,128)}, u32[]{:S(2)}, u32[]{:S(2)}) %collective-permute-start) | collective-permute-done | bytes 1048608 | tf_op jit(solution)/shard_map/ppermute | solution.py:11
  204.7 2.3 %bitcast_add_fusion = f32[1024,256]{1,0:T(8,128)} fusion(f32[1024,256]{1,0:T(8,128)} %collective-permute-done, f32[64,16,256]{2,1,0:T(8,128)S(1)} %gather_fusion.3), kind=kLoop, calls=%fused_computation.15 | loop fusion | flops 262144 | bytes 3145728 | tf_op jit(solution)/shard_map/add | solution.py:102
  (32 shorter events, 1.7 us)
Async XLA Ops:
  6.5 168.4 %copy-start = (f32[1,2048,256]{2,1,0:T(8,128)S(1)}, f32[1,2048,256]{2,1,0:T(8,128)}, u32[]{:S(2)}) copy-start(f32[1,2048,256]{2,1,0:T(8,128)} %param.6) | copy-start | bytes 6291460
  6.5 80.8 %copy-start.1 = (s32[1,512]{1,0:T(1,128)S(1)}, s32[1,512]{1,0:T(1,128)}, u32[]{:S(2)}) copy-start(s32[1,512]{1,0:T(1,128)} %param.7) | copy-start | bytes 6148
  6.5 80.7 %all-gather.9.cloned.1.call-start = ((), (), s32[]{:S(2)}) async-start(), calls=%async_computation | async-start | bytes 2228224 | tf_op jit(solution)/shard_map/all_gather | solution.py:40
  7.3 117.7 %all-gather.13.cloned.1.call-start = ((), (), s32[]{:S(2)}) async-start(), calls=%async_computation.2 | async-start | bytes 2621440 | tf_op jit(solution)/shard_map/all_gather | solution.py:31
  51.7 99.6 %all-gather.11.cloned.1.call-start = ((), (), s32[]{:S(2)}) async-start(), calls=%async_computation.1 | async-start | bytes 6291456 | tf_op jit(solution)/shard_map/all_gather | solution.py:41
  158.8 13.2 %copy-start.2 = (bf16[2048,1024]{1,0:T(8,128)(2,1)}, bf16[2048,1024]{1,0:T(8,128)(2,1)S(1)}, u32[]{:S(2)}) copy-start(bf16[2048,1024]{1,0:T(8,128)(2,1)S(1)} %fusion.2) | copy-start | bytes 12582916
  179.3 25.4 %collective-permute-start = (f32[1024,256]{1,0:T(8,128)}, f32[1024,256]{1,0:T(8,128)}, u32[]{:S(2)}, u32[]{:S(2)}) collective-permute-start(f32[1024,256]{1,0:T(8,128)} %bitcast.57), channel_id=1, source_target_pairs={{0,128},{128,0},{256,384},{384,256},{1,129},{129,1},{257,385},{385... | collective-permute-start | bytes 3145736 | tf_op jit(solution)/shard_map/ppermute | solution.py:11
Sparse Core Ops, SparseCore 0:
  9.4 77.7 all-gather.8
  89.4 35.5 all-gather.12
  127.1 24.2 all-gather.10

commit v2 on v1

--- a/solution.py
+++ b/solution.py
@@ -17,6 +17,28 @@
     )
 
 
+def ring_gather(value, axis, index, n):
+    ahead = [(source, (source + 1) % n) for source in range(n)]
+    behind = [(source, (source - 1) % n) for source in range(n)]
+    held = [value]
+    forward = value
+    backward = value
+    for step in range(1, n):
+        if step % 2:
+            forward = lax.ppermute(forward, axis, ahead)
+            held.append(forward)
+        else:
+            backward = lax.ppermute(backward, axis, behind)
+            held.append(backward)
+    offsets = [0] + [(step + 1) // 2 if step % 2 else -(step // 2) for step in range(1, n)]
+    by_offset = [None] * n
+    for offset, block in zip(offsets, held):
+        by_offset[offset % n] = block
+    stacked = jnp.stack(by_offset)
+    sources = jnp.arange(n, dtype=jnp.int32)
+    return stacked[(index - sources) % n]
+
+
 def local(inverse_factor, panel, trailing, extend_map):
     nrow = lax.axis_size("row")
     nz = lax.axis_size("z")
@@ -28,27 +50,23 @@
 
     inverse = lax.all_gather(inverse_factor[0], "core", axis=0, tiled=True)
     inverse = lax.all_gather(inverse, "z", axis=0, tiled=True)
-    inverse = lax.all_gather(inverse, "row", axis=0, tiled=True)
-    order = inverse.shape[0]
-    chunk = order // ncol
-    inverse = (
-        inverse.reshape(nz, ncore, chunk, order)
-        .transpose(1, 0, 2, 3)
-        .reshape(order, order)
-    )
+    inverse = ring_gather(inverse, "row", row_index, nrow)
+    order = inverse.shape[-1]
+    inverse = inverse.reshape(order, order)
 
-    columns = lax.all_gather(panel[0], "z", axis=1, tiled=True)
-    columns = lax.all_gather(columns, "core", axis=1, tiled=True)
-    solved = jnp.dot(columns, inverse, preferred_element_type=jnp.float32).astype(
-        jnp.bfloat16
-    )
+    columns = lax.all_gather(panel[0], ("z", "core"), axis=1, tiled=True)
+
+    def solve(rows):
+        return jnp.dot(rows, inverse, preferred_element_type=jnp.float32).astype(
+            jnp.bfloat16
+        )
 
     local_trailing = trailing[0]
     rows_here = local_trailing.shape[0]
     cols_here = local_trailing.shape[1]
     share = rows_here // ncol
-    piece = lax.dynamic_slice_in_dim(solved, col_index * share, share, 0)
-    col_side = lax.all_gather(piece, "row", axis=0, tiled=True)
+    piece = solve(lax.dynamic_slice_in_dim(columns, col_index * share, share, 0))
+    col_side = ring_gather(piece, "row", row_index, nrow)
 
     block_map = extend_map[0]
     nblocks = block_map.shape[0]
@@ -80,7 +98,7 @@
 
     def half_update(which):
         rows = lax.dynamic_slice_in_dim(local_trailing, which * half, half, 0)
-        low = lax.dynamic_slice_in_dim(solved, which * half, half, 0)
+        low = solve(lax.dynamic_slice_in_dim(columns, which * half, half, 0))
         moved_cols = jnp.dot(
             rows,
             select_cols,

time: 214 us -> 154 us (0.72)
  waiting for transfers between devices: 97.2 us -> 26.6 us
  starting transfers between devices: 2.81 us -> 22.8 us
  blocking collectives: 57.5 us -> 40.4 us
  other arithmetic: 16.1 us -> 19.4 us
    all_gather x3 -> x1, waiting for transfers between devices: 79.7 us -> 4.3 us  [local(): columns = lax.all_gather(panel[0], ('z', 'core'), axis=1, tiled=True)]
    ppermute x0 -> x6, starting transfers between devices: none -> 19.6 us  [the longest x4 12.2 us: ring_gather(): forward = lax.ppermute(forward, axis, ahead)]
    all_gather x1 -> x0, blocking collectives: 13.1 us -> none  [local(): col_side = lax.all_gather(piece, 'row', axis=0, tiled=True)]
    dot_general x2, matrix products: 4.68 us -> 12.6 us  [outer_rows(): lax.dot_general(left, right, (((1,), (1,)), ((), ())), preferred_element_...]
    ppermute x0 -> x6, waiting for transfers between devices: none -> 7.88 us  [the longest x4 6.34 us: ring_gather(): forward = lax.ppermute(forward, axis, ahead)]
    dot_general x1, matrix products: 7.43 us -> 2.31 us  [solve(): jnp.dot(rows, inverse, preferred_element_type=jnp.float32)]
    gather x0 -> x2, local copies, waits for them, and re-layouts: none -> 4.2 us  [ring_gather(): return stacked[(index - sources) % n]]
    all_gather x1, blocking collectives: 42.4 us -> 38.4 us  [local(): inverse = lax.all_gather(inverse, 'z', axis=0, tiled=True)]
  transfers between devices with their start and end apart: 4 -> 8, of which waited for: 4 -> 5; matrix products, arithmetic and copies ran while one was open for 12% -> 23% of each run, Pallas kernels for 0% -> 0%
where the time goes in v2:
time: 154 us; the launch traced here: 153 us
  blocking collectives  40.4 us (26%)
  waiting for transfers between devices  26.6 us (17%)
  starting transfers between devices  22.8 us (15%)
  other arithmetic  19.4 us (13%)
  matrix products  17.1 us (11%)
  between operations  13.6 us (9%)
  local copies, waits for them, and re-layouts  12.8 us (8%)
    all_gather x1, blocking collectives, local(): inverse = lax.all_gather(inverse, 'z', axis=0, tiled=True)  38.4 us
    ppermute x1, waiting for transfers between devices, from_partner(): return lax.ppermute(value, axis, pairs)  13.7 us
    dot_general x2, matrix products, outer_rows(): lax.dot_general(left, right, (((1,), (1,)), ((), ())), preferred_element_...  12.6 us
    ppermute x4, starting transfers between devices, ring_gather(): forward = lax.ppermute(forward, axis, ahead)  12.2 us
    ppermute x2, starting transfers between devices, ring_gather(): backward = lax.ppermute(backward, axis, behind)  7.36 us
    ppermute x4, waiting for transfers between devices, ring_gather(): forward = lax.ppermute(forward, axis, ahead)  6.34 us
    add x1, other arithmetic, local(): picked = gather_col[lane // width] * width + lane % width  5.75 us
    gather x6, other arithmetic, local(): picked = gather_col[lane // width] * width + lane % width  4.47 us
  transfers between devices with their start and end apart: 8, of which 5 were waited for; matrix products, arithmetic and copies ran while one was open for 23% of the time, Pallas kernels for 0%

profile of v2, /device:TPU:24, one launch (start us, length us, event | category | flops | bytes accessed | tf_op | source)
XLA Modules:
  0.0 152.7 jit_solution(12370641346807167266)
XLA Ops:
  7.3 2.0 %all-gather.1 = bf16[1,16,1024]{2,1,0:T(8,128)(2,1)S(1)} all-gather(bf16[1,8,1024]{2,1,0:T(8,128)(2,1)} %param.4), channel_id=3, replica_groups=mesh['front'=4,'row'=4,'z'=16,'core'=2] {'core'}, dimensions={1}, use_global_device_ids=true | all-gather | bytes 49152 | tf_op jit(solution)/shard_map/all_gather | solution.py:51
  9.3 38.4 %all-gather.2 = bf16[1,256,1024]{2,1,0:T(8,128)(2,1)S(1)} all-gather(bf16[1,16,1024]{2,1,0:T(8,128)(2,1)S(1)} %all-gather.1), channel_id=4, replica_groups=mesh['front'=4,'row'=4,'z'=16,'core'=2] {'z'}, dimensions={1}, use_global_device_ids=true | all-gather | bytes 557056 | tf_op jit(solution)/shard_map/all_gather | solution.py:52
  47.7 3.4 %collective-permute-start = (bf16[256,1024]{1,0:T(8,128)(2,1)S(1)}, bf16[256,1024]{1,0:T(8,128)(2,1)S(1)}, u32[]{:S(2)}, u32[]{:S(2)}) collective-permute-start(bf16[256,1024]{1,0:T(8,128)(2,1)S(1)} %bitcast.75), channel_id=1, source_target_pairs={{0,32},{32,64},{64,96},{96,0},{1,33},{33,65},{65,97},{97,1},{2,34}... | collective-permute-start | bytes 1572872 | tf_op jit(solution)/shard_map/ppermute | solution.py:28
  51.1 3.7 %collective-permute-start.2 = (bf16[256,1024]{1,0:T(8,128)(2,1)S(1)}, bf16[256,1024]{1,0:T(8,128)(2,1)}, u32[]{:S(2)}, u32[]{:S(2)}) collective-permute-start(bf16[256,1024]{1,0:T(8,128)(2,1)S(1)} %bitcast.76), channel_id=1, source_target_pairs={{0,96},{32,0},{64,32},{96,64},{1,97},{33,1},{65,33},{97,65},{2,98}... | collective-permute-start | bytes 1572872 | tf_op jit(solution)/shard_map/ppermute | solution.py:31
  58.2 1.9 %collective-permute-done = bf16[256,1024]{1,0:T(8,128)(2,1)S(1)} collective-permute-done((bf16[256,1024]{1,0:T(8,128)(2,1)S(1)}, bf16[256,1024]{1,0:T(8,128)(2,1)S(1)}, u32[]{:S(2)}, u32[]{:S(2)}) %collective-permute-start) | collective-permute-done | bytes 524320 | tf_op jit(solution)/shard_map/ppermute | solution.py:28
  60.1 3.4 %collective-permute-start.1 = (bf16[256,1024]{1,0:T(8,128)(2,1)S(1)}, bf16[256,1024]{1,0:T(8,128)(2,1)}, u32[]{:S(2)}, u32[]{:S(2)}) collective-permute-start(bf16[256,1024]{1,0:T(8,128)(2,1)S(1)} %collective-permute-done), channel_id=1, source_target_pairs={{0,32},{32,64},{64,96},{96,0},{1,33},{33,65},{65,97},{97,1},{2,34}... | collective-permute-start | bytes 1572872 | tf_op jit(solution)/shard_map/ppermute | solution.py:28
  63.5 4.3 %compare_select_fusion.1 = s32[256,1]{0,1:T(1,128)S(1)} fusion(s32[]{:T(128)} %bitcast.12, s32[]{:T(128)} %bitcast.13, s32[]{:T(128)} %bitcast.14, s32[]{:T(128)} %bitcast.15, s32[]{:T(128)} %bitcast.16, s32[]{:T(128)} %bitcast.18, s32[]{:T(128)} %bitcast.17), kind=kLoop, calls=%fused_computation.50 | loop fusion | flops 5888 | bytes 1052 | tf_op jit(solution)/shard_map/gather | solution.py:92
  67.8 1.6 %gather_fusion.4 = s32[128]{0:T(128)S(1)} fusion(s32[512]{0:T(512)} %bitcast.70, s32[1024]{0:T(1024)S(1)} %pad_clamp_fusion.2), kind=kCustom, calls=%fused_computation.4 | custom fusion | bytes 1536 | tf_op jit(solution)/shard_map/gather | solution.py:79
  69.6 5.7 %fusion.41 = s32[256]{0:T(256)S(1)} fusion(pred[256]{0:T(512)(128)(4,1)S(1)} %get-tuple-element.27, pred[256]{0:T(512)(128)(4,1)S(1)} %get-tuple-element.28, pred[256]{0:T(512)(128)(4,1)S(1)} %get-tuple-element.29, pred[256]{0:T(512)(128)(4,1)S(1)} %get-tuple-element.30, pred[256]{0:T(512)(128)(4,1)S(1)} %get-tuple-element.31, ...), kind=kLoop, calls=%fused_computation.89 | loop fusion | flops 4352 | bytes 4388 | tf_op jit(solution)/shard_map/add | solution.py:92
  77.0 2.8 %pad_maximum_fusion = bf16[4,256,1024]{2,1,0:T(8,128)(2,1)} fusion(bf16[1,256,1024]{2,1,0:T(8,128)(2,1)} %bitcast.24, bf16[1,256,1024]{2,1,0:T(8,128)(2,1)} %bitcast.23, bf16[1,256,1024]{2,1,0:T(8,128)(2,1)S(1)} %bitcast.81, bf16[1,256,1024]{2,1,0:T(8,128)(2,1)S(1)} %all-gather.2), kind=kLoop, calls=%fused_computation.7 | loop fusion | flops 3145728 | bytes 4194304 | tf_op jit(solution)/shard_map/stack | solution.py:37
  79.8 3.6 %gather_fusion.1 = bf16[4,256,1024]{2,1,0:T(8,128)(2,1)} fusion(bf16[4,256,1024]{2,1,0:T(8,128)(2,1)} %pad_maximum_fusion, s32[1024]{0:T(1024)S(1)} %pad_clamp_fusion.4), kind=kCustom, calls=%fused_computation.1 | custom fusion | bytes 4194320 | tf_op jit(solution)/shard_map/gather | solution.py:39
  83.4 4.3 %all-gather.5.cloned.1.call-done = bf16[1,2048,1024]{1,2,0:T(8,128)(2,1)} async-done(((bf16[1,2048,32]{1,2,0:T(8,128)(2,1)}), bf16[1,2048,1024]{1,2,0:T(8,128)(2,1)}) %all-gather.5.cloned.1.call-update) | async-done | bytes 4194320 | tf_op jit(solution)/shard_map/all_gather | solution.py:57
  87.7 2.3 %convolution_convert_fusion = bf16[64,1024]{1,0:T(8,128)(2,1)S(1)} fusion(bf16[1024,1024]{1,0:T(8,128)(2,1)} %bitcast.71, bf16[1,2048,1024]{1,2,0:T(8,128)(2,1)} %all-gather.5.cloned.1.call-done, s32[]{:T(128)S(6)} %select_n.183), kind=kOutput, calls=%fused_computation.20 | convolution fusion | flops 134283264 | bytes 2490372 | tf_op jit(solution)/shard_map/dot_general | solution.py:60
  90.0 3.3 %collective-permute-start.3 = (bf16[64,1024]{1,0:T(8,128)(2,1)S(1)}, bf16[64,1024]{1,0:T(8,128)(2,1)S(1)}, u32[]{:S(2)}, u32[]{:S(2)}) collective-permute-start(bf16[64,1024]{1,0:T(8,128)(2,1)S(1)} %convolution_convert_fusion), channel_id=1, source_target_pairs={{0,32},{32,64},{64,96},{96,0},{1,33},{33,65},{65,97},{97,1},{2,34}... | collective-permute-start | bytes 393224 | tf_op jit(solution)/shard_map/ppermute | solution.py:28
  93.4 2.5 %sort.35 = (s32[128]{0:T(128)}, s32[128]{0:T(128)S(1)}) sort(s32[128]{0:T(128)S(1)} %fusion.50, s32[128]{0:T(128)S(1)} %iota.47), dimensions={0}, to_apply=%region_1.2 | sort | flops 896 | bytes 2048 | tf_op jit(solution)/shard_map/jit(argsort)/sort | solution.py:80
  96.0 3.7 %collective-permute-start.5 = (bf16[64,1024]{1,0:T(8,128)(2,1)S(1)}, bf16[64,1024]{1,0:T(8,128)(2,1)S(1)}, u32[]{:S(2)}, u32[]{:S(2)}) collective-permute-start(bf16[64,1024]{1,0:T(8,128)(2,1)S(1)} %convolution_convert_fusion), channel_id=1, source_target_pairs={{0,96},{32,0},{64,32},{96,64},{1,97},{33,1},{65,33},{97,65},{2,98}... | collective-permute-start | bytes 393224 | tf_op jit(solution)/shard_map/ppermute | solution.py:31
  99.7 2.1 %collective-permute-start.4 = (bf16[64,1024]{1,0:T(8,128)(2,1)S(1)}, bf16[64,1024]{1,0:T(8,128)(2,1)S(1)}, u32[]{:S(2)}, u32[]{:S(2)}) collective-permute-start(bf16[64,1024]{1,0:T(8,128)(2,1)S(1)} %collective-permute-done.3), channel_id=1, source_target_pairs={{0,32},{32,64},{64,96},{96,0},{1,33},{33,65},{65,97},{97,1},{2,34}... | collective-permute-start | bytes 393224 | tf_op jit(solution)/shard_map/ppermute | solution.py:28
  103.4 4.4 %collective-permute-done.4 = bf16[64,1024]{1,0:T(8,128)(2,1)S(1)} collective-permute-done((bf16[64,1024]{1,0:T(8,128)(2,1)S(1)}, bf16[64,1024]{1,0:T(8,128)(2,1)S(1)}, u32[]{:S(2)}, u32[]{:S(2)}) %collective-permute-start.4) | collective-permute-done | bytes 131104 | tf_op jit(solution)/shard_map/ppermute | solution.py:28
  110.0 6.0 %fusion.13 = f32[1024,256]{1,0:T(8,128)S(1)} fusion(f32[1024,256]{1,0:T(8,128)} %fusion.24, bf16[256,1024]{1,0:T(8,128)(2,1)} %bitcast.79, bf16[1024,1024]{1,0:T(8,128)(2,1)} %bitcast.72, bf16[1,2048,1024]{1,2,0:T(8,128)(2,1)} %all-gather.5.cloned.1.call-done, s32[]{:T(128)S(6)} %select_n.192), kind=kOutput, calls=%fused_computation.19 | convolution fusion | flops 2685665280 | bytes 6815748 | tf_op jit(solution)/shard_map/dot_general | solution.py:15
  117.5 3.3 %collective-permute-start.6 = (f32[1024,256]{1,0:T(8,128)}, f32[1024,256]{1,0:T(8,128)}, u32[]{:S(2)}, u32[]{:S(2)}) collective-permute-start(f32[1024,256]{1,0:T(8,128)} %bitcast.40), channel_id=1, source_target_pairs={{0,128},{128,0},{256,384},{384,256},{1,129},{129,1},{257,385},{385... | collective-permute-start | bytes 3145736 | tf_op jit(solution)/shard_map/ppermute | solution.py:11
  121.5 6.6 %fusion.10 = f32[1024,256]{1,0:T(8,128)} fusion(f32[1024,256]{1,0:T(8,128)S(1)} %fusion.26, bf16[256,1024]{1,0:T(8,128)(2,1)} %bitcast.80, bf16[1024,1024]{1,0:T(8,128)(2,1)} %bitcast.73, bf16[1,2048,1024]{1,2,0:T(8,128)(2,1)} %all-gather.5.cloned.1.call-done, s32[]{:T(128)S(6)} %select_n.172), kind=kOutput, calls=%fused_computation.18 | convolution fusion | flops 2685665280 | bytes 6815748 | tf_op jit(solution)/shard_map/dot_general | solution.py:15
  128.1 1.8 %gather_fusion.5 = f32[64,16,256]{2,1,0:T(8,128)S(1)} fusion(f32[64,16,256]{2,1,0:T(8,128)} %bitcast.77, s32[1024]{0:T(1024)S(1)} %pad_clamp_fusion.1), kind=kCustom, calls=%fused_computation.5 | custom fusion | bytes 2097408 | tf_op jit(solution)/shard_map/gather | solution.py:113
  129.9 13.7 %collective-permute-done.6 = f32[1024,256]{1,0:T(8,128)} collective-permute-done((f32[1024,256]{1,0:T(8,128)}, f32[1024,256]{1,0:T(8,128)}, u32[]{:S(2)}, u32[]{:S(2)}) %collective-permute-start.6) | collective-permute-done | bytes 1048608 | tf_op jit(solution)/shard_map/ppermute | solution.py:11
  143.6 2.3 %bitcast_add_fusion = f32[1024,256]{1,0:T(8,128)} fusion(f32[1024,256]{1,0:T(8,128)} %collective-permute-done.6, f32[64,16,256]{2,1,0:T(8,128)S(1)} %gather_fusion.5), kind=kLoop, calls=%fused_computation.23 | loop fusion | flops 262144 | bytes 3145728 | tf_op jit(solution)/shard_map/add | solution.py:120
  (37 shorter events, 11.8 us)
Async XLA Ops:
  6.5 68.8 %copy-start = (f32[1,2048,256]{2,1,0:T(8,128)S(1)}, f32[1,2048,256]{2,1,0:T(8,128)}, u32[]{:S(2)}) copy-start(f32[1,2048,256]{2,1,0:T(8,128)} %param.6) | copy-start | bytes 6291460
  6.5 81.2 %all-gather.5.cloned.1.call-start = ((), (), s32[]{:S(2)}) async-start(), calls=%async_computation | async-start | bytes 4325376 | tf_op jit(solution)/shard_map/all_gather | solution.py:57
  47.7 12.4 %collective-permute-start = (bf16[256,1024]{1,0:T(8,128)(2,1)S(1)}, bf16[256,1024]{1,0:T(8,128)(2,1)S(1)}, u32[]{:S(2)}, u32[]{:S(2)}) collective-permute-start(bf16[256,1024]{1,0:T(8,128)(2,1)S(1)} %bitcast.75), channel_id=1, source_target_pairs={{0,32},{32,64},{64,96},{96,0},{1,33},{33,65},{65,97},{97,1},{2,34}... | collective-permute-start | bytes 1572872 | tf_op jit(solution)/shard_map/ppermute | solution.py:28
  51.1 25.9 %collective-permute-start.2 = (bf16[256,1024]{1,0:T(8,128)(2,1)S(1)}, bf16[256,1024]{1,0:T(8,128)(2,1)}, u32[]{:S(2)}, u32[]{:S(2)}) collective-permute-start(bf16[256,1024]{1,0:T(8,128)(2,1)S(1)} %bitcast.76), channel_id=1, source_target_pairs={{0,96},{32,0},{64,32},{96,64},{1,97},{33,1},{65,33},{97,65},{2,98}... | collective-permute-start | bytes 1572872 | tf_op jit(solution)/shard_map/ppermute | solution.py:31
  60.1 16.9 %collective-permute-start.1 = (bf16[256,1024]{1,0:T(8,128)(2,1)S(1)}, bf16[256,1024]{1,0:T(8,128)(2,1)}, u32[]{:S(2)}, u32[]{:S(2)}) collective-permute-start(bf16[256,1024]{1,0:T(8,128)(2,1)S(1)} %collective-permute-done), channel_id=1, source_target_pairs={{0,32},{32,64},{64,96},{96,0},{1,33},{33,65},{65,97},{97,1},{2,34}... | collective-permute-start | bytes 1572872 | tf_op jit(solution)/shard_map/ppermute | solution.py:28
  90.0 9.6 %collective-permute-start.3 = (bf16[64,1024]{1,0:T(8,128)(2,1)S(1)}, bf16[64,1024]{1,0:T(8,128)(2,1)S(1)}, u32[]{:S(2)}, u32[]{:S(2)}) collective-permute-start(bf16[64,1024]{1,0:T(8,128)(2,1)S(1)} %convolution_convert_fusion), channel_id=1, source_target_pairs={{0,32},{32,64},{64,96},{96,0},{1,33},{33,65},{65,97},{97,1},{2,34}... | collective-permute-start | bytes 393224 | tf_op jit(solution)/shard_map/ppermute | solution.py:28
  96.0 7.5 %collective-permute-start.5 = (bf16[64,1024]{1,0:T(8,128)(2,1)S(1)}, bf16[64,1024]{1,0:T(8,128)(2,1)S(1)}, u32[]{:S(2)}, u32[]{:S(2)}) collective-permute-start(bf16[64,1024]{1,0:T(8,128)(2,1)S(1)} %convolution_convert_fusion), channel_id=1, source_target_pairs={{0,96},{32,0},{64,32},{96,64},{1,97},{33,1},{65,33},{97,65},{2,98}... | collective-permute-start | bytes 393224 | tf_op jit(solution)/shard_map/ppermute | solution.py:31
  99.7 8.2 %collective-permute-start.4 = (bf16[64,1024]{1,0:T(8,128)(2,1)S(1)}, bf16[64,1024]{1,0:T(8,128)(2,1)S(1)}, u32[]{:S(2)}, u32[]{:S(2)}) collective-permute-start(bf16[64,1024]{1,0:T(8,128)(2,1)S(1)} %collective-permute-done.3), channel_id=1, source_target_pairs={{0,32},{32,64},{64,96},{96,0},{1,33},{33,65},{65,97},{97,1},{2,34}... | collective-permute-start | bytes 393224 | tf_op jit(solution)/shard_map/ppermute | solution.py:28
  117.5 26.1 %collective-permute-start.6 = (f32[1024,256]{1,0:T(8,128)}, f32[1024,256]{1,0:T(8,128)}, u32[]{:S(2)}, u32[]{:S(2)}) collective-permute-start(f32[1024,256]{1,0:T(8,128)} %bitcast.40), channel_id=1, source_target_pairs={{0,128},{128,0},{256,384},{384,256},{1,129},{129,1},{257,385},{385... | collective-permute-start | bytes 3145736 | tf_op jit(solution)/shard_map/ppermute | solution.py:11
Sparse Core Ops, SparseCore 0:
  9.5 78.1 all-gather.4

commit v3 on v2

--- a/solution.py
+++ b/solution.py
@@ -54,19 +54,24 @@
     order = inverse.shape[-1]
     inverse = inverse.reshape(order, order)
 
-    columns = lax.all_gather(panel[0], ("z", "core"), axis=1, tiled=True)
-
     def solve(rows):
         return jnp.dot(rows, inverse, preferred_element_type=jnp.float32).astype(
             jnp.bfloat16
         )
 
+    local_panel = panel[0]
     local_trailing = trailing[0]
     rows_here = local_trailing.shape[0]
     cols_here = local_trailing.shape[1]
-    share = rows_here // ncol
-    piece = solve(lax.dynamic_slice_in_dim(columns, col_index * share, share, 0))
-    col_side = ring_gather(piece, "row", row_index, nrow)
+    member = lax.axis_index("front") % 2
+    half = rows_here // 2
+    cols = ("z", "core")
+    piece_panel = lax.all_to_all(local_panel, cols, 0, 1, tiled=True)
+    col_side = solve(ring_gather(piece_panel, "row", row_index, nrow).reshape(-1, order))
+    away = lax.dynamic_slice_in_dim(local_panel, (1 - member) * half, half, 0)
+    away = lax.all_gather(away, cols, axis=1, tiled=True)
+    home = lax.dynamic_slice_in_dim(local_panel, member * half, half, 0)
+    home = lax.all_gather(home, cols, axis=1, tiled=True)
 
     block_map = extend_map[0]
     nblocks = block_map.shape[0]
@@ -92,13 +97,11 @@
     picked = gather_col[lane // width] * width + lane % width
     select_cols = (lane[:, None] == picked[None, :]).astype(jnp.float32)
 
-    member = lax.axis_index("front") % 2
-    half = rows_here // 2
     half_blocks = half // width
 
-    def half_update(which):
+    def half_update(which, columns):
         rows = lax.dynamic_slice_in_dim(local_trailing, which * half, half, 0)
-        low = solve(lax.dynamic_slice_in_dim(columns, which * half, half, 0))
+        low = solve(columns)
         moved_cols = jnp.dot(
             rows,
             select_cols,
@@ -114,10 +117,10 @@
             half, cols_here
         )
 
-    outgoing = half_update(1 - member)
+    outgoing = half_update(1 - member, away).astype(jnp.bfloat16)
     incoming = from_partner(outgoing, "front", 0)
-    keep = half_update(member)
-    return (keep + incoming)[None]
+    keep = half_update(member, home)
+    return (keep + incoming.astype(jnp.float32))[None]
 
 
 def solution(mesh):

time: 154 us -> 179 us (1.16)
  local copies, waits for them, and re-layouts: 12.8 us -> 19.1 us
  waiting for transfers between devices: 26.6 us -> 32.9 us
  starting transfers between devices: 22.8 us -> 27.6 us
  blocking collectives: 40.4 us -> 43.2 us
  matrix products: 17.1 us -> 19.1 us
    ppermute x1, waiting for transfers between devices: 13.7 us -> 0.01 us  [from_partner(): return lax.ppermute(value, axis, pairs)]
    all_gather x1 -> x2, waiting for transfers between devices: 4.3 us -> 15.2 us  [the longest x1 15.2 us: local(): home = lax.all_gather(home, cols, axis=1, tiled=True)]
    ppermute x4, waiting for transfers between devices: 6.34 us -> 14.5 us  [ring_gather(): forward = lax.ppermute(forward, axis, ahead)]
    all_to_all x0 -> x1, starting transfers between devices: none -> 6.84 us  [local(): piece_panel = lax.all_to_all(local_panel, cols, 0, 1, tiled=True)]
    all_gather x1, blocking collectives: 38.4 us -> 41.2 us  [local(): inverse = lax.all_gather(inverse, 'z', axis=0, tiled=True)]
    gather x2 -> x3, local copies, waits for them, and re-layouts: 4.2 us -> 6.75 us  [ring_gather(): return stacked[(index - sources) % n]]
    ppermute x4, starting transfers between devices: 12.2 us -> 9.87 us  [ring_gather(): forward = lax.ppermute(forward, axis, ahead)]
  transfers between devices with their start and end apart: 8 -> 10, of which waited for: 5 -> 4; matrix products, arithmetic and copies ran while one was open for 23% -> 31% of each run, Pallas kernels for 0% -> 0%
where the time goes in v3:
time: 179 us; the launch traced here: 176 us
  blocking collectives  43.2 us (24%)
  waiting for transfers between devices  32.9 us (18%)
  starting transfers between devices  27.6 us (15%)
  other arithmetic  20.7 us (12%)
  local copies, waits for them, and re-layouts  19.1 us (11%)
  matrix products  19.1 us (11%)
  between operations  13.7 us (8%)
    all_gather x1, blocking collectives, local(): inverse = lax.all_gather(inverse, 'z', axis=0, tiled=True)  41.2 us
    all_gather x1, waiting for transfers between devices, local(): home = lax.all_gather(home, cols, axis=1, tiled=True)  15.2 us
    ppermute x4, waiting for transfers between devices, ring_gather(): forward = lax.ppermute(forward, axis, ahead)  14.5 us
    dot_general x2, matrix products, outer_rows(): lax.dot_general(left, right, (((1,), (1,)), ((), ())), preferred_element_...  13.5 us
    ppermute x4, starting transfers between devices, ring_gather(): forward = lax.ppermute(forward, axis, ahead)  9.87 us
    ppermute x2, starting transfers between devices, ring_gather(): backward = lax.ppermute(backward, axis, behind)  8.14 us
    all_to_all x1, starting transfers between devices, local(): piece_panel = lax.all_to_all(local_panel, cols, 0, 1, tiled=True)  6.84 us
    gather x3, local copies, waits for them, and re-layouts, ring_gather(): return stacked[(index - sources) % n]  6.75 us
  transfers between devices with their start and end apart: 10, of which 4 were waited for; matrix products, arithmetic and copies ran while one was open for 31% of the time, Pallas kernels for 0%

profile of v3, /device:TPU:24, one launch (start us, length us, event | category | flops | bytes accessed | tf_op | source)
XLA Modules:
  0.0 176.4 jit_solution(10807764174956880249)
XLA Ops:
  8.2 2.0 %all-gather.1 = bf16[1,16,1024]{2,1,0:T(8,128)(2,1)S(1)} all-gather(bf16[1,8,1024]{2,1,0:T(8,128)(2,1)} %param.4), channel_id=3, replica_groups=mesh['front'=4,'row'=4,'z'=16,'core'=2] {'core'}, dimensions={1}, use_global_device_ids=true | all-gather | bytes 49152 | tf_op jit(solution)/shard_map/all_gather | solution.py:51
  10.3 41.2 %all-gather.2 = bf16[1,256,1024]{2,1,0:T(8,128)(2,1)} all-gather(bf16[1,16,1024]{2,1,0:T(8,128)(2,1)S(1)} %all-gather.1), channel_id=4, replica_groups=mesh['front'=4,'row'=4,'z'=16,'core'=2] {'z'}, dimensions={1}, use_global_device_ids=true | all-gather | bytes 557056 | tf_op jit(solution)/shard_map/all_gather | solution.py:52
  51.5 4.5 %collective-permute-start.2 = (bf16[256,1024]{1,0:T(8,128)(2,1)}, bf16[256,1024]{1,0:T(8,128)(2,1)}, u32[]{:S(2)}, u32[]{:S(2)}) collective-permute-start(bf16[256,1024]{1,0:T(8,128)(2,1)} %bitcast.21), channel_id=1, source_target_pairs={{0,96},{32,0},{64,32},{96,64},{1,97},{33,1},{65,33},{97,65},{2,98}... | collective-permute-start | bytes 1572872 | tf_op jit(solution)/shard_map/ppermute | solution.py:31
  56.0 1.9 %collective-permute-start = (bf16[256,1024]{1,0:T(8,128)(2,1)}, bf16[256,1024]{1,0:T(8,128)(2,1)}, u32[]{:S(2)}, u32[]{:S(2)}) collective-permute-start(bf16[256,1024]{1,0:T(8,128)(2,1)} %bitcast.21), channel_id=1, source_target_pairs={{0,32},{32,64},{64,96},{96,0},{1,33},{33,65},{65,97},{97,1},{2,34}... | collective-permute-start | bytes 1572872 | tf_op jit(solution)/shard_map/ppermute | solution.py:28
  60.1 6.8 %all-to-all-start = ((bf16[32,2,1024]{2,1,0:T(2,128)(2,1)}), bf16[32,2,1024]{2,1,0:T(2,128)(2,1)S(1)}, u32[]{:S(2)}, u32[]{:S(2)}) async-start(bf16[32,2,1024]{2,1,0:T(2,128)(2,1)} %reshape.425), calls=%async_computation | async-start | bytes 262144 | tf_op jit(solution)/shard_map/all_to_all | solution.py:69
  71.8 4.4 %compare_select_fusion.1 = s32[256,1]{0,1:T(1,128)S(1)} fusion(s32[]{:T(128)} %bitcast.12, s32[]{:T(128)} %bitcast.13, s32[]{:T(128)} %bitcast.14, s32[]{:T(128)} %bitcast.15, s32[]{:T(128)} %bitcast.16, s32[]{:T(128)} %bitcast.18, s32[]{:T(128)} %bitcast.17), kind=kLoop, calls=%fused_computation.46 | loop fusion | flops 5888 | bytes 1052 | tf_op jit(solution)/shard_map/gather | solution.py:97
  76.3 5.7 %fusion.30 = s32[256]{0:T(256)S(1)} fusion(pred[256]{0:T(512)(128)(4,1)S(1)} %get-tuple-element.29, pred[256]{0:T(512)(128)(4,1)S(1)} %get-tuple-element.30, pred[256]{0:T(512)(128)(4,1)S(1)} %get-tuple-element.31, pred[256]{0:T(512)(128)(4,1)S(1)} %get-tuple-element.32, pred[256]{0:T(512)(128)(4,1)S(1)} %get-tuple-element.33, ...), kind=kLoop, calls=%fused_computation.80 | loop fusion | flops 4352 | bytes 4388 | tf_op jit(solution)/shard_map/add | solution.py:97
  82.0 2.5 %sort.35 = (s32[128]{0:T(128)}, s32[128]{0:T(128)S(1)}) sort(s32[128]{0:T(128)S(1)} %fusion.41, s32[128]{0:T(128)S(1)} %iota.47), dimensions={0}, to_apply=%region_1.2 | sort | flops 896 | bytes 2048 | tf_op jit(solution)/shard_map/jit(argsort)/sort | solution.py:85
  88.0 2.6 %collective-permute-start.3 = (bf16[64,1024]{0,1:T(8,128)(2,1)S(1)}, bf16[64,1024]{0,1:T(8,128)(2,1)S(1)}, u32[]{:S(2)}, u32[]{:S(2)}) collective-permute-start(bf16[64,1024]{0,1:T(8,128)(2,1)S(1)} %bitcast.85), channel_id=1, source_target_pairs={{0,32},{32,64},{64,96},{96,0},{1,33},{33,65},{65,97},{97,1},{2,34}... | collective-permute-start | bytes 393224 | tf_op jit(solution)/shard_map/ppermute | solution.py:28
  90.7 3.4 %collective-permute-start.1 = (bf16[256,1024]{1,0:T(8,128)(2,1)}, bf16[256,1024]{1,0:T(8,128)(2,1)}, u32[]{:S(2)}, u32[]{:S(2)}) collective-permute-start(bf16[256,1024]{1,0:T(8,128)(2,1)} %collective-permute-done), channel_id=1, source_target_pairs={{0,32},{32,64},{64,96},{96,0},{1,33},{33,65},{65,97},{97,1},{2,34}... | collective-permute-start | bytes 1572872 | tf_op jit(solution)/shard_map/ppermute | solution.py:28
  94.2 3.6 %collective-permute-start.5 = (bf16[64,1024]{0,1:T(8,128)(2,1)S(1)}, bf16[64,1024]{0,1:T(8,128)(2,1)S(1)}, u32[]{:S(2)}, u32[]{:S(2)}) collective-permute-start(bf16[64,1024]{0,1:T(8,128)(2,1)S(1)} %bitcast.86), channel_id=1, source_target_pairs={{0,96},{32,0},{64,32},{96,64},{1,97},{33,1},{65,33},{97,65},{2,98}... | collective-permute-start | bytes 393224 | tf_op jit(solution)/shard_map/ppermute | solution.py:31
  97.8 2.4 %collective-permute-done.3 = bf16[64,1024]{0,1:T(8,128)(2,1)S(1)} collective-permute-done((bf16[64,1024]{0,1:T(8,128)(2,1)S(1)}, bf16[64,1024]{0,1:T(8,128)(2,1)S(1)}, u32[]{:S(2)}, u32[]{:S(2)}) %collective-permute-start.3) | collective-permute-done | bytes 131104 | tf_op jit(solution)/shard_map/ppermute | solution.py:28
  102.2 2.5 %collective-permute-done.5 = bf16[64,1024]{0,1:T(8,128)(2,1)S(1)} collective-permute-done((bf16[64,1024]{0,1:T(8,128)(2,1)S(1)}, bf16[64,1024]{0,1:T(8,128)(2,1)S(1)}, u32[]{:S(2)}, u32[]{:S(2)}) %collective-permute-start.5) | collective-permute-done | bytes 131104 | tf_op jit(solution)/shard_map/ppermute | solution.py:31
  104.7 12.1 %collective-permute-done.4 = bf16[64,1024]{0,1:T(8,128)(2,1)S(1)} collective-permute-done((bf16[64,1024]{0,1:T(8,128)(2,1)S(1)}, bf16[64,1024]{0,1:T(8,128)(2,1)S(1)}, u32[]{:S(2)}, u32[]{:S(2)}) %collective-permute-start.4) | collective-permute-done | bytes 131104 | tf_op jit(solution)/shard_map/ppermute | solution.py:28
  118.0 2.0 %gather_fusion.2 = bf16[4,64,1024]{1,2,0:T(8,128)(2,1)S(1)} fusion(bf16[4,64,1024]{1,2,0:T(8,128)(2,1)} %pad_maximum_fusion.1, s32[1024]{0:T(1024)S(1)} %pad_clamp_fusion.4), kind=kCustom, calls=%fused_computation.2 | custom fusion | bytes 1048592 | tf_op jit(solution)/shard_map/gather | solution.py:39
  121.1 3.1 %pad_maximum_fusion = bf16[4,256,1024]{2,1,0:T(8,128)(2,1)} fusion(bf16[1,256,1024]{2,1,0:T(8,128)(2,1)} %bitcast.24, bf16[1,256,1024]{2,1,0:T(8,128)(2,1)} %bitcast.23, bf16[1,256,1024]{2,1,0:T(8,128)(2,1)} %bitcast.22, bf16[1,256,1024]{2,1,0:T(8,128)(2,1)} %all-gather.2), kind=kLoop, calls=%fused_computation.7 | loop fusion | flops 3145728 | bytes 4194304 | tf_op jit(solution)/shard_map/stack | solution.py:37
  124.2 3.7 %gather_fusion.1 = bf16[4,256,1024]{2,1,0:T(8,128)(2,1)} fusion(bf16[4,256,1024]{2,1,0:T(8,128)(2,1)} %pad_maximum_fusion, s32[1024]{0:T(1024)S(1)} %pad_clamp_fusion.4), kind=kCustom, calls=%fused_computation.1 | custom fusion | bytes 4194320 | tf_op jit(solution)/shard_map/gather | solution.py:39
  127.9 2.3 %convolution_convert_fusion = bf16[256,1024]{1,0:T(8,128)(2,1)S(1)} fusion(bf16[256,1024]{1,0:T(8,128)(2,1)S(1)} %bitcast.88, bf16[1024,1024]{1,0:T(8,128)(2,1)} %bitcast.80), kind=kOutput, calls=%fused_computation.18 | convolution fusion | flops 537133056 | bytes 3145728 | tf_op jit(solution)/shard_map/dot_general | solution.py:58
  131.6 6.9 %fusion.11 = bf16[1024,256]{1,0:T(8,128)(2,1)} fusion(f32[1024,256]{1,0:T(8,128)} %fusion.22, bf16[256,1024]{1,0:T(8,128)(2,1)} %bitcast.89, bf16[1024,1024]{1,0:T(8,128)(2,1)} %bitcast.81, bf16[1,1024,1024]{1,2,0:T(8,128)(2,1)} %all-gather.9.cloned.1.call-done), kind=kOutput, calls=%fused_computation.17 | convolution fusion | flops 2685927424 | bytes 6291456 | tf_op jit(solution)/shard_map/dot_general | solution.py:15
  138.5 2.4 %gather_fusion.6 = bf16[64,16,256]{2,1,0:T(8,128)(2,1)} fusion(bf16[64,16,256]{2,1,0:T(8,128)(2,1)} %bitcast.92, s32[1024]{0:T(1024)S(1)} %pad_clamp_fusion), kind=kCustom, calls=%fused_computation.6 | custom fusion | bytes 1048832 | tf_op jit(solution)/shard_map/gather | solution.py:116
  140.9 2.7 %collective-permute-start.6 = (bf16[1024,256]{1,0:T(8,128)(2,1)}, bf16[1024,256]{1,0:T(8,128)(2,1)}, u32[]{:S(2)}, u32[]{:S(2)}) collective-permute-start(bf16[1024,256]{1,0:T(8,128)(2,1)} %bitcast.91), channel_id=1, source_target_pairs={{0,128},{128,0},{256,384},{384,256},{1,129},{129,1},{257,385},{385... | collective-permute-start | bytes 1572872 | tf_op jit(solution)/shard_map/ppermute | solution.py:11
  143.6 15.2 %all-gather.7.cloned.1.call-done = bf16[1,1024,1024]{1,2,0:T(8,128)(2,1)} async-done(((bf16[1,1024,32]{1,2,0:T(8,128)(2,1)}), bf16[1,1024,1024]{1,2,0:T(8,128)(2,1)}) %all-gather.7.cloned.1.call-update) | async-done | bytes 2097168 | tf_op jit(solution)/shard_map/all_gather | solution.py:74
  158.9 6.6 %fusion.8 = f32[1024,256]{1,0:T(8,128)} fusion(f32[1024,256]{1,0:T(8,128)S(1)} %copy-done.2, bf16[256,1024]{1,0:T(8,128)(2,1)} %bitcast.90, bf16[1024,1024]{1,0:T(8,128)(2,1)} %bitcast.82, bf16[1,1024,1024]{1,2,0:T(8,128)(2,1)} %all-gather.7.cloned.1.call-done), kind=kOutput, calls=%fused_computation.16 | convolution fusion | flops 2685665280 | bytes 6815744 | tf_op jit(solution)/shard_map/dot_general | solution.py:15
  167.3 2.2 %bitcast_add_fusion = f32[1024,256]{1,0:T(8,128)} fusion(f32[64,16,256]{2,1,0:T(8,128)S(1)} %gather_fusion.5, bf16[1024,256]{1,0:T(8,128)(2,1)} %collective-permute-done.6), kind=kLoop, calls=%fused_computation.22 | loop fusion | flops 524288 | bytes 2621440 | tf_op jit(solution)/shard_map/add | solution.py:123
  (54 shorter events, 19.8 us)
Async XLA Ops:
  6.5 78.0 %copy-start = (f32[1,2048,256]{2,1,0:T(8,128)S(1)}, f32[1,2048,256]{2,1,0:T(8,128)}, u32[]{:S(2)}) copy-start(f32[1,2048,256]{2,1,0:T(8,128)} %param.6) | copy-start | bytes 6291460
  6.5 61.2 %copy-start.1 = (s32[1,512]{1,0:T(1,128)S(1)}, s32[1,512]{1,0:T(1,128)}, u32[]{:S(2)}) copy-start(s32[1,512]{1,0:T(1,128)} %param.7) | copy-start | bytes 6148
  6.5 125.1 %all-gather.9.cloned.1.call-start = ((), (), s32[]{:S(2)}) async-start(), calls=%async_computation.2 | async-start | bytes 2162688 | tf_op jit(solution)/shard_map/all_gather | solution.py:72
  51.5 69.6 %collective-permute-start.2 = (bf16[256,1024]{1,0:T(8,128)(2,1)}, bf16[256,1024]{1,0:T(8,128)(2,1)}, u32[]{:S(2)}, u32[]{:S(2)}) collective-permute-start(bf16[256,1024]{1,0:T(8,128)(2,1)} %bitcast.21), channel_id=1, source_target_pairs={{0,96},{32,0},{64,32},{96,64},{1,97},{33,1},{65,33},{97,65},{2,98}... | collective-permute-start | bytes 1572872 | tf_op jit(solution)/shard_map/ppermute | solution.py:31
  56.0 34.7 %collective-permute-start = (bf16[256,1024]{1,0:T(8,128)(2,1)}, bf16[256,1024]{1,0:T(8,128)(2,1)}, u32[]{:S(2)}, u32[]{:S(2)}) collective-permute-start(bf16[256,1024]{1,0:T(8,128)(2,1)} %bitcast.21), channel_id=1, source_target_pairs={{0,32},{32,64},{64,96},{96,0},{1,33},{33,65},{65,97},{97,1},{2,34}... | collective-permute-start | bytes 1572872 | tf_op jit(solution)/shard_map/ppermute | solution.py:28
  60.1 27.7 %all-to-all-start = ((bf16[32,2,1024]{2,1,0:T(2,128)(2,1)}), bf16[32,2,1024]{2,1,0:T(2,128)(2,1)S(1)}, u32[]{:S(2)}, u32[]{:S(2)}) async-start(bf16[32,2,1024]{2,1,0:T(2,128)(2,1)} %reshape.425), calls=%async_computation | async-start | bytes 262144 | tf_op jit(solution)/shard_map/all_to_all | solution.py:69
  66.9 92.0 %all-gather.7.cloned.1.call-start = ((), (), s32[]{:S(2)}) async-start(), calls=%async_computation.1 | async-start | bytes 2162688 | tf_op jit(solution)/shard_map/all_gather | solution.py:74
  88.0 12.2 %collective-permute-start.3 = (bf16[64,1024]{0,1:T(8,128)(2,1)S(1)}, bf16[64,1024]{0,1:T(8,128)(2,1)S(1)}, u32[]{:S(2)}, u32[]{:S(2)}) collective-permute-start(bf16[64,1024]{0,1:T(8,128)(2,1)S(1)} %bitcast.85), channel_id=1, source_target_pairs={{0,32},{32,64},{64,96},{96,0},{1,33},{33,65},{65,97},{97,1},{2,34}... | collective-permute-start | bytes 393224 | tf_op jit(solution)/shard_map/ppermute | solution.py:28
  90.7 30.4 %collective-permute-start.1 = (bf16[256,1024]{1,0:T(8,128)(2,1)}, bf16[256,1024]{1,0:T(8,128)(2,1)}, u32[]{:S(2)}, u32[]{:S(2)}) collective-permute-start(bf16[256,1024]{1,0:T(8,128)(2,1)} %collective-permute-done), channel_id=1, source_target_pairs={{0,32},{32,64},{64,96},{96,0},{1,33},{33,65},{65,97},{97,1},{2,34}... | collective-permute-start | bytes 1572872 | tf_op jit(solution)/shard_map/ppermute | solution.py:28
  94.2 10.5 %collective-permute-start.5 = (bf16[64,1024]{0,1:T(8,128)(2,1)S(1)}, bf16[64,1024]{0,1:T(8,128)(2,1)S(1)}, u32[]{:S(2)}, u32[]{:S(2)}) collective-permute-start(bf16[64,1024]{0,1:T(8,128)(2,1)S(1)} %bitcast.86), channel_id=1, source_target_pairs={{0,96},{32,0},{64,32},{96,64},{1,97},{33,1},{65,33},{97,65},{2,98}... | collective-permute-start | bytes 393224 | tf_op jit(solution)/shard_map/ppermute | solution.py:31
  100.2 16.5 %collective-permute-start.4 = (bf16[64,1024]{0,1:T(8,128)(2,1)S(1)}, bf16[64,1024]{0,1:T(8,128)(2,1)S(1)}, u32[]{:S(2)}, u32[]{:S(2)}) collective-permute-start(bf16[64,1024]{0,1:T(8,128)(2,1)S(1)} %collective-permute-done.3), channel_id=1, source_target_pairs={{0,32},{32,64},{64,96},{96,0},{1,33},{33,65},{65,97},{97,1},{2,34}... | collective-permute-start | bytes 393224 | tf_op jit(solution)/shard_map/ppermute | solution.py:28
  124.2 3.7 %copy-start.3 = (bf16[4,64,1024]{2,1,0:T(8,128)(2,1)S(1)}, bf16[4,64,1024]{2,1,0:T(8,128)(2,1)}, u32[]{:S(2)}) copy-start(bf16[4,64,1024]{2,1,0:T(8,128)(2,1)} %copy.7) | copy-start | bytes 1572868
  131.6 27.3 %copy-start.2 = (f32[1024,256]{1,0:T(8,128)S(1)}, f32[1024,256]{1,0:T(8,128)}, u32[]{:S(2)}) copy-start(f32[1024,256]{1,0:T(8,128)} %fusion.24) | copy-start | bytes 3145732
  140.9 26.4 %collective-permute-start.6 = (bf16[1024,256]{1,0:T(8,128)(2,1)}, bf16[1024,256]{1,0:T(8,128)(2,1)}, u32[]{:S(2)}, u32[]{:S(2)}) collective-permute-start(bf16[1024,256]{1,0:T(8,128)(2,1)} %bitcast.91), channel_id=1, source_target_pairs={{0,128},{128,0},{256,384},{384,256},{1,129},{129,1},{257,385},{385... | collective-permute-start | bytes 1572872 | tf_op jit(solution)/shard_map/ppermute | solution.py:11
Sparse Core Ops, SparseCore 0:
  9.5 77.6 all-gather.8
  89.3 69.5 all-gather.6

commit v4 on v1

--- a/solution.py
+++ b/solution.py
@@ -26,29 +26,37 @@
     row_index = lax.axis_index("row")
     col_index = lax.axis_index("z") * ncore + lax.axis_index("core")
 
-    inverse = lax.all_gather(inverse_factor[0], "core", axis=0, tiled=True)
-    inverse = lax.all_gather(inverse, "z", axis=0, tiled=True)
-    inverse = lax.all_gather(inverse, "row", axis=0, tiled=True)
-    order = inverse.shape[0]
-    chunk = order // ncol
+    local_panel = panel[0]
+    local_trailing = trailing[0]
+    rows_here = local_trailing.shape[0]
+    cols_here = local_trailing.shape[1]
+    chunk = local_panel.shape[1]
+    cols = ("z", "core")
+
+    inverse = lax.all_gather(inverse_factor[0], "row", axis=0, tiled=True)
+    order = inverse.shape[1]
+    held = inverse.shape[0]
+    payload = jnp.concatenate([local_panel, inverse.reshape(-1, chunk)], axis=0)
+    gathered = lax.all_gather(payload, cols, axis=1, tiled=True)
+    columns = gathered[:rows_here]
     inverse = (
-        inverse.reshape(nz, ncore, chunk, order)
-        .transpose(1, 0, 2, 3)
+        gathered[rows_here:]
+        .reshape(nrow, held // nrow, order // chunk, ncol, chunk)
+        .transpose(0, 3, 1, 2, 4)
         .reshape(order, order)
     )
 
-    columns = lax.all_gather(panel[0], "z", axis=1, tiled=True)
-    columns = lax.all_gather(columns, "core", axis=1, tiled=True)
-    solved = jnp.dot(columns, inverse, preferred_element_type=jnp.float32).astype(
-        jnp.bfloat16
-    )
+    def solve(rows):
+        return jnp.dot(rows, inverse, preferred_element_type=jnp.float32).astype(
+            jnp.bfloat16
+        )
 
-    local_trailing = trailing[0]
-    rows_here = local_trailing.shape[0]
-    cols_here = local_trailing.shape[1]
-    share = rows_here // ncol
-    piece = lax.dynamic_slice_in_dim(solved, col_index * share, share, 0)
-    col_side = lax.all_gather(piece, "row", axis=0, tiled=True)
+    member = lax.axis_index("front") % 2
+    half = rows_here // 2
+    piece_panel = lax.all_to_all(local_panel, cols, 0, 1, tiled=True)
+    col_side = solve(lax.all_gather(piece_panel, "row", axis=0, tiled=True))
+    away = lax.dynamic_slice_in_dim(columns, (1 - member) * half, half, 0)
+    home = lax.dynamic_slice_in_dim(columns, member * half, half, 0)
 
     block_map = extend_map[0]
     nblocks = block_map.shape[0]
@@ -74,13 +82,11 @@
     picked = gather_col[lane // width] * width + lane % width
     select_cols = (lane[:, None] == picked[None, :]).astype(jnp.float32)
 
-    member = lax.axis_index("front") % 2
-    half = rows_here // 2
     half_blocks = half // width
 
-    def half_update(which):
+    def half_update(which, columns):
         rows = lax.dynamic_slice_in_dim(local_trailing, which * half, half, 0)
-        low = lax.dynamic_slice_in_dim(solved, which * half, half, 0)
+        low = solve(columns)
         moved_cols = jnp.dot(
             rows,
             select_cols,
@@ -96,10 +102,10 @@
             half, cols_here
         )
 
-    outgoing = half_update(1 - member)
+    outgoing = half_update(1 - member, away).astype(jnp.bfloat16)
     incoming = from_partner(outgoing, "front", 0)
-    keep = half_update(member)
-    return (keep + incoming)[None]
+    keep = half_update(member, home)
+    return (keep + incoming.astype(jnp.float32))[None]
 
 
 def solution(mesh):

time: 214 us -> 192 us (0.90)
  waiting for transfers between devices: 97.2 us -> 37.6 us
  local copies, waits for them, and re-layouts: 11.2 us -> 57.1 us
  blocking collectives: 57.5 us -> 26.3 us
  starting transfers between devices: 2.81 us -> 18.1 us
  matrix products: 15.4 us -> 18.8 us
    all_gather x3 -> x1, waiting for transfers between devices: 79.7 us -> 32.4 us  [local(): gathered = lax.all_gather(payload, cols, axis=1, tiled=True)]
    reshape x0 -> x5, local copies, waits for them, and re-layouts: none -> 37.4 us  [the longest x3 37.1 us: local(): inverse = gathered[rows_here:].reshape(nrow, held // nrow, order // chunk...]
    all_gather x3 -> x2, blocking collectives: 57.5 us -> 26.3 us  [the longest x1 13.7 us: local(): col_side = solve(lax.all_gather(piece_panel, 'row', axis=0, tiled=True))]
    all_to_all x0 -> x1, starting transfers between devices: none -> 15.5 us  [local(): piece_panel = lax.all_to_all(local_panel, cols, 0, 1, tiled=True)]
    ppermute x1, waiting for transfers between devices: 16.8 us -> 5.16 us  [from_partner(): return lax.ppermute(value, axis, pairs)]
    dot_general x2, matrix products: 4.68 us -> 13.4 us  [outer_rows(): lax.dot_general(left, right, (((1,), (1,)), ((), ())), preferred_element_...]
    slice x0 -> x2, local copies, waits for them, and re-layouts: none -> 7.85 us  [the longest x1 4.7 us: local(): columns = gathered[:rows_here]]
    dot_general x1, matrix products: 7.43 us -> 3.27 us  [solve(): jnp.dot(rows, inverse, preferred_element_type=jnp.float32)]
  transfers between devices with their start and end apart: 4 -> 3, of which waited for: 4 -> 2; matrix products, arithmetic and copies ran while one was open for 12% -> 15% of each run, Pallas kernels for 0% -> 0%
where the time goes in v4:
time: 192 us; the launch traced here: 190 us
  local copies, waits for them, and re-layouts  57.1 us (30%)
  waiting for transfers between devices  37.6 us (20%)
  blocking collectives  26.3 us (14%)
  matrix products  18.8 us (10%)
  starting transfers between devices  18.1 us (9%)
  other arithmetic  18 us (9%)
  between operations  13.6 us (7%)
    reshape x3, local copies, waits for them, and re-layouts, local(): inverse = gathered[rows_here:].reshape(nrow, held // nrow, order // chunk...  37.1 us
    all_gather x1, waiting for transfers between devices, local(): gathered = lax.all_gather(payload, cols, axis=1, tiled=True)  32.4 us
    all_to_all x1, starting transfers between devices, local(): piece_panel = lax.all_to_all(local_panel, cols, 0, 1, tiled=True)  15.5 us
    all_gather x1, blocking collectives, local(): col_side = solve(lax.all_gather(piece_panel, 'row', axis=0, tiled=True))  13.7 us
    dot_general x2, matrix products, outer_rows(): lax.dot_general(left, right, (((1,), (1,)), ((), ())), preferred_element_...  13.4 us
    all_gather x1, blocking collectives, local(): inverse = lax.all_gather(inverse_factor[0], 'row', axis=0, tiled=True)  12.5 us
    add x1, other arithmetic, local(): picked = gather_col[lane // width] * width + lane % width  5.66 us
    ppermute x1, waiting for transfers between devices, from_partner(): return lax.ppermute(value, axis, pairs)  5.16 us
  transfers between devices with their start and end apart: 3, of which 2 were waited for; matrix products, arithmetic and copies ran while one was open for 15% of the time, Pallas kernels for 0%

profile of v4, /device:TPU:24, one launch (start us, length us, event | category | flops | bytes accessed | tf_op | source)
XLA Modules:
  0.0 189.6 jit_solution(10457263910888537700)
XLA Ops:
  6.5 12.5 %all-gather = bf16[1,32,1024]{2,1,0:T(8,128)(2,1)S(1)} all-gather(bf16[1,8,1024]{2,1,0:T(8,128)(2,1)} %param.4), channel_id=2, replica_groups=mesh['front'=4,'row'=4,'z'=16,'core'=2] {'row'}, dimensions={1}, use_global_device_ids=true | all-gather | bytes 81920 | tf_op jit(solution)/shard_map/all_gather | solution.py:36
  19.4 1.6 pad_maximum_fusion
  23.1 15.5 %all-to-all-start = ((bf16[32,2,1024]{2,1,0:T(2,128)(2,1)}), bf16[32,2,1024]{2,1,0:T(2,128)(2,1)S(1)}, u32[]{:S(2)}, u32[]{:S(2)}) async-start(bf16[32,2,1024]{2,1,0:T(2,128)(2,1)} %reshape.358), calls=%async_computation | async-start | bytes 262144 | tf_op jit(solution)/shard_map/all_to_all | solution.py:56
  38.7 1.3 gather_fusion.2
  40.7 2.5 %sort.35 = (s32[128]{0:T(128)}, s32[128]{0:T(128)S(1)}) sort(s32[128]{0:T(128)S(1)} %fusion.45, s32[128]{0:T(128)S(1)} %iota.41), dimensions={0}, to_apply=%region_1.2 | sort | flops 896 | bytes 2048 | tf_op jit(solution)/shard_map/jit(argsort)/sort | solution.py:70
  45.4 4.5 %compare_select_fusion.1 = s32[256,1]{0,1:T(1,128)S(1)} fusion(s32[]{:T(128)} %bitcast.12, s32[]{:T(128)} %bitcast.13, s32[]{:T(128)} %bitcast.14, s32[]{:T(128)} %bitcast.15, s32[]{:T(128)} %bitcast.16, s32[]{:T(128)} %bitcast.18, s32[]{:T(128)} %bitcast.17), kind=kLoop, calls=%fused_computation.42 | loop fusion | flops 5888 | bytes 1052 | tf_op jit(solution)/shard_map/gather | solution.py:82
  50.0 5.7 %fusion.30 = s32[256]{0:T(256)S(1)} fusion(pred[256]{0:T(512)(128)(4,1)S(1)} %get-tuple-element.27, pred[256]{0:T(512)(128)(4,1)S(1)} %get-tuple-element.28, pred[256]{0:T(512)(128)(4,1)S(1)} %get-tuple-element.29, pred[256]{0:T(512)(128)(4,1)S(1)} %get-tuple-element.30, pred[256]{0:T(512)(128)(4,1)S(1)} %get-tuple-element.31, ...), kind=kLoop, calls=%fused_computation.72 | loop fusion | flops 4352 | bytes 4388 | tf_op jit(solution)/shard_map/add | solution.py:82
  55.7 1.6 fusion.22
  58.3 13.7 %all_gather.11 = bf16[256,1024]{1,0:T(8,128)(2,1)} all-gather(bf16[64,1024]{1,0:T(8,128)(2,1)S(1)} %copy.11), channel_id=1, replica_groups=mesh['front'=4,'row'=4,'z'=16,'core'=2] {'row'}, dimensions={0}, use_global_device_ids=true | all-gather | bytes 655360 | tf_op jit(solution)/shard_map/all_gather | solution.py:57
  72.0 32.4 %all-gather.3.cloned.1.call-done = bf16[3072,1024]{0,1:T(8,128)(2,1)} async-done(((bf16[3072,32]{0,1:T(8,128)(2,1)}), bf16[3072,1024]{0,1:T(8,128)(2,1)}) %all-gather.3.cloned.1.call-update) | async-done | bytes 6291472 | tf_op jit(solution)/shard_map/all_gather | solution.py:40
  104.4 3.2 %slice.36 = bf16[1024,1024]{0,1:T(8,128)(2,1)} slice(bf16[3072,1024]{0,1:T(8,128)(2,1)} %all-gather.3.cloned.1.call-done), slice={[2048:3072], [0:1024]} | slice | bytes 4194304 | tf_op jit(solution)/shard_map/slice | solution.py:43
  107.6 10.9 %reshape.229 = bf16[4,8,32,32,32]{2,1,0,4,3:T(8,128)(2,1)} reshape(bf16[1024,1024]{0,1:T(8,128)(2,1)} %slice.36) | data formatting | bytes 4194304 | tf_op jit(solution)/shard_map/reshape | solution.py:44
  118.4 13.8 %copy.9 = bf16[4,8,32,32,32]{4,2,1,3,0:T(8,128)(2,1)} copy(bf16[4,8,32,32,32]{2,1,0,4,3:T(8,128)(2,1)} %reshape.229) | data formatting | bytes 4194304 | tf_op jit(solution)/shard_map/reshape | solution.py:44
  132.2 12.4 %reshape.230 = bf16[1024,1024]{1,0:T(8,128)(2,1)} reshape(bf16[4,32,8,32,32]{4,3,2,1,0:T(8,128)(2,1)} %bitcast.61) | data formatting | bytes 4194304 | tf_op jit(solution)/shard_map/reshape | solution.py:46
  144.7 3.3 %convolution_convert_fusion = bf16[1024,256]{0,1:T(8,128)(2,1)} fusion(bf16[256,1024]{1,0:T(8,128)(2,1)} %all_gather.11, bf16[1024,1024]{1,0:T(8,128)(2,1)} %reshape.230), kind=kOutput, calls=%fused_computation.15 | convolution fusion | flops 537133056 | bytes 3145728 | tf_op jit(solution)/shard_map/dot_general | solution.py:50
  147.9 2.4 %gather_fusion.1 = bf16[16,16,1024]{2,1,0:T(8,128)(2,1)} fusion(bf16[16,16,1024]{2,1,0:T(8,128)(2,1)} %bitcast.70, s32[1024]{0:T(1024)S(1)} %pad_clamp_fusion.3), kind=kCustom, calls=%fused_computation.1 | custom fusion | bytes 1048640 | tf_op jit(solution)/shard_map/gather | solution.py:78
  150.3 4.7 %slice.35 = bf16[2048,1024]{0,1:T(8,128)(2,1)} slice(bf16[3072,1024]{0,1:T(8,128)(2,1)} %all-gather.3.cloned.1.call-done), slice={[0:2048], [0:1024]} | slice | bytes 8388608 | tf_op jit(solution)/shard_map/slice | solution.py:41
  155.0 6.8 %fusion.11 = bf16[1024,256]{1,0:T(8,128)(2,1)} fusion(f32[1024,256]{1,0:T(8,128)} %fusion.22, bf16[256,1024]{1,0:T(8,128)(2,1)} %bitcast.66, bf16[1024,1024]{1,0:T(8,128)(2,1)} %reshape.230, bf16[2048,1024]{0,1:T(8,128)(2,1)} %slice.35, s32[]{:T(128)S(6)} %select_n.160), kind=kOutput, calls=%fused_computation.14 | convolution fusion | flops 2685927424 | bytes 6291460 | tf_op jit(solution)/shard_map/dot_general | solution.py:15
  161.8 2.5 %gather_fusion.4 = bf16[64,16,256]{2,1,0:T(8,128)(2,1)} fusion(bf16[64,16,256]{2,1,0:T(8,128)(2,1)} %bitcast.69, s32[1024]{0:T(1024)S(1)} %pad_clamp_fusion), kind=kCustom, calls=%fused_computation.4 | custom fusion | bytes 1048832 | tf_op jit(solution)/shard_map/gather | solution.py:101
  164.3 2.7 %collective-permute-start = (bf16[1024,256]{1,0:T(8,128)(2,1)}, bf16[1024,256]{1,0:T(8,128)(2,1)}, u32[]{:S(2)}, u32[]{:S(2)}) collective-permute-start(bf16[1024,256]{1,0:T(8,128)(2,1)} %bitcast.68), channel_id=1, source_target_pairs={{0,128},{128,0},{256,384},{384,256},{1,129},{129,1},{257,385},{385... | collective-permute-start | bytes 1572872 | tf_op jit(solution)/shard_map/ppermute | solution.py:11
  166.9 6.6 %fusion.8 = f32[1024,256]{1,0:T(8,128)} fusion(f32[1024,256]{1,0:T(8,128)S(1)} %fusion.24, bf16[256,1024]{1,0:T(8,128)(2,1)} %bitcast.67, bf16[1024,1024]{1,0:T(8,128)(2,1)} %reshape.230, bf16[2048,1024]{0,1:T(8,128)(2,1)} %slice.35, s32[]{:T(128)S(6)} %select_n.143), kind=kOutput, calls=%fused_computation.13 | convolution fusion | flops 2685665280 | bytes 6815748 | tf_op jit(solution)/shard_map/dot_general | solution.py:15
  173.5 1.8 gather_fusion.3
  175.4 5.2 %collective-permute-done = bf16[1024,256]{1,0:T(8,128)(2,1)} collective-permute-done((bf16[1024,256]{1,0:T(8,128)(2,1)}, bf16[1024,256]{1,0:T(8,128)(2,1)}, u32[]{:S(2)}, u32[]{:S(2)}) %collective-permute-start) | collective-permute-done | bytes 524320 | tf_op jit(solution)/shard_map/ppermute | solution.py:11
  180.5 2.2 %bitcast_add_fusion = f32[1024,256]{1,0:T(8,128)} fusion(f32[64,16,256]{2,1,0:T(8,128)S(1)} %gather_fusion.3, bf16[1024,256]{1,0:T(8,128)(2,1)} %collective-permute-done), kind=kLoop, calls=%fused_computation.18 | loop fusion | flops 524288 | bytes 2621440 | tf_op jit(solution)/shard_map/add | solution.py:108
  (36 shorter events, 6.4 us)
Async XLA Ops:
  6.5 49.1 %copy-start = (f32[1,2048,256]{2,1,0:T(8,128)S(1)}, f32[1,2048,256]{2,1,0:T(8,128)}, u32[]{:S(2)}) copy-start(f32[1,2048,256]{2,1,0:T(8,128)} %param.6) | copy-start | bytes 6291460
  6.5 32.1 %copy-start.1 = (s32[1,512]{1,0:T(1,128)S(1)}, s32[1,512]{1,0:T(1,128)}, u32[]{:S(2)}) copy-start(s32[1,512]{1,0:T(1,128)} %param.7) | copy-start | bytes 6148
  6.5 97.9 %all-gather.3.cloned.1.call-start = ((), (), s32[]{:S(2)}) async-start(), calls=%async_computation.1 | async-start | bytes 6488064 | tf_op jit(solution)/shard_map/all_gather | solution.py:40
  23.1 34.8 %all-to-all-start = ((bf16[32,2,1024]{2,1,0:T(2,128)(2,1)}), bf16[32,2,1024]{2,1,0:T(2,128)(2,1)S(1)}, u32[]{:S(2)}, u32[]{:S(2)}) async-start(bf16[32,2,1024]{2,1,0:T(2,128)(2,1)} %reshape.358), calls=%async_computation | async-start | bytes 262144 | tf_op jit(solution)/shard_map/all_to_all | solution.py:56
  164.3 16.3 %collective-permute-start = (bf16[1024,256]{1,0:T(8,128)(2,1)}, bf16[1024,256]{1,0:T(8,128)(2,1)}, u32[]{:S(2)}, u32[]{:S(2)}) collective-permute-start(bf16[1024,256]{1,0:T(8,128)(2,1)} %bitcast.68), channel_id=1, source_target_pairs={{0,128},{128,0},{256,384},{384,256},{1,129},{129,1},{257,385},{385... | collective-permute-start | bytes 1572872 | tf_op jit(solution)/shard_map/ppermute | solution.py:11
Sparse Core Ops, SparseCore 0:
  21.1 83.2 all-gather.2

commit v5 on v2

--- a/solution.py
+++ b/solution.py
@@ -99,6 +99,7 @@
     def half_update(which):
         rows = lax.dynamic_slice_in_dim(local_trailing, which * half, half, 0)
         low = solve(lax.dynamic_slice_in_dim(columns, which * half, half, 0))
+        rows, low = lax.optimization_barrier((rows, low))
         moved_cols = jnp.dot(
             rows,
             select_cols,
@@ -114,10 +115,10 @@
             half, cols_here
         )
 
-    outgoing = half_update(1 - member)
+    outgoing = half_update(1 - member).astype(jnp.bfloat16)
     incoming = from_partner(outgoing, "front", 0)
     keep = half_update(member)
-    return (keep + incoming)[None]
+    return (keep + incoming.astype(jnp.float32))[None]
 
 
 def solution(mesh):

time: 154 us -> 140 us (0.909)
  waiting for transfers between devices: 26.6 us -> 19.5 us
  local copies, waits for them, and re-layouts: 12.8 us -> 9.99 us
  other arithmetic: 19.4 us -> 16.8 us
  starting transfers between devices: 22.8 us -> 20.3 us
    dot_general x1 -> x3, matrix products: 2.31 us -> 10.8 us  [solve(): jnp.dot(rows, inverse, preferred_element_type=jnp.float32)]
    dot_general x2, matrix products: 12.6 us -> 4.68 us  [outer_rows(): lax.dot_general(left, right, (((1,), (1,)), ((), ())), preferred_element_...]
    ppermute x1, waiting for transfers between devices: 13.7 us -> 7.11 us  [from_partner(): return lax.ppermute(value, axis, pairs)]
    all_gather x1, waiting for transfers between devices: 4.3 us -> 8.55 us  [local(): columns = lax.all_gather(panel[0], ('z', 'core'), axis=1, tiled=True)]
    ppermute x4, waiting for transfers between devices: 6.34 us -> 3.08 us  [ring_gather(): forward = lax.ppermute(forward, axis, ahead)]
    dynamic_slice x0 -> x1, local copies, waits for them, and re-layouts: none -> 2.65 us  [half_update(): rows = lax.dynamic_slice_in_dim(local_trailing, which * half, half, 0)]
    ppermute x4, starting transfers between devices: 12.2 us -> 9.83 us  [ring_gather(): forward = lax.ppermute(forward, axis, ahead)]
    gather x2, local copies, waits for them, and re-layouts: 3.44 us -> 1.23 us  [half_update(): schur.reshape(half_blocks, width, cols_here)[blocks]]
  transfers between devices with their start and end apart: 8 -> 8, of which waited for: 5 -> 4; matrix products, arithmetic and copies ran while one was open for 23% -> 26% of each run, Pallas kernels for 0% -> 0%
where the time goes in v5:
time: 140 us; the launch traced here: 137 us
  blocking collectives  40.4 us (29%)
  starting transfers between devices  20.3 us (14%)
  waiting for transfers between devices  19.5 us (14%)
  other arithmetic  16.8 us (12%)
  matrix products  16.7 us (12%)
  between operations  13.7 us (10%)
  local copies, waits for them, and re-layouts  9.99 us (7%)
    all_gather x1, blocking collectives, local(): inverse = lax.all_gather(inverse, 'z', axis=0, tiled=True)  38.4 us
    dot_general x3, matrix products, solve(): jnp.dot(rows, inverse, preferred_element_type=jnp.float32)  10.8 us
    ppermute x4, starting transfers between devices, ring_gather(): forward = lax.ppermute(forward, axis, ahead)  9.83 us
    all_gather x1, waiting for transfers between devices, local(): columns = lax.all_gather(panel[0], ('z', 'core'), axis=1, tiled=True)  8.55 us
    ppermute x2, starting transfers between devices, ring_gather(): backward = lax.ppermute(backward, axis, behind)  7.41 us
    ppermute x1, waiting for transfers between devices, from_partner(): return lax.ppermute(value, axis, pairs)  7.11 us
    add x1, other arithmetic, local(): picked = gather_col[lane // width] * width + lane % width  5.66 us
    dot_general x2, matrix products, outer_rows(): lax.dot_general(left, right, (((1,), (1,)), ((), ())), preferred_element_...  4.68 us
  transfers between devices with their start and end apart: 8, of which 4 were waited for; matrix products, arithmetic and copies ran while one was open for 26% of the time, Pallas kernels for 0%

profile of v5, /device:TPU:24, one launch (start us, length us, event | category | flops | bytes accessed | tf_op | source)
XLA Modules:
  0.0 137.4 jit_solution(6326988579324521490)
XLA Ops:
  7.3 2.0 %all-gather.1 = bf16[1,16,1024]{2,1,0:T(8,128)(2,1)S(1)} all-gather(bf16[1,8,1024]{2,1,0:T(8,128)(2,1)} %param.4), channel_id=3, replica_groups=mesh['front'=4,'row'=4,'z'=16,'core'=2] {'core'}, dimensions={1}, use_global_device_ids=true | all-gather | bytes 49152 | tf_op jit(solution)/shard_map/all_gather | solution.py:51
  9.3 38.4 %all-gather.2 = bf16[1,256,1024]{2,1,0:T(8,128)(2,1)S(1)} all-gather(bf16[1,16,1024]{2,1,0:T(8,128)(2,1)S(1)} %all-gather.1), channel_id=4, replica_groups=mesh['front'=4,'row'=4,'z'=16,'core'=2] {'z'}, dimensions={1}, use_global_device_ids=true | all-gather | bytes 557056 | tf_op jit(solution)/shard_map/all_gather | solution.py:52
  47.7 3.4 %collective-permute-start = (bf16[256,1024]{1,0:T(8,128)(2,1)S(1)}, bf16[256,1024]{1,0:T(8,128)(2,1)S(1)}, u32[]{:S(2)}, u32[]{:S(2)}) collective-permute-start(bf16[256,1024]{1,0:T(8,128)(2,1)S(1)} %bitcast.75), channel_id=1, source_target_pairs={{0,32},{32,64},{64,96},{96,0},{1,33},{33,65},{65,97},{97,1},{2,34}... | collective-permute-start | bytes 1572872 | tf_op jit(solution)/shard_map/ppermute | solution.py:28
  51.1 3.7 %collective-permute-start.2 = (bf16[256,1024]{1,0:T(8,128)(2,1)S(1)}, bf16[256,1024]{1,0:T(8,128)(2,1)S(1)}, u32[]{:S(2)}, u32[]{:S(2)}) collective-permute-start(bf16[256,1024]{1,0:T(8,128)(2,1)S(1)} %bitcast.76), channel_id=1, source_target_pairs={{0,96},{32,0},{64,32},{96,64},{1,97},{33,1},{65,33},{97,65},{2,98}... | collective-permute-start | bytes 1572872 | tf_op jit(solution)/shard_map/ppermute | solution.py:31
  54.8 1.3 gather_fusion.4
  56.8 2.5 %sort.35 = (s32[128]{0:T(128)}, s32[128]{0:T(128)S(1)}) sort(s32[128]{0:T(128)S(1)} %fusion.28, s32[128]{0:T(128)S(1)} %iota.47), dimensions={0}, to_apply=%region_1.2 | sort | flops 896 | bytes 2048 | tf_op jit(solution)/shard_map/jit(argsort)/sort | solution.py:80
  61.5 2.2 %collective-permute-start.1 = (bf16[256,1024]{1,0:T(8,128)(2,1)S(1)}, bf16[256,1024]{1,0:T(8,128)(2,1)S(1)}, u32[]{:S(2)}, u32[]{:S(2)}) collective-permute-start(bf16[256,1024]{1,0:T(8,128)(2,1)S(1)} %collective-permute-done), channel_id=1, source_target_pairs={{0,32},{32,64},{64,96},{96,0},{1,33},{33,65},{65,97},{97,1},{2,34}... | collective-permute-start | bytes 1572872 | tf_op jit(solution)/shard_map/ppermute | solution.py:28
  63.7 4.3 %compare_select_fusion.1 = s32[256,1]{0,1:T(1,128)S(1)} fusion(s32[]{:T(128)} %bitcast.19, s32[]{:T(128)} %bitcast.20, s32[]{:T(128)} %bitcast.21, s32[]{:T(128)} %bitcast.22, s32[]{:T(128)} %bitcast.23, s32[]{:T(128)} %bitcast.25, s32[]{:T(128)} %bitcast.24), kind=kLoop, calls=%fused_computation.44 | loop fusion | flops 5888 | bytes 1052 | tf_op jit(solution)/shard_map/gather | solution.py:92
  68.2 2.7 %dynamic-slice_bitcast_fusion = (f32[1024,256]{1,0:T(8,128)S(1)}, f32[1024,256]{1,0:T(8,128)}) fusion(f32[1,2048,256]{2,1,0:T(8,128)} %param.6, s32[]{:T(128)S(6)} %select_n.192, s32[]{:T(128)S(6)} %select_n.172), kind=kLoop, calls=%fused_computation.20 | loop fusion | bytes 4194312 | tf_op jit(solution)/shard_map/dynamic_slice | solution.py:100
  70.8 5.7 %fusion.19 = s32[256]{0:T(256)S(1)} fusion(pred[256]{0:T(512)(128)(4,1)S(1)} %get-tuple-element.37, pred[256]{0:T(512)(128)(4,1)S(1)} %get-tuple-element.38, pred[256]{0:T(512)(128)(4,1)S(1)} %get-tuple-element.39, pred[256]{0:T(512)(128)(4,1)S(1)} %get-tuple-element.40, pred[256]{0:T(512)(128)(4,1)S(1)} %get-tuple-element.41, ...), kind=kLoop, calls=%fused_computation.81 | loop fusion | flops 4352 | bytes 4388 | tf_op jit(solution)/shard_map/add | solution.py:92
  76.5 1.6 %pad_maximum_fusion = bf16[4,256,1024]{2,1,0:T(8,128)(2,1)} fusion(bf16[1,256,1024]{2,1,0:T(8,128)(2,1)S(1)} %bitcast.81, bf16[1,256,1024]{2,1,0:T(8,128)(2,1)S(1)} %bitcast.82, bf16[1,256,1024]{2,1,0:T(8,128)(2,1)S(1)} %bitcast.80, bf16[1,256,1024]{2,1,0:T(8,128)(2,1)S(1)} %all-gather.2), kind=kLoop, calls=%fused_computation.7 | loop fusion | flops 3145728 | bytes 4194304 | tf_op jit(solution)/shard_map/stack | solution.py:37
  78.1 2.3 %gather_fusion = bf16[4,256,1024]{2,1,0:T(8,128)(2,1)S(1)} fusion(bf16[4,256,1024]{2,1,0:T(8,128)(2,1)} %pad_maximum_fusion, s32[1024]{0:T(1024)S(1)} %pad_clamp_fusion.5), kind=kCustom, calls=%fused_computation | custom fusion | bytes 4194320 | tf_op jit(solution)/shard_map/gather | solution.py:39
  80.4 8.6 %all-gather.5.cloned.1.call-done = bf16[1,2048,1024]{1,2,0:T(8,128)(2,1)} async-done(((bf16[1,2048,32]{1,2,0:T(8,128)(2,1)}), bf16[1,2048,1024]{1,2,0:T(8,128)(2,1)}) %all-gather.5.cloned.1.call-update) | async-done | bytes 4194320 | tf_op jit(solution)/shard_map/all_gather | solution.py:57
  88.9 1.6 %convolution_convert_fusion = bf16[64,1024]{1,0:T(8,128)(2,1)S(1)} fusion(bf16[1024,1024]{1,0:T(8,128)(2,1)S(1)} %bitcast.69, bf16[1,2048,1024]{1,2,0:T(8,128)(2,1)} %all-gather.5.cloned.1.call-done, s32[]{:T(128)S(6)} %select_n.183), kind=kOutput, calls=%fused_computation.18 | convolution fusion | flops 134283264 | bytes 2490372 | tf_op jit(solution)/shard_map/dot_general | solution.py:60
  90.5 3.8 %collective-permute-start.5 = (bf16[64,1024]{1,0:T(8,128)(2,1)S(1)}, bf16[64,1024]{1,0:T(8,128)(2,1)S(1)}, u32[]{:S(2)}, u32[]{:S(2)}) collective-permute-start(bf16[64,1024]{1,0:T(8,128)(2,1)S(1)} %convolution_convert_fusion), channel_id=1, source_target_pairs={{0,96},{32,0},{64,32},{96,64},{1,97},{33,1},{65,33},{97,65},{2,98}... | collective-permute-start | bytes 393224 | tf_op jit(solution)/shard_map/ppermute | solution.py:31
  94.3 2.3 %collective-permute-start.3 = (bf16[64,1024]{1,0:T(8,128)(2,1)S(1)}, bf16[64,1024]{1,0:T(8,128)(2,1)S(1)}, u32[]{:S(2)}, u32[]{:S(2)}) collective-permute-start(bf16[64,1024]{1,0:T(8,128)(2,1)S(1)} %convolution_convert_fusion), channel_id=1, source_target_pairs={{0,32},{32,64},{64,96},{96,0},{1,33},{33,65},{65,97},{97,1},{2,34}... | collective-permute-start | bytes 393224 | tf_op jit(solution)/shard_map/ppermute | solution.py:28
  96.7 5.4 %fusion.9 = bf16[1024,1024]{1,0:T(8,128)(2,1)} fusion(bf16[1024,1024]{1,0:T(8,128)(2,1)S(1)} %bitcast.70, bf16[1,2048,1024]{1,2,0:T(8,128)(2,1)} %all-gather.5.cloned.1.call-done, s32[]{:T(128)S(6)} %select_n.192), kind=kOutput, calls=%fused_computation.15 | convolution fusion | flops 2148532224 | bytes 6291460 | tf_op jit(solution)/shard_map/dot_general | solution.py:60
  102.8 1.9 %collective-permute-start.4 = (bf16[64,1024]{1,0:T(8,128)(2,1)S(1)}, bf16[64,1024]{1,0:T(8,128)(2,1)S(1)}, u32[]{:S(2)}, u32[]{:S(2)}) collective-permute-start(bf16[64,1024]{1,0:T(8,128)(2,1)S(1)} %collective-permute-done.3), channel_id=1, source_target_pairs={{0,32},{32,64},{64,96},{96,0},{1,33},{33,65},{65,97},{97,1},{2,34}... | collective-permute-start | bytes 393224 | tf_op jit(solution)/shard_map/ppermute | solution.py:28
  104.7 3.8 %fusion.6 = bf16[1024,1024]{1,0:T(8,128)(2,1)} fusion(bf16[1024,1024]{1,0:T(8,128)(2,1)S(1)} %bitcast.71, bf16[1,2048,1024]{1,2,0:T(8,128)(2,1)S(1)} %copy-done.2, s32[]{:T(128)S(6)} %select_n.172), kind=kOutput, calls=%fused_computation.14 | convolution fusion | flops 2148532224 | bytes 6291460 | tf_op jit(solution)/shard_map/dot_general | solution.py:60
  108.5 2.3 %collective-permute-done.4 = bf16[64,1024]{1,0:T(8,128)(2,1)S(1)} collective-permute-done((bf16[64,1024]{1,0:T(8,128)(2,1)S(1)}, bf16[64,1024]{1,0:T(8,128)(2,1)S(1)}, u32[]{:S(2)}, u32[]{:S(2)}) %collective-permute-start.4) | collective-permute-done | bytes 131104 | tf_op jit(solution)/shard_map/ppermute | solution.py:28
  112.1 2.3 %fusion.38 = f32[1024,256]{1,0:T(8,128)S(1)} fusion(bf16[1024,1024]{1,0:T(8,128)(2,1)} %fusion.9, bf16[256,1024]{1,0:T(8,128)(2,1)S(1)} %bitcast.77), kind=kOutput, calls=%fused_computation.112 | convolution fusion | flops 536870912 | bytes 3670016 | tf_op jit(solution)/shard_map/dot_general | solution.py:15
  115.7 3.1 %collective-permute-start.6 = (bf16[1024,256]{1,0:T(8,128)(2,1)S(1)}, bf16[1024,256]{1,0:T(8,128)(2,1)S(1)}, u32[]{:S(2)}, u32[]{:S(2)}) collective-permute-start(bf16[1024,256]{1,0:T(8,128)(2,1)S(1)} %bitcast.79), channel_id=1, source_target_pairs={{0,128},{128,0},{256,384},{384,256},{1,129},{129,1},{257,385},{385... | collective-permute-start | bytes 1572872 | tf_op jit(solution)/shard_map/ppermute | solution.py:11
  118.8 2.3 %fusion.37 = f32[1024,256]{1,0:T(8,128)S(1)} fusion(bf16[1024,1024]{1,0:T(8,128)(2,1)} %fusion.6, bf16[256,1024]{1,0:T(8,128)(2,1)S(1)} %bitcast.78), kind=kOutput, calls=%fused_computation.111 | convolution fusion | flops 536870912 | bytes 3670016 | tf_op jit(solution)/shard_map/dot_general | solution.py:15
  122.4 7.1 %collective-permute-done.6 = bf16[1024,256]{1,0:T(8,128)(2,1)S(1)} collective-permute-done((bf16[1024,256]{1,0:T(8,128)(2,1)S(1)}, bf16[1024,256]{1,0:T(8,128)(2,1)S(1)}, u32[]{:S(2)}, u32[]{:S(2)}) %collective-permute-start.6) | collective-permute-done | bytes 524320 | tf_op jit(solution)/shard_map/ppermute | solution.py:11
  (44 shorter events, 9.3 us)
Async XLA Ops:
  6.5 48.2 %copy-start = (s32[1,512]{1,0:T(1,128)S(1)}, s32[1,512]{1,0:T(1,128)}, u32[]{:S(2)}) copy-start(s32[1,512]{1,0:T(1,128)} %param.7) | copy-start | bytes 6148
  6.5 82.4 %all-gather.5.cloned.1.call-start = ((), (), s32[]{:S(2)}) async-start(), calls=%async_computation | async-start | bytes 4325376 | tf_op jit(solution)/shard_map/all_gather | solution.py:57
  47.7 13.8 %collective-permute-start = (bf16[256,1024]{1,0:T(8,128)(2,1)S(1)}, bf16[256,1024]{1,0:T(8,128)(2,1)S(1)}, u32[]{:S(2)}, u32[]{:S(2)}) collective-permute-start(bf16[256,1024]{1,0:T(8,128)(2,1)S(1)} %bitcast.75), channel_id=1, source_target_pairs={{0,32},{32,64},{64,96},{96,0},{1,33},{33,65},{65,97},{97,1},{2,34}... | collective-permute-start | bytes 1572872 | tf_op jit(solution)/shard_map/ppermute | solution.py:28
  51.1 25.4 %collective-permute-start.2 = (bf16[256,1024]{1,0:T(8,128)(2,1)S(1)}, bf16[256,1024]{1,0:T(8,128)(2,1)S(1)}, u32[]{:S(2)}, u32[]{:S(2)}) collective-permute-start(bf16[256,1024]{1,0:T(8,128)(2,1)S(1)} %bitcast.76), channel_id=1, source_target_pairs={{0,96},{32,0},{64,32},{96,64},{1,97},{33,1},{65,33},{97,65},{2,98}... | collective-permute-start | bytes 1572872 | tf_op jit(solution)/shard_map/ppermute | solution.py:31
  61.5 15.0 %collective-permute-start.1 = (bf16[256,1024]{1,0:T(8,128)(2,1)S(1)}, bf16[256,1024]{1,0:T(8,128)(2,1)S(1)}, u32[]{:S(2)}, u32[]{:S(2)}) collective-permute-start(bf16[256,1024]{1,0:T(8,128)(2,1)S(1)} %collective-permute-done), channel_id=1, source_target_pairs={{0,32},{32,64},{64,96},{96,0},{1,33},{33,65},{65,97},{97,1},{2,34}... | collective-permute-start | bytes 1572872 | tf_op jit(solution)/shard_map/ppermute | solution.py:28
  90.5 14.2 %copy-start.2 = (bf16[1,2048,1024]{1,2,0:T(8,128)(2,1)S(1)}, bf16[1,2048,1024]{1,2,0:T(8,128)(2,1)}, u32[]{:S(2)}) copy-start(bf16[1,2048,1024]{1,2,0:T(8,128)(2,1)} %all-gather.5.cloned.1.call-done) | copy-start | bytes 12582916
  90.5 18.0 %collective-permute-start.5 = (bf16[64,1024]{1,0:T(8,128)(2,1)S(1)}, bf16[64,1024]{1,0:T(8,128)(2,1)S(1)}, u32[]{:S(2)}, u32[]{:S(2)}) collective-permute-start(bf16[64,1024]{1,0:T(8,128)(2,1)S(1)} %convolution_convert_fusion), channel_id=1, source_target_pairs={{0,96},{32,0},{64,32},{96,64},{1,97},{33,1},{65,33},{97,65},{2,98}... | collective-permute-start | bytes 393224 | tf_op jit(solution)/shard_map/ppermute | solution.py:31
  94.3 8.5 %collective-permute-start.3 = (bf16[64,1024]{1,0:T(8,128)(2,1)S(1)}, bf16[64,1024]{1,0:T(8,128)(2,1)S(1)}, u32[]{:S(2)}, u32[]{:S(2)}) collective-permute-start(bf16[64,1024]{1,0:T(8,128)(2,1)S(1)} %convolution_convert_fusion), channel_id=1, source_target_pairs={{0,32},{32,64},{64,96},{96,0},{1,33},{33,65},{65,97},{97,1},{2,34}... | collective-permute-start | bytes 393224 | tf_op jit(solution)/shard_map/ppermute | solution.py:28
  102.8 8.1 %collective-permute-start.4 = (bf16[64,1024]{1,0:T(8,128)(2,1)S(1)}, bf16[64,1024]{1,0:T(8,128)(2,1)S(1)}, u32[]{:S(2)}, u32[]{:S(2)}) collective-permute-start(bf16[64,1024]{1,0:T(8,128)(2,1)S(1)} %collective-permute-done.3), channel_id=1, source_target_pairs={{0,32},{32,64},{64,96},{96,0},{1,33},{33,65},{65,97},{97,1},{2,34}... | collective-permute-start | bytes 393224 | tf_op jit(solution)/shard_map/ppermute | solution.py:28
  115.7 5.4 %copy-start.1 = (f32[1024,256]{1,0:T(8,128)S(1)}, f32[1024,256]{1,0:T(8,128)}, u32[]{:S(2)}) copy-start(f32[1024,256]{1,0:T(8,128)} %get-tuple-element.11) | copy-start | bytes 3145732
  115.7 13.8 %collective-permute-start.6 = (bf16[1024,256]{1,0:T(8,128)(2,1)S(1)}, bf16[1024,256]{1,0:T(8,128)(2,1)S(1)}, u32[]{:S(2)}, u32[]{:S(2)}) collective-permute-start(bf16[1024,256]{1,0:T(8,128)(2,1)S(1)} %bitcast.79), channel_id=1, source_target_pairs={{0,128},{128,0},{256,384},{384,256},{1,129},{129,1},{257,385},{385... | collective-permute-start | bytes 1572872 | tf_op jit(solution)/shard_map/ppermute | solution.py:11
Sparse Core Ops, SparseCore 0:
  9.5 79.4 all-gather.4

commit v6 on v5

--- a/solution.py
+++ b/solution.py
@@ -39,6 +39,12 @@
     return stacked[(index - sources) % n]
 
 
+def inverse_order(target):
+    slots = jnp.arange(target.shape[0], dtype=jnp.int32)
+    hit = target[None, :] == slots[:, None]
+    return jnp.sum(jnp.where(hit, slots[None, :], 0), axis=1, dtype=jnp.int32)
+
+
 def local(inverse_factor, panel, trailing, extend_map):
     nrow = lax.axis_size("row")
     nz = lax.axis_size("z")
@@ -64,9 +70,8 @@
     local_trailing = trailing[0]
     rows_here = local_trailing.shape[0]
     cols_here = local_trailing.shape[1]
-    share = rows_here // ncol
-    piece = solve(lax.dynamic_slice_in_dim(columns, col_index * share, share, 0))
-    col_side = ring_gather(piece, "row", row_index, nrow)
+    piece_panel = lax.all_to_all(panel[0], ("z", "core"), 0, 1, tiled=True)
+    piece_panel = lax.all_gather(piece_panel, "row", axis=0, tiled=True)
 
     block_map = extend_map[0]
     nblocks = block_map.shape[0]
@@ -77,20 +82,23 @@
     depth_row = slots_row % per_class
     source_row = (depth_row * ncol + class_row) * nrow + row_index
     target_row = class_row * per_class + block_map[source_row] // group
-    gather_row = jnp.argsort(target_row)
+    gather_row = inverse_order(target_row)
     slots_col = jnp.arange(nrow * per_class, dtype=jnp.int32)
     class_col = slots_col // per_class
     depth_col = slots_col % per_class
     source_col = (depth_col * ncol + col_index) * nrow + class_col
     target_col = class_col * per_class + block_map[source_col] // group
-    gather_col = jnp.argsort(target_col)
+    gather_col = inverse_order(target_col)
 
+    col_side = solve(piece_panel)
     col_side = col_side.reshape(nrow * per_class, width, order)[gather_col].reshape(
         cols_here, order
     )
-    lane = jnp.arange(cols_here, dtype=jnp.int32)
-    picked = gather_col[lane // width] * width + lane % width
-    select_cols = (lane[:, None] == picked[None, :]).astype(jnp.float32)
+    blocks_col = slots_col[:, None] == gather_col[None, :]
+    same = jnp.arange(width)[:, None] == jnp.arange(width)[None, :]
+    select_cols = (blocks_col[:, None, :, None] & same[None, :, None, :]).reshape(
+        cols_here, cols_here
+    ).astype(jnp.float32)
 
     member = lax.axis_index("front") % 2
     half = rows_here // 2

time: 140 us -> 145 us (1.036)
  blocking collectives: 40.4 us -> 58.5 us
  other arithmetic: 16.8 us -> 4.71 us
  local copies, waits for them, and re-layouts: 9.99 us -> 13.3 us
    all_gather x0 -> x1, blocking collectives: none -> 14 us  [local(): piece_panel = lax.all_gather(piece_panel, 'row', axis=0, tiled=True)]
    all_to_all x0 -> x1, waiting for transfers between devices: none -> 11.4 us  [local(): piece_panel = lax.all_to_all(panel[0], ('z', 'core'), 0, 1, tiled=True)]
    all_gather x1, waiting for transfers between devices: 8.55 us -> 0.01 us  [local(): columns = lax.all_gather(panel[0], ('z', 'core'), axis=1, tiled=True)]
    all_to_all x0 -> x1, starting transfers between devices: none -> 7.2 us  [local(): piece_panel = lax.all_to_all(panel[0], ('z', 'core'), 0, 1, tiled=True)]
    add x1 -> x0, other arithmetic: 5.66 us -> none  [local(): picked = gather_col[lane // width] * width + lane % width]
    gather x6 -> x0, other arithmetic: 4.48 us -> none  [local(): picked = gather_col[lane // width] * width + lane % width]
    ppermute x4 -> x2, starting transfers between devices: 9.83 us -> 5.52 us  [ring_gather(): forward = lax.ppermute(forward, axis, ahead)]
    all_gather x1, blocking collectives: 38.4 us -> 42.5 us  [local(): inverse = lax.all_gather(inverse, 'z', axis=0, tiled=True)]
  transfers between devices with their start and end apart: 8 -> 6, of which waited for: 4 -> 2; matrix products, arithmetic and copies ran while one was open for 26% -> 13% of each run, Pallas kernels for 0% -> 0%
where the time goes in v6:
time: 145 us; the launch traced here: 144 us
  blocking collectives  58.5 us (40%)
  starting transfers between devices  19.3 us (13%)
  waiting for transfers between devices  18.3 us (13%)
  matrix products  15.8 us (11%)
  between operations  13.7 us (9%)
  local copies, waits for them, and re-layouts  13.3 us (9%)
  other arithmetic  4.71 us (3%)
    all_gather x1, blocking collectives, local(): inverse = lax.all_gather(inverse, 'z', axis=0, tiled=True)  42.5 us
    all_gather x1, blocking collectives, local(): piece_panel = lax.all_gather(piece_panel, 'row', axis=0, tiled=True)  14 us
    all_to_all x1, waiting for transfers between devices, local(): piece_panel = lax.all_to_all(panel[0], ('z', 'core'), 0, 1, tiled=True)  11.4 us
    dot_general x3, matrix products, solve(): jnp.dot(rows, inverse, preferred_element_type=jnp.float32)  11.4 us
    all_to_all x1, starting transfers between devices, local(): piece_panel = lax.all_to_all(panel[0], ('z', 'core'), 0, 1, tiled=True)  7.2 us
    ppermute x1, waiting for transfers between devices, from_partner(): return lax.ppermute(value, axis, pairs)  6.2 us
    ppermute x2, starting transfers between devices, ring_gather(): forward = lax.ppermute(forward, axis, ahead)  5.52 us
    ppermute x1, starting transfers between devices, ring_gather(): backward = lax.ppermute(backward, axis, behind)  3.69 us
  transfers between devices with their start and end apart: 6, of which 2 were waited for; matrix products, arithmetic and copies ran while one was open for 13% of the time, Pallas kernels for 0%

profile of v6, /device:TPU:24, one launch (start us, length us, event | category | flops | bytes accessed | tf_op | source)
XLA Modules:
  0.0 143.7 jit_solution(15598702942103204462)
XLA Ops:
  7.3 2.0 %all-gather.1 = bf16[1,16,1024]{2,1,0:T(8,128)(2,1)S(1)} all-gather(bf16[1,8,1024]{2,1,0:T(8,128)(2,1)} %param.4), channel_id=3, replica_groups=mesh['front'=4,'row'=4,'z'=16,'core'=2] {'core'}, dimensions={1}, use_global_device_ids=true | all-gather | bytes 49152 | tf_op jit(solution)/shard_map/all_gather | solution.py:57
  9.3 42.5 %all-gather.2 = bf16[1,256,1024]{2,1,0:T(8,128)(2,1)} all-gather(bf16[1,16,1024]{2,1,0:T(8,128)(2,1)S(1)} %all-gather.1), channel_id=4, replica_groups=mesh['front'=4,'row'=4,'z'=16,'core'=2] {'z'}, dimensions={1}, use_global_device_ids=true | all-gather | bytes 557056 | tf_op jit(solution)/shard_map/all_gather | solution.py:58
  51.8 3.4 %collective-permute-start = (bf16[256,1024]{1,0:T(8,128)(2,1)}, bf16[256,1024]{1,0:T(8,128)(2,1)}, u32[]{:S(2)}, u32[]{:S(2)}) collective-permute-start(bf16[256,1024]{1,0:T(8,128)(2,1)} %bitcast.2), channel_id=1, source_target_pairs={{0,32},{32,64},{64,96},{96,0},{1,33},{33,65},{65,97},{97,1},{2,34}... | collective-permute-start | bytes 1572872 | tf_op jit(solution)/shard_map/ppermute | solution.py:28
  55.2 3.7 %collective-permute-start.2 = (bf16[256,1024]{1,0:T(8,128)(2,1)}, bf16[256,1024]{1,0:T(8,128)(2,1)}, u32[]{:S(2)}, u32[]{:S(2)}) collective-permute-start(bf16[256,1024]{1,0:T(8,128)(2,1)} %bitcast.2), channel_id=1, source_target_pairs={{0,96},{32,0},{64,32},{96,64},{1,97},{33,1},{65,33},{97,65},{2,98}... | collective-permute-start | bytes 1572872 | tf_op jit(solution)/shard_map/ppermute | solution.py:31
  58.9 1.2 all_to_all.14
  60.2 0.8 reshape.388
  61.0 7.2 %all-to-all-start = ((bf16[32,2,1024]{2,1,0:T(2,128)(2,1)}), bf16[32,2,1024]{2,1,0:T(2,128)(2,1)S(1)}, u32[]{:S(2)}, u32[]{:S(2)}) async-start(bf16[32,2,1024]{2,1,0:T(2,128)(2,1)} %reshape.388), calls=%async_computation | async-start | bytes 262144 | tf_op jit(solution)/shard_map/all_to_all | solution.py:73
  68.3 1.3 gather_fusion.3
  71.0 2.2 %collective-permute-start.1 = (bf16[256,1024]{1,0:T(8,128)(2,1)}, bf16[256,1024]{1,0:T(8,128)(2,1)}, u32[]{:S(2)}, u32[]{:S(2)}) collective-permute-start(bf16[256,1024]{1,0:T(8,128)(2,1)} %collective-permute-done), channel_id=1, source_target_pairs={{0,32},{32,64},{64,96},{96,0},{1,33},{33,65},{65,97},{97,1},{2,34}... | collective-permute-start | bytes 1572872 | tf_op jit(solution)/shard_map/ppermute | solution.py:28
  73.2 0.9 and.163
  74.1 1.1 dynamic-slice_bitcast_fusion
  75.2 11.4 %all-to-all-done = bf16[32,2,1024]{2,1,0:T(2,128)(2,1)S(1)} async-done(((bf16[32,2,1024]{2,1,0:T(2,128)(2,1)}), bf16[32,2,1024]{2,1,0:T(2,128)(2,1)S(1)}, u32[]{:S(2)}, u32[]{:S(2)}) %all-to-all-start) | async-done | bytes 131104 | tf_op jit(solution)/shard_map/all_to_all | solution.py:73
  87.0 14.0 %all_gather.15 = bf16[256,1024]{1,0:T(8,128)(2,1)} all-gather(bf16[64,1024]{1,0:T(8,128)(2,1)S(1)} %copy.9), channel_id=1, replica_groups=mesh['front'=4,'row'=4,'z'=16,'core'=2] {'row'}, dimensions={0}, use_global_device_ids=true | all-gather | bytes 655360 | tf_op jit(solution)/shard_map/all_gather | solution.py:74
  100.9 1.8 %pad_maximum_fusion = bf16[4,256,1024]{2,1,0:T(8,128)(2,1)S(1)} fusion(bf16[1,256,1024]{2,1,0:T(8,128)(2,1)} %bitcast.5, bf16[1,256,1024]{2,1,0:T(8,128)(2,1)} %bitcast.4, bf16[1,256,1024]{2,1,0:T(8,128)(2,1)} %bitcast.3, bf16[1,256,1024]{2,1,0:T(8,128)(2,1)} %all-gather.2), kind=kLoop, calls=%fused_computation.6 | loop fusion | flops 3145728 | bytes 4194304 | tf_op jit(solution)/shard_map/stack | solution.py:37
  102.7 2.0 %gather_fusion = bf16[4,256,1024]{2,1,0:T(8,128)(2,1)} fusion(bf16[4,256,1024]{2,1,0:T(8,128)(2,1)S(1)} %pad_maximum_fusion, s32[1024]{0:T(1024)S(1)} %pad_clamp_fusion.5), kind=kCustom, calls=%fused_computation | custom fusion | bytes 4194320 | tf_op jit(solution)/shard_map/gather | solution.py:39
  104.7 3.4 %convolution_convert_fusion = bf16[1024,256]{0,1:T(8,128)(2,1)} fusion(bf16[256,1024]{1,0:T(8,128)(2,1)} %all_gather.15, bf16[1024,1024]{1,0:T(8,128)(2,1)} %bitcast.66), kind=kOutput, calls=%fused_computation.17 | convolution fusion | flops 537133056 | bytes 3145728 | tf_op jit(solution)/shard_map/dot_general | solution.py:66
  108.1 2.4 %gather_fusion.2 = bf16[16,16,1024]{2,1,0:T(8,128)(2,1)} fusion(bf16[16,16,1024]{2,1,0:T(8,128)(2,1)} %bitcast.74, s32[1024]{0:T(1024)S(1)} %pad_clamp_fusion.3), kind=kCustom, calls=%fused_computation.2 | custom fusion | bytes 1048640 | tf_op jit(solution)/shard_map/gather | solution.py:94
  110.5 4.2 %fusion.9 = bf16[1024,1024]{1,0:T(8,128)(2,1)S(1)} fusion(bf16[1024,1024]{1,0:T(8,128)(2,1)S(1)} %bitcast.67, bf16[1,2048,1024]{1,2,0:T(8,128)(2,1)} %all-gather.5.cloned.1.call-done, s32[]{:T(128)S(6)} %select_n.183), kind=kOutput, calls=%fused_computation.14 | convolution fusion | flops 2148532224 | bytes 6291460 | tf_op jit(solution)/shard_map/dot_general | solution.py:66
  114.7 3.8 %fusion.6 = bf16[1024,1024]{1,0:T(8,128)(2,1)} fusion(bf16[1024,1024]{1,0:T(8,128)(2,1)S(1)} %bitcast.68, bf16[1,2048,1024]{1,2,0:T(8,128)(2,1)S(1)} %copy-done.5, s32[]{:T(128)S(6)} %select_n.165), kind=kOutput, calls=%fused_computation.13 | convolution fusion | flops 2148532224 | bytes 6291460 | tf_op jit(solution)/shard_map/dot_general | solution.py:66
  120.4 1.4 gather_fusion.5
  121.8 2.9 %collective-permute-start.3 = (bf16[1024,256]{1,0:T(8,128)(2,1)}, bf16[1024,256]{1,0:T(8,128)(2,1)}, u32[]{:S(2)}, u32[]{:S(2)}) collective-permute-start(bf16[1024,256]{1,0:T(8,128)(2,1)} %bitcast.23), channel_id=1, source_target_pairs={{0,128},{128,0},{256,384},{384,256},{1,129},{129,1},{257,385},{385... | collective-permute-start | bytes 1572872 | tf_op jit(solution)/shard_map/ppermute | solution.py:11
  124.7 2.4 %fusion.31 = f32[1024,256]{1,0:T(8,128)S(1)} fusion(bf16[1024,1024]{1,0:T(8,128)(2,1)} %fusion.6, bf16[256,1024]{1,0:T(8,128)(2,1)} %bitcast.72), kind=kOutput, calls=%fused_computation.88 | convolution fusion | flops 536870912 | bytes 3670016 | tf_op jit(solution)/shard_map/dot_general | solution.py:15
  128.4 6.2 %collective-permute-done.3 = bf16[1024,256]{1,0:T(8,128)(2,1)} collective-permute-done((bf16[1024,256]{1,0:T(8,128)(2,1)}, bf16[1024,256]{1,0:T(8,128)(2,1)}, u32[]{:S(2)}, u32[]{:S(2)}) %collective-permute-start.3) | collective-permute-done | bytes 524320 | tf_op jit(solution)/shard_map/ppermute | solution.py:11
  134.6 2.2 %bitcast_add_fusion = f32[1024,256]{1,0:T(8,128)} fusion(f32[64,16,256]{2,1,0:T(8,128)S(1)} %gather_fusion.4, bf16[1024,256]{1,0:T(8,128)(2,1)} %collective-permute-done.3), kind=kLoop, calls=%fused_computation.18 | loop fusion | flops 524288 | bytes 2621440 | tf_op jit(solution)/shard_map/add | solution.py:129
  (43 shorter events, 5.8 us)
Async XLA Ops:
  6.5 61.7 %copy-start = (s32[1,512]{1,0:T(1,128)S(1)}, s32[1,512]{1,0:T(1,128)}, u32[]{:S(2)}) copy-start(s32[1,512]{1,0:T(1,128)} %param.7) | copy-start | bytes 6148
  6.5 104.0 %all-gather.5.cloned.1.call-start = ((), (), s32[]{:S(2)}) async-start(), calls=%async_computation.1 | async-start | bytes 4325376 | tf_op jit(solution)/shard_map/all_gather | solution.py:63
  9.3 64.8 %copy-start.2 = (f32[1,2048,256]{2,1,0:T(8,128)S(1)}, f32[1,2048,256]{2,1,0:T(8,128)}, u32[]{:S(2)}) copy-start(f32[1,2048,256]{2,1,0:T(8,128)} %param.6) | copy-start | bytes 6291460
  51.8 19.2 %collective-permute-start = (bf16[256,1024]{1,0:T(8,128)(2,1)}, bf16[256,1024]{1,0:T(8,128)(2,1)}, u32[]{:S(2)}, u32[]{:S(2)}) collective-permute-start(bf16[256,1024]{1,0:T(8,128)(2,1)} %bitcast.2), channel_id=1, source_target_pairs={{0,32},{32,64},{64,96},{96,0},{1,33},{33,65},{65,97},{97,1},{2,34}... | collective-permute-start | bytes 1572872 | tf_op jit(solution)/shard_map/ppermute | solution.py:28
  55.2 45.8 %collective-permute-start.2 = (bf16[256,1024]{1,0:T(8,128)(2,1)}, bf16[256,1024]{1,0:T(8,128)(2,1)}, u32[]{:S(2)}, u32[]{:S(2)}) collective-permute-start(bf16[256,1024]{1,0:T(8,128)(2,1)} %bitcast.2), channel_id=1, source_target_pairs={{0,96},{32,0},{64,32},{96,64},{1,97},{33,1},{65,33},{97,65},{2,98}... | collective-permute-start | bytes 1572872 | tf_op jit(solution)/shard_map/ppermute | solution.py:31
  61.0 25.6 %all-to-all-start = ((bf16[32,2,1024]{2,1,0:T(2,128)(2,1)}), bf16[32,2,1024]{2,1,0:T(2,128)(2,1)S(1)}, u32[]{:S(2)}, u32[]{:S(2)}) async-start(bf16[32,2,1024]{2,1,0:T(2,128)(2,1)} %reshape.388), calls=%async_computation | async-start | bytes 262144 | tf_op jit(solution)/shard_map/all_to_all | solution.py:73
  71.0 29.9 %collective-permute-start.1 = (bf16[256,1024]{1,0:T(8,128)(2,1)}, bf16[256,1024]{1,0:T(8,128)(2,1)}, u32[]{:S(2)}, u32[]{:S(2)}) collective-permute-start(bf16[256,1024]{1,0:T(8,128)(2,1)} %collective-permute-done), channel_id=1, source_target_pairs={{0,32},{32,64},{64,96},{96,0},{1,33},{33,65},{65,97},{97,1},{2,34}... | collective-permute-start | bytes 1572872 | tf_op jit(solution)/shard_map/ppermute | solution.py:28
  104.7 5.8 %copy-start.3 = (bf16[4,256,1024]{2,1,0:T(8,128)(2,1)S(1)}, bf16[4,256,1024]{2,1,0:T(8,128)(2,1)}, u32[]{:S(2)}) copy-start(bf16[4,256,1024]{2,1,0:T(8,128)(2,1)} %gather_fusion) | copy-start | bytes 6291460
  110.5 4.2 %copy-start.5 = (bf16[1,2048,1024]{1,2,0:T(8,128)(2,1)S(1)}, bf16[1,2048,1024]{1,2,0:T(8,128)(2,1)}, u32[]{:S(2)}) copy-start(bf16[1,2048,1024]{1,2,0:T(8,128)(2,1)} %all-gather.5.cloned.1.call-done) | copy-start | bytes 12582916
  114.7 3.8 %copy-start.4 = (bf16[16,16,1024]{2,1,0:T(8,128)(2,1)S(1)}, bf16[16,16,1024]{2,1,0:T(8,128)(2,1)}, u32[]{:S(2)}) copy-start(bf16[16,16,1024]{2,1,0:T(8,128)(2,1)} %gather_fusion.2) | copy-start | bytes 1572868
  118.5 1.2 copy-start.1
  121.8 12.8 %collective-permute-start.3 = (bf16[1024,256]{1,0:T(8,128)(2,1)}, bf16[1024,256]{1,0:T(8,128)(2,1)}, u32[]{:S(2)}, u32[]{:S(2)}) collective-permute-start(bf16[1024,256]{1,0:T(8,128)(2,1)} %bitcast.23), channel_id=1, source_target_pairs={{0,128},{128,0},{256,384},{384,256},{1,129},{129,1},{257,385},{385... | collective-permute-start | bytes 1572872 | tf_op jit(solution)/shard_map/ppermute | solution.py:11
Sparse Core Ops, SparseCore 0:
  9.5 81.4 all-gather.4

commit v7 on v6

--- a/solution.py
+++ b/solution.py
@@ -62,6 +62,12 @@
 
     columns = lax.all_gather(panel[0], ("z", "core"), axis=1, tiled=True)
 
+    def solve_first(rows):
+        ready, _ = lax.optimization_barrier((inverse, moved_cols))
+        return jnp.dot(rows, ready, preferred_element_type=jnp.float32).astype(
+            jnp.bfloat16
+        )
+
     def solve(rows):
         return jnp.dot(rows, inverse, preferred_element_type=jnp.float32).astype(
             jnp.bfloat16
@@ -70,9 +76,7 @@
     local_trailing = trailing[0]
     rows_here = local_trailing.shape[0]
     cols_here = local_trailing.shape[1]
-    piece_panel = lax.all_to_all(panel[0], ("z", "core"), 0, 1, tiled=True)
-    piece_panel = lax.all_gather(piece_panel, "row", axis=0, tiled=True)
-
+    share = rows_here // ncol
     block_map = extend_map[0]
     nblocks = block_map.shape[0]
     per_class = nblocks // group
@@ -90,31 +94,33 @@
     target_col = class_col * per_class + block_map[source_col] // group
     gather_col = inverse_order(target_col)
 
-    col_side = solve(piece_panel)
-    col_side = col_side.reshape(nrow * per_class, width, order)[gather_col].reshape(
-        cols_here, order
-    )
     blocks_col = slots_col[:, None] == gather_col[None, :]
     same = jnp.arange(width)[:, None] == jnp.arange(width)[None, :]
     select_cols = (blocks_col[:, None, :, None] & same[None, :, None, :]).reshape(
         cols_here, cols_here
     ).astype(jnp.float32)
+    moved_cols = jnp.dot(
+        local_trailing,
+        select_cols,
+        precision=lax.Precision.HIGHEST,
+        preferred_element_type=jnp.float32,
+    )
+    piece = solve_first(lax.dynamic_slice_in_dim(columns, col_index * share, share, 0))
+    col_side = ring_gather(piece, "row", row_index, nrow)
+
+    col_side = col_side.reshape(nrow * per_class, width, order)[gather_col].reshape(
+        cols_here, order
+    )
 
     member = lax.axis_index("front") % 2
     half = rows_here // 2
     half_blocks = half // width
 
     def half_update(which):
-        rows = lax.dynamic_slice_in_dim(local_trailing, which * half, half, 0)
+        rows = lax.dynamic_slice_in_dim(moved_cols, which * half, half, 0)
         low = solve(lax.dynamic_slice_in_dim(columns, which * half, half, 0))
         rows, low = lax.optimization_barrier((rows, low))
-        moved_cols = jnp.dot(
-            rows,
-            select_cols,
-            precision=lax.Precision.HIGHEST,
-            preferred_element_type=jnp.float32,
-        )
-        schur = moved_cols - outer_rows(low, col_side)
+        schur = rows - outer_rows(low, col_side)
         blocks = (
             lax.dynamic_slice_in_dim(gather_row, which * half_blocks, half_blocks, 0)
             - which * half_blocks

time: 145 us -> 148 us (1.021)
  blocking collectives: 58.5 us -> 45.1 us
  local copies, waits for them, and re-layouts: 13.3 us -> 22.4 us
  matrix products: 15.8 us -> 19.1 us
  other arithmetic: 4.71 us -> 6.98 us
    ppermute x2 -> x4, waiting for transfers between devices: 0.01 us -> 19 us  [ring_gather(): forward = lax.ppermute(forward, axis, ahead)]
    all_gather x1 -> x0, blocking collectives: 14 us -> none  [local(): piece_panel = lax.all_gather(piece_panel, 'row', axis=0, tiled=True)]
    all_to_all x1 -> x0, waiting for transfers between devices: 11.4 us -> none  [local(): piece_panel = lax.all_to_all(panel[0], ('z', 'core'), 0, 1, tiled=True)]
    all_to_all x1 -> x0, starting transfers between devices: 7.2 us -> none  [local(): piece_panel = lax.all_to_all(panel[0], ('z', 'core'), 0, 1, tiled=True)]
    ppermute x1, waiting for transfers between devices: 6.2 us -> 0.01 us  [from_partner(): return lax.ppermute(value, axis, pairs)]
    ppermute x1 -> x2, starting transfers between devices: 3.69 us -> 9.58 us  [ring_gather(): backward = lax.ppermute(backward, axis, behind)]
    sub x0 -> x2, local copies, waits for them, and re-layouts: none -> 4.57 us  [half_update(): schur = rows - outer_rows(low, col_side)]
    gather x1 -> x2, local copies, waits for them, and re-layouts: 2 us -> 6.07 us  [ring_gather(): return stacked[(index - sources) % n]]
  transfers between devices with their start and end apart: 6 -> 8, of which waited for: 2 -> 4; matrix products, arithmetic and copies ran while one was open for 13% -> 20% of each run, Pallas kernels for 0% -> 0%
where the time goes in v7:
time: 148 us; the launch traced here: 146 us
  blocking collectives  45.1 us (30%)
  local copies, waits for them, and re-layouts  22.4 us (15%)
  waiting for transfers between devices  19.7 us (13%)
  starting transfers between devices  19.3 us (13%)
  matrix products  19.1 us (13%)
  between operations  13.7 us (9%)
  other arithmetic  6.98 us (5%)
    all_gather x1, blocking collectives, local(): inverse = lax.all_gather(inverse, 'z', axis=0, tiled=True)  43.1 us
    ppermute x4, waiting for transfers between devices, ring_gather(): forward = lax.ppermute(forward, axis, ahead)  19 us
    dot_general x2, matrix products, solve(): jnp.dot(rows, inverse, preferred_element_type=jnp.float32)  9.97 us
    ppermute x2, starting transfers between devices, ring_gather(): backward = lax.ppermute(backward, axis, behind)  9.58 us
    ppermute x4, starting transfers between devices, ring_gather(): forward = lax.ppermute(forward, axis, ahead)  7.66 us
    gather x2, local copies, waits for them, and re-layouts, ring_gather(): return stacked[(index - sources) % n]  6.07 us
    dot_general x2, matrix products, outer_rows(): lax.dot_general(left, right, (((1,), (1,)), ((), ())), preferred_element_...  5.35 us
    sub x2, local copies, waits for them, and re-layouts, half_update(): schur = rows - outer_rows(low, col_side)  4.57 us
  transfers between devices with their start and end apart: 8, of which 4 were waited for; matrix products, arithmetic and copies ran while one was open for 20% of the time, Pallas kernels for 0%

profile of v7, /device:TPU:24, one launch (start us, length us, event | category | flops | bytes accessed | tf_op | source)
XLA Modules:
  0.0 146.2 jit_solution(379952319195674657)
XLA Ops:
  7.3 2.0 %all-gather.1 = bf16[1,16,1024]{2,1,0:T(8,128)(2,1)S(1)} all-gather(bf16[1,8,1024]{2,1,0:T(8,128)(2,1)} %param.4), channel_id=3, replica_groups=mesh['front'=4,'row'=4,'z'=16,'core'=2] {'core'}, dimensions={1}, use_global_device_ids=true | all-gather | bytes 49152 | tf_op jit(solution)/shard_map/all_gather | solution.py:57
  9.3 43.1 %all-gather.2 = bf16[1,256,1024]{2,1,0:T(8,128)(2,1)} all-gather(bf16[1,16,1024]{2,1,0:T(8,128)(2,1)S(1)} %all-gather.1), channel_id=4, replica_groups=mesh['front'=4,'row'=4,'z'=16,'core'=2] {'z'}, dimensions={1}, use_global_device_ids=true | all-gather | bytes 557056 | tf_op jit(solution)/shard_map/all_gather | solution.py:58
  52.4 4.5 %collective-permute-start.2 = (bf16[256,1024]{1,0:T(8,128)(2,1)}, bf16[256,1024]{1,0:T(8,128)(2,1)}, u32[]{:S(2)}, u32[]{:S(2)}) collective-permute-start(bf16[256,1024]{1,0:T(8,128)(2,1)} %bitcast.5), channel_id=1, source_target_pairs={{0,96},{32,0},{64,32},{96,64},{1,97},{33,1},{65,33},{97,65},{2,98}... | collective-permute-start | bytes 1572872 | tf_op jit(solution)/shard_map/ppermute | solution.py:31
  56.8 1.9 %collective-permute-start = (bf16[256,1024]{1,0:T(8,128)(2,1)}, bf16[256,1024]{1,0:T(8,128)(2,1)}, u32[]{:S(2)}, u32[]{:S(2)}) collective-permute-start(bf16[256,1024]{1,0:T(8,128)(2,1)} %bitcast.5), channel_id=1, source_target_pairs={{0,32},{32,64},{64,96},{96,0},{1,33},{33,65},{65,97},{97,1},{2,34}... | collective-permute-start | bytes 1572872 | tf_op jit(solution)/shard_map/ppermute | solution.py:28
  62.5 10.0 %collective-permute-done = bf16[256,1024]{1,0:T(8,128)(2,1)} collective-permute-done((bf16[256,1024]{1,0:T(8,128)(2,1)}, bf16[256,1024]{1,0:T(8,128)(2,1)}, u32[]{:S(2)}, u32[]{:S(2)}) %collective-permute-start) | collective-permute-done | bytes 524320 | tf_op jit(solution)/shard_map/ppermute | solution.py:28
  72.5 1.9 %collective-permute-start.1 = (bf16[256,1024]{1,0:T(8,128)(2,1)}, bf16[256,1024]{1,0:T(8,128)(2,1)}, u32[]{:S(2)}, u32[]{:S(2)}) collective-permute-start(bf16[256,1024]{1,0:T(8,128)(2,1)} %collective-permute-done), channel_id=1, source_target_pairs={{0,32},{32,64},{64,96},{96,0},{1,33},{33,65},{65,97},{97,1},{2,34}... | collective-permute-start | bytes 1572872 | tf_op jit(solution)/shard_map/ppermute | solution.py:28
  77.9 7.2 %collective-permute-done.1 = bf16[256,1024]{1,0:T(8,128)(2,1)} collective-permute-done((bf16[256,1024]{1,0:T(8,128)(2,1)}, bf16[256,1024]{1,0:T(8,128)(2,1)}, u32[]{:S(2)}, u32[]{:S(2)}) %collective-permute-start.1) | collective-permute-done | bytes 524320 | tf_op jit(solution)/shard_map/ppermute | solution.py:28
  85.1 3.1 %pad_maximum_fusion = bf16[4,256,1024]{2,1,0:T(8,128)(2,1)} fusion(bf16[1,256,1024]{2,1,0:T(8,128)(2,1)} %bitcast.8, bf16[1,256,1024]{2,1,0:T(8,128)(2,1)} %bitcast.7, bf16[1,256,1024]{2,1,0:T(8,128)(2,1)} %bitcast.6, bf16[1,256,1024]{2,1,0:T(8,128)(2,1)} %all-gather.2), kind=kLoop, calls=%fused_computation.7 | loop fusion | flops 3145728 | bytes 4194304 | tf_op jit(solution)/shard_map/stack | solution.py:37
  88.3 3.6 %gather_fusion.1 = bf16[4,256,1024]{2,1,0:T(8,128)(2,1)} fusion(bf16[4,256,1024]{2,1,0:T(8,128)(2,1)} %pad_maximum_fusion, s32[1024]{0:T(1024)S(1)} %pad_clamp_fusion.4), kind=kCustom, calls=%fused_computation.1 | custom fusion | bytes 4194320 | tf_op jit(solution)/shard_map/gather | solution.py:39
  91.9 2.4 %convolution_convert_fusion = bf16[64,1024]{1,0:T(8,128)(2,1)S(1)} fusion(bf16[1024,1024]{1,0:T(8,128)(2,1)} %bitcast.59, bf16[1,2048,1024]{1,2,0:T(8,128)(2,1)} %all-gather.5.cloned.1.call-done, s32[]{:T(128)S(6)} %select_n.180), kind=kOutput, calls=%fused_computation.20 | convolution fusion | flops 134283264 | bytes 2490372 | tf_op jit(solution)/shard_map/dot_general | solution.py:67
  94.3 1.9 %collective-permute-start.3 = (bf16[64,1024]{1,0:T(8,128)(2,1)S(1)}, bf16[64,1024]{1,0:T(8,128)(2,1)S(1)}, u32[]{:S(2)}, u32[]{:S(2)}) collective-permute-start(bf16[64,1024]{1,0:T(8,128)(2,1)S(1)} %convolution_convert_fusion), channel_id=1, source_target_pairs={{0,32},{32,64},{64,96},{96,0},{1,33},{33,65},{65,97},{97,1},{2,34}... | collective-permute-start | bytes 393224 | tf_op jit(solution)/shard_map/ppermute | solution.py:28
  96.3 5.1 %collective-permute-start.5 = (bf16[64,1024]{1,0:T(8,128)(2,1)S(1)}, bf16[64,1024]{1,0:T(8,128)(2,1)S(1)}, u32[]{:S(2)}, u32[]{:S(2)}) collective-permute-start(bf16[64,1024]{1,0:T(8,128)(2,1)S(1)} %convolution_convert_fusion), channel_id=1, source_target_pairs={{0,96},{32,0},{64,32},{96,64},{1,97},{33,1},{65,33},{97,65},{2,98}... | collective-permute-start | bytes 393224 | tf_op jit(solution)/shard_map/ppermute | solution.py:31
  102.4 1.9 %collective-permute-start.4 = (bf16[64,1024]{1,0:T(8,128)(2,1)S(1)}, bf16[64,1024]{1,0:T(8,128)(2,1)S(1)}, u32[]{:S(2)}, u32[]{:S(2)}) collective-permute-start(bf16[64,1024]{1,0:T(8,128)(2,1)S(1)} %collective-permute-done.3), channel_id=1, source_target_pairs={{0,32},{32,64},{64,96},{96,0},{1,33},{33,65},{65,97},{97,1},{2,34}... | collective-permute-start | bytes 393224 | tf_op jit(solution)/shard_map/ppermute | solution.py:28
  104.3 5.4 %fusion.11 = bf16[1024,1024]{1,0:T(8,128)(2,1)} fusion(bf16[1024,1024]{1,0:T(8,128)(2,1)S(1)} %bitcast.61, bf16[1,2048,1024]{1,2,0:T(8,128)(2,1)} %all-gather.5.cloned.1.call-done, s32[]{:T(128)S(6)} %select_n.190), kind=kOutput, calls=%fused_computation.17 | convolution fusion | flops 2148532224 | bytes 6291460 | tf_op jit(solution)/shard_map/dot_general | solution.py:72
  111.4 2.5 %gather_fusion.2 = bf16[4,64,1024]{2,1,0:T(8,128)(2,1)} fusion(bf16[4,64,1024]{2,1,0:T(8,128)(2,1)} %pad_maximum_fusion.1, s32[1024]{0:T(1024)S(1)} %pad_clamp_fusion.4), kind=kCustom, calls=%fused_computation.2 | custom fusion | bytes 1048592 | tf_op jit(solution)/shard_map/gather | solution.py:39
  113.8 2.5 %gather_fusion.3 = bf16[16,16,1024]{2,1,0:T(8,128)(2,1)} fusion(bf16[16,16,1024]{2,1,0:T(8,128)(2,1)} %bitcast.64, s32[1024]{0:T(1024)S(1)} %pad_clamp_fusion.3), kind=kCustom, calls=%fused_computation.3 | custom fusion | bytes 1048640 | tf_op jit(solution)/shard_map/gather | solution.py:111
  116.3 3.6 %convolution_subtract_fusion = bf16[1024,256]{0,1:T(8,128)(2,1)} fusion(f32[1024,256]{0,1:T(8,128)} %get-tuple-element.11, bf16[1024,1024]{1,0:T(8,128)(2,1)} %fusion.11, bf16[256,1024]{1,0:T(8,128)(2,1)} %bitcast.65), kind=kOutput, calls=%fused_computation.18 | convolution fusion | flops 537395200 | bytes 4194304 | tf_op jit(solution)/shard_map/dot_general | solution.py:15
  119.9 2.0 %copy.16 = bf16[1024,256]{1,0:T(8,128)(2,1)} copy(bf16[1024,256]{0,1:T(8,128)(2,1)} %convolution_subtract_fusion) | data formatting | bytes 1048576 | tf_op jit(solution)/shard_map/sub | solution.py:123
  121.9 2.5 %gather_fusion.6 = bf16[64,16,256]{2,1,0:T(8,128)(2,1)} fusion(bf16[64,16,256]{2,1,0:T(8,128)(2,1)} %bitcast.63, s32[1024]{0:T(1024)S(1)} %pad_clamp_fusion), kind=kCustom, calls=%fused_computation.6 | custom fusion | bytes 1048832 | tf_op jit(solution)/shard_map/gather | solution.py:128
  124.4 2.0 %collective-permute-start.6 = (bf16[1024,256]{1,0:T(8,128)(2,1)}, bf16[1024,256]{1,0:T(8,128)(2,1)}, u32[]{:S(2)}, u32[]{:S(2)}) collective-permute-start(bf16[1024,256]{1,0:T(8,128)(2,1)} %bitcast.67), channel_id=1, source_target_pairs={{0,128},{128,0},{256,384},{384,256},{1,129},{129,1},{257,385},{385... | collective-permute-start | bytes 1572872 | tf_op jit(solution)/shard_map/ppermute | solution.py:11
  126.4 4.6 %fusion.8 = bf16[1024,1024]{1,0:T(8,128)(2,1)S(1)} fusion(bf16[1024,1024]{1,0:T(8,128)(2,1)} %bitcast.60, bf16[1,2048,1024]{1,2,0:T(8,128)(2,1)} %all-gather.5.cloned.1.call-done, s32[]{:T(128)S(6)} %select_n.177), kind=kOutput, calls=%fused_computation.16 | convolution fusion | flops 2148532224 | bytes 6291460 | tf_op jit(solution)/shard_map/dot_general | solution.py:72
  132.8 2.5 %copy.14 = f32[1024,256]{1,0:T(8,128)} copy(f32[1024,256]{0,1:T(8,128)} %convolution_subtract_fusion.1) | data formatting | bytes 2097152 | tf_op jit(solution)/shard_map/sub | solution.py:123
  135.3 1.8 %gather_fusion.5 = f32[64,16,256]{2,1,0:T(8,128)S(1)} fusion(f32[64,16,256]{2,1,0:T(8,128)} %bitcast.62, s32[1024]{0:T(1024)S(1)} %pad_clamp_fusion.1), kind=kCustom, calls=%fused_computation.5 | custom fusion | bytes 2097408 | tf_op jit(solution)/shard_map/gather | solution.py:128
  137.2 2.2 %bitcast_add_fusion = f32[1024,256]{1,0:T(8,128)} fusion(f32[64,16,256]{2,1,0:T(8,128)S(1)} %gather_fusion.5, bf16[1024,256]{1,0:T(8,128)(2,1)} %collective-permute-done.6), kind=kLoop, calls=%fused_computation.21 | loop fusion | flops 524288 | bytes 2621440 | tf_op jit(solution)/shard_map/add | solution.py:135
  (38 shorter events, 12.2 us)
Async XLA Ops:
  6.5 68.8 %copy-start = (f32[1,2048,256]{2,1,0:T(8,128)S(1)}, f32[1,2048,256]{2,1,0:T(8,128)}, u32[]{:S(2)}) copy-start(f32[1,2048,256]{2,1,0:T(8,128)} %param.6) | copy-start | bytes 6291460
  6.5 85.3 %all-gather.5.cloned.1.call-start = ((), (), s32[]{:S(2)}) async-start(), calls=%async_computation | async-start | bytes 4325376 | tf_op jit(solution)/shard_map/all_gather | solution.py:63
  52.4 25.5 %collective-permute-start.2 = (bf16[256,1024]{1,0:T(8,128)(2,1)}, bf16[256,1024]{1,0:T(8,128)(2,1)}, u32[]{:S(2)}, u32[]{:S(2)}) collective-permute-start(bf16[256,1024]{1,0:T(8,128)(2,1)} %bitcast.5), channel_id=1, source_target_pairs={{0,96},{32,0},{64,32},{96,64},{1,97},{33,1},{65,33},{97,65},{2,98}... | collective-permute-start | bytes 1572872 | tf_op jit(solution)/shard_map/ppermute | solution.py:31
  56.8 15.7 %collective-permute-start = (bf16[256,1024]{1,0:T(8,128)(2,1)}, bf16[256,1024]{1,0:T(8,128)(2,1)}, u32[]{:S(2)}, u32[]{:S(2)}) collective-permute-start(bf16[256,1024]{1,0:T(8,128)(2,1)} %bitcast.5), channel_id=1, source_target_pairs={{0,32},{32,64},{64,96},{96,0},{1,33},{33,65},{65,97},{97,1},{2,34}... | collective-permute-start | bytes 1572872 | tf_op jit(solution)/shard_map/ppermute | solution.py:28
  72.5 12.6 %collective-permute-start.1 = (bf16[256,1024]{1,0:T(8,128)(2,1)}, bf16[256,1024]{1,0:T(8,128)(2,1)}, u32[]{:S(2)}, u32[]{:S(2)}) collective-permute-start(bf16[256,1024]{1,0:T(8,128)(2,1)} %collective-permute-done), channel_id=1, source_target_pairs={{0,32},{32,64},{64,96},{96,0},{1,33},{33,65},{65,97},{97,1},{2,34}... | collective-permute-start | bytes 1572872 | tf_op jit(solution)/shard_map/ppermute | solution.py:28
  91.9 12.4 %copy-start.1 = (bf16[4,256,1024]{2,1,0:T(8,128)(2,1)S(1)}, bf16[4,256,1024]{2,1,0:T(8,128)(2,1)}, u32[]{:S(2)}) copy-start(bf16[4,256,1024]{2,1,0:T(8,128)(2,1)} %gather_fusion.1) | copy-start | bytes 6291460
  94.3 8.1 %collective-permute-start.3 = (bf16[64,1024]{1,0:T(8,128)(2,1)S(1)}, bf16[64,1024]{1,0:T(8,128)(2,1)S(1)}, u32[]{:S(2)}, u32[]{:S(2)}) collective-permute-start(bf16[64,1024]{1,0:T(8,128)(2,1)S(1)} %convolution_convert_fusion), channel_id=1, source_target_pairs={{0,32},{32,64},{64,96},{96,0},{1,33},{33,65},{65,97},{97,1},{2,34}... | collective-permute-start | bytes 393224 | tf_op jit(solution)/shard_map/ppermute | solution.py:28
  96.3 13.4 %collective-permute-start.5 = (bf16[64,1024]{1,0:T(8,128)(2,1)S(1)}, bf16[64,1024]{1,0:T(8,128)(2,1)S(1)}, u32[]{:S(2)}, u32[]{:S(2)}) collective-permute-start(bf16[64,1024]{1,0:T(8,128)(2,1)S(1)} %convolution_convert_fusion), channel_id=1, source_target_pairs={{0,96},{32,0},{64,32},{96,64},{1,97},{33,1},{65,33},{97,65},{2,98}... | collective-permute-start | bytes 393224 | tf_op jit(solution)/shard_map/ppermute | solution.py:31
  102.4 8.1 %collective-permute-start.4 = (bf16[64,1024]{1,0:T(8,128)(2,1)S(1)}, bf16[64,1024]{1,0:T(8,128)(2,1)S(1)}, u32[]{:S(2)}, u32[]{:S(2)}) collective-permute-start(bf16[64,1024]{1,0:T(8,128)(2,1)S(1)} %collective-permute-done.3), channel_id=1, source_target_pairs={{0,32},{32,64},{64,96},{96,0},{1,33},{33,65},{65,97},{97,1},{2,34}... | collective-permute-start | bytes 393224 | tf_op jit(solution)/shard_map/ppermute | solution.py:28
  124.4 6.7 %copy-start.2 = (bf16[16,16,1024]{2,1,0:T(8,128)(2,1)S(1)}, bf16[16,16,1024]{2,1,0:T(8,128)(2,1)}, u32[]{:S(2)}) copy-start(bf16[16,16,1024]{2,1,0:T(8,128)(2,1)} %gather_fusion.3) | copy-start | bytes 1572868
  124.4 12.8 %collective-permute-start.6 = (bf16[1024,256]{1,0:T(8,128)(2,1)}, bf16[1024,256]{1,0:T(8,128)(2,1)}, u32[]{:S(2)}, u32[]{:S(2)}) collective-permute-start(bf16[1024,256]{1,0:T(8,128)(2,1)} %bitcast.67), channel_id=1, source_target_pairs={{0,128},{128,0},{256,384},{384,256},{1,129},{129,1},{257,385},{385... | collective-permute-start | bytes 1572872 | tf_op jit(solution)/shard_map/ppermute | solution.py:11
Sparse Core Ops, SparseCore 0:
  9.5 78.5 all-gather.4

commit v8 on v5

--- a/solution.py
+++ b/solution.py
@@ -39,6 +39,16 @@
     return stacked[(index - sources) % n]
 
 
+def direct_gather(value, axis, index, n):
+    held = [value]
+    for offset in range(1, n):
+        pairs = [(source, (source + offset) % n) for source in range(n)]
+        held.append(lax.ppermute(value, axis, pairs))
+    stacked = jnp.stack(held)
+    sources = jnp.arange(n, dtype=jnp.int32)
+    return stacked[(index - sources) % n]
+
+
 def local(inverse_factor, panel, trailing, extend_map):
     nrow = lax.axis_size("row")
     nz = lax.axis_size("z")
@@ -66,7 +76,7 @@
     cols_here = local_trailing.shape[1]
     share = rows_here // ncol
     piece = solve(lax.dynamic_slice_in_dim(columns, col_index * share, share, 0))
-    col_side = ring_gather(piece, "row", row_index, nrow)
+    col_side = direct_gather(piece, "row", row_index, nrow)
 
     block_map = extend_map[0]
     nblocks = block_map.shape[0]

time: 140 us -> 140 us (level)
  waiting for transfers between devices: 19.5 us -> 17.4 us
  starting transfers between devices: 20.3 us -> 22.3 us
    ppermute x0 -> x3, starting transfers between devices: none -> 9.57 us  [direct_gather(): held.append(lax.ppermute(value, axis, pairs))]
    ppermute x4 -> x2, starting transfers between devices: 9.83 us -> 5.58 us  [ring_gather(): forward = lax.ppermute(forward, axis, ahead)]
    ppermute x2 -> x1, starting transfers between devices: 7.41 us -> 3.65 us  [ring_gather(): backward = lax.ppermute(backward, axis, behind)]
    ppermute x4 -> x2, waiting for transfers between devices: 3.08 us -> 0.01 us  [ring_gather(): forward = lax.ppermute(forward, axis, ahead)]
    gather x2 -> x1, local copies, waits for them, and re-layouts: 2.85 us -> 2.27 us  [ring_gather(): return stacked[(index - sources) % n]]
  transfers between devices with their start and end apart: 8 -> 8, of which waited for: 4 -> 2; matrix products, arithmetic and copies ran while one was open for 26% -> 26% of each run, Pallas kernels for 0% -> 0%
where the time goes in v8:
time: 140 us; the launch traced here: 137 us
  blocking collectives  40.4 us (29%)
  starting transfers between devices  22.3 us (16%)
  waiting for transfers between devices  17.4 us (12%)
  other arithmetic  16.8 us (12%)
  matrix products  16.7 us (12%)
  between operations  13.7 us (10%)
  local copies, waits for them, and re-layouts  9.99 us (7%)
    all_gather x1, blocking collectives, local(): inverse = lax.all_gather(inverse, 'z', axis=0, tiled=True)  38.4 us
    dot_general x3, matrix products, solve(): jnp.dot(rows, inverse, preferred_element_type=jnp.float32)  10.8 us
    ppermute x3, starting transfers between devices, direct_gather(): held.append(lax.ppermute(value, axis, pairs))  9.57 us
    all_gather x1, waiting for transfers between devices, local(): columns = lax.all_gather(panel[0], ('z', 'core'), axis=1, tiled=True)  8.55 us
    ppermute x1, waiting for transfers between devices, from_partner(): return lax.ppermute(value, axis, pairs)  8.11 us
    add x1, other arithmetic, local(): picked = gather_col[lane // width] * width + lane % width  5.66 us
    ppermute x2, starting transfers between devices, ring_gather(): forward = lax.ppermute(forward, axis, ahead)  5.58 us
    dot_general x2, matrix products, outer_rows(): lax.dot_general(left, right, (((1,), (1,)), ((), ())), preferred_element_...  4.67 us
  transfers between devices with their start and end apart: 8, of which 2 were waited for; matrix products, arithmetic and copies ran while one was open for 26% of the time, Pallas kernels for 0%

profile of v8, /device:TPU:24, one launch (start us, length us, event | category | flops | bytes accessed | tf_op | source)
XLA Modules:
  0.0 137.4 jit_solution(3528086649519723305)
XLA Ops:
  7.3 2.0 %all-gather.1 = bf16[1,16,1024]{2,1,0:T(8,128)(2,1)S(1)} all-gather(bf16[1,8,1024]{2,1,0:T(8,128)(2,1)} %param.4), channel_id=3, replica_groups=mesh['front'=4,'row'=4,'z'=16,'core'=2] {'core'}, dimensions={1}, use_global_device_ids=true | all-gather | bytes 49152 | tf_op jit(solution)/shard_map/all_gather | solution.py:61
  9.3 38.4 %all-gather.2 = bf16[1,256,1024]{2,1,0:T(8,128)(2,1)S(1)} all-gather(bf16[1,16,1024]{2,1,0:T(8,128)(2,1)S(1)} %all-gather.1), channel_id=4, replica_groups=mesh['front'=4,'row'=4,'z'=16,'core'=2] {'z'}, dimensions={1}, use_global_device_ids=true | all-gather | bytes 557056 | tf_op jit(solution)/shard_map/all_gather | solution.py:62
  47.7 3.4 %collective-permute-start = (bf16[256,1024]{1,0:T(8,128)(2,1)S(1)}, bf16[256,1024]{1,0:T(8,128)(2,1)S(1)}, u32[]{:S(2)}, u32[]{:S(2)}) collective-permute-start(bf16[256,1024]{1,0:T(8,128)(2,1)S(1)} %bitcast.75), channel_id=1, source_target_pairs={{0,32},{32,64},{64,96},{96,0},{1,33},{33,65},{65,97},{97,1},{2,34}... | collective-permute-start | bytes 1572872 | tf_op jit(solution)/shard_map/ppermute | solution.py:28
  51.1 3.7 %collective-permute-start.2 = (bf16[256,1024]{1,0:T(8,128)(2,1)S(1)}, bf16[256,1024]{1,0:T(8,128)(2,1)S(1)}, u32[]{:S(2)}, u32[]{:S(2)}) collective-permute-start(bf16[256,1024]{1,0:T(8,128)(2,1)S(1)} %bitcast.76), channel_id=1, source_target_pairs={{0,96},{32,0},{64,32},{96,64},{1,97},{33,1},{65,33},{97,65},{2,98}... | collective-permute-start | bytes 1572872 | tf_op jit(solution)/shard_map/ppermute | solution.py:31
  54.8 1.3 gather_fusion.4
  56.8 2.5 %sort.35 = (s32[128]{0:T(128)}, s32[128]{0:T(128)S(1)}) sort(s32[128]{0:T(128)S(1)} %fusion.28, s32[128]{0:T(128)S(1)} %iota.47), dimensions={0}, to_apply=%region_1.2 | sort | flops 896 | bytes 2048 | tf_op jit(solution)/shard_map/jit(argsort)/sort | solution.py:90
  59.3 1.2 sort.34
  61.5 2.2 %collective-permute-start.1 = (bf16[256,1024]{1,0:T(8,128)(2,1)S(1)}, bf16[256,1024]{1,0:T(8,128)(2,1)S(1)}, u32[]{:S(2)}, u32[]{:S(2)}) collective-permute-start(bf16[256,1024]{1,0:T(8,128)(2,1)S(1)} %collective-permute-done), channel_id=1, source_target_pairs={{0,32},{32,64},{64,96},{96,0},{1,33},{33,65},{65,97},{97,1},{2,34}... | collective-permute-start | bytes 1572872 | tf_op jit(solution)/shard_map/ppermute | solution.py:28
  63.7 4.3 %compare_select_fusion.1 = s32[256,1]{0,1:T(1,128)S(1)} fusion(s32[]{:T(128)} %bitcast.19, s32[]{:T(128)} %bitcast.20, s32[]{:T(128)} %bitcast.21, s32[]{:T(128)} %bitcast.22, s32[]{:T(128)} %bitcast.23, s32[]{:T(128)} %bitcast.25, s32[]{:T(128)} %bitcast.24), kind=kLoop, calls=%fused_computation.44 | loop fusion | flops 5888 | bytes 1052 | tf_op jit(solution)/shard_map/gather | solution.py:102
  68.2 2.7 %dynamic-slice_bitcast_fusion = (f32[1024,256]{1,0:T(8,128)S(1)}, f32[1024,256]{1,0:T(8,128)}) fusion(f32[1,2048,256]{2,1,0:T(8,128)} %param.6, s32[]{:T(128)S(6)} %select_n.192, s32[]{:T(128)S(6)} %select_n.172), kind=kLoop, calls=%fused_computation.20 | loop fusion | bytes 4194312 | tf_op jit(solution)/shard_map/dynamic_slice | solution.py:110
  70.8 5.7 %fusion.19 = s32[256]{0:T(256)S(1)} fusion(pred[256]{0:T(512)(128)(4,1)S(1)} %get-tuple-element.37, pred[256]{0:T(512)(128)(4,1)S(1)} %get-tuple-element.38, pred[256]{0:T(512)(128)(4,1)S(1)} %get-tuple-element.39, pred[256]{0:T(512)(128)(4,1)S(1)} %get-tuple-element.40, pred[256]{0:T(512)(128)(4,1)S(1)} %get-tuple-element.41, ...), kind=kLoop, calls=%fused_computation.81 | loop fusion | flops 4352 | bytes 4388 | tf_op jit(solution)/shard_map/add | solution.py:102
  76.5 1.6 %pad_maximum_fusion = bf16[4,256,1024]{2,1,0:T(8,128)(2,1)} fusion(bf16[1,256,1024]{2,1,0:T(8,128)(2,1)S(1)} %bitcast.81, bf16[1,256,1024]{2,1,0:T(8,128)(2,1)S(1)} %bitcast.82, bf16[1,256,1024]{2,1,0:T(8,128)(2,1)S(1)} %bitcast.80, bf16[1,256,1024]{2,1,0:T(8,128)(2,1)S(1)} %all-gather.2), kind=kLoop, calls=%fused_computation.7 | loop fusion | flops 3145728 | bytes 4194304 | tf_op jit(solution)/shard_map/stack | solution.py:37
  78.1 2.3 %gather_fusion = bf16[4,256,1024]{2,1,0:T(8,128)(2,1)S(1)} fusion(bf16[4,256,1024]{2,1,0:T(8,128)(2,1)} %pad_maximum_fusion, s32[1024]{0:T(1024)S(1)} %pad_clamp_fusion.5), kind=kCustom, calls=%fused_computation | custom fusion | bytes 4194320 | tf_op jit(solution)/shard_map/gather | solution.py:39
  80.4 8.6 %all-gather.5.cloned.1.call-done = bf16[1,2048,1024]{1,2,0:T(8,128)(2,1)} async-done(((bf16[1,2048,32]{1,2,0:T(8,128)(2,1)}), bf16[1,2048,1024]{1,2,0:T(8,128)(2,1)}) %all-gather.5.cloned.1.call-update) | async-done | bytes 4194320 | tf_op jit(solution)/shard_map/all_gather | solution.py:67
  88.9 1.6 %convolution_convert_fusion = bf16[64,1024]{1,0:T(8,128)(2,1)S(1)} fusion(bf16[1024,1024]{1,0:T(8,128)(2,1)S(1)} %bitcast.69, bf16[1,2048,1024]{1,2,0:T(8,128)(2,1)} %all-gather.5.cloned.1.call-done, s32[]{:T(128)S(6)} %select_n.183), kind=kOutput, calls=%fused_computation.18 | convolution fusion | flops 134283264 | bytes 2490372 | tf_op jit(solution)/shard_map/dot_general | solution.py:70
  90.5 3.8 %collective-permute-start.5 = (bf16[64,1024]{1,0:T(8,128)(2,1)S(1)}, bf16[64,1024]{1,0:T(8,128)(2,1)S(1)}, u32[]{:S(2)}, u32[]{:S(2)}) collective-permute-start(bf16[64,1024]{1,0:T(8,128)(2,1)S(1)} %convolution_convert_fusion), channel_id=1, source_target_pairs={{0,96},{32,0},{64,32},{96,64},{1,97},{33,1},{65,33},{97,65},{2,98}... | collective-permute-start | bytes 393224 | tf_op jit(solution)/shard_map/ppermute | solution.py:46
  94.3 2.6 %collective-permute-start.4 = (bf16[64,1024]{1,0:T(8,128)(2,1)S(1)}, bf16[64,1024]{1,0:T(8,128)(2,1)S(1)}, u32[]{:S(2)}, u32[]{:S(2)}) collective-permute-start(bf16[64,1024]{1,0:T(8,128)(2,1)S(1)} %convolution_convert_fusion), channel_id=1, source_target_pairs={{0,64},{32,96},{64,0},{96,32},{1,65},{33,97},{65,1},{97,33},{2,66}... | collective-permute-start | bytes 393224 | tf_op jit(solution)/shard_map/ppermute | solution.py:46
  96.9 3.2 %collective-permute-start.3 = (bf16[64,1024]{1,0:T(8,128)(2,1)S(1)}, bf16[64,1024]{1,0:T(8,128)(2,1)S(1)}, u32[]{:S(2)}, u32[]{:S(2)}) collective-permute-start(bf16[64,1024]{1,0:T(8,128)(2,1)S(1)} %convolution_convert_fusion), channel_id=1, source_target_pairs={{0,32},{32,64},{64,96},{96,0},{1,33},{33,65},{65,97},{97,1},{2,34}... | collective-permute-start | bytes 393224 | tf_op jit(solution)/shard_map/ppermute | solution.py:46
  100.1 5.4 %fusion.9 = bf16[1024,1024]{1,0:T(8,128)(2,1)} fusion(bf16[1024,1024]{1,0:T(8,128)(2,1)S(1)} %bitcast.70, bf16[1,2048,1024]{1,2,0:T(8,128)(2,1)} %all-gather.5.cloned.1.call-done, s32[]{:T(128)S(6)} %select_n.192), kind=kOutput, calls=%fused_computation.15 | convolution fusion | flops 2148532224 | bytes 6291460 | tf_op jit(solution)/shard_map/dot_general | solution.py:70
  105.5 3.8 %fusion.6 = bf16[1024,1024]{1,0:T(8,128)(2,1)} fusion(bf16[1024,1024]{1,0:T(8,128)(2,1)S(1)} %bitcast.71, bf16[1,2048,1024]{1,2,0:T(8,128)(2,1)S(1)} %copy-done.2, s32[]{:T(128)S(6)} %select_n.172), kind=kOutput, calls=%fused_computation.14 | convolution fusion | flops 2148532224 | bytes 6291460 | tf_op jit(solution)/shard_map/dot_general | solution.py:70
  110.6 2.3 %fusion.38 = f32[1024,256]{1,0:T(8,128)S(1)} fusion(bf16[1024,1024]{1,0:T(8,128)(2,1)} %fusion.9, bf16[256,1024]{1,0:T(8,128)(2,1)S(1)} %bitcast.77), kind=kOutput, calls=%fused_computation.112 | convolution fusion | flops 536870912 | bytes 3670016 | tf_op jit(solution)/shard_map/dot_general | solution.py:15
  114.2 3.5 %collective-permute-start.6 = (bf16[1024,256]{1,0:T(8,128)(2,1)S(1)}, bf16[1024,256]{1,0:T(8,128)(2,1)S(1)}, u32[]{:S(2)}, u32[]{:S(2)}) collective-permute-start(bf16[1024,256]{1,0:T(8,128)(2,1)S(1)} %bitcast.79), channel_id=1, source_target_pairs={{0,128},{128,0},{256,384},{384,256},{1,129},{129,1},{257,385},{385... | collective-permute-start | bytes 1572872 | tf_op jit(solution)/shard_map/ppermute | solution.py:11
  117.7 2.3 %fusion.37 = f32[1024,256]{1,0:T(8,128)S(1)} fusion(bf16[1024,1024]{1,0:T(8,128)(2,1)} %fusion.6, bf16[256,1024]{1,0:T(8,128)(2,1)S(1)} %bitcast.78), kind=kOutput, calls=%fused_computation.111 | convolution fusion | flops 536870912 | bytes 3670016 | tf_op jit(solution)/shard_map/dot_general | solution.py:15
  121.3 8.1 %collective-permute-done.6 = bf16[1024,256]{1,0:T(8,128)(2,1)S(1)} collective-permute-done((bf16[1024,256]{1,0:T(8,128)(2,1)S(1)}, bf16[1024,256]{1,0:T(8,128)(2,1)S(1)}, u32[]{:S(2)}, u32[]{:S(2)}) %collective-permute-start.6) | collective-permute-done | bytes 524320 | tf_op jit(solution)/shard_map/ppermute | solution.py:11
  (44 shorter events, 7.3 us)
Async XLA Ops:
  6.5 48.2 %copy-start = (s32[1,512]{1,0:T(1,128)S(1)}, s32[1,512]{1,0:T(1,128)}, u32[]{:S(2)}) copy-start(s32[1,512]{1,0:T(1,128)} %param.7) | copy-start | bytes 6148
  6.5 82.4 %all-gather.5.cloned.1.call-start = ((), (), s32[]{:S(2)}) async-start(), calls=%async_computation | async-start | bytes 4325376 | tf_op jit(solution)/shard_map/all_gather | solution.py:67
  47.7 13.8 %collective-permute-start = (bf16[256,1024]{1,0:T(8,128)(2,1)S(1)}, bf16[256,1024]{1,0:T(8,128)(2,1)S(1)}, u32[]{:S(2)}, u32[]{:S(2)}) collective-permute-start(bf16[256,1024]{1,0:T(8,128)(2,1)S(1)} %bitcast.75), channel_id=1, source_target_pairs={{0,32},{32,64},{64,96},{96,0},{1,33},{33,65},{65,97},{97,1},{2,34}... | collective-permute-start | bytes 1572872 | tf_op jit(solution)/shard_map/ppermute | solution.py:28
  51.1 25.4 %collective-permute-start.2 = (bf16[256,1024]{1,0:T(8,128)(2,1)S(1)}, bf16[256,1024]{1,0:T(8,128)(2,1)S(1)}, u32[]{:S(2)}, u32[]{:S(2)}) collective-permute-start(bf16[256,1024]{1,0:T(8,128)(2,1)S(1)} %bitcast.76), channel_id=1, source_target_pairs={{0,96},{32,0},{64,32},{96,64},{1,97},{33,1},{65,33},{97,65},{2,98}... | collective-permute-start | bytes 1572872 | tf_op jit(solution)/shard_map/ppermute | solution.py:31
  61.5 15.0 %collective-permute-start.1 = (bf16[256,1024]{1,0:T(8,128)(2,1)S(1)}, bf16[256,1024]{1,0:T(8,128)(2,1)S(1)}, u32[]{:S(2)}, u32[]{:S(2)}) collective-permute-start(bf16[256,1024]{1,0:T(8,128)(2,1)S(1)} %collective-permute-done), channel_id=1, source_target_pairs={{0,32},{32,64},{64,96},{96,0},{1,33},{33,65},{65,97},{97,1},{2,34}... | collective-permute-start | bytes 1572872 | tf_op jit(solution)/shard_map/ppermute | solution.py:28
  90.5 15.0 %copy-start.2 = (bf16[1,2048,1024]{1,2,0:T(8,128)(2,1)S(1)}, bf16[1,2048,1024]{1,2,0:T(8,128)(2,1)}, u32[]{:S(2)}) copy-start(bf16[1,2048,1024]{1,2,0:T(8,128)(2,1)} %all-gather.5.cloned.1.call-done) | copy-start | bytes 12582916
  90.5 18.8 %collective-permute-start.5 = (bf16[64,1024]{1,0:T(8,128)(2,1)S(1)}, bf16[64,1024]{1,0:T(8,128)(2,1)S(1)}, u32[]{:S(2)}, u32[]{:S(2)}) collective-permute-start(bf16[64,1024]{1,0:T(8,128)(2,1)S(1)} %convolution_convert_fusion), channel_id=1, source_target_pairs={{0,96},{32,0},{64,32},{96,64},{1,97},{33,1},{65,33},{97,65},{2,98}... | collective-permute-start | bytes 393224 | tf_op jit(solution)/shard_map/ppermute | solution.py:46
  94.3 15.0 %collective-permute-start.4 = (bf16[64,1024]{1,0:T(8,128)(2,1)S(1)}, bf16[64,1024]{1,0:T(8,128)(2,1)S(1)}, u32[]{:S(2)}, u32[]{:S(2)}) collective-permute-start(bf16[64,1024]{1,0:T(8,128)(2,1)S(1)} %convolution_convert_fusion), channel_id=1, source_target_pairs={{0,64},{32,96},{64,0},{96,32},{1,65},{33,97},{65,1},{97,33},{2,66}... | collective-permute-start | bytes 393224 | tf_op jit(solution)/shard_map/ppermute | solution.py:46
  96.9 12.4 %collective-permute-start.3 = (bf16[64,1024]{1,0:T(8,128)(2,1)S(1)}, bf16[64,1024]{1,0:T(8,128)(2,1)S(1)}, u32[]{:S(2)}, u32[]{:S(2)}) collective-permute-start(bf16[64,1024]{1,0:T(8,128)(2,1)S(1)} %convolution_convert_fusion), channel_id=1, source_target_pairs={{0,32},{32,64},{64,96},{96,0},{1,33},{33,65},{65,97},{97,1},{2,34}... | collective-permute-start | bytes 393224 | tf_op jit(solution)/shard_map/ppermute | solution.py:46
  114.2 5.9 %copy-start.1 = (f32[1024,256]{1,0:T(8,128)S(1)}, f32[1024,256]{1,0:T(8,128)}, u32[]{:S(2)}) copy-start(f32[1024,256]{1,0:T(8,128)} %get-tuple-element.11) | copy-start | bytes 3145732
  114.2 15.3 %collective-permute-start.6 = (bf16[1024,256]{1,0:T(8,128)(2,1)S(1)}, bf16[1024,256]{1,0:T(8,128)(2,1)S(1)}, u32[]{:S(2)}, u32[]{:S(2)}) collective-permute-start(bf16[1024,256]{1,0:T(8,128)(2,1)S(1)} %bitcast.79), channel_id=1, source_target_pairs={{0,128},{128,0},{256,384},{384,256},{1,129},{129,1},{257,385},{385... | collective-permute-start | bytes 1572872 | tf_op jit(solution)/shard_map/ppermute | solution.py:11
Sparse Core Ops, SparseCore 0:
  9.5 79.4 all-gather.4

commit v9 on v8

--- a/solution.py
+++ b/solution.py
@@ -106,9 +106,12 @@
     half = rows_here // 2
     half_blocks = half // width
 
-    def half_update(which):
+    def half_update(which, after=None):
         rows = lax.dynamic_slice_in_dim(local_trailing, which * half, half, 0)
-        low = solve(lax.dynamic_slice_in_dim(columns, which * half, half, 0))
+        own = lax.dynamic_slice_in_dim(columns, which * half, half, 0)
+        if after is not None:
+            own, _ = lax.optimization_barrier((own, after))
+        low = solve(own)
         rows, low = lax.optimization_barrier((rows, low))
         moved_cols = jnp.dot(
             rows,
@@ -127,7 +130,7 @@
 
     outgoing = half_update(1 - member).astype(jnp.bfloat16)
     incoming = from_partner(outgoing, "front", 0)
-    keep = half_update(member)
+    keep = half_update(member, outgoing)
     return (keep + incoming.astype(jnp.float32))[None]
 
 

time: 140 us -> 147 us (1.050)
  the two profiles are of different devices: /device:TPU:24 before, /device:TPU:2 now
where the time goes in v9:
time: 147 us; the launch traced here: 146 us
  blocking collectives  40.4 us (27%)
  starting transfers between devices  23.5 us (16%)
  other arithmetic  18.8 us (13%)
  local copies, waits for them, and re-layouts  17.6 us (12%)
  matrix products  16.2 us (11%)
  waiting for transfers between devices  15.7 us (11%)
  between operations  13.7 us (9%)
    all_gather x1, blocking collectives, local(): inverse = lax.all_gather(inverse, 'z', axis=0, tiled=True)  38.4 us
    dot_general x3, matrix products, solve(): jnp.dot(rows, inverse, preferred_element_type=jnp.float32)  11 us
    ppermute x3, starting transfers between devices, direct_gather(): held.append(lax.ppermute(value, axis, pairs))  10.8 us
    all_gather x1, waiting for transfers between devices, local(): columns = lax.all_gather(panel[0], ('z', 'core'), axis=1, tiled=True)  9.45 us
    ppermute x2, starting transfers between devices, ring_gather(): forward = lax.ppermute(forward, axis, ahead)  6.79 us
    add x1, other arithmetic, local(): picked = gather_col[lane // width] * width + lane % width  5.65 us
    ppermute x1, waiting for transfers between devices, from_partner(): return lax.ppermute(value, axis, pairs)  5.52 us
    gather x6, other arithmetic, local(): picked = gather_col[lane // width] * width + lane % width  4.48 us
  transfers between devices with their start and end apart: 8, of which 2 were waited for; matrix products, arithmetic and copies ran while one was open for 25% of the time, Pallas kernels for 0%

profile of v9, /device:TPU:2, one launch (start us, length us, event | category | flops | bytes accessed | tf_op | source)
XLA Modules:
  0.0 145.8 jit_solution(445260705129007054)
XLA Ops:
  7.3 2.0 %all-gather.1 = bf16[1,16,1024]{2,1,0:T(8,128)(2,1)S(1)} all-gather(bf16[1,8,1024]{2,1,0:T(8,128)(2,1)} %param.4), channel_id=3, replica_groups=mesh['front'=4,'row'=4,'z'=16,'core'=2] {'core'}, dimensions={1}, use_global_device_ids=true | all-gather | bytes 49152 | tf_op jit(solution)/shard_map/all_gather | solution.py:61
  9.3 38.4 %all-gather.2 = bf16[1,256,1024]{2,1,0:T(8,128)(2,1)S(1)} all-gather(bf16[1,16,1024]{2,1,0:T(8,128)(2,1)S(1)} %all-gather.1), channel_id=4, replica_groups=mesh['front'=4,'row'=4,'z'=16,'core'=2] {'z'}, dimensions={1}, use_global_device_ids=true | all-gather | bytes 557056 | tf_op jit(solution)/shard_map/all_gather | solution.py:62
  47.7 3.4 %collective-permute-start = (bf16[256,1024]{1,0:T(8,128)(2,1)S(1)}, bf16[256,1024]{1,0:T(8,128)(2,1)S(1)}, u32[]{:S(2)}, u32[]{:S(2)}) collective-permute-start(bf16[256,1024]{1,0:T(8,128)(2,1)S(1)} %bitcast.73), channel_id=1, source_target_pairs={{0,32},{32,64},{64,96},{96,0},{1,33},{33,65},{65,97},{97,1},{2,34}... | collective-permute-start | bytes 1572872 | tf_op jit(solution)/shard_map/ppermute | solution.py:28
  51.1 2.4 %collective-permute-start.2 = (bf16[256,1024]{1,0:T(8,128)(2,1)S(1)}, bf16[256,1024]{1,0:T(8,128)(2,1)S(1)}, u32[]{:S(2)}, u32[]{:S(2)}) collective-permute-start(bf16[256,1024]{1,0:T(8,128)(2,1)S(1)} %bitcast.74), channel_id=1, source_target_pairs={{0,96},{32,0},{64,32},{96,64},{1,97},{33,1},{65,33},{97,65},{2,98}... | collective-permute-start | bytes 1572872 | tf_op jit(solution)/shard_map/ppermute | solution.py:31
  55.6 2.5 %sort.35 = (s32[128]{0:T(128)}, s32[128]{0:T(128)S(1)}) sort(s32[128]{0:T(128)S(1)} %fusion.21, s32[128]{0:T(128)S(1)} %iota.47), dimensions={0}, to_apply=%region_1.2 | sort | flops 896 | bytes 2048 | tf_op jit(solution)/shard_map/jit(argsort)/sort | solution.py:90
  60.3 3.4 %collective-permute-start.1 = (bf16[256,1024]{1,0:T(8,128)(2,1)S(1)}, bf16[256,1024]{1,0:T(8,128)(2,1)S(1)}, u32[]{:S(2)}, u32[]{:S(2)}) collective-permute-start(bf16[256,1024]{1,0:T(8,128)(2,1)S(1)} %collective-permute-done), channel_id=1, source_target_pairs={{0,32},{32,64},{64,96},{96,0},{1,33},{33,65},{65,97},{97,1},{2,34}... | collective-permute-start | bytes 1572872 | tf_op jit(solution)/shard_map/ppermute | solution.py:28
  63.7 4.3 %compare_select_fusion.1 = s32[256,1]{0,1:T(1,128)S(1)} fusion(s32[]{:T(128)} %bitcast.21, s32[]{:T(128)} %bitcast.22, s32[]{:T(128)} %bitcast.23, s32[]{:T(128)} %bitcast.24, s32[]{:T(128)} %bitcast.25, s32[]{:T(128)} %bitcast.27, s32[]{:T(128)} %bitcast.26), kind=kLoop, calls=%fused_computation.42 | loop fusion | flops 5888 | bytes 1052 | tf_op jit(solution)/shard_map/gather | solution.py:102
  68.2 2.7 %dynamic-slice_bitcast_fusion.1 = (f32[1024,256]{1,0:T(8,128)S(1)}, f32[1024,256]{1,0:T(8,128)}) fusion(f32[1,2048,256]{2,1,0:T(8,128)} %param.6, s32[]{:T(128)S(6)} %select_n.173, s32[]{:T(128)S(6)} %select_n.172), kind=kLoop, calls=%fused_computation.18 | loop fusion | bytes 4194312 | tf_op jit(solution)/shard_map/dynamic_slice | solution.py:110
  70.8 5.7 %fusion.12 = s32[256]{0:T(256)S(1)} fusion(pred[256]{0:T(512)(128)(4,1)S(1)} %get-tuple-element.39, pred[256]{0:T(512)(128)(4,1)S(1)} %get-tuple-element.40, pred[256]{0:T(512)(128)(4,1)S(1)} %get-tuple-element.41, pred[256]{0:T(512)(128)(4,1)S(1)} %get-tuple-element.42, pred[256]{0:T(512)(128)(4,1)S(1)} %get-tuple-element.43, ...), kind=kLoop, calls=%fused_computation.78 | loop fusion | flops 4352 | bytes 4388 | tf_op jit(solution)/shard_map/add | solution.py:102
  76.5 1.6 %pad_maximum_fusion = bf16[4,256,1024]{2,1,0:T(8,128)(2,1)} fusion(bf16[1,256,1024]{2,1,0:T(8,128)(2,1)S(1)} %bitcast.78, bf16[1,256,1024]{2,1,0:T(8,128)(2,1)S(1)} %bitcast.79, bf16[1,256,1024]{2,1,0:T(8,128)(2,1)S(1)} %bitcast.77, bf16[1,256,1024]{2,1,0:T(8,128)(2,1)S(1)} %all-gather.2), kind=kLoop, calls=%fused_computation.7 | loop fusion | flops 3145728 | bytes 4194304 | tf_op jit(solution)/shard_map/stack | solution.py:37
  78.1 2.3 %gather_fusion = bf16[4,256,1024]{2,1,0:T(8,128)(2,1)S(1)} fusion(bf16[4,256,1024]{2,1,0:T(8,128)(2,1)} %pad_maximum_fusion, s32[1024]{0:T(1024)S(1)} %pad_clamp_fusion.5), kind=kCustom, calls=%fused_computation | custom fusion | bytes 4194320 | tf_op jit(solution)/shard_map/gather | solution.py:39
  80.4 9.5 %all-gather.5.cloned.1.call-done = bf16[1,2048,1024]{1,2,0:T(8,128)(2,1)} async-done(((bf16[1,2048,32]{1,2,0:T(8,128)(2,1)}), bf16[1,2048,1024]{1,2,0:T(8,128)(2,1)}) %all-gather.5.cloned.1.call-update) | async-done | bytes 4194320 | tf_op jit(solution)/shard_map/all_gather | solution.py:67
  91.4 2.2 %collective-permute-start.5 = (bf16[64,1024]{1,0:T(8,128)(2,1)S(1)}, bf16[64,1024]{1,0:T(8,128)(2,1)S(1)}, u32[]{:S(2)}, u32[]{:S(2)}) collective-permute-start(bf16[64,1024]{1,0:T(8,128)(2,1)S(1)} %convolution_convert_fusion.1), channel_id=1, source_target_pairs={{0,96},{32,0},{64,32},{96,64},{1,97},{33,1},{65,33},{97,65},{2,98}... | collective-permute-start | bytes 393224 | tf_op jit(solution)/shard_map/ppermute | solution.py:46
  93.6 4.6 %collective-permute-start.4 = (bf16[64,1024]{1,0:T(8,128)(2,1)S(1)}, bf16[64,1024]{1,0:T(8,128)(2,1)S(1)}, u32[]{:S(2)}, u32[]{:S(2)}) collective-permute-start(bf16[64,1024]{1,0:T(8,128)(2,1)S(1)} %convolution_convert_fusion.1), channel_id=1, source_target_pairs={{0,64},{32,96},{64,0},{96,32},{1,65},{33,97},{65,1},{97,33},{2,66}... | collective-permute-start | bytes 393224 | tf_op jit(solution)/shard_map/ppermute | solution.py:46
  98.2 4.1 %collective-permute-start.3 = (bf16[64,1024]{1,0:T(8,128)(2,1)S(1)}, bf16[64,1024]{1,0:T(8,128)(2,1)S(1)}, u32[]{:S(2)}, u32[]{:S(2)}) collective-permute-start(bf16[64,1024]{1,0:T(8,128)(2,1)S(1)} %convolution_convert_fusion.1), channel_id=1, source_target_pairs={{0,32},{32,64},{64,96},{96,0},{1,33},{33,65},{65,97},{97,1},{2,34}... | collective-permute-start | bytes 393224 | tf_op jit(solution)/shard_map/ppermute | solution.py:46
  102.3 5.4 %fusion.3 = bf16[1024,1024]{1,0:T(8,128)(2,1)} fusion(bf16[1024,1024]{1,0:T(8,128)(2,1)S(1)} %bitcast.68, bf16[1,2048,1024]{1,2,0:T(8,128)(2,1)} %all-gather.5.cloned.1.call-done, s32[]{:T(128)S(6)} %select_n.173), kind=kOutput, calls=%fused_computation.12 | convolution fusion | flops 2148532224 | bytes 6291460 | tf_op jit(solution)/shard_map/dot_general | solution.py:70
  110.1 2.4 %gather_fusion.2 = bf16[4,64,1024]{2,1,0:T(8,128)(2,1)} fusion(bf16[4,64,1024]{2,1,0:T(8,128)(2,1)} %pad_maximum_fusion.1, s32[1024]{0:T(1024)S(1)} %pad_clamp_fusion.5), kind=kCustom, calls=%fused_computation.2 | custom fusion | bytes 1048592 | tf_op jit(solution)/shard_map/gather | solution.py:49
  112.5 2.4 %gather_fusion.3 = bf16[16,16,1024]{2,1,0:T(8,128)(2,1)} fusion(bf16[16,16,1024]{2,1,0:T(8,128)(2,1)} %bitcast.72, s32[1024]{0:T(1024)S(1)} %pad_clamp_fusion.3), kind=kCustom, calls=%fused_computation.3 | custom fusion | bytes 1048640 | tf_op jit(solution)/shard_map/gather | solution.py:98
  114.9 2.4 %fusion.30 = f32[1024,256]{1,0:T(8,128)S(1)} fusion(bf16[1024,1024]{1,0:T(8,128)(2,1)} %fusion.3, bf16[256,1024]{1,0:T(8,128)(2,1)} %bitcast.75), kind=kOutput, calls=%fused_computation.108 | convolution fusion | flops 536870912 | bytes 3670016 | tf_op jit(solution)/shard_map/dot_general | solution.py:15
  118.8 2.4 %gather_fusion.5 = bf16[64,16,256]{2,1,0:T(8,128)(2,1)} fusion(bf16[64,16,256]{2,1,0:T(8,128)(2,1)} %bitcast.71, s32[1024]{0:T(1024)S(1)} %pad_clamp_fusion.1), kind=kCustom, calls=%fused_computation.5 | custom fusion | bytes 1048832 | tf_op jit(solution)/shard_map/gather | solution.py:127
  121.2 3.5 %collective-permute-start.6 = (bf16[1024,256]{1,0:T(8,128)(2,1)}, bf16[1024,256]{1,0:T(8,128)(2,1)}, u32[]{:S(2)}, u32[]{:S(2)}) collective-permute-start(bf16[1024,256]{1,0:T(8,128)(2,1)} %bitcast.38), channel_id=1, source_target_pairs={{0,128},{128,0},{256,384},{384,256},{1,129},{129,1},{257,385},{385... | collective-permute-start | bytes 1572872 | tf_op jit(solution)/shard_map/ppermute | solution.py:11
  124.7 4.0 %convolution_convert_fusion = bf16[1024,1024]{1,0:T(8,128)(2,1)S(1)} fusion(bf16[1024,1024]{0,1:T(8,128)(2,1)} %dynamic-slice_bitcast_fusion, bf16[1024,1024]{1,0:T(8,128)(2,1)S(1)} %bitcast.69), kind=kOutput, calls=%fused_computation.13 | convolution fusion | flops 2148532224 | bytes 6291456 | tf_op jit(solution)/shard_map/dot_general | solution.py:70
  131.3 5.5 %collective-permute-done.6 = bf16[1024,256]{1,0:T(8,128)(2,1)} collective-permute-done((bf16[1024,256]{1,0:T(8,128)(2,1)}, bf16[1024,256]{1,0:T(8,128)(2,1)}, u32[]{:S(2)}, u32[]{:S(2)}) %collective-permute-start.6) | collective-permute-done | bytes 524320 | tf_op jit(solution)/shard_map/ppermute | solution.py:11
  136.8 2.2 %bitcast_add_fusion = f32[1024,256]{1,0:T(8,128)} fusion(f32[64,16,256]{2,1,0:T(8,128)S(1)} %gather_fusion.6, bf16[1024,256]{1,0:T(8,128)(2,1)} %collective-permute-done.6), kind=kLoop, calls=%fused_computation.17 | loop fusion | flops 524288 | bytes 2621440 | tf_op jit(solution)/shard_map/add | solution.py:134
  (47 shorter events, 12.9 us)
Async XLA Ops:
  6.5 47.0 %copy-start = (s32[1,512]{1,0:T(1,128)S(1)}, s32[1,512]{1,0:T(1,128)}, u32[]{:S(2)}) copy-start(s32[1,512]{1,0:T(1,128)} %param.7) | copy-start | bytes 6148
  6.5 83.3 %all-gather.5.cloned.1.call-start = ((), (), s32[]{:S(2)}) async-start(), calls=%async_computation | async-start | bytes 4325376 | tf_op jit(solution)/shard_map/all_gather | solution.py:67
  47.7 12.6 %collective-permute-start = (bf16[256,1024]{1,0:T(8,128)(2,1)S(1)}, bf16[256,1024]{1,0:T(8,128)(2,1)S(1)}, u32[]{:S(2)}, u32[]{:S(2)}) collective-permute-start(bf16[256,1024]{1,0:T(8,128)(2,1)S(1)} %bitcast.73), channel_id=1, source_target_pairs={{0,32},{32,64},{64,96},{96,0},{1,33},{33,65},{65,97},{97,1},{2,34}... | collective-permute-start | bytes 1572872 | tf_op jit(solution)/shard_map/ppermute | solution.py:28
  51.1 25.4 %collective-permute-start.2 = (bf16[256,1024]{1,0:T(8,128)(2,1)S(1)}, bf16[256,1024]{1,0:T(8,128)(2,1)S(1)}, u32[]{:S(2)}, u32[]{:S(2)}) collective-permute-start(bf16[256,1024]{1,0:T(8,128)(2,1)S(1)} %bitcast.74), channel_id=1, source_target_pairs={{0,96},{32,0},{64,32},{96,64},{1,97},{33,1},{65,33},{97,65},{2,98}... | collective-permute-start | bytes 1572872 | tf_op jit(solution)/shard_map/ppermute | solution.py:31
  60.3 16.2 %collective-permute-start.1 = (bf16[256,1024]{1,0:T(8,128)(2,1)S(1)}, bf16[256,1024]{1,0:T(8,128)(2,1)S(1)}, u32[]{:S(2)}, u32[]{:S(2)}) collective-permute-start(bf16[256,1024]{1,0:T(8,128)(2,1)S(1)} %collective-permute-done), channel_id=1, source_target_pairs={{0,32},{32,64},{64,96},{96,0},{1,33},{33,65},{65,97},{97,1},{2,34}... | collective-permute-start | bytes 1572872 | tf_op jit(solution)/shard_map/ppermute | solution.py:28
  91.4 16.2 %copy-start.2 = (bf16[1,2048,1024]{1,2,0:T(8,128)(2,1)S(1)}, bf16[1,2048,1024]{1,2,0:T(8,128)(2,1)}, u32[]{:S(2)}) copy-start(bf16[1,2048,1024]{1,2,0:T(8,128)(2,1)} %all-gather.5.cloned.1.call-done) | copy-start | bytes 12582916
  91.4 17.8 %collective-permute-start.5 = (bf16[64,1024]{1,0:T(8,128)(2,1)S(1)}, bf16[64,1024]{1,0:T(8,128)(2,1)S(1)}, u32[]{:S(2)}, u32[]{:S(2)}) collective-permute-start(bf16[64,1024]{1,0:T(8,128)(2,1)S(1)} %convolution_convert_fusion.1), channel_id=1, source_target_pairs={{0,96},{32,0},{64,32},{96,64},{1,97},{33,1},{65,33},{97,65},{2,98}... | collective-permute-start | bytes 393224 | tf_op jit(solution)/shard_map/ppermute | solution.py:46
  93.6 15.6 %collective-permute-start.4 = (bf16[64,1024]{1,0:T(8,128)(2,1)S(1)}, bf16[64,1024]{1,0:T(8,128)(2,1)S(1)}, u32[]{:S(2)}, u32[]{:S(2)}) collective-permute-start(bf16[64,1024]{1,0:T(8,128)(2,1)S(1)} %convolution_convert_fusion.1), channel_id=1, source_target_pairs={{0,64},{32,96},{64,0},{96,32},{1,65},{33,97},{65,1},{97,33},{2,66}... | collective-permute-start | bytes 393224 | tf_op jit(solution)/shard_map/ppermute | solution.py:46
  98.2 11.0 %collective-permute-start.3 = (bf16[64,1024]{1,0:T(8,128)(2,1)S(1)}, bf16[64,1024]{1,0:T(8,128)(2,1)S(1)}, u32[]{:S(2)}, u32[]{:S(2)}) collective-permute-start(bf16[64,1024]{1,0:T(8,128)(2,1)S(1)} %convolution_convert_fusion.1), channel_id=1, source_target_pairs={{0,32},{32,64},{64,96},{96,0},{1,33},{33,65},{65,97},{97,1},{2,34}... | collective-permute-start | bytes 393224 | tf_op jit(solution)/shard_map/ppermute | solution.py:46
  121.2 7.5 %copy-start.3 = (bf16[16,16,1024]{2,1,0:T(8,128)(2,1)S(1)}, bf16[16,16,1024]{2,1,0:T(8,128)(2,1)}, u32[]{:S(2)}) copy-start(bf16[16,16,1024]{2,1,0:T(8,128)(2,1)} %gather_fusion.3) | copy-start | bytes 1572868
  121.2 15.6 %collective-permute-start.6 = (bf16[1024,256]{1,0:T(8,128)(2,1)}, bf16[1024,256]{1,0:T(8,128)(2,1)}, u32[]{:S(2)}, u32[]{:S(2)}) collective-permute-start(bf16[1024,256]{1,0:T(8,128)(2,1)} %bitcast.38), channel_id=1, source_target_pairs={{0,128},{128,0},{256,384},{384,256},{1,129},{129,1},{257,385},{385... | collective-permute-start | bytes 1572872 | tf_op jit(solution)/shard_map/ppermute | solution.py:11
  128.8 1.2 copy-start.1
Sparse Core Ops, SparseCore 0:
  9.5 80.3 all-gather.4

commit v10 on v5

--- a/solution.py
+++ b/solution.py
@@ -66,7 +66,9 @@
     cols_here = local_trailing.shape[1]
     share = rows_here // ncol
     piece = solve(lax.dynamic_slice_in_dim(columns, col_index * share, share, 0))
-    col_side = ring_gather(piece, "row", row_index, nrow)
+    col_side = lax.all_to_all(
+        jnp.broadcast_to(piece[None], (nrow,) + piece.shape), "row", 0, 0, tiled=True
+    )
 
     block_map = extend_map[0]
     nblocks = block_map.shape[0]

time: 140 us -> 136 us (0.971)
  starting transfers between devices: 20.3 us -> 16.5 us
    ppermute x4 -> x2, starting transfers between devices: 9.83 us -> 5.58 us  [ring_gather(): forward = lax.ppermute(forward, axis, ahead)]
    all_to_all x0 -> x1, starting transfers between devices: none -> 4.13 us  [local(): lax.all_to_all(jnp.broadcast_to(piece[None], (nrow,) + piece.shape), 'row...]
    ppermute x2 -> x1, starting transfers between devices: 7.41 us -> 3.65 us  [ring_gather(): backward = lax.ppermute(backward, axis, behind)]
    ppermute x4 -> x2, waiting for transfers between devices: 3.08 us -> 0.01 us  [ring_gather(): forward = lax.ppermute(forward, axis, ahead)]
    ppermute x1, waiting for transfers between devices: 7.11 us -> 8.52 us  [from_partner(): return lax.ppermute(value, axis, pairs)]
    gather x2 -> x1, local copies, waits for them, and re-layouts: 2.85 us -> 2.27 us  [ring_gather(): return stacked[(index - sources) % n]]
  transfers between devices with their start and end apart: 8 -> 6, of which waited for: 4 -> 3; matrix products, arithmetic and copies ran while one was open for 26% -> 27% of each run, Pallas kernels for 0% -> 0%
where the time goes in v10:
time: 136 us; the launch traced here: 134 us
  blocking collectives  40.4 us (30%)
  waiting for transfers between devices  18.7 us (14%)
  matrix products  16.9 us (12%)
  other arithmetic  16.8 us (12%)
  starting transfers between devices  16.5 us (12%)
  between operations  13.7 us (10%)
  local copies, waits for them, and re-layouts  11.3 us (8%)
    all_gather x1, blocking collectives, local(): inverse = lax.all_gather(inverse, 'z', axis=0, tiled=True)  38.4 us
    dot_general x3, matrix products, solve(): jnp.dot(rows, inverse, preferred_element_type=jnp.float32)  10.9 us
    all_gather x1, waiting for transfers between devices, local(): columns = lax.all_gather(panel[0], ('z', 'core'), axis=1, tiled=True)  8.55 us
    ppermute x1, waiting for transfers between devices, from_partner(): return lax.ppermute(value, axis, pairs)  8.52 us
    add x1, other arithmetic, local(): picked = gather_col[lane // width] * width + lane % width  5.66 us
    ppermute x2, starting transfers between devices, ring_gather(): forward = lax.ppermute(forward, axis, ahead)  5.58 us
    dot_general x2, matrix products, outer_rows(): lax.dot_general(left, right, (((1,), (1,)), ((), ())), preferred_element_...  4.67 us
    gather x6, other arithmetic, local(): picked = gather_col[lane // width] * width + lane % width  4.48 us
  transfers between devices with their start and end apart: 6, of which 3 were waited for; matrix products, arithmetic and copies ran while one was open for 27% of the time, Pallas kernels for 0%

profile of v10, /device:TPU:24, one launch (start us, length us, event | category | flops | bytes accessed | tf_op | source)
XLA Modules:
  0.0 134.2 jit_solution(12672380951604042354)
XLA Ops:
  7.3 2.0 %all-gather.1 = bf16[1,16,1024]{2,1,0:T(8,128)(2,1)S(1)} all-gather(bf16[1,8,1024]{2,1,0:T(8,128)(2,1)} %param.4), channel_id=3, replica_groups=mesh['front'=4,'row'=4,'z'=16,'core'=2] {'core'}, dimensions={1}, use_global_device_ids=true | all-gather | bytes 49152 | tf_op jit(solution)/shard_map/all_gather | solution.py:51
  9.3 38.4 %all-gather.2 = bf16[1,256,1024]{2,1,0:T(8,128)(2,1)S(1)} all-gather(bf16[1,16,1024]{2,1,0:T(8,128)(2,1)S(1)} %all-gather.1), channel_id=4, replica_groups=mesh['front'=4,'row'=4,'z'=16,'core'=2] {'z'}, dimensions={1}, use_global_device_ids=true | all-gather | bytes 557056 | tf_op jit(solution)/shard_map/all_gather | solution.py:52
  47.7 3.4 %collective-permute-start = (bf16[256,1024]{1,0:T(8,128)(2,1)S(1)}, bf16[256,1024]{1,0:T(8,128)(2,1)S(1)}, u32[]{:S(2)}, u32[]{:S(2)}) collective-permute-start(bf16[256,1024]{1,0:T(8,128)(2,1)S(1)} %bitcast.70), channel_id=1, source_target_pairs={{0,32},{32,64},{64,96},{96,0},{1,33},{33,65},{65,97},{97,1},{2,34}... | collective-permute-start | bytes 1572872 | tf_op jit(solution)/shard_map/ppermute | solution.py:28
  51.1 3.7 %collective-permute-start.2 = (bf16[256,1024]{1,0:T(8,128)(2,1)S(1)}, bf16[256,1024]{1,0:T(8,128)(2,1)S(1)}, u32[]{:S(2)}, u32[]{:S(2)}) collective-permute-start(bf16[256,1024]{1,0:T(8,128)(2,1)S(1)} %bitcast.71), channel_id=1, source_target_pairs={{0,96},{32,0},{64,32},{96,64},{1,97},{33,1},{65,33},{97,65},{2,98}... | collective-permute-start | bytes 1572872 | tf_op jit(solution)/shard_map/ppermute | solution.py:31
  54.8 1.3 gather_fusion.3
  56.8 2.5 %sort.35 = (s32[128]{0:T(128)}, s32[128]{0:T(128)S(1)}) sort(s32[128]{0:T(128)S(1)} %fusion.28, s32[128]{0:T(128)S(1)} %iota.46), dimensions={0}, to_apply=%region_1.2 | sort | flops 896 | bytes 2048 | tf_op jit(solution)/shard_map/jit(argsort)/sort | solution.py:82
  59.3 1.2 sort.34
  61.5 2.2 %collective-permute-start.1 = (bf16[256,1024]{1,0:T(8,128)(2,1)S(1)}, bf16[256,1024]{1,0:T(8,128)(2,1)S(1)}, u32[]{:S(2)}, u32[]{:S(2)}) collective-permute-start(bf16[256,1024]{1,0:T(8,128)(2,1)S(1)} %collective-permute-done), channel_id=1, source_target_pairs={{0,32},{32,64},{64,96},{96,0},{1,33},{33,65},{65,97},{97,1},{2,34}... | collective-permute-start | bytes 1572872 | tf_op jit(solution)/shard_map/ppermute | solution.py:28
  63.7 4.3 %compare_select_fusion.1 = s32[256,1]{0,1:T(1,128)S(1)} fusion(s32[]{:T(128)} %bitcast.19, s32[]{:T(128)} %bitcast.20, s32[]{:T(128)} %bitcast.21, s32[]{:T(128)} %bitcast.22, s32[]{:T(128)} %bitcast.23, s32[]{:T(128)} %bitcast.25, s32[]{:T(128)} %bitcast.24), kind=kLoop, calls=%fused_computation.42 | loop fusion | flops 5888 | bytes 1052 | tf_op jit(solution)/shard_map/gather | solution.py:94
  68.2 2.7 %dynamic-slice_bitcast_fusion = (f32[1024,256]{1,0:T(8,128)S(1)}, f32[1024,256]{1,0:T(8,128)}) fusion(f32[1,2048,256]{2,1,0:T(8,128)} %param.6, s32[]{:T(128)S(6)} %select_n.189, s32[]{:T(128)S(6)} %select_n.169), kind=kLoop, calls=%fused_computation.19 | loop fusion | bytes 4194312 | tf_op jit(solution)/shard_map/dynamic_slice | solution.py:102
  70.8 5.7 %fusion.19 = s32[256]{0:T(256)S(1)} fusion(pred[256]{0:T(512)(128)(4,1)S(1)} %get-tuple-element.37, pred[256]{0:T(512)(128)(4,1)S(1)} %get-tuple-element.38, pred[256]{0:T(512)(128)(4,1)S(1)} %get-tuple-element.39, pred[256]{0:T(512)(128)(4,1)S(1)} %get-tuple-element.40, pred[256]{0:T(512)(128)(4,1)S(1)} %get-tuple-element.41, ...), kind=kLoop, calls=%fused_computation.79 | loop fusion | flops 4352 | bytes 4388 | tf_op jit(solution)/shard_map/add | solution.py:94
  76.5 1.6 %pad_maximum_fusion = bf16[4,256,1024]{2,1,0:T(8,128)(2,1)} fusion(bf16[1,256,1024]{2,1,0:T(8,128)(2,1)S(1)} %bitcast.76, bf16[1,256,1024]{2,1,0:T(8,128)(2,1)S(1)} %bitcast.77, bf16[1,256,1024]{2,1,0:T(8,128)(2,1)S(1)} %bitcast.75, bf16[1,256,1024]{2,1,0:T(8,128)(2,1)S(1)} %all-gather.2), kind=kLoop, calls=%fused_computation.6 | loop fusion | flops 3145728 | bytes 4194304 | tf_op jit(solution)/shard_map/stack | solution.py:37
  78.1 2.3 %gather_fusion = bf16[4,256,1024]{2,1,0:T(8,128)(2,1)S(1)} fusion(bf16[4,256,1024]{2,1,0:T(8,128)(2,1)} %pad_maximum_fusion, s32[1024]{0:T(1024)S(1)} %pad_clamp_fusion.5), kind=kCustom, calls=%fused_computation | custom fusion | bytes 4194320 | tf_op jit(solution)/shard_map/gather | solution.py:39
  80.4 8.6 %all-gather.5.cloned.1.call-done = bf16[1,2048,1024]{1,2,0:T(8,128)(2,1)} async-done(((bf16[1,2048,32]{1,2,0:T(8,128)(2,1)}), bf16[1,2048,1024]{1,2,0:T(8,128)(2,1)}) %all-gather.5.cloned.1.call-update) | async-done | bytes 4194320 | tf_op jit(solution)/shard_map/all_gather | solution.py:57
  88.9 1.6 %convolution_convert_fusion = bf16[64,1024]{1,0:T(8,128)(2,1)S(1)} fusion(bf16[1024,1024]{1,0:T(8,128)(2,1)S(1)} %bitcast.65, bf16[1,2048,1024]{1,2,0:T(8,128)(2,1)} %all-gather.5.cloned.1.call-done, s32[]{:T(128)S(6)} %select_n.180), kind=kOutput, calls=%fused_computation.17 | convolution fusion | flops 134283264 | bytes 2490372 | tf_op jit(solution)/shard_map/dot_general | solution.py:60
  91.4 4.1 %all-to-all-start = ((bf16[4,64,1024]{2,1,0:T(8,128)(2,1)}), bf16[4,64,1024]{2,1,0:T(8,128)(2,1)}, u32[]{:S(2)}, u32[]{:S(2)}) async-start(bf16[4,64,1024]{2,1,0:T(8,128)(2,1)} %broadcast_in_dim.10), calls=%async_computation | async-start | bytes 1048576 | tf_op jit(solution)/shard_map/all_to_all | solution.py:69
  95.5 5.5 %fusion.9 = bf16[1024,1024]{1,0:T(8,128)(2,1)} fusion(bf16[1024,1024]{1,0:T(8,128)(2,1)S(1)} %bitcast.66, bf16[1,2048,1024]{1,2,0:T(8,128)(2,1)} %all-gather.5.cloned.1.call-done, s32[]{:T(128)S(6)} %select_n.189), kind=kOutput, calls=%fused_computation.14 | convolution fusion | flops 2148532224 | bytes 6291460 | tf_op jit(solution)/shard_map/dot_general | solution.py:60
  101.1 3.8 %fusion.6 = bf16[1024,1024]{1,0:T(8,128)(2,1)} fusion(bf16[1024,1024]{1,0:T(8,128)(2,1)S(1)} %bitcast.67, bf16[1,2048,1024]{1,2,0:T(8,128)(2,1)S(1)} %copy-done.2, s32[]{:T(128)S(6)} %select_n.169), kind=kOutput, calls=%fused_computation.13 | convolution fusion | flops 2148532224 | bytes 6291460 | tf_op jit(solution)/shard_map/dot_general | solution.py:60
  105.8 1.6 %gather_fusion.2 = bf16[16,16,1024]{2,1,0:T(8,128)(2,1)S(1)} fusion(bf16[16,16,1024]{2,1,0:T(8,128)(2,1)} %bitcast.28, s32[1024]{0:T(1024)S(1)} %pad_clamp_fusion.3), kind=kCustom, calls=%fused_computation.2 | custom fusion | bytes 1048640 | tf_op jit(solution)/shard_map/gather | solution.py:90
  107.4 2.3 %fusion.38 = f32[1024,256]{1,0:T(8,128)S(1)} fusion(bf16[1024,1024]{1,0:T(8,128)(2,1)} %fusion.9, bf16[256,1024]{1,0:T(8,128)(2,1)S(1)} %bitcast.72), kind=kOutput, calls=%fused_computation.110 | convolution fusion | flops 536870912 | bytes 3670016 | tf_op jit(solution)/shard_map/dot_general | solution.py:15
  111.0 3.1 %collective-permute-start.3 = (bf16[1024,256]{1,0:T(8,128)(2,1)S(1)}, bf16[1024,256]{1,0:T(8,128)(2,1)S(1)}, u32[]{:S(2)}, u32[]{:S(2)}) collective-permute-start(bf16[1024,256]{1,0:T(8,128)(2,1)S(1)} %bitcast.74), channel_id=1, source_target_pairs={{0,128},{128,0},{256,384},{384,256},{1,129},{129,1},{257,385},{385... | collective-permute-start | bytes 1572872 | tf_op jit(solution)/shard_map/ppermute | solution.py:11
  114.1 2.3 %fusion.37 = f32[1024,256]{1,0:T(8,128)S(1)} fusion(bf16[1024,1024]{1,0:T(8,128)(2,1)} %fusion.6, bf16[256,1024]{1,0:T(8,128)(2,1)S(1)} %bitcast.73), kind=kOutput, calls=%fused_computation.109 | convolution fusion | flops 536870912 | bytes 3670016 | tf_op jit(solution)/shard_map/dot_general | solution.py:15
  117.8 8.5 %collective-permute-done.3 = bf16[1024,256]{1,0:T(8,128)(2,1)S(1)} collective-permute-done((bf16[1024,256]{1,0:T(8,128)(2,1)S(1)}, bf16[1024,256]{1,0:T(8,128)(2,1)S(1)}, u32[]{:S(2)}, u32[]{:S(2)}) %collective-permute-start.3) | collective-permute-done | bytes 524320 | tf_op jit(solution)/shard_map/ppermute | solution.py:11
  126.3 1.1 bitcast_add_fusion
  (39 shorter events, 6.7 us)
Async XLA Ops:
  6.5 48.2 %copy-start = (s32[1,512]{1,0:T(1,128)S(1)}, s32[1,512]{1,0:T(1,128)}, u32[]{:S(2)}) copy-start(s32[1,512]{1,0:T(1,128)} %param.7) | copy-start | bytes 6148
  6.5 82.4 %all-gather.5.cloned.1.call-start = ((), (), s32[]{:S(2)}) async-start(), calls=%async_computation.1 | async-start | bytes 4325376 | tf_op jit(solution)/shard_map/all_gather | solution.py:57
  47.7 13.8 %collective-permute-start = (bf16[256,1024]{1,0:T(8,128)(2,1)S(1)}, bf16[256,1024]{1,0:T(8,128)(2,1)S(1)}, u32[]{:S(2)}, u32[]{:S(2)}) collective-permute-start(bf16[256,1024]{1,0:T(8,128)(2,1)S(1)} %bitcast.70), channel_id=1, source_target_pairs={{0,32},{32,64},{64,96},{96,0},{1,33},{33,65},{65,97},{97,1},{2,34}... | collective-permute-start | bytes 1572872 | tf_op jit(solution)/shard_map/ppermute | solution.py:28
  51.1 25.4 %collective-permute-start.2 = (bf16[256,1024]{1,0:T(8,128)(2,1)S(1)}, bf16[256,1024]{1,0:T(8,128)(2,1)S(1)}, u32[]{:S(2)}, u32[]{:S(2)}) collective-permute-start(bf16[256,1024]{1,0:T(8,128)(2,1)S(1)} %bitcast.71), channel_id=1, source_target_pairs={{0,96},{32,0},{64,32},{96,64},{1,97},{33,1},{65,33},{97,65},{2,98}... | collective-permute-start | bytes 1572872 | tf_op jit(solution)/shard_map/ppermute | solution.py:31
  61.5 15.0 %collective-permute-start.1 = (bf16[256,1024]{1,0:T(8,128)(2,1)S(1)}, bf16[256,1024]{1,0:T(8,128)(2,1)S(1)}, u32[]{:S(2)}, u32[]{:S(2)}) collective-permute-start(bf16[256,1024]{1,0:T(8,128)(2,1)S(1)} %collective-permute-done), channel_id=1, source_target_pairs={{0,32},{32,64},{64,96},{96,0},{1,33},{33,65},{65,97},{97,1},{2,34}... | collective-permute-start | bytes 1572872 | tf_op jit(solution)/shard_map/ppermute | solution.py:28
  91.4 14.4 %all-to-all-start = ((bf16[4,64,1024]{2,1,0:T(8,128)(2,1)}), bf16[4,64,1024]{2,1,0:T(8,128)(2,1)}, u32[]{:S(2)}, u32[]{:S(2)}) async-start(bf16[4,64,1024]{2,1,0:T(8,128)(2,1)} %broadcast_in_dim.10), calls=%async_computation | async-start | bytes 1048576 | tf_op jit(solution)/shard_map/all_to_all | solution.py:69
  95.5 5.5 %copy-start.2 = (bf16[1,2048,1024]{1,2,0:T(8,128)(2,1)S(1)}, bf16[1,2048,1024]{1,2,0:T(8,128)(2,1)}, u32[]{:S(2)}) copy-start(bf16[1,2048,1024]{1,2,0:T(8,128)(2,1)} %all-gather.5.cloned.1.call-done) | copy-start | bytes 12582916
  111.0 5.5 %copy-start.1 = (f32[1024,256]{1,0:T(8,128)S(1)}, f32[1024,256]{1,0:T(8,128)}, u32[]{:S(2)}) copy-start(f32[1024,256]{1,0:T(8,128)} %get-tuple-element.11) | copy-start | bytes 3145732
  111.0 15.3 %collective-permute-start.3 = (bf16[1024,256]{1,0:T(8,128)(2,1)S(1)}, bf16[1024,256]{1,0:T(8,128)(2,1)S(1)}, u32[]{:S(2)}, u32[]{:S(2)}) collective-permute-start(bf16[1024,256]{1,0:T(8,128)(2,1)S(1)} %bitcast.74), channel_id=1, source_target_pairs={{0,128},{128,0},{256,384},{384,256},{1,129},{129,1},{257,385},{385... | collective-permute-start | bytes 1572872 | tf_op jit(solution)/shard_map/ppermute | solution.py:11
Sparse Core Ops, SparseCore 0:
  9.5 79.4 all-gather.4

commit v11 on v10

--- a/solution.py
+++ b/solution.py
@@ -56,10 +56,18 @@
 
     columns = lax.all_gather(panel[0], ("z", "core"), axis=1, tiled=True)
 
+    step = order // 4
+
     def solve(rows):
-        return jnp.dot(rows, inverse, preferred_element_type=jnp.float32).astype(
-            jnp.bfloat16
-        )
+        parts = [
+            jnp.dot(
+                rows[:, : end + step],
+                inverse[: end + step, end : end + step],
+                preferred_element_type=jnp.float32,
+            ).astype(jnp.bfloat16)
+            for end in range(0, order, step)
+        ]
+        return jnp.concatenate(parts, axis=1)
 
     local_trailing = trailing[0]
     rows_here = local_trailing.shape[0]

time: 136 us -> 151 us (1.11)
  waiting for transfers between devices: 18.7 us -> 24.2 us
  local copies, waits for them, and re-layouts: 11.3 us -> 16.1 us
  other arithmetic: 16.8 us -> 19.8 us
  matrix products: 16.9 us -> 19.7 us
    all_to_all x1, waiting for transfers between devices: 0.9 us -> 5.47 us  [local(): lax.all_to_all(jnp.broadcast_to(piece[None], (nrow,) + piece.shape), 'row...]
    dot_general x3 -> x12, matrix products: 10.9 us -> 15.2 us  [solve(): jnp.dot(rows[:, :end + step], inverse[:end + step, end:end + step], prefe...]
    dynamic_slice x0 -> x2, local copies, waits for them, and re-layouts: none -> 3.9 us  [the longest x1 2.82 us: half_update(): low = solve(lax.dynamic_slice_in_dim(columns, which * half, half, 0))]
    concatenate x0 -> x3, other arithmetic: none -> 3.21 us  [solve(): return jnp.concatenate(parts, axis=1)]
    ppermute x1, waiting for transfers between devices: 8.52 us -> 10.4 us  [from_partner(): return lax.ppermute(value, axis, pairs)]
  transfers between devices with their start and end apart: 6 -> 6, of which waited for: 3 -> 3; matrix products, arithmetic and copies ran while one was open for 27% -> 20% of each run, Pallas kernels for 0% -> 0%
where the time goes in v11:
time: 151 us; the launch traced here: 150 us
  blocking collectives  40.4 us (27%)
  waiting for transfers between devices  24.2 us (16%)
  other arithmetic  19.8 us (13%)
  matrix products  19.7 us (13%)
  local copies, waits for them, and re-layouts  16.1 us (11%)
  starting transfers between devices  15.7 us (10%)
  between operations  13.8 us (9%)
    all_gather x1, blocking collectives, local(): inverse = lax.all_gather(inverse, 'z', axis=0, tiled=True)  38.4 us
    dot_general x12, matrix products, solve(): jnp.dot(rows[:, :end + step], inverse[:end + step, end:end + step], prefe...  15.2 us
    ppermute x1, waiting for transfers between devices, from_partner(): return lax.ppermute(value, axis, pairs)  10.4 us
    all_gather x1, waiting for transfers between devices, local(): columns = lax.all_gather(panel[0], ('z', 'core'), axis=1, tiled=True)  7.66 us
    ppermute x2, starting transfers between devices, ring_gather(): forward = lax.ppermute(forward, axis, ahead)  5.58 us
    add x1, other arithmetic, local(): picked = gather_col[lane // width] * width + lane % width  5.54 us
    all_to_all x1, waiting for transfers between devices, local(): lax.all_to_all(jnp.broadcast_to(piece[None], (nrow,) + piece.shape), 'row...  5.47 us
    gather x6, other arithmetic, local(): picked = gather_col[lane // width] * width + lane % width  4.59 us
  transfers between devices with their start and end apart: 6, of which 3 were waited for; matrix products, arithmetic and copies ran while one was open for 20% of the time, Pallas kernels for 0%

profile of v11, /device:TPU:24, one launch (start us, length us, event | category | flops | bytes accessed | tf_op | source)
XLA Modules:
  0.0 149.8 jit_solution(11932269541784774910)
XLA Ops:
  7.3 2.0 %all-gather.1 = bf16[1,16,1024]{2,1,0:T(8,128)(2,1)S(1)} all-gather(bf16[1,8,1024]{2,1,0:T(8,128)(2,1)} %param.4), channel_id=3, replica_groups=mesh['front'=4,'row'=4,'z'=16,'core'=2] {'core'}, dimensions={1}, use_global_device_ids=true | all-gather | bytes 49152 | tf_op jit(solution)/shard_map/all_gather | solution.py:51
  9.3 38.4 %all-gather.2 = bf16[1,256,1024]{2,1,0:T(8,128)(2,1)S(1)} all-gather(bf16[1,16,1024]{2,1,0:T(8,128)(2,1)S(1)} %all-gather.1), channel_id=4, replica_groups=mesh['front'=4,'row'=4,'z'=16,'core'=2] {'z'}, dimensions={1}, use_global_device_ids=true | all-gather | bytes 557056 | tf_op jit(solution)/shard_map/all_gather | solution.py:52
  47.7 3.4 %collective-permute-start = (bf16[256,1024]{1,0:T(8,128)(2,1)S(1)}, bf16[256,1024]{1,0:T(8,128)(2,1)S(1)}, u32[]{:S(2)}, u32[]{:S(2)}) collective-permute-start(bf16[256,1024]{1,0:T(8,128)(2,1)S(1)} %bitcast.75), channel_id=1, source_target_pairs={{0,32},{32,64},{64,96},{96,0},{1,33},{33,65},{65,97},{97,1},{2,34}... | collective-permute-start | bytes 1572872 | tf_op jit(solution)/shard_map/ppermute | solution.py:28
  51.1 3.7 %collective-permute-start.2 = (bf16[256,1024]{1,0:T(8,128)(2,1)S(1)}, bf16[256,1024]{1,0:T(8,128)(2,1)S(1)}, u32[]{:S(2)}, u32[]{:S(2)}) collective-permute-start(bf16[256,1024]{1,0:T(8,128)(2,1)S(1)} %bitcast.76), channel_id=1, source_target_pairs={{0,96},{32,0},{64,32},{96,64},{1,97},{33,1},{65,33},{97,65},{2,98}... | collective-permute-start | bytes 1572872 | tf_op jit(solution)/shard_map/ppermute | solution.py:31
  56.8 2.5 %sort.35 = (s32[128]{0:T(128)}, s32[128]{0:T(128)S(1)}) sort(s32[128]{0:T(128)S(1)} %fusion.40, s32[128]{0:T(128)S(1)} %iota.46), dimensions={0}, to_apply=%region_1.2 | sort | flops 896 | bytes 2048 | tf_op jit(solution)/shard_map/jit(argsort)/sort | solution.py:90
  61.5 2.2 %collective-permute-start.1 = (bf16[256,1024]{1,0:T(8,128)(2,1)S(1)}, bf16[256,1024]{1,0:T(8,128)(2,1)S(1)}, u32[]{:S(2)}, u32[]{:S(2)}) collective-permute-start(bf16[256,1024]{1,0:T(8,128)(2,1)S(1)} %collective-permute-done), channel_id=1, source_target_pairs={{0,32},{32,64},{64,96},{96,0},{1,33},{33,65},{65,97},{97,1},{2,34}... | collective-permute-start | bytes 1572872 | tf_op jit(solution)/shard_map/ppermute | solution.py:28
  63.7 4.4 %compare_select_fusion.1 = s32[256,1]{0,1:T(1,128)S(1)} fusion(s32[]{:T(128)} %bitcast.19, s32[]{:T(128)} %bitcast.20, s32[]{:T(128)} %bitcast.21, s32[]{:T(128)} %bitcast.22, s32[]{:T(128)} %bitcast.23, s32[]{:T(128)} %bitcast.25, s32[]{:T(128)} %bitcast.24), kind=kLoop, calls=%fused_computation.72 | loop fusion | flops 5888 | bytes 1052 | tf_op jit(solution)/shard_map/gather | solution.py:102
  68.3 3.0 %dynamic-slice_bitcast_fusion.2 = (f32[1024,256]{1,0:T(8,128)}, f32[1024,256]{1,0:T(8,128)}) fusion(f32[1,2048,256]{2,1,0:T(8,128)} %param.6, s32[]{:T(128)S(6)} %select_n.189, s32[]{:T(128)S(6)} %select_n.169), kind=kLoop, calls=%fused_computation.32 | loop fusion | bytes 4194312 | tf_op jit(solution)/shard_map/dynamic_slice | solution.py:110
  71.3 5.5 %fusion.31 = s32[256]{0:T(256)S(1)} fusion(pred[256]{0:T(512)(128)(4,1)S(1)} %get-tuple-element.39, pred[256]{0:T(512)(128)(4,1)S(1)} %get-tuple-element.40, pred[256]{0:T(512)(128)(4,1)S(1)} %get-tuple-element.41, pred[256]{0:T(512)(128)(4,1)S(1)} %get-tuple-element.42, pred[256]{0:T(512)(128)(4,1)S(1)} %get-tuple-element.43, ...), kind=kLoop, calls=%fused_computation.106 | loop fusion | flops 4352 | bytes 4388 | tf_op jit(solution)/shard_map/add | solution.py:102
  77.9 1.5 pad_maximum_fusion
  79.3 2.0 %gather_fusion = bf16[4,256,1024]{2,1,0:T(8,128)(2,1)} fusion(bf16[4,256,1024]{2,1,0:T(8,128)(2,1)S(1)} %pad_maximum_fusion, s32[1024]{0:T(1024)S(1)} %pad_clamp_fusion.5), kind=kCustom, calls=%fused_computation | custom fusion | bytes 4194320 | tf_op jit(solution)/shard_map/gather | solution.py:39
  81.3 7.7 %all-gather.5.cloned.1.call-done = bf16[1,2048,1024]{1,2,0:T(8,128)(2,1)} async-done(((bf16[1,2048,32]{1,2,0:T(8,128)(2,1)}), bf16[1,2048,1024]{1,2,0:T(8,128)(2,1)}) %all-gather.5.cloned.1.call-update) | async-done | bytes 4194320 | tf_op jit(solution)/shard_map/all_gather | solution.py:57
  94.9 2.8 %dynamic-slice_bitcast_fusion = (bf16[1024,1024]{0,1:T(8,128)(2,1)S(1)}, bf16[1024,1024]{0,1:T(8,128)(2,1)S(1)}) fusion(bf16[1,2048,1024]{1,2,0:T(8,128)(2,1)} %all-gather.5.cloned.1.call-done, s32[]{:T(128)S(6)} %select_n.189, s32[]{:T(128)S(6)} %select_n.169), kind=kLoop, calls=%fused_computation.9 | loop fusion | bytes 8388616 | tf_op jit(solution)/shard_map/dynamic_slice | solution.py:111
  99.4 1.4 fusion.7
  100.9 1.6 %convolution_convert_fusion.4 = bf16[1024,256]{0,1:T(8,128)(2,1)} fusion(bf16[1024,1024]{0,1:T(8,128)(2,1)S(1)} %get-tuple-element.17, bf16[1024,1024]{1,0:T(8,128)(2,1)S(1)} %bitcast.65), kind=kOutput, calls=%fused_computation.21 | convolution fusion | flops 537133056 | bytes 3145728 | tf_op jit(solution)/shard_map/dot_general | solution.py:63
  102.4 1.6 %convolution_convert_fusion.5 = bf16[1024,256]{0,1:T(8,128)(2,1)} fusion(bf16[1024,1024]{0,1:T(8,128)(2,1)S(1)} %get-tuple-element.18, bf16[1024,1024]{1,0:T(8,128)(2,1)S(1)} %bitcast.66), kind=kOutput, calls=%fused_computation.22 | convolution fusion | flops 537133056 | bytes 3145728 | tf_op jit(solution)/shard_map/dot_general | solution.py:63
  104.0 1.4 fusion.4
  107.6 3.5 %all-to-all-start = ((bf16[4,64,1024]{2,1,0:T(8,128)(2,1)}), bf16[4,64,1024]{2,1,0:T(8,128)(2,1)S(1)}, u32[]{:S(2)}, u32[]{:S(2)}) async-start(bf16[4,64,1024]{2,1,0:T(8,128)(2,1)} %broadcast_in_dim.10), calls=%async_computation | async-start | bytes 1048576 | tf_op jit(solution)/shard_map/all_to_all | solution.py:77
  111.1 3.0 %pad_maximum_fusion.2 = bf16[1024,1024]{0,1:T(8,128)(2,1)} fusion(bf16[1024,256]{0,1:T(8,128)(2,1)} %convolution_convert_fusion.4, bf16[1024,256]{0,1:T(8,128)(2,1)} %fusion.7, bf16[1024,256]{0,1:T(8,128)(2,1)} %convolution_convert_fusion, bf16[1024,256]{0,1:T(8,128)(2,1)S(1)} %convolution_convert_fusion.1), kind=kLoop, calls=%fused_computation.8 | loop fusion | flops 8388608 | bytes 4194304 | tf_op jit(solution)/shard_map/concatenate | solution.py:70
  114.2 1.4 convolution_convert_fusion.3
  115.8 5.5 %all-to-all-done = bf16[4,64,1024]{2,1,0:T(8,128)(2,1)S(1)} async-done(((bf16[4,64,1024]{2,1,0:T(8,128)(2,1)}), bf16[4,64,1024]{2,1,0:T(8,128)(2,1)S(1)}, u32[]{:S(2)}, u32[]{:S(2)}) %all-to-all-start) | async-done | bytes 524320 | tf_op jit(solution)/shard_map/all_to_all | solution.py:77
  121.8 2.5 %fusion.50 = f32[1024,256]{1,0:T(8,128)S(1)} fusion(bf16[1024,1024]{0,1:T(8,128)(2,1)} %pad_maximum_fusion.2, bf16[256,1024]{1,0:T(8,128)(2,1)S(1)} %bitcast.70), kind=kOutput, calls=%fused_computation.137 | convolution fusion | flops 536870912 | bytes 3670016 | tf_op jit(solution)/shard_map/dot_general | solution.py:15
  126.4 3.0 %collective-permute-start.3 = (bf16[1024,256]{1,0:T(8,128)(2,1)}, bf16[1024,256]{1,0:T(8,128)(2,1)S(1)}, u32[]{:S(2)}, u32[]{:S(2)}) collective-permute-start(bf16[1024,256]{1,0:T(8,128)(2,1)} %bitcast.77), channel_id=1, source_target_pairs={{0,128},{128,0},{256,384},{384,256},{1,129},{129,1},{257,385},{385... | collective-permute-start | bytes 1572872 | tf_op jit(solution)/shard_map/ppermute | solution.py:11
  131.5 10.4 %collective-permute-done.3 = bf16[1024,256]{1,0:T(8,128)(2,1)S(1)} collective-permute-done((bf16[1024,256]{1,0:T(8,128)(2,1)}, bf16[1024,256]{1,0:T(8,128)(2,1)S(1)}, u32[]{:S(2)}, u32[]{:S(2)}) %collective-permute-start.3) | collective-permute-done | bytes 524320 | tf_op jit(solution)/shard_map/ppermute | solution.py:11
  (67 shorter events, 21.6 us)
Async XLA Ops:
  6.5 48.2 %copy-start = (s32[1,512]{1,0:T(1,128)S(1)}, s32[1,512]{1,0:T(1,128)}, u32[]{:S(2)}) copy-start(s32[1,512]{1,0:T(1,128)} %param.7) | copy-start | bytes 6148
  6.5 82.5 %all-gather.5.cloned.1.call-start = ((), (), s32[]{:S(2)}) async-start(), calls=%async_computation.1 | async-start | bytes 4325376 | tf_op jit(solution)/shard_map/all_gather | solution.py:57
  47.7 13.8 %collective-permute-start = (bf16[256,1024]{1,0:T(8,128)(2,1)S(1)}, bf16[256,1024]{1,0:T(8,128)(2,1)S(1)}, u32[]{:S(2)}, u32[]{:S(2)}) collective-permute-start(bf16[256,1024]{1,0:T(8,128)(2,1)S(1)} %bitcast.75), channel_id=1, source_target_pairs={{0,32},{32,64},{64,96},{96,0},{1,33},{33,65},{65,97},{97,1},{2,34}... | collective-permute-start | bytes 1572872 | tf_op jit(solution)/shard_map/ppermute | solution.py:28
  51.1 25.8 %collective-permute-start.2 = (bf16[256,1024]{1,0:T(8,128)(2,1)S(1)}, bf16[256,1024]{1,0:T(8,128)(2,1)S(1)}, u32[]{:S(2)}, u32[]{:S(2)}) collective-permute-start(bf16[256,1024]{1,0:T(8,128)(2,1)S(1)} %bitcast.76), channel_id=1, source_target_pairs={{0,96},{32,0},{64,32},{96,64},{1,97},{33,1},{65,33},{97,65},{2,98}... | collective-permute-start | bytes 1572872 | tf_op jit(solution)/shard_map/ppermute | solution.py:31
  61.5 15.4 %collective-permute-start.1 = (bf16[256,1024]{1,0:T(8,128)(2,1)S(1)}, bf16[256,1024]{1,0:T(8,128)(2,1)S(1)}, u32[]{:S(2)}, u32[]{:S(2)}) collective-permute-start(bf16[256,1024]{1,0:T(8,128)(2,1)S(1)} %collective-permute-done), channel_id=1, source_target_pairs={{0,32},{32,64},{64,96},{96,0},{1,33},{33,65},{65,97},{97,1},{2,34}... | collective-permute-start | bytes 1572872 | tf_op jit(solution)/shard_map/ppermute | solution.py:28
  76.9 0.8 copy-start.5
  76.9 1.0 copy-start.6
  94.9 2.9 %copy-start.1 = (bf16[4,256,1024]{2,1,0:T(8,128)(2,1)S(1)}, bf16[4,256,1024]{2,1,0:T(8,128)(2,1)}, u32[]{:S(2)}) copy-start(bf16[4,256,1024]{2,1,0:T(8,128)(2,1)} %gather_fusion) | copy-start | bytes 6291460
  97.7 7.7 %copy-start.4 = (bf16[1024,1024]{0,1:T(8,128)(2,1)}, bf16[1024,1024]{0,1:T(8,128)(2,1)S(1)}, u32[]{:S(2)}) copy-start(bf16[1024,1024]{0,1:T(8,128)(2,1)S(1)} %get-tuple-element.18) | copy-start | bytes 6291460
  107.6 13.6 %all-to-all-start = ((bf16[4,64,1024]{2,1,0:T(8,128)(2,1)}), bf16[4,64,1024]{2,1,0:T(8,128)(2,1)S(1)}, u32[]{:S(2)}, u32[]{:S(2)}) async-start(bf16[4,64,1024]{2,1,0:T(8,128)(2,1)} %broadcast_in_dim.10), calls=%async_computation | async-start | bytes 1048576 | tf_op jit(solution)/shard_map/all_to_all | solution.py:77
  111.1 4.5 %copy-start.7 = (bf16[1024,256]{0,1:T(8,128)(2,1)S(1)}, bf16[1024,256]{0,1:T(8,128)(2,1)}, u32[]{:S(2)}) copy-start(bf16[1024,256]{0,1:T(8,128)(2,1)} %convolution_convert_fusion.5) | copy-start | bytes 1572868
  111.1 4.5 %copy-start.8 = (bf16[1024,256]{0,1:T(8,128)(2,1)S(1)}, bf16[1024,256]{0,1:T(8,128)(2,1)}, u32[]{:S(2)}) copy-start(bf16[1024,256]{0,1:T(8,128)(2,1)} %fusion.4) | copy-start | bytes 1572868
  111.1 4.5 %copy-start.9 = (bf16[1024,256]{0,1:T(8,128)(2,1)S(1)}, bf16[1024,256]{0,1:T(8,128)(2,1)}, u32[]{:S(2)}) copy-start(bf16[1024,256]{0,1:T(8,128)(2,1)} %convolution_convert_fusion.2) | copy-start | bytes 1572868
  121.8 2.5 %copy-start.2 = (f32[1024,256]{1,0:T(8,128)S(1)}, f32[1024,256]{1,0:T(8,128)}, u32[]{:S(2)}) copy-start(f32[1024,256]{1,0:T(8,128)} %get-tuple-element.15) | copy-start | bytes 3145732
  126.4 3.8 %copy-start.3 = (f32[1024,256]{1,0:T(8,128)S(1)}, f32[1024,256]{1,0:T(8,128)}, u32[]{:S(2)}) copy-start(f32[1024,256]{1,0:T(8,128)} %get-tuple-element.11) | copy-start | bytes 3145732
  126.4 15.5 %collective-permute-start.3 = (bf16[1024,256]{1,0:T(8,128)(2,1)}, bf16[1024,256]{1,0:T(8,128)(2,1)S(1)}, u32[]{:S(2)}, u32[]{:S(2)}) collective-permute-start(bf16[1024,256]{1,0:T(8,128)(2,1)} %bitcast.77), channel_id=1, source_target_pairs={{0,128},{128,0},{256,384},{384,256},{1,129},{129,1},{257,385},{385... | collective-permute-start | bytes 1572872 | tf_op jit(solution)/shard_map/ppermute | solution.py:11
Sparse Core Ops, SparseCore 0:
  9.5 79.4 all-gather.4

commit v12 on v5

--- a/solution.py
+++ b/solution.py
@@ -66,7 +66,6 @@
     cols_here = local_trailing.shape[1]
     share = rows_here // ncol
     piece = solve(lax.dynamic_slice_in_dim(columns, col_index * share, share, 0))
-    col_side = ring_gather(piece, "row", row_index, nrow)
 
     block_map = extend_map[0]
     nblocks = block_map.shape[0]
@@ -85,9 +84,14 @@
     target_col = class_col * per_class + block_map[source_col] // group
     gather_col = jnp.argsort(target_col)
 
-    col_side = col_side.reshape(nrow * per_class, width, order)[gather_col].reshape(
-        cols_here, order
+    own_blocks = (
+        lax.dynamic_slice_in_dim(gather_col, row_index * per_class, per_class, 0)
+        - row_index * per_class
     )
+    piece = piece.reshape(per_class, width, order)[own_blocks].reshape(share, order)
+    col_side = lax.all_to_all(
+        jnp.broadcast_to(piece[None], (nrow,) + piece.shape), "row", 0, 0, tiled=True
+    ).reshape(cols_here, order)
     lane = jnp.arange(cols_here, dtype=jnp.int32)
     picked = gather_col[lane // width] * width + lane % width
     select_cols = (lane[:, None] == picked[None, :]).astype(jnp.float32)

time: 140 us -> 135 us (0.964)
  starting transfers between devices: 20.3 us -> 16.4 us
    ppermute x4 -> x2, starting transfers between devices: 9.83 us -> 5.58 us  [ring_gather(): forward = lax.ppermute(forward, axis, ahead)]
    all_to_all x0 -> x1, starting transfers between devices: none -> 4.13 us  [local(): lax.all_to_all(jnp.broadcast_to(piece[None], (nrow,) + piece.shape), 'row...]
    ppermute x2 -> x1, starting transfers between devices: 7.41 us -> 3.65 us  [ring_gather(): backward = lax.ppermute(backward, axis, behind)]
    ppermute x4 -> x2, waiting for transfers between devices: 3.08 us -> 0.01 us  [ring_gather(): forward = lax.ppermute(forward, axis, ahead)]
    ppermute x1, waiting for transfers between devices: 7.11 us -> 8.54 us  [from_partner(): return lax.ppermute(value, axis, pairs)]
    gather x2 -> x1, local copies, waits for them, and re-layouts: 2.85 us -> 2.27 us  [ring_gather(): return stacked[(index - sources) % n]]
  transfers between devices with their start and end apart: 8 -> 6, of which waited for: 4 -> 3; matrix products, arithmetic and copies ran while one was open for 26% -> 27% of each run, Pallas kernels for 0% -> 0%
where the time goes in v12:
time: 135 us; the launch traced here: 133 us
  blocking collectives  40.4 us (30%)
  waiting for transfers between devices  18.7 us (14%)
  matrix products  17 us (13%)
  other arithmetic  16.8 us (12%)
  starting transfers between devices  16.4 us (12%)
  between operations  13.7 us (10%)
  local copies, waits for them, and re-layouts  10.3 us (8%)
    all_gather x1, blocking collectives, local(): inverse = lax.all_gather(inverse, 'z', axis=0, tiled=True)  38.4 us
    dot_general x3, matrix products, solve(): jnp.dot(rows, inverse, preferred_element_type=jnp.float32)  10.9 us
    all_gather x1, waiting for transfers between devices, local(): columns = lax.all_gather(panel[0], ('z', 'core'), axis=1, tiled=True)  8.6 us
    ppermute x1, waiting for transfers between devices, from_partner(): return lax.ppermute(value, axis, pairs)  8.54 us
    add x1, other arithmetic, local(): picked = gather_col[lane // width] * width + lane % width  5.69 us
    ppermute x2, starting transfers between devices, ring_gather(): forward = lax.ppermute(forward, axis, ahead)  5.58 us
    dot_general x2, matrix products, outer_rows(): lax.dot_general(left, right, (((1,), (1,)), ((), ())), preferred_element_...  4.83 us
    gather x6, other arithmetic, local(): picked = gather_col[lane // width] * width + lane % width  4.45 us
  transfers between devices with their start and end apart: 6, of which 3 were waited for; matrix products, arithmetic and copies ran while one was open for 27% of the time, Pallas kernels for 0%

profile of v12, /device:TPU:24, one launch (start us, length us, event | category | flops | bytes accessed | tf_op | source)
XLA Modules:
  0.0 133.3 jit_solution(15449167133978030716)
XLA Ops:
  7.3 2.0 %all-gather.1 = bf16[1,16,1024]{2,1,0:T(8,128)(2,1)S(1)} all-gather(bf16[1,8,1024]{2,1,0:T(8,128)(2,1)} %param.4), channel_id=3, replica_groups=mesh['front'=4,'row'=4,'z'=16,'core'=2] {'core'}, dimensions={1}, use_global_device_ids=true | all-gather | bytes 49152 | tf_op jit(solution)/shard_map/all_gather | solution.py:51
  9.3 38.4 %all-gather.2 = bf16[1,256,1024]{2,1,0:T(8,128)(2,1)S(1)} all-gather(bf16[1,16,1024]{2,1,0:T(8,128)(2,1)S(1)} %all-gather.1), channel_id=4, replica_groups=mesh['front'=4,'row'=4,'z'=16,'core'=2] {'z'}, dimensions={1}, use_global_device_ids=true | all-gather | bytes 557056 | tf_op jit(solution)/shard_map/all_gather | solution.py:52
  47.7 3.4 %collective-permute-start = (bf16[256,1024]{1,0:T(8,128)(2,1)S(1)}, bf16[256,1024]{1,0:T(8,128)(2,1)S(1)}, u32[]{:S(2)}, u32[]{:S(2)}) collective-permute-start(bf16[256,1024]{1,0:T(8,128)(2,1)S(1)} %bitcast.71), channel_id=1, source_target_pairs={{0,32},{32,64},{64,96},{96,0},{1,33},{33,65},{65,97},{97,1},{2,34}... | collective-permute-start | bytes 1572872 | tf_op jit(solution)/shard_map/ppermute | solution.py:28
  51.1 3.7 %collective-permute-start.2 = (bf16[256,1024]{1,0:T(8,128)(2,1)S(1)}, bf16[256,1024]{1,0:T(8,128)(2,1)S(1)}, u32[]{:S(2)}, u32[]{:S(2)}) collective-permute-start(bf16[256,1024]{1,0:T(8,128)(2,1)S(1)} %bitcast.72), channel_id=1, source_target_pairs={{0,96},{32,0},{64,32},{96,64},{1,97},{33,1},{65,33},{97,65},{2,98}... | collective-permute-start | bytes 1572872 | tf_op jit(solution)/shard_map/ppermute | solution.py:31
  54.8 1.3 gather_fusion.3
  56.8 2.5 %sort.35 = (s32[128]{0:T(128)}, s32[128]{0:T(128)S(1)}) sort(s32[128]{0:T(128)S(1)} %fusion.28, s32[128]{0:T(128)S(1)} %iota.46), dimensions={0}, to_apply=%region_1.2 | sort | flops 896 | bytes 2048 | tf_op jit(solution)/shard_map/jit(argsort)/sort | solution.py:79
  59.3 1.2 sort.34
  61.5 2.2 %collective-permute-start.1 = (bf16[256,1024]{1,0:T(8,128)(2,1)S(1)}, bf16[256,1024]{1,0:T(8,128)(2,1)S(1)}, u32[]{:S(2)}, u32[]{:S(2)}) collective-permute-start(bf16[256,1024]{1,0:T(8,128)(2,1)S(1)} %collective-permute-done), channel_id=1, source_target_pairs={{0,32},{32,64},{64,96},{96,0},{1,33},{33,65},{65,97},{97,1},{2,34}... | collective-permute-start | bytes 1572872 | tf_op jit(solution)/shard_map/ppermute | solution.py:28
  63.7 4.3 %compare_select_fusion.1 = s32[256,1]{0,1:T(1,128)S(1)} fusion(s32[]{:T(128)} %bitcast.19, s32[]{:T(128)} %bitcast.20, s32[]{:T(128)} %bitcast.21, s32[]{:T(128)} %bitcast.22, s32[]{:T(128)} %bitcast.23, s32[]{:T(128)} %bitcast.25, s32[]{:T(128)} %bitcast.24), kind=kLoop, calls=%fused_computation.42 | loop fusion | flops 5888 | bytes 1052 | tf_op jit(solution)/shard_map/gather | solution.py:96
  68.2 2.7 %dynamic-slice_bitcast_fusion = (f32[1024,256]{1,0:T(8,128)S(1)}, f32[1024,256]{1,0:T(8,128)}) fusion(f32[1,2048,256]{2,1,0:T(8,128)} %param.6, s32[]{:T(128)S(6)} %select_n.193, s32[]{:T(128)S(6)} %select_n.172), kind=kLoop, calls=%fused_computation.19 | loop fusion | bytes 4194312 | tf_op jit(solution)/shard_map/dynamic_slice | solution.py:104
  70.9 5.7 %fusion.19 = s32[256]{0:T(256)S(1)} fusion(pred[256]{0:T(512)(128)(4,1)S(1)} %get-tuple-element.37, pred[256]{0:T(512)(128)(4,1)S(1)} %get-tuple-element.38, pred[256]{0:T(512)(128)(4,1)S(1)} %get-tuple-element.39, pred[256]{0:T(512)(128)(4,1)S(1)} %get-tuple-element.40, pred[256]{0:T(512)(128)(4,1)S(1)} %get-tuple-element.41, ...), kind=kLoop, calls=%fused_computation.79 | loop fusion | flops 4352 | bytes 4388 | tf_op jit(solution)/shard_map/add | solution.py:96
  76.6 1.6 %pad_maximum_fusion = bf16[4,256,1024]{2,1,0:T(8,128)(2,1)} fusion(bf16[1,256,1024]{2,1,0:T(8,128)(2,1)S(1)} %bitcast.76, bf16[1,256,1024]{2,1,0:T(8,128)(2,1)S(1)} %bitcast.77, bf16[1,256,1024]{2,1,0:T(8,128)(2,1)S(1)} %bitcast.75, bf16[1,256,1024]{2,1,0:T(8,128)(2,1)S(1)} %all-gather.2), kind=kLoop, calls=%fused_computation.6 | loop fusion | flops 3145728 | bytes 4194304 | tf_op jit(solution)/shard_map/stack | solution.py:37
  78.2 2.3 %gather_fusion = bf16[4,256,1024]{2,1,0:T(8,128)(2,1)S(1)} fusion(bf16[4,256,1024]{2,1,0:T(8,128)(2,1)} %pad_maximum_fusion, s32[1024]{0:T(1024)S(1)} %pad_clamp_fusion.5), kind=kCustom, calls=%fused_computation | custom fusion | bytes 4194320 | tf_op jit(solution)/shard_map/gather | solution.py:39
  80.4 8.6 %all-gather.5.cloned.1.call-done = bf16[1,2048,1024]{1,2,0:T(8,128)(2,1)} async-done(((bf16[1,2048,32]{1,2,0:T(8,128)(2,1)}), bf16[1,2048,1024]{1,2,0:T(8,128)(2,1)}) %all-gather.5.cloned.1.call-update) | async-done | bytes 4194320 | tf_op jit(solution)/shard_map/all_gather | solution.py:57
  89.0 1.6 %convolution_convert_fusion = bf16[64,1024]{1,0:T(8,128)(2,1)S(1)} fusion(bf16[1024,1024]{1,0:T(8,128)(2,1)S(1)} %bitcast.66, bf16[1,2048,1024]{1,2,0:T(8,128)(2,1)} %all-gather.5.cloned.1.call-done, s32[]{:T(128)S(6)} %select_n.183), kind=kOutput, calls=%fused_computation.17 | convolution fusion | flops 134283264 | bytes 2490372 | tf_op jit(solution)/shard_map/dot_general | solution.py:60
  92.1 4.1 %all-to-all-start = ((bf16[4,64,1024]{2,1,0:T(8,128)(2,1)}), bf16[4,64,1024]{2,1,0:T(8,128)(2,1)}, u32[]{:S(2)}, u32[]{:S(2)}) async-start(bf16[4,64,1024]{2,1,0:T(8,128)(2,1)} %broadcast_in_dim.27), calls=%async_computation | async-start | bytes 1048576 | tf_op jit(solution)/shard_map/all_to_all | solution.py:92
  96.2 5.5 %fusion.9 = bf16[1024,1024]{1,0:T(8,128)(2,1)} fusion(bf16[1024,1024]{1,0:T(8,128)(2,1)S(1)} %bitcast.67, bf16[1,2048,1024]{1,2,0:T(8,128)(2,1)} %all-gather.5.cloned.1.call-done, s32[]{:T(128)S(6)} %select_n.193), kind=kOutput, calls=%fused_computation.14 | convolution fusion | flops 2148532224 | bytes 6291460 | tf_op jit(solution)/shard_map/dot_general | solution.py:60
  101.7 3.8 %fusion.6 = bf16[1024,1024]{1,0:T(8,128)(2,1)} fusion(bf16[1024,1024]{1,0:T(8,128)(2,1)S(1)} %bitcast.68, bf16[1,2048,1024]{1,2,0:T(8,128)(2,1)S(1)} %copy-done.2, s32[]{:T(128)S(6)} %select_n.172), kind=kOutput, calls=%fused_computation.13 | convolution fusion | flops 2148532224 | bytes 6291460 | tf_op jit(solution)/shard_map/dot_general | solution.py:60
  105.6 0.9 all-to-all-done
  106.4 2.4 %fusion.38 = f32[1024,256]{1,0:T(8,128)S(1)} fusion(bf16[1024,1024]{1,0:T(8,128)(2,1)} %fusion.9, bf16[256,1024]{1,0:T(8,128)(2,1)} %bitcast.30), kind=kOutput, calls=%fused_computation.110 | convolution fusion | flops 536870912 | bytes 3670016 | tf_op jit(solution)/shard_map/dot_general | solution.py:15
  110.1 3.0 %collective-permute-start.3 = (bf16[1024,256]{1,0:T(8,128)(2,1)S(1)}, bf16[1024,256]{1,0:T(8,128)(2,1)S(1)}, u32[]{:S(2)}, u32[]{:S(2)}) collective-permute-start(bf16[1024,256]{1,0:T(8,128)(2,1)S(1)} %bitcast.74), channel_id=1, source_target_pairs={{0,128},{128,0},{256,384},{384,256},{1,129},{129,1},{257,385},{385... | collective-permute-start | bytes 1572872 | tf_op jit(solution)/shard_map/ppermute | solution.py:11
  113.2 2.4 %fusion.37 = f32[1024,256]{1,0:T(8,128)S(1)} fusion(bf16[1024,1024]{1,0:T(8,128)(2,1)} %fusion.6, bf16[256,1024]{1,0:T(8,128)(2,1)} %bitcast.30), kind=kOutput, calls=%fused_computation.109 | convolution fusion | flops 536870912 | bytes 3670016 | tf_op jit(solution)/shard_map/dot_general | solution.py:15
  116.9 8.5 %collective-permute-done.3 = bf16[1024,256]{1,0:T(8,128)(2,1)S(1)} collective-permute-done((bf16[1024,256]{1,0:T(8,128)(2,1)S(1)}, bf16[1024,256]{1,0:T(8,128)(2,1)S(1)}, u32[]{:S(2)}, u32[]{:S(2)}) %collective-permute-start.3) | collective-permute-done | bytes 524320 | tf_op jit(solution)/shard_map/ppermute | solution.py:11
  125.4 1.1 bitcast_add_fusion
  (39 shorter events, 6.5 us)
Async XLA Ops:
  6.5 48.2 %copy-start = (s32[1,512]{1,0:T(1,128)S(1)}, s32[1,512]{1,0:T(1,128)}, u32[]{:S(2)}) copy-start(s32[1,512]{1,0:T(1,128)} %param.7) | copy-start | bytes 6148
  6.5 82.5 %all-gather.5.cloned.1.call-start = ((), (), s32[]{:S(2)}) async-start(), calls=%async_computation.1 | async-start | bytes 4325376 | tf_op jit(solution)/shard_map/all_gather | solution.py:57
  47.7 13.9 %collective-permute-start = (bf16[256,1024]{1,0:T(8,128)(2,1)S(1)}, bf16[256,1024]{1,0:T(8,128)(2,1)S(1)}, u32[]{:S(2)}, u32[]{:S(2)}) collective-permute-start(bf16[256,1024]{1,0:T(8,128)(2,1)S(1)} %bitcast.71), channel_id=1, source_target_pairs={{0,32},{32,64},{64,96},{96,0},{1,33},{33,65},{65,97},{97,1},{2,34}... | collective-permute-start | bytes 1572872 | tf_op jit(solution)/shard_map/ppermute | solution.py:28
  51.1 25.5 %collective-permute-start.2 = (bf16[256,1024]{1,0:T(8,128)(2,1)S(1)}, bf16[256,1024]{1,0:T(8,128)(2,1)S(1)}, u32[]{:S(2)}, u32[]{:S(2)}) collective-permute-start(bf16[256,1024]{1,0:T(8,128)(2,1)S(1)} %bitcast.72), channel_id=1, source_target_pairs={{0,96},{32,0},{64,32},{96,64},{1,97},{33,1},{65,33},{97,65},{2,98}... | collective-permute-start | bytes 1572872 | tf_op jit(solution)/shard_map/ppermute | solution.py:31
  61.5 15.0 %collective-permute-start.1 = (bf16[256,1024]{1,0:T(8,128)(2,1)S(1)}, bf16[256,1024]{1,0:T(8,128)(2,1)S(1)}, u32[]{:S(2)}, u32[]{:S(2)}) collective-permute-start(bf16[256,1024]{1,0:T(8,128)(2,1)S(1)} %collective-permute-done), channel_id=1, source_target_pairs={{0,32},{32,64},{64,96},{96,0},{1,33},{33,65},{65,97},{97,1},{2,34}... | collective-permute-start | bytes 1572872 | tf_op jit(solution)/shard_map/ppermute | solution.py:28
  92.1 14.4 %all-to-all-start = ((bf16[4,64,1024]{2,1,0:T(8,128)(2,1)}), bf16[4,64,1024]{2,1,0:T(8,128)(2,1)}, u32[]{:S(2)}, u32[]{:S(2)}) async-start(bf16[4,64,1024]{2,1,0:T(8,128)(2,1)} %broadcast_in_dim.27), calls=%async_computation | async-start | bytes 1048576 | tf_op jit(solution)/shard_map/all_to_all | solution.py:92
  96.2 5.5 %copy-start.2 = (bf16[1,2048,1024]{1,2,0:T(8,128)(2,1)S(1)}, bf16[1,2048,1024]{1,2,0:T(8,128)(2,1)}, u32[]{:S(2)}) copy-start(bf16[1,2048,1024]{1,2,0:T(8,128)(2,1)} %all-gather.5.cloned.1.call-done) | copy-start | bytes 12582916
  110.1 5.5 %copy-start.1 = (f32[1024,256]{1,0:T(8,128)S(1)}, f32[1024,256]{1,0:T(8,128)}, u32[]{:S(2)}) copy-start(f32[1024,256]{1,0:T(8,128)} %get-tuple-element.11) | copy-start | bytes 3145732
  110.1 15.3 %collective-permute-start.3 = (bf16[1024,256]{1,0:T(8,128)(2,1)S(1)}, bf16[1024,256]{1,0:T(8,128)(2,1)S(1)}, u32[]{:S(2)}, u32[]{:S(2)}) collective-permute-start(bf16[1024,256]{1,0:T(8,128)(2,1)S(1)} %bitcast.74), channel_id=1, source_target_pairs={{0,128},{128,0},{256,384},{384,256},{1,129},{129,1},{257,385},{385... | collective-permute-start | bytes 1572872 | tf_op jit(solution)/shard_map/ppermute | solution.py:11
Sparse Core Ops, SparseCore 0:
  9.5 79.5 all-gather.4

commit v13 on v12

--- a/solution.py
+++ b/solution.py
@@ -100,9 +100,12 @@
     half = rows_here // 2
     half_blocks = half // width
 
-    def half_update(which):
+    def half_update(which, after=None):
         rows = lax.dynamic_slice_in_dim(local_trailing, which * half, half, 0)
-        low = solve(lax.dynamic_slice_in_dim(columns, which * half, half, 0))
+        own = lax.dynamic_slice_in_dim(columns, which * half, half, 0)
+        if after is not None:
+            own, _ = lax.optimization_barrier((own, after))
+        low = solve(own)
         rows, low = lax.optimization_barrier((rows, low))
         moved_cols = jnp.dot(
             rows,
@@ -121,7 +124,7 @@
 
     outgoing = half_update(1 - member).astype(jnp.bfloat16)
     incoming = from_partner(outgoing, "front", 0)
-    keep = half_update(member)
+    keep = half_update(member, outgoing)
     return (keep + incoming.astype(jnp.float32))[None]
 
 

time: 135 us -> 138 us (1.022)
  local copies, waits for them, and re-layouts: 10.3 us -> 13.7 us
    ppermute x1, waiting for transfers between devices: 8.54 us -> 5.35 us  [from_partner(): return lax.ppermute(value, axis, pairs)]
    all_to_all x1, waiting for transfers between devices: 0.89 us -> 3.14 us  [local(): lax.all_to_all(jnp.broadcast_to(piece[None], (nrow,) + piece.shape), 'row...]
    gather x2, local copies, waits for them, and re-layouts: 1.23 us -> 3.06 us  [half_update(): schur.reshape(half_blocks, width, cols_here)[blocks]]
    dynamic_slice x0 -> x1, local copies, waits for them, and re-layouts: none -> 1.56 us  [half_update(): own = lax.dynamic_slice_in_dim(columns, which * half, half, 0)]
where the time goes in v13:
time: 138 us; the launch traced here: 137 us
  blocking collectives  40.4 us (29%)
  other arithmetic  18 us (13%)
  waiting for transfers between devices  17.8 us (13%)
  matrix products  17.5 us (13%)
  starting transfers between devices  16.2 us (12%)
  local copies, waits for them, and re-layouts  13.7 us (10%)
  between operations  13.7 us (10%)
    all_gather x1, blocking collectives, local(): inverse = lax.all_gather(inverse, 'z', axis=0, tiled=True)  38.4 us
    dot_general x3, matrix products, solve(): jnp.dot(rows, inverse, preferred_element_type=jnp.float32)  11.1 us
    all_gather x1, waiting for transfers between devices, local(): columns = lax.all_gather(panel[0], ('z', 'core'), axis=1, tiled=True)  8.6 us
    add x1, other arithmetic, local(): picked = gather_col[lane // width] * width + lane % width  5.69 us
    ppermute x2, starting transfers between devices, ring_gather(): forward = lax.ppermute(forward, axis, ahead)  5.58 us
    ppermute x1, waiting for transfers between devices, from_partner(): return lax.ppermute(value, axis, pairs)  5.35 us
    gather x6, other arithmetic, local(): picked = gather_col[lane // width] * width + lane % width  4.45 us
    dot_general x2, matrix products, outer_rows(): lax.dot_general(left, right, (((1,), (1,)), ((), ())), preferred_element_...  4.29 us
  transfers between devices with their start and end apart: 6, of which 3 were waited for; matrix products, arithmetic and copies ran while one was open for 27% of the time, Pallas kernels for 0%

profile of v13, /device:TPU:24, one launch (start us, length us, event | category | flops | bytes accessed | tf_op | source)
XLA Modules:
  0.0 137.3 jit_solution(821998032756021603)
XLA Ops:
  7.3 2.0 %all-gather.1 = bf16[1,16,1024]{2,1,0:T(8,128)(2,1)S(1)} all-gather(bf16[1,8,1024]{2,1,0:T(8,128)(2,1)} %param.4), channel_id=3, replica_groups=mesh['front'=4,'row'=4,'z'=16,'core'=2] {'core'}, dimensions={1}, use_global_device_ids=true | all-gather | bytes 49152 | tf_op jit(solution)/shard_map/all_gather | solution.py:51
  9.3 38.4 %all-gather.2 = bf16[1,256,1024]{2,1,0:T(8,128)(2,1)S(1)} all-gather(bf16[1,16,1024]{2,1,0:T(8,128)(2,1)S(1)} %all-gather.1), channel_id=4, replica_groups=mesh['front'=4,'row'=4,'z'=16,'core'=2] {'z'}, dimensions={1}, use_global_device_ids=true | all-gather | bytes 557056 | tf_op jit(solution)/shard_map/all_gather | solution.py:52
  47.7 3.4 %collective-permute-start = (bf16[256,1024]{1,0:T(8,128)(2,1)S(1)}, bf16[256,1024]{1,0:T(8,128)(2,1)S(1)}, u32[]{:S(2)}, u32[]{:S(2)}) collective-permute-start(bf16[256,1024]{1,0:T(8,128)(2,1)S(1)} %bitcast.69), channel_id=1, source_target_pairs={{0,32},{32,64},{64,96},{96,0},{1,33},{33,65},{65,97},{97,1},{2,34}... | collective-permute-start | bytes 1572872 | tf_op jit(solution)/shard_map/ppermute | solution.py:28
  51.1 3.7 %collective-permute-start.2 = (bf16[256,1024]{1,0:T(8,128)(2,1)S(1)}, bf16[256,1024]{1,0:T(8,128)(2,1)S(1)}, u32[]{:S(2)}, u32[]{:S(2)}) collective-permute-start(bf16[256,1024]{1,0:T(8,128)(2,1)S(1)} %bitcast.70), channel_id=1, source_target_pairs={{0,96},{32,0},{64,32},{96,64},{1,97},{33,1},{65,33},{97,65},{2,98}... | collective-permute-start | bytes 1572872 | tf_op jit(solution)/shard_map/ppermute | solution.py:31
  56.8 2.5 %sort.35 = (s32[128]{0:T(128)}, s32[128]{0:T(128)S(1)}) sort(s32[128]{0:T(128)S(1)} %fusion.21, s32[128]{0:T(128)S(1)} %iota.46), dimensions={0}, to_apply=%region_1.2 | sort | flops 896 | bytes 2048 | tf_op jit(solution)/shard_map/jit(argsort)/sort | solution.py:79
  61.5 2.2 %collective-permute-start.1 = (bf16[256,1024]{1,0:T(8,128)(2,1)S(1)}, bf16[256,1024]{1,0:T(8,128)(2,1)S(1)}, u32[]{:S(2)}, u32[]{:S(2)}) collective-permute-start(bf16[256,1024]{1,0:T(8,128)(2,1)S(1)} %collective-permute-done), channel_id=1, source_target_pairs={{0,32},{32,64},{64,96},{96,0},{1,33},{33,65},{65,97},{97,1},{2,34}... | collective-permute-start | bytes 1572872 | tf_op jit(solution)/shard_map/ppermute | solution.py:28
  63.7 4.3 %compare_select_fusion.1 = s32[256,1]{0,1:T(1,128)S(1)} fusion(s32[]{:T(128)} %bitcast.21, s32[]{:T(128)} %bitcast.22, s32[]{:T(128)} %bitcast.23, s32[]{:T(128)} %bitcast.24, s32[]{:T(128)} %bitcast.25, s32[]{:T(128)} %bitcast.27, s32[]{:T(128)} %bitcast.26), kind=kLoop, calls=%fused_computation.40 | loop fusion | flops 5888 | bytes 1052 | tf_op jit(solution)/shard_map/gather | solution.py:96
  68.2 2.7 %dynamic-slice_bitcast_fusion.1 = (f32[1024,256]{1,0:T(8,128)S(1)}, f32[1024,256]{1,0:T(8,128)}) fusion(f32[1,2048,256]{2,1,0:T(8,128)} %param.6, s32[]{:T(128)S(6)} %select_n.173, s32[]{:T(128)S(6)} %select_n.172), kind=kLoop, calls=%fused_computation.17 | loop fusion | bytes 4194312 | tf_op jit(solution)/shard_map/dynamic_slice | solution.py:104
  70.9 5.7 %fusion.12 = s32[256]{0:T(256)S(1)} fusion(pred[256]{0:T(512)(128)(4,1)S(1)} %get-tuple-element.39, pred[256]{0:T(512)(128)(4,1)S(1)} %get-tuple-element.40, pred[256]{0:T(512)(128)(4,1)S(1)} %get-tuple-element.41, pred[256]{0:T(512)(128)(4,1)S(1)} %get-tuple-element.42, pred[256]{0:T(512)(128)(4,1)S(1)} %get-tuple-element.43, ...), kind=kLoop, calls=%fused_computation.76 | loop fusion | flops 4352 | bytes 4388 | tf_op jit(solution)/shard_map/add | solution.py:96
  76.6 1.6 %pad_maximum_fusion = bf16[4,256,1024]{2,1,0:T(8,128)(2,1)} fusion(bf16[1,256,1024]{2,1,0:T(8,128)(2,1)S(1)} %bitcast.73, bf16[1,256,1024]{2,1,0:T(8,128)(2,1)S(1)} %bitcast.74, bf16[1,256,1024]{2,1,0:T(8,128)(2,1)S(1)} %bitcast.72, bf16[1,256,1024]{2,1,0:T(8,128)(2,1)S(1)} %all-gather.2), kind=kLoop, calls=%fused_computation.6 | loop fusion | flops 3145728 | bytes 4194304 | tf_op jit(solution)/shard_map/stack | solution.py:37
  78.2 2.3 %gather_fusion = bf16[4,256,1024]{2,1,0:T(8,128)(2,1)S(1)} fusion(bf16[4,256,1024]{2,1,0:T(8,128)(2,1)} %pad_maximum_fusion, s32[1024]{0:T(1024)S(1)} %pad_clamp_fusion.5), kind=kCustom, calls=%fused_computation | custom fusion | bytes 4194320 | tf_op jit(solution)/shard_map/gather | solution.py:39
  80.4 8.6 %all-gather.5.cloned.1.call-done = bf16[1,2048,1024]{1,2,0:T(8,128)(2,1)} async-done(((bf16[1,2048,32]{1,2,0:T(8,128)(2,1)}), bf16[1,2048,1024]{1,2,0:T(8,128)(2,1)}) %all-gather.5.cloned.1.call-update) | async-done | bytes 4194320 | tf_op jit(solution)/shard_map/all_gather | solution.py:57
  89.0 1.6 %convolution_convert_fusion.1 = bf16[64,1024]{1,0:T(8,128)(2,1)S(1)} fusion(bf16[1024,1024]{1,0:T(8,128)(2,1)S(1)} %bitcast.64, bf16[1,2048,1024]{1,2,0:T(8,128)(2,1)} %all-gather.5.cloned.1.call-done, s32[]{:T(128)S(6)} %select_n.184), kind=kOutput, calls=%fused_computation.15 | convolution fusion | flops 134283264 | bytes 2490372 | tf_op jit(solution)/shard_map/dot_general | solution.py:60
  92.1 4.1 %all-to-all-start = ((bf16[4,64,1024]{2,1,0:T(8,128)(2,1)}), bf16[4,64,1024]{2,1,0:T(8,128)(2,1)}, u32[]{:S(2)}, u32[]{:S(2)}) async-start(bf16[4,64,1024]{2,1,0:T(8,128)(2,1)} %broadcast_in_dim.27), calls=%async_computation | async-start | bytes 1048576 | tf_op jit(solution)/shard_map/all_to_all | solution.py:92
  96.2 5.5 %fusion.3 = bf16[1024,1024]{1,0:T(8,128)(2,1)} fusion(bf16[1024,1024]{1,0:T(8,128)(2,1)S(1)} %bitcast.65, bf16[1,2048,1024]{1,2,0:T(8,128)(2,1)} %all-gather.5.cloned.1.call-done, s32[]{:T(128)S(6)} %select_n.173), kind=kOutput, calls=%fused_computation.11 | convolution fusion | flops 2148532224 | bytes 6291460 | tf_op jit(solution)/shard_map/dot_general | solution.py:60
  101.7 1.6 %dynamic-slice_bitcast_fusion = bf16[1024,1024]{0,1:T(8,128)(2,1)} fusion(bf16[1,2048,1024]{1,2,0:T(8,128)(2,1)S(1)} %copy-done.2, s32[]{:T(128)S(6)} %select_n.172), kind=kLoop, calls=%fused_computation.10 | loop fusion | bytes 4194308 | tf_op jit(solution)/shard_map/dynamic_slice | solution.py:105
  103.3 3.1 %all-to-all-done = bf16[4,64,1024]{2,1,0:T(8,128)(2,1)} async-done(((bf16[4,64,1024]{2,1,0:T(8,128)(2,1)}), bf16[4,64,1024]{2,1,0:T(8,128)(2,1)}, u32[]{:S(2)}, u32[]{:S(2)}) %all-to-all-start) | async-done | bytes 524320 | tf_op jit(solution)/shard_map/all_to_all | solution.py:92
  106.4 2.4 %fusion.30 = f32[1024,256]{1,0:T(8,128)S(1)} fusion(bf16[1024,1024]{1,0:T(8,128)(2,1)} %fusion.3, bf16[256,1024]{1,0:T(8,128)(2,1)} %bitcast.32), kind=kOutput, calls=%fused_computation.106 | convolution fusion | flops 536870912 | bytes 3670016 | tf_op jit(solution)/shard_map/dot_general | solution.py:15
  110.3 2.4 %gather_fusion.4 = bf16[64,16,256]{2,1,0:T(8,128)(2,1)} fusion(bf16[64,16,256]{2,1,0:T(8,128)(2,1)} %bitcast.68, s32[1024]{0:T(1024)S(1)} %pad_clamp_fusion.1), kind=kCustom, calls=%fused_computation.4 | custom fusion | bytes 1048832 | tf_op jit(solution)/shard_map/gather | solution.py:121
  112.8 2.9 %collective-permute-start.3 = (bf16[1024,256]{1,0:T(8,128)(2,1)}, bf16[1024,256]{1,0:T(8,128)(2,1)}, u32[]{:S(2)}, u32[]{:S(2)}) collective-permute-start(bf16[1024,256]{1,0:T(8,128)(2,1)} %bitcast.35), channel_id=1, source_target_pairs={{0,128},{128,0},{256,384},{384,256},{1,129},{129,1},{257,385},{385... | collective-permute-start | bytes 1572872 | tf_op jit(solution)/shard_map/ppermute | solution.py:11
  115.6 4.0 %convolution_convert_fusion = bf16[1024,1024]{1,0:T(8,128)(2,1)S(1)} fusion(bf16[1024,1024]{0,1:T(8,128)(2,1)} %dynamic-slice_bitcast_fusion, bf16[1024,1024]{1,0:T(8,128)(2,1)S(1)} %bitcast.66), kind=kOutput, calls=%fused_computation.12 | convolution fusion | flops 2148532224 | bytes 6291456 | tf_op jit(solution)/shard_map/dot_general | solution.py:60
  119.7 1.9 %fusion.31 = f32[1024,256]{1,0:T(8,128)S(1)} fusion(bf16[1024,1024]{1,0:T(8,128)(2,1)S(1)} %convolution_convert_fusion, bf16[256,1024]{1,0:T(8,128)(2,1)} %bitcast.32), kind=kOutput, calls=%fused_computation.107 | convolution fusion | flops 536870912 | bytes 3670016 | tf_op jit(solution)/shard_map/dot_general | solution.py:15
  122.9 5.4 %collective-permute-done.3 = bf16[1024,256]{1,0:T(8,128)(2,1)} collective-permute-done((bf16[1024,256]{1,0:T(8,128)(2,1)}, bf16[1024,256]{1,0:T(8,128)(2,1)}, u32[]{:S(2)}, u32[]{:S(2)}) %collective-permute-start.3) | collective-permute-done | bytes 524320 | tf_op jit(solution)/shard_map/ppermute | solution.py:11
  128.2 2.2 %bitcast_add_fusion = f32[1024,256]{1,0:T(8,128)} fusion(f32[64,16,256]{2,1,0:T(8,128)S(1)} %gather_fusion.5, bf16[1024,256]{1,0:T(8,128)(2,1)} %collective-permute-done.3), kind=kLoop, calls=%fused_computation.16 | loop fusion | flops 524288 | bytes 2621440 | tf_op jit(solution)/shard_map/add | solution.py:128
  (40 shorter events, 9.2 us)
Async XLA Ops:
  6.5 48.2 %copy-start = (s32[1,512]{1,0:T(1,128)S(1)}, s32[1,512]{1,0:T(1,128)}, u32[]{:S(2)}) copy-start(s32[1,512]{1,0:T(1,128)} %param.7) | copy-start | bytes 6148
  6.5 82.5 %all-gather.5.cloned.1.call-start = ((), (), s32[]{:S(2)}) async-start(), calls=%async_computation.1 | async-start | bytes 4325376 | tf_op jit(solution)/shard_map/all_gather | solution.py:57
  47.7 13.9 %collective-permute-start = (bf16[256,1024]{1,0:T(8,128)(2,1)S(1)}, bf16[256,1024]{1,0:T(8,128)(2,1)S(1)}, u32[]{:S(2)}, u32[]{:S(2)}) collective-permute-start(bf16[256,1024]{1,0:T(8,128)(2,1)S(1)} %bitcast.69), channel_id=1, source_target_pairs={{0,32},{32,64},{64,96},{96,0},{1,33},{33,65},{65,97},{97,1},{2,34}... | collective-permute-start | bytes 1572872 | tf_op jit(solution)/shard_map/ppermute | solution.py:28
  51.1 25.5 %collective-permute-start.2 = (bf16[256,1024]{1,0:T(8,128)(2,1)S(1)}, bf16[256,1024]{1,0:T(8,128)(2,1)S(1)}, u32[]{:S(2)}, u32[]{:S(2)}) collective-permute-start(bf16[256,1024]{1,0:T(8,128)(2,1)S(1)} %bitcast.70), channel_id=1, source_target_pairs={{0,96},{32,0},{64,32},{96,64},{1,97},{33,1},{65,33},{97,65},{2,98}... | collective-permute-start | bytes 1572872 | tf_op jit(solution)/shard_map/ppermute | solution.py:31
  61.5 15.0 %collective-permute-start.1 = (bf16[256,1024]{1,0:T(8,128)(2,1)S(1)}, bf16[256,1024]{1,0:T(8,128)(2,1)S(1)}, u32[]{:S(2)}, u32[]{:S(2)}) collective-permute-start(bf16[256,1024]{1,0:T(8,128)(2,1)S(1)} %collective-permute-done), channel_id=1, source_target_pairs={{0,32},{32,64},{64,96},{96,0},{1,33},{33,65},{65,97},{97,1},{2,34}... | collective-permute-start | bytes 1572872 | tf_op jit(solution)/shard_map/ppermute | solution.py:28
  92.1 14.4 %all-to-all-start = ((bf16[4,64,1024]{2,1,0:T(8,128)(2,1)}), bf16[4,64,1024]{2,1,0:T(8,128)(2,1)}, u32[]{:S(2)}, u32[]{:S(2)}) async-start(bf16[4,64,1024]{2,1,0:T(8,128)(2,1)} %broadcast_in_dim.27), calls=%async_computation | async-start | bytes 1048576 | tf_op jit(solution)/shard_map/all_to_all | solution.py:92
  96.2 5.5 %copy-start.2 = (bf16[1,2048,1024]{1,2,0:T(8,128)(2,1)S(1)}, bf16[1,2048,1024]{1,2,0:T(8,128)(2,1)}, u32[]{:S(2)}) copy-start(bf16[1,2048,1024]{1,2,0:T(8,128)(2,1)} %all-gather.5.cloned.1.call-done) | copy-start | bytes 12582916
  112.8 15.5 %collective-permute-start.3 = (bf16[1024,256]{1,0:T(8,128)(2,1)}, bf16[1024,256]{1,0:T(8,128)(2,1)}, u32[]{:S(2)}, u32[]{:S(2)}) collective-permute-start(bf16[1024,256]{1,0:T(8,128)(2,1)} %bitcast.35), channel_id=1, source_target_pairs={{0,128},{128,0},{256,384},{384,256},{1,129},{129,1},{257,385},{385... | collective-permute-start | bytes 1572872 | tf_op jit(solution)/shard_map/ppermute | solution.py:11
  119.7 1.9 %copy-start.1 = (f32[1024,256]{1,0:T(8,128)S(1)}, f32[1024,256]{1,0:T(8,128)}, u32[]{:S(2)}) copy-start(f32[1024,256]{1,0:T(8,128)} %get-tuple-element.17) | copy-start | bytes 3145732
Sparse Core Ops, SparseCore 0:
  9.5 79.5 all-gather.4

commit v14 on v12

--- a/solution.py
+++ b/solution.py
@@ -96,13 +96,14 @@
     picked = gather_col[lane // width] * width + lane % width
     select_cols = (lane[:, None] == picked[None, :]).astype(jnp.float32)
 
+    solved = solve(columns)
     member = lax.axis_index("front") % 2
     half = rows_here // 2
     half_blocks = half // width
 
     def half_update(which):
         rows = lax.dynamic_slice_in_dim(local_trailing, which * half, half, 0)
-        low = solve(lax.dynamic_slice_in_dim(columns, which * half, half, 0))
+        low = lax.dynamic_slice_in_dim(solved, which * half, half, 0)
         rows, low = lax.optimization_barrier((rows, low))
         moved_cols = jnp.dot(
             rows,

time: 135 us -> 135 us (level)
  matrix products: 17 us -> 13.1 us
  local copies, waits for them, and re-layouts: 10.3 us -> 13.2 us
  waiting for transfers between devices: 18.7 us -> 20.6 us
    dot_general x3 -> x2, matrix products: 10.9 us -> 8.62 us  [solve(): jnp.dot(rows, inverse, preferred_element_type=jnp.float32)]
    ppermute x1, waiting for transfers between devices: 8.54 us -> 10.4 us  [from_partner(): return lax.ppermute(value, axis, pairs)]
    dynamic_slice x0 -> x1, local copies, waits for them, and re-layouts: none -> 1.82 us  [half_update(): low = lax.dynamic_slice_in_dim(solved, which * half, half, 0)]
    dot_general x2, matrix products: 4.83 us -> 3.22 us  [outer_rows(): lax.dot_general(left, right, (((1,), (1,)), ((), ())), preferred_element_...]
  transfers between devices with their start and end apart: 6 -> 6, of which waited for: 3 -> 3; matrix products, arithmetic and copies ran while one was open for 27% -> 26% of each run, Pallas kernels for 0% -> 0%
where the time goes in v14:
time: 135 us; the launch traced here: 134 us
  blocking collectives  40.4 us (30%)
  waiting for transfers between devices  20.6 us (15%)
  other arithmetic  16.8 us (12%)
  starting transfers between devices  15.7 us (12%)
  between operations  13.7 us (10%)
  local copies, waits for them, and re-layouts  13.2 us (10%)
  matrix products  13.1 us (10%)
    all_gather x1, blocking collectives, local(): inverse = lax.all_gather(inverse, 'z', axis=0, tiled=True)  38.4 us
    ppermute x1, waiting for transfers between devices, from_partner(): return lax.ppermute(value, axis, pairs)  10.4 us
    dot_general x2, matrix products, solve(): jnp.dot(rows, inverse, preferred_element_type=jnp.float32)  8.62 us
    all_gather x1, waiting for transfers between devices, local(): columns = lax.all_gather(panel[0], ('z', 'core'), axis=1, tiled=True)  8.2 us
    ppermute x2, starting transfers between devices, ring_gather(): forward = lax.ppermute(forward, axis, ahead)  5.58 us
    add x1, other arithmetic, local(): picked = gather_col[lane // width] * width + lane % width  5.54 us
    gather x6, other arithmetic, local(): picked = gather_col[lane // width] * width + lane % width  4.59 us
    ppermute x1, starting transfers between devices, ring_gather(): backward = lax.ppermute(backward, axis, behind)  3.65 us
  transfers between devices with their start and end apart: 6, of which 3 were waited for; matrix products, arithmetic and copies ran while one was open for 26% of the time, Pallas kernels for 0%

profile of v14, /device:TPU:24, one launch (start us, length us, event | category | flops | bytes accessed | tf_op | source)
XLA Modules:
  0.0 133.6 jit_solution(1006870976834022299)
XLA Ops:
  7.3 2.0 %all-gather = bf16[1,16,1024]{2,1,0:T(8,128)(2,1)S(1)} all-gather(bf16[1,8,1024]{2,1,0:T(8,128)(2,1)} %param.4), channel_id=2, replica_groups=mesh['front'=4,'row'=4,'z'=16,'core'=2] {'core'}, dimensions={1}, use_global_device_ids=true | all-gather | bytes 49152 | tf_op jit(solution)/shard_map/all_gather | solution.py:51
  9.3 38.4 %all-gather.1 = bf16[1,256,1024]{2,1,0:T(8,128)(2,1)S(1)} all-gather(bf16[1,16,1024]{2,1,0:T(8,128)(2,1)S(1)} %all-gather), channel_id=3, replica_groups=mesh['front'=4,'row'=4,'z'=16,'core'=2] {'z'}, dimensions={1}, use_global_device_ids=true | all-gather | bytes 557056 | tf_op jit(solution)/shard_map/all_gather | solution.py:52
  47.7 3.4 %collective-permute-start = (bf16[256,1024]{1,0:T(8,128)(2,1)S(1)}, bf16[256,1024]{1,0:T(8,128)(2,1)S(1)}, u32[]{:S(2)}, u32[]{:S(2)}) collective-permute-start(bf16[256,1024]{1,0:T(8,128)(2,1)S(1)} %bitcast.70), channel_id=1, source_target_pairs={{0,32},{32,64},{64,96},{96,0},{1,33},{33,65},{65,97},{97,1},{2,34}... | collective-permute-start | bytes 1572872 | tf_op jit(solution)/shard_map/ppermute | solution.py:28
  51.1 3.7 %collective-permute-start.2 = (bf16[256,1024]{1,0:T(8,128)(2,1)S(1)}, bf16[256,1024]{1,0:T(8,128)(2,1)S(1)}, u32[]{:S(2)}, u32[]{:S(2)}) collective-permute-start(bf16[256,1024]{1,0:T(8,128)(2,1)S(1)} %bitcast.71), channel_id=1, source_target_pairs={{0,96},{32,0},{64,32},{96,64},{1,97},{33,1},{65,33},{97,65},{2,98}... | collective-permute-start | bytes 1572872 | tf_op jit(solution)/shard_map/ppermute | solution.py:31
  54.8 1.3 gather_fusion.3
  56.8 2.5 %sort.35 = (s32[128]{0:T(128)}, s32[128]{0:T(128)S(1)}) sort(s32[128]{0:T(128)S(1)} %fusion.19, s32[128]{0:T(128)S(1)} %iota.46), dimensions={0}, to_apply=%region_1.2 | sort | flops 896 | bytes 2048 | tf_op jit(solution)/shard_map/jit(argsort)/sort | solution.py:79
  59.3 1.2 sort.34
  61.5 2.2 %collective-permute-start.1 = (bf16[256,1024]{1,0:T(8,128)(2,1)S(1)}, bf16[256,1024]{1,0:T(8,128)(2,1)S(1)}, u32[]{:S(2)}, u32[]{:S(2)}) collective-permute-start(bf16[256,1024]{1,0:T(8,128)(2,1)S(1)} %collective-permute-done), channel_id=1, source_target_pairs={{0,32},{32,64},{64,96},{96,0},{1,33},{33,65},{65,97},{97,1},{2,34}... | collective-permute-start | bytes 1572872 | tf_op jit(solution)/shard_map/ppermute | solution.py:28
  63.7 4.4 %compare_select_fusion.1 = s32[256,1]{0,1:T(1,128)S(1)} fusion(s32[]{:T(128)} %bitcast.20, s32[]{:T(128)} %bitcast.21, s32[]{:T(128)} %bitcast.22, s32[]{:T(128)} %bitcast.23, s32[]{:T(128)} %bitcast.24, s32[]{:T(128)} %bitcast.26, s32[]{:T(128)} %bitcast.25), kind=kLoop, calls=%fused_computation.39 | loop fusion | flops 5888 | bytes 1052 | tf_op jit(solution)/shard_map/gather | solution.py:96
  68.3 3.0 %dynamic-slice_bitcast_fusion.2 = (f32[1024,256]{1,0:T(8,128)}, f32[1024,256]{1,0:T(8,128)}) fusion(f32[1,2048,256]{2,1,0:T(8,128)} %param.6, s32[]{:T(128)S(6)} %select_n.193, s32[]{:T(128)S(6)} %select_n.172), kind=kLoop, calls=%fused_computation.16 | loop fusion | bytes 4194312 | tf_op jit(solution)/shard_map/dynamic_slice | solution.py:105
  71.4 5.5 %fusion.10 = s32[256]{0:T(256)S(1)} fusion(pred[256]{0:T(512)(128)(4,1)S(1)} %get-tuple-element.39, pred[256]{0:T(512)(128)(4,1)S(1)} %get-tuple-element.40, pred[256]{0:T(512)(128)(4,1)S(1)} %get-tuple-element.41, pred[256]{0:T(512)(128)(4,1)S(1)} %get-tuple-element.42, pred[256]{0:T(512)(128)(4,1)S(1)} %get-tuple-element.43, ...), kind=kLoop, calls=%fused_computation.74 | loop fusion | flops 4352 | bytes 4388 | tf_op jit(solution)/shard_map/add | solution.py:96
  76.9 1.6 %pad_maximum_fusion = bf16[4,256,1024]{2,1,0:T(8,128)(2,1)} fusion(bf16[1,256,1024]{2,1,0:T(8,128)(2,1)S(1)} %bitcast.75, bf16[1,256,1024]{2,1,0:T(8,128)(2,1)S(1)} %bitcast.76, bf16[1,256,1024]{2,1,0:T(8,128)(2,1)S(1)} %bitcast.74, bf16[1,256,1024]{2,1,0:T(8,128)(2,1)S(1)} %all-gather.1), kind=kLoop, calls=%fused_computation.9 | loop fusion | flops 3145728 | bytes 4194304 | tf_op jit(solution)/shard_map/stack | solution.py:37
  78.5 2.3 %gather_fusion = bf16[4,256,1024]{2,1,0:T(8,128)(2,1)S(1)} fusion(bf16[4,256,1024]{2,1,0:T(8,128)(2,1)} %pad_maximum_fusion, s32[1024]{0:T(1024)S(1)} %pad_clamp_fusion.5), kind=kCustom, calls=%fused_computation | custom fusion | bytes 4194320 | tf_op jit(solution)/shard_map/gather | solution.py:39
  80.8 8.2 %all-gather.5.cloned.1.call-done = bf16[1,2048,1024]{1,2,0:T(8,128)(2,1)} async-done(((bf16[1,2048,32]{1,2,0:T(8,128)(2,1)}), bf16[1,2048,1024]{1,2,0:T(8,128)(2,1)}) %all-gather.5.cloned.1.call-update) | async-done | bytes 4194320 | tf_op jit(solution)/shard_map/all_gather | solution.py:57
  89.0 1.6 %convolution_convert_fusion = bf16[64,1024]{1,0:T(8,128)(2,1)S(1)} fusion(bf16[1024,1024]{1,0:T(8,128)(2,1)S(1)} %bitcast.64, bf16[1,2048,1024]{1,2,0:T(8,128)(2,1)} %all-gather.5.cloned.1.call-done, s32[]{:T(128)S(6)} %select_n.183), kind=kOutput, calls=%fused_computation.14 | convolution fusion | flops 134283264 | bytes 2490372 | tf_op jit(solution)/shard_map/dot_general | solution.py:60
  92.0 3.5 %all-to-all-start = ((bf16[4,64,1024]{2,1,0:T(8,128)(2,1)}), bf16[4,64,1024]{2,1,0:T(8,128)(2,1)S(1)}, u32[]{:S(2)}, u32[]{:S(2)}) async-start(bf16[4,64,1024]{2,1,0:T(8,128)(2,1)} %broadcast_in_dim.27), calls=%async_computation | async-start | bytes 1048576 | tf_op jit(solution)/shard_map/all_to_all | solution.py:92
  95.5 7.0 %fusion.2 = bf16[1024,2048]{1,0:T(8,128)(2,1)S(1)} fusion(bf16[1024,1024]{1,0:T(8,128)(2,1)S(1)} %bitcast.65, bf16[1,2048,1024]{1,2,0:T(8,128)(2,1)} %all-gather.5.cloned.1.call-done), kind=kOutput, calls=%fused_computation.8 | convolution fusion | flops 4297064448 | bytes 10485760 | tf_op jit(solution)/shard_map/dot_general | solution.py:60
  102.6 1.8 %dynamic-slice_bitcast_fusion = (bf16[1024,1024]{0,1:T(8,128)(2,1)}, bf16[1024,1024]{0,1:T(8,128)(2,1)S(1)}) fusion(bf16[1024,2048]{1,0:T(8,128)(2,1)S(1)} %fusion.2, s32[]{:T(128)S(6)} %select_n.193, s32[]{:T(128)S(6)} %select_n.172), kind=kLoop, calls=%fused_computation.10 | loop fusion | bytes 8388616 | tf_op jit(solution)/shard_map/dynamic_slice | solution.py:106
  104.4 1.3 all-to-all-done
  105.7 2.5 %fusion.29 = f32[1024,256]{1,0:T(8,128)S(1)} fusion(bf16[1024,1024]{0,1:T(8,128)(2,1)} %get-tuple-element.16, bf16[256,1024]{1,0:T(8,128)(2,1)S(1)} %bitcast.66), kind=kOutput, calls=%fused_computation.105 | convolution fusion | flops 536870912 | bytes 3670016 | tf_op jit(solution)/shard_map/dot_general | solution.py:15
  108.8 1.4 %gather_fusion.5 = bf16[64,16,256]{2,1,0:T(8,128)(2,1)} fusion(bf16[64,16,256]{2,1,0:T(8,128)(2,1)S(1)} %bitcast.69, s32[1024]{0:T(1024)S(1)} %pad_clamp_fusion), kind=kCustom, calls=%fused_computation.5 | custom fusion | bytes 1048832 | tf_op jit(solution)/shard_map/gather | solution.py:119
  110.2 3.0 %collective-permute-start.3 = (bf16[1024,256]{1,0:T(8,128)(2,1)}, bf16[1024,256]{1,0:T(8,128)(2,1)S(1)}, u32[]{:S(2)}, u32[]{:S(2)}) collective-permute-start(bf16[1024,256]{1,0:T(8,128)(2,1)} %bitcast.73), channel_id=1, source_target_pairs={{0,128},{128,0},{256,384},{384,256},{1,129},{129,1},{257,385},{385... | collective-permute-start | bytes 1572872 | tf_op jit(solution)/shard_map/ppermute | solution.py:11
  115.3 10.4 %collective-permute-done.3 = bf16[1024,256]{1,0:T(8,128)(2,1)S(1)} collective-permute-done((bf16[1024,256]{1,0:T(8,128)(2,1)}, bf16[1024,256]{1,0:T(8,128)(2,1)S(1)}, u32[]{:S(2)}, u32[]{:S(2)}) %collective-permute-start.3) | collective-permute-done | bytes 524320 | tf_op jit(solution)/shard_map/ppermute | solution.py:11
  125.7 1.1 bitcast_add_fusion
  (39 shorter events, 6.6 us)
Async XLA Ops:
  6.5 48.2 %copy-start = (s32[1,512]{1,0:T(1,128)S(1)}, s32[1,512]{1,0:T(1,128)}, u32[]{:S(2)}) copy-start(s32[1,512]{1,0:T(1,128)} %param.7) | copy-start | bytes 6148
  6.5 82.5 %all-gather.5.cloned.1.call-start = ((), (), s32[]{:S(2)}) async-start(), calls=%async_computation.1 | async-start | bytes 4325376 | tf_op jit(solution)/shard_map/all_gather | solution.py:57
  47.7 13.9 %collective-permute-start = (bf16[256,1024]{1,0:T(8,128)(2,1)S(1)}, bf16[256,1024]{1,0:T(8,128)(2,1)S(1)}, u32[]{:S(2)}, u32[]{:S(2)}) collective-permute-start(bf16[256,1024]{1,0:T(8,128)(2,1)S(1)} %bitcast.70), channel_id=1, source_target_pairs={{0,32},{32,64},{64,96},{96,0},{1,33},{33,65},{65,97},{97,1},{2,34}... | collective-permute-start | bytes 1572872 | tf_op jit(solution)/shard_map/ppermute | solution.py:28
  51.1 25.9 %collective-permute-start.2 = (bf16[256,1024]{1,0:T(8,128)(2,1)S(1)}, bf16[256,1024]{1,0:T(8,128)(2,1)S(1)}, u32[]{:S(2)}, u32[]{:S(2)}) collective-permute-start(bf16[256,1024]{1,0:T(8,128)(2,1)S(1)} %bitcast.71), channel_id=1, source_target_pairs={{0,96},{32,0},{64,32},{96,64},{1,97},{33,1},{65,33},{97,65},{2,98}... | collective-permute-start | bytes 1572872 | tf_op jit(solution)/shard_map/ppermute | solution.py:31
  61.5 15.4 %collective-permute-start.1 = (bf16[256,1024]{1,0:T(8,128)(2,1)S(1)}, bf16[256,1024]{1,0:T(8,128)(2,1)S(1)}, u32[]{:S(2)}, u32[]{:S(2)}) collective-permute-start(bf16[256,1024]{1,0:T(8,128)(2,1)S(1)} %collective-permute-done), channel_id=1, source_target_pairs={{0,32},{32,64},{64,96},{96,0},{1,33},{33,65},{65,97},{97,1},{2,34}... | collective-permute-start | bytes 1572872 | tf_op jit(solution)/shard_map/ppermute | solution.py:28
  92.0 13.6 %all-to-all-start = ((bf16[4,64,1024]{2,1,0:T(8,128)(2,1)}), bf16[4,64,1024]{2,1,0:T(8,128)(2,1)S(1)}, u32[]{:S(2)}, u32[]{:S(2)}) async-start(bf16[4,64,1024]{2,1,0:T(8,128)(2,1)} %broadcast_in_dim.27), calls=%async_computation | async-start | bytes 1048576 | tf_op jit(solution)/shard_map/all_to_all | solution.py:92
  105.7 2.5 %copy-start.1 = (f32[1024,256]{1,0:T(8,128)S(1)}, f32[1024,256]{1,0:T(8,128)}, u32[]{:S(2)}) copy-start(f32[1024,256]{1,0:T(8,128)} %get-tuple-element.15) | copy-start | bytes 3145732
  110.2 3.8 %copy-start.2 = (f32[1024,256]{1,0:T(8,128)S(1)}, f32[1024,256]{1,0:T(8,128)}, u32[]{:S(2)}) copy-start(f32[1024,256]{1,0:T(8,128)} %get-tuple-element.11) | copy-start | bytes 3145732
  110.2 15.5 %collective-permute-start.3 = (bf16[1024,256]{1,0:T(8,128)(2,1)}, bf16[1024,256]{1,0:T(8,128)(2,1)S(1)}, u32[]{:S(2)}, u32[]{:S(2)}) collective-permute-start(bf16[1024,256]{1,0:T(8,128)(2,1)} %bitcast.73), channel_id=1, source_target_pairs={{0,128},{128,0},{256,384},{384,256},{1,129},{129,1},{257,385},{385... | collective-permute-start | bytes 1572872 | tf_op jit(solution)/shard_map/ppermute | solution.py:11
Sparse Core Ops, SparseCore 0:
  9.5 79.5 all-gather.4

commit v15 on v14

--- a/solution.py
+++ b/solution.py
@@ -88,10 +88,9 @@
         lax.dynamic_slice_in_dim(gather_col, row_index * per_class, per_class, 0)
         - row_index * per_class
     )
-    piece = piece.reshape(per_class, width, order)[own_blocks].reshape(share, order)
-    col_side = lax.all_to_all(
-        jnp.broadcast_to(piece[None], (nrow,) + piece.shape), "row", 0, 0, tiled=True
-    ).reshape(cols_here, order)
+    copies = jnp.tile(own_blocks, nrow)
+    piece = piece.reshape(per_class, width, order)[copies].reshape(nrow, share, order)
+    col_side = lax.all_to_all(piece, "row", 0, 0, tiled=True).reshape(cols_here, order)
     lane = jnp.arange(cols_here, dtype=jnp.int32)
     picked = gather_col[lane // width] * width + lane % width
     select_cols = (lane[:, None] == picked[None, :]).astype(jnp.float32)

time: 135 us -> 135 us (level)
  starting transfers between devices: 15.7 us -> 17.5 us
  waiting for transfers between devices: 20.6 us -> 18.9 us
    all_to_all x1, starting transfers between devices: 3.47 us -> 5.65 us  [local(): lax.all_to_all(piece, 'row', 0, 0, tiled=True).reshape(cols_here, order)]
    all_gather x1, waiting for transfers between devices: 8.2 us -> 6.78 us  [local(): columns = lax.all_gather(panel[0], ('z', 'core'), axis=1, tiled=True)]
where the time goes in v15:
time: 135 us; the launch traced here: 134 us
  blocking collectives  40.4 us (30%)
  waiting for transfers between devices  18.9 us (14%)
  starting transfers between devices  17.5 us (13%)
  other arithmetic  16.8 us (12%)
  between operations  13.7 us (10%)
  local copies, waits for them, and re-layouts  13.3 us (10%)
  matrix products  13.1 us (10%)
    all_gather x1, blocking collectives, local(): inverse = lax.all_gather(inverse, 'z', axis=0, tiled=True)  38.4 us
    ppermute x1, waiting for transfers between devices, from_partner(): return lax.ppermute(value, axis, pairs)  10.4 us
    dot_general x2, matrix products, solve(): jnp.dot(rows, inverse, preferred_element_type=jnp.float32)  8.6 us
    all_gather x1, waiting for transfers between devices, local(): columns = lax.all_gather(panel[0], ('z', 'core'), axis=1, tiled=True)  6.78 us
    all_to_all x1, starting transfers between devices, local(): lax.all_to_all(piece, 'row', 0, 0, tiled=True).reshape(cols_here, order)  5.65 us
    ppermute x2, starting transfers between devices, ring_gather(): forward = lax.ppermute(forward, axis, ahead)  5.58 us
    add x1, other arithmetic, local(): picked = gather_col[lane // width] * width + lane % width  5.55 us
    gather x6, other arithmetic, local(): picked = gather_col[lane // width] * width + lane % width  4.59 us
  transfers between devices with their start and end apart: 6, of which 3 were waited for; matrix products, arithmetic and copies ran while one was open for 26% of the time, Pallas kernels for 0%

profile of v15, /device:TPU:24, one launch (start us, length us, event | category | flops | bytes accessed | tf_op | source)
XLA Modules:
  0.0 133.8 jit_solution(7582487865372526733)
XLA Ops:
  7.3 2.0 %all-gather = bf16[1,16,1024]{2,1,0:T(8,128)(2,1)S(1)} all-gather(bf16[1,8,1024]{2,1,0:T(8,128)(2,1)} %param.4), channel_id=2, replica_groups=mesh['front'=4,'row'=4,'z'=16,'core'=2] {'core'}, dimensions={1}, use_global_device_ids=true | all-gather | bytes 49152 | tf_op jit(solution)/shard_map/all_gather | solution.py:51
  9.3 38.4 %all-gather.1 = bf16[1,256,1024]{2,1,0:T(8,128)(2,1)S(1)} all-gather(bf16[1,16,1024]{2,1,0:T(8,128)(2,1)S(1)} %all-gather), channel_id=3, replica_groups=mesh['front'=4,'row'=4,'z'=16,'core'=2] {'z'}, dimensions={1}, use_global_device_ids=true | all-gather | bytes 557056 | tf_op jit(solution)/shard_map/all_gather | solution.py:52
  47.7 3.4 %collective-permute-start = (bf16[256,1024]{1,0:T(8,128)(2,1)S(1)}, bf16[256,1024]{1,0:T(8,128)(2,1)S(1)}, u32[]{:S(2)}, u32[]{:S(2)}) collective-permute-start(bf16[256,1024]{1,0:T(8,128)(2,1)S(1)} %bitcast.73), channel_id=1, source_target_pairs={{0,32},{32,64},{64,96},{96,0},{1,33},{33,65},{65,97},{97,1},{2,34}... | collective-permute-start | bytes 1572872 | tf_op jit(solution)/shard_map/ppermute | solution.py:28
  51.1 3.7 %collective-permute-start.2 = (bf16[256,1024]{1,0:T(8,128)(2,1)S(1)}, bf16[256,1024]{1,0:T(8,128)(2,1)S(1)}, u32[]{:S(2)}, u32[]{:S(2)}) collective-permute-start(bf16[256,1024]{1,0:T(8,128)(2,1)S(1)} %bitcast.74), channel_id=1, source_target_pairs={{0,96},{32,0},{64,32},{96,64},{1,97},{33,1},{65,33},{97,65},{2,98}... | collective-permute-start | bytes 1572872 | tf_op jit(solution)/shard_map/ppermute | solution.py:31
  54.8 1.3 gather_fusion.3
  56.8 1.2 sort.34
  58.2 2.5 %sort.35 = (s32[128]{0:T(128)}, s32[128]{0:T(128)S(1)}) sort(s32[128]{0:T(128)S(1)} %fusion.19, s32[128]{0:T(128)S(1)} %iota.46), dimensions={0}, to_apply=%region_1.2 | sort | flops 896 | bytes 2048 | tf_op jit(solution)/shard_map/jit(argsort)/sort | solution.py:79
  61.6 2.2 %collective-permute-start.1 = (bf16[256,1024]{1,0:T(8,128)(2,1)S(1)}, bf16[256,1024]{1,0:T(8,128)(2,1)S(1)}, u32[]{:S(2)}, u32[]{:S(2)}) collective-permute-start(bf16[256,1024]{1,0:T(8,128)(2,1)S(1)} %collective-permute-done), channel_id=1, source_target_pairs={{0,32},{32,64},{64,96},{96,0},{1,33},{33,65},{65,97},{97,1},{2,34}... | collective-permute-start | bytes 1572872 | tf_op jit(solution)/shard_map/ppermute | solution.py:28
  63.8 4.4 %compare_select_fusion.1 = s32[256,1]{0,1:T(1,128)S(1)} fusion(s32[]{:T(128)} %bitcast.20, s32[]{:T(128)} %bitcast.21, s32[]{:T(128)} %bitcast.22, s32[]{:T(128)} %bitcast.23, s32[]{:T(128)} %bitcast.24, s32[]{:T(128)} %bitcast.26, s32[]{:T(128)} %bitcast.25), kind=kLoop, calls=%fused_computation.39 | loop fusion | flops 5888 | bytes 1052 | tf_op jit(solution)/shard_map/gather | solution.py:95
  68.4 3.0 %dynamic-slice_bitcast_fusion.2 = (f32[1024,256]{1,0:T(8,128)}, f32[1024,256]{1,0:T(8,128)}) fusion(f32[1,2048,256]{2,1,0:T(8,128)} %param.6, s32[]{:T(128)S(6)} %select_n.200, s32[]{:T(128)S(6)} %select_n.179), kind=kLoop, calls=%fused_computation.16 | loop fusion | bytes 4194312 | tf_op jit(solution)/shard_map/dynamic_slice | solution.py:104
  71.5 5.5 %fusion.10 = s32[256]{0:T(256)S(1)} fusion(pred[256]{0:T(512)(128)(4,1)S(1)} %get-tuple-element.39, pred[256]{0:T(512)(128)(4,1)S(1)} %get-tuple-element.40, pred[256]{0:T(512)(128)(4,1)S(1)} %get-tuple-element.41, pred[256]{0:T(512)(128)(4,1)S(1)} %get-tuple-element.42, pred[256]{0:T(512)(128)(4,1)S(1)} %get-tuple-element.43, ...), kind=kLoop, calls=%fused_computation.74 | loop fusion | flops 4352 | bytes 4388 | tf_op jit(solution)/shard_map/add | solution.py:95
  77.1 1.6 %pad_maximum_fusion = bf16[4,256,1024]{2,1,0:T(8,128)(2,1)} fusion(bf16[1,256,1024]{2,1,0:T(8,128)(2,1)S(1)} %bitcast.77, bf16[1,256,1024]{2,1,0:T(8,128)(2,1)S(1)} %bitcast.78, bf16[1,256,1024]{2,1,0:T(8,128)(2,1)S(1)} %bitcast.76, bf16[1,256,1024]{2,1,0:T(8,128)(2,1)S(1)} %all-gather.1), kind=kLoop, calls=%fused_computation.9 | loop fusion | flops 3145728 | bytes 4194304 | tf_op jit(solution)/shard_map/stack | solution.py:37
  78.7 2.3 %gather_fusion = bf16[4,256,1024]{2,1,0:T(8,128)(2,1)S(1)} fusion(bf16[4,256,1024]{2,1,0:T(8,128)(2,1)} %pad_maximum_fusion, s32[1024]{0:T(1024)S(1)} %pad_clamp_fusion.5), kind=kCustom, calls=%fused_computation | custom fusion | bytes 4194320 | tf_op jit(solution)/shard_map/gather | solution.py:39
  81.0 6.8 %all-gather.5.cloned.1.call-done = bf16[1,2048,1024]{1,2,0:T(8,128)(2,1)} async-done(((bf16[1,2048,32]{1,2,0:T(8,128)(2,1)}), bf16[1,2048,1024]{1,2,0:T(8,128)(2,1)}) %all-gather.5.cloned.1.call-update) | async-done | bytes 4194320 | tf_op jit(solution)/shard_map/all_gather | solution.py:57
  87.7 1.6 %convolution_convert_fusion = bf16[64,1024]{1,0:T(8,128)(2,1)S(1)} fusion(bf16[1024,1024]{1,0:T(8,128)(2,1)S(1)} %bitcast.66, bf16[1,2048,1024]{1,2,0:T(8,128)(2,1)} %all-gather.5.cloned.1.call-done, s32[]{:T(128)S(6)} %select_n.190), kind=kOutput, calls=%fused_computation.14 | convolution fusion | flops 134283264 | bytes 2490372 | tf_op jit(solution)/shard_map/dot_general | solution.py:60
  89.3 1.4 %gather_fusion.2 = bf16[16,16,1024]{2,1,0:T(8,128)(2,1)} fusion(bf16[4,16,1024]{2,1,0:T(8,128)(2,1)S(1)} %bitcast.71, s32[1024]{0:T(1024)S(1)} %pad_clamp_fusion.3), kind=kCustom, calls=%fused_computation.2 | custom fusion | bytes 1048640 | tf_op jit(solution)/shard_map/gather | solution.py:92
  90.7 5.7 %all-to-all-start = ((bf16[4,64,1024]{2,1,0:T(8,128)(2,1)}), bf16[4,64,1024]{2,1,0:T(8,128)(2,1)S(1)}, u32[]{:S(2)}, u32[]{:S(2)}) async-start(bf16[4,64,1024]{2,1,0:T(8,128)(2,1)} %bitcast.31), calls=%async_computation | async-start | bytes 1048576 | tf_op jit(solution)/shard_map/all_to_all | solution.py:93
  96.3 7.0 %fusion.2 = bf16[1024,2048]{1,0:T(8,128)(2,1)S(1)} fusion(bf16[1024,1024]{1,0:T(8,128)(2,1)S(1)} %bitcast.67, bf16[1,2048,1024]{1,2,0:T(8,128)(2,1)} %all-gather.5.cloned.1.call-done), kind=kOutput, calls=%fused_computation.8 | convolution fusion | flops 4297064448 | bytes 10485760 | tf_op jit(solution)/shard_map/dot_general | solution.py:60
  103.4 1.8 %dynamic-slice_bitcast_fusion = (bf16[1024,1024]{0,1:T(8,128)(2,1)}, bf16[1024,1024]{0,1:T(8,128)(2,1)S(1)}) fusion(bf16[1024,2048]{1,0:T(8,128)(2,1)S(1)} %fusion.2, s32[]{:T(128)S(6)} %select_n.200, s32[]{:T(128)S(6)} %select_n.179), kind=kLoop, calls=%fused_computation.10 | loop fusion | bytes 8388616 | tf_op jit(solution)/shard_map/dynamic_slice | solution.py:105
  106.2 2.5 %fusion.30 = f32[1024,256]{1,0:T(8,128)S(1)} fusion(bf16[1024,1024]{0,1:T(8,128)(2,1)} %get-tuple-element.16, bf16[256,1024]{1,0:T(8,128)(2,1)S(1)} %bitcast.68), kind=kOutput, calls=%fused_computation.107 | convolution fusion | flops 536870912 | bytes 3670016 | tf_op jit(solution)/shard_map/dot_general | solution.py:15
  109.4 1.4 %gather_fusion.5 = bf16[64,16,256]{2,1,0:T(8,128)(2,1)} fusion(bf16[64,16,256]{2,1,0:T(8,128)(2,1)S(1)} %bitcast.72, s32[1024]{0:T(1024)S(1)} %pad_clamp_fusion), kind=kCustom, calls=%fused_computation.5 | custom fusion | bytes 1048832 | tf_op jit(solution)/shard_map/gather | solution.py:118
  110.7 2.7 %collective-permute-start.3 = (bf16[1024,256]{1,0:T(8,128)(2,1)}, bf16[1024,256]{1,0:T(8,128)(2,1)S(1)}, u32[]{:S(2)}, u32[]{:S(2)}) collective-permute-start(bf16[1024,256]{1,0:T(8,128)(2,1)} %bitcast.75), channel_id=1, source_target_pairs={{0,128},{128,0},{256,384},{384,256},{1,129},{129,1},{257,385},{385... | collective-permute-start | bytes 1572872 | tf_op jit(solution)/shard_map/ppermute | solution.py:11
  115.5 10.4 %collective-permute-done.3 = bf16[1024,256]{1,0:T(8,128)(2,1)S(1)} collective-permute-done((bf16[1024,256]{1,0:T(8,128)(2,1)}, bf16[1024,256]{1,0:T(8,128)(2,1)S(1)}, u32[]{:S(2)}, u32[]{:S(2)}) %collective-permute-start.3) | collective-permute-done | bytes 524320 | tf_op jit(solution)/shard_map/ppermute | solution.py:11
  125.9 1.1 bitcast_add_fusion
  (41 shorter events, 6.3 us)
Async XLA Ops:
  6.5 48.2 %copy-start = (s32[1,512]{1,0:T(1,128)S(1)}, s32[1,512]{1,0:T(1,128)}, u32[]{:S(2)}) copy-start(s32[1,512]{1,0:T(1,128)} %param.7) | copy-start | bytes 6148
  6.5 81.2 %all-gather.5.cloned.1.call-start = ((), (), s32[]{:S(2)}) async-start(), calls=%async_computation.1 | async-start | bytes 4325376 | tf_op jit(solution)/shard_map/all_gather | solution.py:57
  47.7 14.0 %collective-permute-start = (bf16[256,1024]{1,0:T(8,128)(2,1)S(1)}, bf16[256,1024]{1,0:T(8,128)(2,1)S(1)}, u32[]{:S(2)}, u32[]{:S(2)}) collective-permute-start(bf16[256,1024]{1,0:T(8,128)(2,1)S(1)} %bitcast.73), channel_id=1, source_target_pairs={{0,32},{32,64},{64,96},{96,0},{1,33},{33,65},{65,97},{97,1},{2,34}... | collective-permute-start | bytes 1572872 | tf_op jit(solution)/shard_map/ppermute | solution.py:28
  51.1 26.0 %collective-permute-start.2 = (bf16[256,1024]{1,0:T(8,128)(2,1)S(1)}, bf16[256,1024]{1,0:T(8,128)(2,1)S(1)}, u32[]{:S(2)}, u32[]{:S(2)}) collective-permute-start(bf16[256,1024]{1,0:T(8,128)(2,1)S(1)} %bitcast.74), channel_id=1, source_target_pairs={{0,96},{32,0},{64,32},{96,64},{1,97},{33,1},{65,33},{97,65},{2,98}... | collective-permute-start | bytes 1572872 | tf_op jit(solution)/shard_map/ppermute | solution.py:31
  61.6 15.4 %collective-permute-start.1 = (bf16[256,1024]{1,0:T(8,128)(2,1)S(1)}, bf16[256,1024]{1,0:T(8,128)(2,1)S(1)}, u32[]{:S(2)}, u32[]{:S(2)}) collective-permute-start(bf16[256,1024]{1,0:T(8,128)(2,1)S(1)} %collective-permute-done), channel_id=1, source_target_pairs={{0,32},{32,64},{64,96},{96,0},{1,33},{33,65},{65,97},{97,1},{2,34}... | collective-permute-start | bytes 1572872 | tf_op jit(solution)/shard_map/ppermute | solution.py:28
  90.7 15.5 %all-to-all-start = ((bf16[4,64,1024]{2,1,0:T(8,128)(2,1)}), bf16[4,64,1024]{2,1,0:T(8,128)(2,1)S(1)}, u32[]{:S(2)}, u32[]{:S(2)}) async-start(bf16[4,64,1024]{2,1,0:T(8,128)(2,1)} %bitcast.31), calls=%async_computation | async-start | bytes 1048576 | tf_op jit(solution)/shard_map/all_to_all | solution.py:93
  106.2 2.5 %copy-start.1 = (f32[1024,256]{1,0:T(8,128)S(1)}, f32[1024,256]{1,0:T(8,128)}, u32[]{:S(2)}) copy-start(f32[1024,256]{1,0:T(8,128)} %get-tuple-element.15) | copy-start | bytes 3145732
  110.7 3.4 %copy-start.2 = (f32[1024,256]{1,0:T(8,128)S(1)}, f32[1024,256]{1,0:T(8,128)}, u32[]{:S(2)}) copy-start(f32[1024,256]{1,0:T(8,128)} %get-tuple-element.11) | copy-start | bytes 3145732
  110.7 15.2 %collective-permute-start.3 = (bf16[1024,256]{1,0:T(8,128)(2,1)}, bf16[1024,256]{1,0:T(8,128)(2,1)S(1)}, u32[]{:S(2)}, u32[]{:S(2)}) collective-permute-start(bf16[1024,256]{1,0:T(8,128)(2,1)} %bitcast.75), channel_id=1, source_target_pairs={{0,128},{128,0},{256,384},{384,256},{1,129},{129,1},{257,385},{385... | collective-permute-start | bytes 1572872 | tf_op jit(solution)/shard_map/ppermute | solution.py:11
Sparse Core Ops, SparseCore 0:
  9.5 78.2 all-gather.4

commit v16 on v15

--- a/solution.py
+++ b/solution.py
@@ -100,9 +100,11 @@
     half = rows_here // 2
     half_blocks = half // width
 
-    def half_update(which):
-        rows = lax.dynamic_slice_in_dim(local_trailing, which * half, half, 0)
-        low = lax.dynamic_slice_in_dim(solved, which * half, half, 0)
+    def half_update(which, part, parts):
+        size = half // parts
+        first = which * half + part * size
+        rows = lax.dynamic_slice_in_dim(local_trailing, first, size, 0)
+        low = lax.dynamic_slice_in_dim(solved, first, size, 0)
         rows, low = lax.optimization_barrier((rows, low))
         moved_cols = jnp.dot(
             rows,
@@ -111,17 +113,19 @@
             preferred_element_type=jnp.float32,
         )
         schur = moved_cols - outer_rows(low, col_side)
+        count = size // width
         blocks = (
-            lax.dynamic_slice_in_dim(gather_row, which * half_blocks, half_blocks, 0)
-            - which * half_blocks
+            lax.dynamic_slice_in_dim(gather_row, first // width, count, 0)
+            - first // width
         )
-        return schur.reshape(half_blocks, width, cols_here)[blocks].reshape(
-            half, cols_here
-        )
+        return schur.reshape(count, width, cols_here)[blocks].reshape(size, cols_here)
 
-    outgoing = half_update(1 - member).astype(jnp.bfloat16)
-    incoming = from_partner(outgoing, "front", 0)
-    keep = half_update(member)
+    incoming = []
+    for part in range(2):
+        outgoing = half_update(1 - member, part, 2).astype(jnp.bfloat16)
+        incoming.append(from_partner(outgoing, "front", 0))
+    incoming = jnp.concatenate(incoming, axis=0)
+    keep = half_update(member, 0, 1)
     return (keep + incoming.astype(jnp.float32))[None]
 
 

time: 135 us -> 144 us (1.067)
  matrix products: 13.1 us -> 17.1 us
  starting transfers between devices: 17.5 us -> 20.8 us
  other arithmetic: 16.8 us -> 19.2 us
    ppermute x1 -> x2, waiting for transfers between devices: 10.4 us -> 4.64 us  [from_partner(): return lax.ppermute(value, axis, pairs)]
    all_to_all x1, waiting for transfers between devices: 1.02 us -> 6.39 us  [local(): lax.all_to_all(piece, 'row', 0, 0, tiled=True).reshape(cols_here, order)]
    ppermute x1 -> x2, starting transfers between devices: 2.65 us -> 5.96 us  [from_partner(): return lax.ppermute(value, axis, pairs)]
    dot_general x2 -> x3, matrix products: 1.28 us -> 4.14 us  [half_update(): jnp.dot(rows, select_cols, precision=lax.Precision.HIGHEST, preferred_ele...]
    dot_general x2 -> x3, matrix products: 3.23 us -> 4.36 us  [outer_rows(): lax.dot_general(left, right, (((1,), (1,)), ((), ())), preferred_element_...]
    dynamic_slice x2 -> x4, local copies, waits for them, and re-layouts: 4.86 us -> 3.8 us  [the longest x2 2.02 us: half_update(): rows = lax.dynamic_slice_in_dim(local_trailing, first, size, 0)]
  transfers between devices with their start and end apart: 6 -> 7, of which waited for: 3 -> 4; matrix products, arithmetic and copies ran while one was open for 26% -> 22% of each run, Pallas kernels for 0% -> 0%
where the time goes in v16:
time: 144 us
  blocking collectives  40.4 us (28%)
  starting transfers between devices  20.8 us (14%)
  other arithmetic  19.2 us (13%)
  waiting for transfers between devices  18.1 us (13%)
  matrix products  17.1 us (12%)
  local copies, waits for them, and re-layouts  14.1 us (10%)
  between operations  13.8 us (10%)
    all_gather x1, blocking collectives, local(): inverse = lax.all_gather(inverse, 'z', axis=0, tiled=True)  38.4 us
    dot_general x2, matrix products, solve(): jnp.dot(rows, inverse, preferred_element_type=jnp.float32)  8.6 us
    all_to_all x1, waiting for transfers between devices, local(): lax.all_to_all(piece, 'row', 0, 0, tiled=True).reshape(cols_here, order)  6.39 us
    all_gather x1, waiting for transfers between devices, local(): columns = lax.all_gather(panel[0], ('z', 'core'), axis=1, tiled=True)  6.33 us
    ppermute x2, starting transfers between devices, from_partner(): return lax.ppermute(value, axis, pairs)  5.96 us
    all_to_all x1, starting transfers between devices, local(): lax.all_to_all(piece, 'row', 0, 0, tiled=True).reshape(cols_here, order)  5.63 us
    add x1, other arithmetic, local(): picked = gather_col[lane // width] * width + lane % width  5.58 us
    ppermute x2, starting transfers between devices, ring_gather(): forward = lax.ppermute(forward, axis, ahead)  5.58 us
  transfers between devices with their start and end apart: 7, of which 4 were waited for; matrix products, arithmetic and copies ran while one was open for 22% of the time, Pallas kernels for 0%

profile of v16, /device:TPU:24, one launch (start us, length us, event | category | flops | bytes accessed | tf_op | source)
XLA Modules:
  0.0 143.5 jit_solution(11484214017025577643)
XLA Ops:
  7.3 2.0 %all-gather = bf16[1,16,1024]{2,1,0:T(8,128)(2,1)S(1)} all-gather(bf16[1,8,1024]{2,1,0:T(8,128)(2,1)} %param.4), channel_id=2, replica_groups=mesh['front'=4,'row'=4,'z'=16,'core'=2] {'core'}, dimensions={1}, use_global_device_ids=true | all-gather | bytes 49152 | tf_op jit(solution)/shard_map/all_gather | solution.py:51
  9.3 38.4 %all-gather.1 = bf16[1,256,1024]{2,1,0:T(8,128)(2,1)S(1)} all-gather(bf16[1,16,1024]{2,1,0:T(8,128)(2,1)S(1)} %all-gather), channel_id=3, replica_groups=mesh['front'=4,'row'=4,'z'=16,'core'=2] {'z'}, dimensions={1}, use_global_device_ids=true | all-gather | bytes 557056 | tf_op jit(solution)/shard_map/all_gather | solution.py:52
  47.7 3.4 %collective-permute-start = (bf16[256,1024]{1,0:T(8,128)(2,1)S(1)}, bf16[256,1024]{1,0:T(8,128)(2,1)}, u32[]{:S(2)}, u32[]{:S(2)}) collective-permute-start(bf16[256,1024]{1,0:T(8,128)(2,1)S(1)} %bitcast.86), channel_id=1, source_target_pairs={{0,32},{32,64},{64,96},{96,0},{1,33},{33,65},{65,97},{97,1},{2,34}... | collective-permute-start | bytes 1572872 | tf_op jit(solution)/shard_map/ppermute | solution.py:28
  51.1 3.7 %collective-permute-start.2 = (bf16[256,1024]{1,0:T(8,128)(2,1)S(1)}, bf16[256,1024]{1,0:T(8,128)(2,1)}, u32[]{:S(2)}, u32[]{:S(2)}) collective-permute-start(bf16[256,1024]{1,0:T(8,128)(2,1)S(1)} %bitcast.87), channel_id=1, source_target_pairs={{0,96},{32,0},{64,32},{96,64},{1,97},{33,1},{65,33},{97,65},{2,98}... | collective-permute-start | bytes 1572872 | tf_op jit(solution)/shard_map/ppermute | solution.py:31
  58.3 2.5 %sort.35 = (s32[128]{0:T(128)}, s32[128]{0:T(128)S(1)}) sort(s32[128]{0:T(128)S(1)} %fusion.22, s32[128]{0:T(128)S(1)} %iota.46), dimensions={0}, to_apply=%region_1.2 | sort | flops 896 | bytes 2048 | tf_op jit(solution)/shard_map/jit(argsort)/sort | solution.py:79
  61.8 2.2 %collective-permute-start.1 = (bf16[256,1024]{1,0:T(8,128)(2,1)}, bf16[256,1024]{1,0:T(8,128)(2,1)}, u32[]{:S(2)}, u32[]{:S(2)}) collective-permute-start(bf16[256,1024]{1,0:T(8,128)(2,1)} %collective-permute-done), channel_id=1, source_target_pairs={{0,32},{32,64},{64,96},{96,0},{1,33},{33,65},{65,97},{97,1},{2,34}... | collective-permute-start | bytes 1572872 | tf_op jit(solution)/shard_map/ppermute | solution.py:28
  64.0 4.4 %compare_select_fusion.1 = s32[256,1]{0,1:T(1,128)S(1)} fusion(s32[]{:T(128)} %bitcast.20, s32[]{:T(128)} %bitcast.21, s32[]{:T(128)} %bitcast.22, s32[]{:T(128)} %bitcast.23, s32[]{:T(128)} %bitcast.24, s32[]{:T(128)} %bitcast.26, s32[]{:T(128)} %bitcast.25), kind=kLoop, calls=%fused_computation.47 | loop fusion | flops 5888 | bytes 1052 | tf_op jit(solution)/shard_map/gather | solution.py:95
  70.6 5.6 %fusion.13 = s32[256]{0:T(256)S(1)} fusion(pred[256]{0:T(512)(128)(4,1)S(1)} %get-tuple-element.43, pred[256]{0:T(512)(128)(4,1)S(1)} %get-tuple-element.44, pred[256]{0:T(512)(128)(4,1)S(1)} %get-tuple-element.45, pred[256]{0:T(512)(128)(4,1)S(1)} %get-tuple-element.46, pred[256]{0:T(512)(128)(4,1)S(1)} %get-tuple-element.47, ...), kind=kLoop, calls=%fused_computation.83 | loop fusion | flops 4352 | bytes 4388 | tf_op jit(solution)/shard_map/add | solution.py:95
  76.2 3.0 %pad_maximum_fusion = bf16[4,256,1024]{2,1,0:T(8,128)(2,1)} fusion(bf16[1,256,1024]{2,1,0:T(8,128)(2,1)} %bitcast.4, bf16[1,256,1024]{2,1,0:T(8,128)(2,1)} %bitcast.3, bf16[1,256,1024]{2,1,0:T(8,128)(2,1)} %bitcast.2, bf16[1,256,1024]{2,1,0:T(8,128)(2,1)S(1)} %all-gather.1), kind=kLoop, calls=%fused_computation.10 | loop fusion | flops 3145728 | bytes 4194304 | tf_op jit(solution)/shard_map/stack | solution.py:37
  79.2 2.3 %gather_fusion = bf16[4,256,1024]{2,1,0:T(8,128)(2,1)S(1)} fusion(bf16[4,256,1024]{2,1,0:T(8,128)(2,1)} %pad_maximum_fusion, s32[1024]{0:T(1024)S(1)} %pad_clamp_fusion.6), kind=kCustom, calls=%fused_computation | custom fusion | bytes 4194320 | tf_op jit(solution)/shard_map/gather | solution.py:39
  81.5 6.3 %all-gather.5.cloned.1.call-done = bf16[1,2048,1024]{1,2,0:T(8,128)(2,1)} async-done(((bf16[1,2048,32]{1,2,0:T(8,128)(2,1)}), bf16[1,2048,1024]{1,2,0:T(8,128)(2,1)}) %all-gather.5.cloned.1.call-update) | async-done | bytes 4194320 | tf_op jit(solution)/shard_map/all_gather | solution.py:57
  87.8 7.0 %fusion.2 = bf16[1024,2048]{1,0:T(8,128)(2,1)S(1)} fusion(bf16[1024,1024]{1,0:T(8,128)(2,1)S(1)} %bitcast.77, bf16[1,2048,1024]{1,2,0:T(8,128)(2,1)} %all-gather.5.cloned.1.call-done), kind=kOutput, calls=%fused_computation.9 | convolution fusion | flops 4297064448 | bytes 10485760 | tf_op jit(solution)/shard_map/dot_general | solution.py:60
  94.8 1.6 %dynamic-slice_bitcast_fusion.2 = (bf16[512,1024]{0,1:T(8,128)(2,1)}, bf16[512,1024]{0,1:T(8,128)(2,1)}) fusion(bf16[1024,2048]{1,0:T(8,128)(2,1)S(1)} %fusion.2, s32[]{:T(128)S(6)} %select_n.224, s32[]{:T(128)S(6)} %select_n.228), kind=kLoop, calls=%fused_computation.18 | loop fusion | bytes 4194312 | tf_op jit(solution)/shard_map/dynamic_slice | solution.py:107
  98.0 1.6 %convolution_convert_fusion = bf16[64,1024]{1,0:T(8,128)(2,1)S(1)} fusion(bf16[1024,1024]{1,0:T(8,128)(2,1)S(1)} %bitcast.78, bf16[1,2048,1024]{1,2,0:T(8,128)(2,1)} %all-gather.5.cloned.1.call-done, s32[]{:T(128)S(6)} %select_n.213), kind=kOutput, calls=%fused_computation.15 | convolution fusion | flops 134283264 | bytes 2490372 | tf_op jit(solution)/shard_map/dot_general | solution.py:60
  99.6 1.4 gather_fusion.2
  100.9 5.6 %all-to-all-start = ((bf16[4,64,1024]{2,1,0:T(8,128)(2,1)}), bf16[4,64,1024]{2,1,0:T(8,128)(2,1)S(1)}, u32[]{:S(2)}, u32[]{:S(2)}) async-start(bf16[4,64,1024]{2,1,0:T(8,128)(2,1)} %bitcast.85), calls=%async_computation | async-start | bytes 1048576 | tf_op jit(solution)/shard_map/all_to_all | solution.py:93
  106.6 2.3 %fusion.8 = f32[512,256]{1,0:T(8,128)} fusion(f32[512,256]{1,0:T(8,128)} %get-tuple-element.17, s32[256]{0:T(256)S(1)} %fusion.13), kind=kOutput, calls=%fused_computation.26 | convolution fusion | flops 402718720 | bytes 1049600 | tf_op jit(solution)/shard_map/dot_general | solution.py:109
  110.1 6.4 %all-to-all-done = bf16[4,64,1024]{2,1,0:T(8,128)(2,1)S(1)} async-done(((bf16[4,64,1024]{2,1,0:T(8,128)(2,1)}), bf16[4,64,1024]{2,1,0:T(8,128)(2,1)S(1)}, u32[]{:S(2)}, u32[]{:S(2)}) %all-to-all-start) | async-done | bytes 524320 | tf_op jit(solution)/shard_map/all_to_all | solution.py:93
  116.5 1.9 %convolution_subtract_fusion.1 = bf16[512,256]{1,0:T(8,128)(2,1)S(1)} fusion(f32[512,256]{1,0:T(8,128)} %fusion.7, bf16[512,1024]{0,1:T(8,128)(2,1)} %get-tuple-element.20, bf16[256,1024]{1,0:T(8,128)(2,1)S(1)} %bitcast.79), kind=kOutput, calls=%fused_computation.13 | convolution fusion | flops 268697600 | bytes 2359296 | tf_op jit(solution)/shard_map/dot_general | solution.py:15
  119.6 2.5 %collective-permute-start.4 = (bf16[512,256]{1,0:T(8,128)(2,1)}, bf16[512,256]{1,0:T(8,128)(2,1)}, u32[]{:S(2)}, u32[]{:S(2)}) collective-permute-start(bf16[512,256]{1,0:T(8,128)(2,1)} %bitcast.91), channel_id=1, source_target_pairs={{0,128},{128,0},{256,384},{384,256},{1,129},{129,1},{257,385},{385... | collective-permute-start | bytes 786440 | tf_op jit(solution)/shard_map/ppermute | solution.py:11
  122.1 1.7 %convolution_subtract_fusion.2 = bf16[512,256]{1,0:T(8,128)(2,1)S(1)} fusion(f32[512,256]{1,0:T(8,128)S(1)} %copy-done.5, bf16[512,1024]{0,1:T(8,128)(2,1)} %get-tuple-element.18, bf16[256,1024]{1,0:T(8,128)(2,1)S(1)} %bitcast.80), kind=kOutput, calls=%fused_computation.14 | convolution fusion | flops 268697600 | bytes 2359296 | tf_op jit(solution)/shard_map/dot_general | solution.py:15
  124.5 3.5 %collective-permute-start.3 = (bf16[512,256]{1,0:T(8,128)(2,1)S(1)}, bf16[512,256]{1,0:T(8,128)(2,1)S(1)}, u32[]{:S(2)}, u32[]{:S(2)}) collective-permute-start(bf16[512,256]{1,0:T(8,128)(2,1)S(1)} %bitcast.92), channel_id=1, source_target_pairs={{0,128},{128,0},{256,384},{384,256},{1,129},{129,1},{257,385},{385... | collective-permute-start | bytes 786440 | tf_op jit(solution)/shard_map/ppermute | solution.py:11
  130.2 4.5 %collective-permute-done.3 = bf16[512,256]{1,0:T(8,128)(2,1)S(1)} collective-permute-done((bf16[512,256]{1,0:T(8,128)(2,1)S(1)}, bf16[512,256]{1,0:T(8,128)(2,1)S(1)}, u32[]{:S(2)}, u32[]{:S(2)}) %collective-permute-start.3) | collective-permute-done | bytes 262176 | tf_op jit(solution)/shard_map/ppermute | solution.py:11
  134.6 2.0 %bitcast_add_fusion = f32[1,1024,256]{2,1,0:T(8,128)} fusion(bf16[1,512,256]{2,1,0:T(8,128)(2,1)} %bitcast.45, bf16[1,512,256]{2,1,0:T(8,128)(2,1)S(1)} %bitcast.90, f32[1,1024,256]{2,1,0:T(8,128)S(1)} %bitcast.82), kind=kLoop, calls=%fused_computation.16 | loop fusion | flops 1310720 | bytes 2621440 | tf_op jit(solution)/shard_map/add | solution.py:129
  (55 shorter events, 14.1 us)
Async XLA Ops:
  6.5 48.3 %copy-start = (s32[1,512]{1,0:T(1,128)S(1)}, s32[1,512]{1,0:T(1,128)}, u32[]{:S(2)}) copy-start(s32[1,512]{1,0:T(1,128)} %param.7) | copy-start | bytes 6148
  6.5 62.0 %copy-start.4 = (f32[1,2048,256]{2,1,0:T(8,128)S(1)}, f32[1,2048,256]{2,1,0:T(8,128)}, u32[]{:S(2)}) copy-start(f32[1,2048,256]{2,1,0:T(8,128)} %param.6) | copy-start | bytes 6291460
  6.5 81.3 %all-gather.5.cloned.1.call-start = ((), (), s32[]{:S(2)}) async-start(), calls=%async_computation.1 | async-start | bytes 4325376 | tf_op jit(solution)/shard_map/all_gather | solution.py:57
  47.7 14.1 %collective-permute-start = (bf16[256,1024]{1,0:T(8,128)(2,1)S(1)}, bf16[256,1024]{1,0:T(8,128)(2,1)}, u32[]{:S(2)}, u32[]{:S(2)}) collective-permute-start(bf16[256,1024]{1,0:T(8,128)(2,1)S(1)} %bitcast.86), channel_id=1, source_target_pairs={{0,32},{32,64},{64,96},{96,0},{1,33},{33,65},{65,97},{97,1},{2,34}... | collective-permute-start | bytes 1572872 | tf_op jit(solution)/shard_map/ppermute | solution.py:28
  51.1 25.1 %collective-permute-start.2 = (bf16[256,1024]{1,0:T(8,128)(2,1)S(1)}, bf16[256,1024]{1,0:T(8,128)(2,1)}, u32[]{:S(2)}, u32[]{:S(2)}) collective-permute-start(bf16[256,1024]{1,0:T(8,128)(2,1)S(1)} %bitcast.87), channel_id=1, source_target_pairs={{0,96},{32,0},{64,32},{96,64},{1,97},{33,1},{65,33},{97,65},{2,98}... | collective-permute-start | bytes 1572872 | tf_op jit(solution)/shard_map/ppermute | solution.py:31
  61.8 14.4 %collective-permute-start.1 = (bf16[256,1024]{1,0:T(8,128)(2,1)}, bf16[256,1024]{1,0:T(8,128)(2,1)}, u32[]{:S(2)}, u32[]{:S(2)}) collective-permute-start(bf16[256,1024]{1,0:T(8,128)(2,1)} %collective-permute-done), channel_id=1, source_target_pairs={{0,32},{32,64},{64,96},{96,0},{1,33},{33,65},{65,97},{97,1},{2,34}... | collective-permute-start | bytes 1572872 | tf_op jit(solution)/shard_map/ppermute | solution.py:28
  81.5 13.4 %copy-start.1 = (bf16[4,256,1024]{2,1,0:T(8,128)(2,1)}, bf16[4,256,1024]{2,1,0:T(8,128)(2,1)S(1)}, u32[]{:S(2)}) copy-start(bf16[4,256,1024]{2,1,0:T(8,128)(2,1)S(1)} %gather_fusion) | copy-start | bytes 6291460
  96.4 1.6 %copy-start.2 = (bf16[4,256,1024]{2,1,0:T(8,128)(2,1)S(1)}, bf16[4,256,1024]{2,1,0:T(8,128)(2,1)}, u32[]{:S(2)}) copy-start(bf16[4,256,1024]{2,1,0:T(8,128)(2,1)} %copy-done.1) | copy-start | bytes 6291460
  100.9 15.5 %all-to-all-start = ((bf16[4,64,1024]{2,1,0:T(8,128)(2,1)}), bf16[4,64,1024]{2,1,0:T(8,128)(2,1)S(1)}, u32[]{:S(2)}, u32[]{:S(2)}) async-start(bf16[4,64,1024]{2,1,0:T(8,128)(2,1)} %bitcast.85), calls=%async_computation | async-start | bytes 1048576 | tf_op jit(solution)/shard_map/all_to_all | solution.py:93
  110.1 12.0 %copy-start.5 = (f32[512,256]{1,0:T(8,128)S(1)}, f32[512,256]{1,0:T(8,128)}, u32[]{:S(2)}) copy-start(f32[512,256]{1,0:T(8,128)} %fusion.8) | copy-start | bytes 1572868
  119.6 10.6 %collective-permute-start.4 = (bf16[512,256]{1,0:T(8,128)(2,1)}, bf16[512,256]{1,0:T(8,128)(2,1)}, u32[]{:S(2)}, u32[]{:S(2)}) collective-permute-start(bf16[512,256]{1,0:T(8,128)(2,1)} %bitcast.91), channel_id=1, source_target_pairs={{0,128},{128,0},{256,384},{384,256},{1,129},{129,1},{257,385},{385... | collective-permute-start | bytes 786440 | tf_op jit(solution)/shard_map/ppermute | solution.py:11
  124.5 4.2 %copy-start.3 = (f32[1024,256]{1,0:T(8,128)S(1)}, f32[1024,256]{1,0:T(8,128)}, u32[]{:S(2)}) copy-start(f32[1024,256]{1,0:T(8,128)} %dynamic-slice_bitcast_fusion.3) | copy-start | bytes 3145732
  124.5 10.2 %collective-permute-start.3 = (bf16[512,256]{1,0:T(8,128)(2,1)S(1)}, bf16[512,256]{1,0:T(8,128)(2,1)S(1)}, u32[]{:S(2)}, u32[]{:S(2)}) collective-permute-start(bf16[512,256]{1,0:T(8,128)(2,1)S(1)} %bitcast.92), channel_id=1, source_target_pairs={{0,128},{128,0},{256,384},{384,256},{1,129},{129,1},{257,385},{385... | collective-permute-start | bytes 786440 | tf_op jit(solution)/shard_map/ppermute | solution.py:11
Sparse Core Ops, SparseCore 0:
  9.5 78.2 all-gather.4

commit v17 on v15

--- a/solution.py
+++ b/solution.py
@@ -100,9 +100,16 @@
     half = rows_here // 2
     half_blocks = half // width
 
+    nblocks_here = rows_here // width
+    trailing_moved = local_trailing.reshape(nblocks_here, width, cols_here)[
+        gather_row
+    ].reshape(rows_here, cols_here)
+    solved_blocks = solved.reshape(nblocks_here, width, order)
+
     def half_update(which):
-        rows = lax.dynamic_slice_in_dim(local_trailing, which * half, half, 0)
-        low = lax.dynamic_slice_in_dim(solved, which * half, half, 0)
+        rows = lax.dynamic_slice_in_dim(trailing_moved, which * half, half, 0)
+        blocks = lax.dynamic_slice_in_dim(gather_row, which * half_blocks, half_blocks, 0)
+        low = solved_blocks[blocks].reshape(half, order)
         rows, low = lax.optimization_barrier((rows, low))
         moved_cols = jnp.dot(
             rows,
@@ -110,14 +117,7 @@
             precision=lax.Precision.HIGHEST,
             preferred_element_type=jnp.float32,
         )
-        schur = moved_cols - outer_rows(low, col_side)
-        blocks = (
-            lax.dynamic_slice_in_dim(gather_row, which * half_blocks, half_blocks, 0)
-            - which * half_blocks
-        )
-        return schur.reshape(half_blocks, width, cols_here)[blocks].reshape(
-            half, cols_here
-        )
+        return moved_cols - outer_rows(low, col_side)
 
     outgoing = half_update(1 - member).astype(jnp.bfloat16)
     incoming = from_partner(outgoing, "front", 0)

time: 135 us -> 146 us (1.081)
  local copies, waits for them, and re-layouts: 13.3 us -> 28.4 us
  waiting for transfers between devices: 18.9 us -> 4.92 us
  matrix products: 13.1 us -> 19.6 us
  blocking collectives: 40.4 us -> 45.1 us
  starting transfers between devices: 17.5 us -> 15.4 us
    gather x2 -> x3, local copies, waits for them, and re-layouts: 2.02 us -> 10.5 us  [the longest x2 8.39 us: half_update(): low = solved_blocks[blocks].reshape(half, order)]
    all_gather x1, waiting for transfers between devices: 6.78 us -> 0.01 us  [local(): columns = lax.all_gather(panel[0], ('z', 'core'), axis=1, tiled=True)]
    convert_element_type x0 -> x1, local copies, waits for them, and re-layouts: none -> 6.4 us  [solve(): jnp.dot(rows, inverse, preferred_element_type=jnp.float32)]
    ppermute x1, waiting for transfers between devices: 10.4 us -> 4.2 us  [from_partner(): return lax.ppermute(value, axis, pairs)]
    all_gather x1, blocking collectives: 38.4 us -> 43.1 us  [local(): inverse = lax.all_gather(inverse, 'z', axis=0, tiled=True)]
    dot_general x2, matrix products: 8.6 us -> 11.7 us  [solve(): jnp.dot(rows, inverse, preferred_element_type=jnp.float32)]
    dynamic_slice x2 -> x1, local copies, waits for them, and re-layouts: 4.86 us -> 2.65 us  [half_update(): rows = lax.dynamic_slice_in_dim(trailing_moved, which * half, half, 0)]
    dot_general x2, matrix products: 1.28 us -> 3.05 us  [half_update(): jnp.dot(rows, select_cols, precision=lax.Precision.HIGHEST, preferred_ele...]
  transfers between devices with their start and end apart: 6 -> 6, of which waited for: 3 -> 1; matrix products, arithmetic and copies ran while one was open for 26% -> 39% of each run, Pallas kernels for 0% -> 0%
where the time goes in v17:
time: 146 us; the launch traced here: 144 us
  blocking collectives  45.1 us (31%)
  local copies, waits for them, and re-layouts  28.4 us (19%)
  matrix products  19.6 us (13%)
  other arithmetic  17.2 us (12%)
  starting transfers between devices  15.4 us (11%)
  between operations  13.6 us (9%)
  waiting for transfers between devices  4.92 us (3%)
    all_gather x1, blocking collectives, local(): inverse = lax.all_gather(inverse, 'z', axis=0, tiled=True)  43.1 us
    dot_general x2, matrix products, solve(): jnp.dot(rows, inverse, preferred_element_type=jnp.float32)  11.7 us
    gather x2, local copies, waits for them, and re-layouts, half_update(): low = solved_blocks[blocks].reshape(half, order)  8.39 us
    convert_element_type x1, local copies, waits for them, and re-layouts, solve(): jnp.dot(rows, inverse, preferred_element_type=jnp.float32)  6.4 us
    add x1, other arithmetic, local(): picked = gather_col[lane // width] * width + lane % width  5.54 us
    dot_general x2, matrix products, outer_rows(): lax.dot_general(left, right, (((1,), (1,)), ((), ())), preferred_element_...  4.92 us
    ppermute x2, starting transfers between devices, ring_gather(): forward = lax.ppermute(forward, axis, ahead)  4.7 us
    gather x6, other arithmetic, local(): picked = gather_col[lane // width] * width + lane % width  4.51 us
  transfers between devices with their start and end apart: 6, of which 1 were waited for; matrix products, arithmetic and copies ran while one was open for 39% of the time, Pallas kernels for 0%

profile of v17, /device:TPU:24, one launch (start us, length us, event | category | flops | bytes accessed | tf_op | source)
XLA Modules:
  0.0 144.3 jit_solution(10561635444255993909)
XLA Ops:
  7.3 2.0 %all-gather = bf16[1,16,1024]{2,1,0:T(8,128)(2,1)S(1)} all-gather(bf16[1,8,1024]{2,1,0:T(8,128)(2,1)} %param.4), channel_id=2, replica_groups=mesh['front'=4,'row'=4,'z'=16,'core'=2] {'core'}, dimensions={1}, use_global_device_ids=true | all-gather | bytes 49152 | tf_op jit(solution)/shard_map/all_gather | solution.py:51
  9.3 43.1 %all-gather.1 = bf16[1,256,1024]{2,1,0:T(8,128)(2,1)} all-gather(bf16[1,16,1024]{2,1,0:T(8,128)(2,1)S(1)} %all-gather), channel_id=3, replica_groups=mesh['front'=4,'row'=4,'z'=16,'core'=2] {'z'}, dimensions={1}, use_global_device_ids=true | all-gather | bytes 557056 | tf_op jit(solution)/shard_map/all_gather | solution.py:52
  52.4 2.8 %collective-permute-start = (bf16[256,1024]{1,0:T(8,128)(2,1)}, bf16[256,1024]{1,0:T(8,128)(2,1)}, u32[]{:S(2)}, u32[]{:S(2)}) collective-permute-start(bf16[256,1024]{1,0:T(8,128)(2,1)} %bitcast.4), channel_id=1, source_target_pairs={{0,32},{32,64},{64,96},{96,0},{1,33},{33,65},{65,97},{97,1},{2,34}... | collective-permute-start | bytes 1572872 | tf_op jit(solution)/shard_map/ppermute | solution.py:28
  55.2 4.3 %collective-permute-start.2 = (bf16[256,1024]{1,0:T(8,128)(2,1)}, bf16[256,1024]{1,0:T(8,128)(2,1)}, u32[]{:S(2)}, u32[]{:S(2)}) collective-permute-start(bf16[256,1024]{1,0:T(8,128)(2,1)} %bitcast.4), channel_id=1, source_target_pairs={{0,96},{32,0},{64,32},{96,64},{1,97},{33,1},{65,33},{97,65},{2,98}... | collective-permute-start | bytes 1572872 | tf_op jit(solution)/shard_map/ppermute | solution.py:31
  59.5 1.6 %gather_fusion = s32[128]{0:T(128)S(1)} fusion(s32[512]{0:T(512)} %bitcast.60, s32[1024]{0:T(1024)S(1)} %pad_clamp_fusion.6), kind=kCustom, calls=%fused_computation | custom fusion | bytes 1536 | tf_op jit(solution)/shard_map/gather | solution.py:78
  64.0 2.5 %sort.34 = (s32[128]{0:T(128)}, s32[128]{0:T(128)S(1)}) sort(s32[128]{0:T(128)S(1)} %fusion.17, s32[128]{0:T(128)S(1)} %iota.39), dimensions={0}, to_apply=%region_0.1 | sort | flops 896 | bytes 2048 | tf_op jit(solution)/shard_map/jit(argsort)/sort | solution.py:79
  67.4 1.9 %collective-permute-start.1 = (bf16[256,1024]{1,0:T(8,128)(2,1)}, bf16[256,1024]{1,0:T(8,128)(2,1)}, u32[]{:S(2)}, u32[]{:S(2)}) collective-permute-start(bf16[256,1024]{1,0:T(8,128)(2,1)} %collective-permute-done), channel_id=1, source_target_pairs={{0,32},{32,64},{64,96},{96,0},{1,33},{33,65},{65,97},{97,1},{2,34}... | collective-permute-start | bytes 1572872 | tf_op jit(solution)/shard_map/ppermute | solution.py:28
  69.3 4.4 %compare_select_fusion.1 = s32[256,1]{0,1:T(1,128)S(1)} fusion(s32[]{:T(128)} %bitcast.24, s32[]{:T(128)} %bitcast.25, s32[]{:T(128)} %bitcast.26, s32[]{:T(128)} %bitcast.27, s32[]{:T(128)} %bitcast.28, s32[]{:T(128)} %bitcast.30, s32[]{:T(128)} %bitcast.29), kind=kLoop, calls=%fused_computation.38 | loop fusion | flops 5888 | bytes 1052 | tf_op jit(solution)/shard_map/gather | solution.py:95
  73.7 2.1 %gather_fusion.1 = f32[128,16,256]{2,1,0:T(8,128)} fusion(f32[128,16,256]{2,1,0:T(8,128)S(1)} %bitcast.59, s32[1024]{0:T(1024)S(1)} %pad_clamp_fusion.5), kind=kCustom, calls=%fused_computation.1 | custom fusion | bytes 4194816 | tf_op jit(solution)/shard_map/gather | solution.py:104
  76.0 2.7 %constant_dynamic-slice_fusion.1 = (f32[1024,256]{1,0:T(8,128)}, f32[1024,256]{1,0:T(8,128)S(1)}) fusion(f32[2048,256]{1,0:T(8,128)} %bitcast.64, s32[]{:T(128)S(6)} %select_n.186, s32[]{:T(128)S(6)} %select_n.202), kind=kLoop, calls=%fused_computation.88 | loop fusion | bytes 4194312 | tf_op jit(solution)/shard_map/dynamic_slice | solution.py:110
  78.6 5.5 %fusion.9 = s32[256]{0:T(256)S(1)} fusion(pred[256]{0:T(512)(128)(4,1)S(1)} %get-tuple-element.37, pred[256]{0:T(512)(128)(4,1)S(1)} %get-tuple-element.38, pred[256]{0:T(512)(128)(4,1)S(1)} %get-tuple-element.39, pred[256]{0:T(512)(128)(4,1)S(1)} %get-tuple-element.40, pred[256]{0:T(512)(128)(4,1)S(1)} %get-tuple-element.41, ...), kind=kLoop, calls=%fused_computation.73 | loop fusion | flops 4352 | bytes 4388 | tf_op jit(solution)/shard_map/add | solution.py:95
  84.2 3.1 %pad_maximum_fusion = bf16[4,256,1024]{2,1,0:T(8,128)(2,1)} fusion(bf16[1,256,1024]{2,1,0:T(8,128)(2,1)} %bitcast.7, bf16[1,256,1024]{2,1,0:T(8,128)(2,1)} %bitcast.6, bf16[1,256,1024]{2,1,0:T(8,128)(2,1)} %bitcast.5, bf16[1,256,1024]{2,1,0:T(8,128)(2,1)} %all-gather.1), kind=kLoop, calls=%fused_computation.10 | loop fusion | flops 3145728 | bytes 4194304 | tf_op jit(solution)/shard_map/stack | solution.py:37
  87.3 3.7 %gather_fusion.2 = bf16[4,256,1024]{2,1,0:T(8,128)(2,1)} fusion(bf16[4,256,1024]{2,1,0:T(8,128)(2,1)} %pad_maximum_fusion, s32[1024]{0:T(1024)S(1)} %pad_clamp_fusion.4), kind=kCustom, calls=%fused_computation.2 | custom fusion | bytes 4194320 | tf_op jit(solution)/shard_map/gather | solution.py:39
  91.0 2.3 %convolution_convert_fusion = bf16[64,1024]{1,0:T(8,128)(2,1)S(1)} fusion(bf16[1024,1024]{1,0:T(8,128)(2,1)} %bitcast.65, bf16[1,2048,1024]{1,2,0:T(8,128)(2,1)} %all-gather.5.cloned.1.call-done, s32[]{:T(128)S(6)} %select_n.199), kind=kOutput, calls=%fused_computation.14 | convolution fusion | flops 134283264 | bytes 2490372 | tf_op jit(solution)/shard_map/dot_general | solution.py:60
  94.7 4.5 %all-to-all-start = ((bf16[4,64,1024]{2,1,0:T(8,128)(2,1)}), bf16[4,64,1024]{2,1,0:T(8,128)(2,1)}, u32[]{:S(2)}, u32[]{:S(2)}) async-start(bf16[4,64,1024]{2,1,0:T(8,128)(2,1)} %bitcast.70), calls=%async_computation | async-start | bytes 1048576 | tf_op jit(solution)/shard_map/all_to_all | solution.py:93
  99.2 9.4 %convert_bitcast_fusion = bf16[2048,1024]{0,1:T(8,128)(2,1)} fusion(bf16[1024,1024]{1,0:T(8,128)(2,1)} %bitcast.66, bf16[1,2048,1024]{1,2,0:T(8,128)(2,1)} %all-gather.5.cloned.1.call-done), kind=kOutput, calls=%fused_computation.9 | convolution fusion | flops 4297064448 | bytes 10485760 | tf_op jit(solution)/shard_map/dot_general | solution.py:60
  108.6 6.4 %copy.5 = bf16[2048,1024]{1,0:T(8,128)(2,1)} copy(bf16[2048,1024]{0,1:T(8,128)(2,1)} %convert_bitcast_fusion) | data formatting | bytes 8388608 | tf_op jit(solution)/shard_map/convert_element_type | solution.py:60
  115.0 4.2 %gather_fusion.6 = bf16[64,16,1024]{2,1,0:T(8,128)(2,1)} fusion(bf16[128,16,1024]{2,1,0:T(8,128)(2,1)} %bitcast.62, s32[1024]{0:T(1024)S(1)} %get-tuple-element.45), kind=kCustom, calls=%fused_computation.6 | custom fusion | bytes 4194560 | tf_op jit(solution)/shard_map/gather | solution.py:112
  119.2 2.4 %fusion.30 = f32[1024,256]{1,0:T(8,128)S(1)} fusion(bf16[1024,1024]{1,0:T(8,128)(2,1)} %bitcast.68, bf16[256,1024]{1,0:T(8,128)(2,1)} %bitcast.36), kind=kOutput, calls=%fused_computation.109 | convolution fusion | flops 536870912 | bytes 3670016 | tf_op jit(solution)/shard_map/dot_general | solution.py:15
  123.0 1.9 %collective-permute-start.3 = (bf16[1024,256]{1,0:T(8,128)(2,1)}, bf16[1024,256]{1,0:T(8,128)(2,1)S(1)}, u32[]{:S(2)}, u32[]{:S(2)}) collective-permute-start(bf16[1024,256]{1,0:T(8,128)(2,1)} %fusion.4), channel_id=1, source_target_pairs={{0,128},{128,0},{256,384},{384,256},{1,129},{129,1},{257,385},{385... | collective-permute-start | bytes 1572872 | tf_op jit(solution)/shard_map/ppermute | solution.py:11
  124.9 4.2 %gather_fusion.3 = bf16[64,16,1024]{2,1,0:T(8,128)(2,1)} fusion(bf16[128,16,1024]{2,1,0:T(8,128)(2,1)} %bitcast.63, s32[1024]{0:T(1024)S(1)} %get-tuple-element.46), kind=kCustom, calls=%fused_computation.3 | custom fusion | bytes 4194560 | tf_op jit(solution)/shard_map/gather | solution.py:112
  129.1 2.5 %fusion.29 = f32[1024,256]{1,0:T(8,128)S(1)} fusion(bf16[1024,1024]{1,0:T(8,128)(2,1)} %bitcast.69, bf16[256,1024]{1,0:T(8,128)(2,1)} %bitcast.36), kind=kOutput, calls=%fused_computation.108 | convolution fusion | flops 536870912 | bytes 3670016 | tf_op jit(solution)/shard_map/dot_general | solution.py:15
  131.7 4.2 %collective-permute-done.3 = bf16[1024,256]{1,0:T(8,128)(2,1)S(1)} collective-permute-done((bf16[1024,256]{1,0:T(8,128)(2,1)}, bf16[1024,256]{1,0:T(8,128)(2,1)S(1)}, u32[]{:S(2)}, u32[]{:S(2)}) %collective-permute-start.3) | collective-permute-done | bytes 524320 | tf_op jit(solution)/shard_map/ppermute | solution.py:11
  135.9 1.6 %add_bitcast_fusion = f32[1,1024,256]{2,1,0:T(8,128)} fusion(bf16[1024,256]{1,0:T(8,128)(2,1)S(1)} %collective-permute-done.3, f32[1024,256]{1,0:T(8,128)S(1)} %fusion.29, f32[1024,256]{1,0:T(8,128)S(1)} %copy-done.1, s32[256]{0:T(256)S(1)} %fusion.9), kind=kOutput, calls=%fused_computation.15 | convolution fusion | flops 806158336 | bytes 3671040 | tf_op jit(solution)/shard_map/dot_general | solution.py:114
  (40 shorter events, 7.4 us)
Async XLA Ops:
  6.5 67.2 %copy-start = (f32[1,2048,256]{2,1,0:T(8,128)S(1)}, f32[1,2048,256]{2,1,0:T(8,128)}, u32[]{:S(2)}) copy-start(f32[1,2048,256]{2,1,0:T(8,128)} %param.6) | copy-start | bytes 6291460
  6.5 84.4 %all-gather.5.cloned.1.call-start = ((), (), s32[]{:S(2)}) async-start(), calls=%async_computation.1 | async-start | bytes 4325376 | tf_op jit(solution)/shard_map/all_gather | solution.py:57
  52.4 15.0 %collective-permute-start = (bf16[256,1024]{1,0:T(8,128)(2,1)}, bf16[256,1024]{1,0:T(8,128)(2,1)}, u32[]{:S(2)}, u32[]{:S(2)}) collective-permute-start(bf16[256,1024]{1,0:T(8,128)(2,1)} %bitcast.4), channel_id=1, source_target_pairs={{0,32},{32,64},{64,96},{96,0},{1,33},{33,65},{65,97},{97,1},{2,34}... | collective-permute-start | bytes 1572872 | tf_op jit(solution)/shard_map/ppermute | solution.py:28
  55.2 29.0 %collective-permute-start.2 = (bf16[256,1024]{1,0:T(8,128)(2,1)}, bf16[256,1024]{1,0:T(8,128)(2,1)}, u32[]{:S(2)}, u32[]{:S(2)}) collective-permute-start(bf16[256,1024]{1,0:T(8,128)(2,1)} %bitcast.4), channel_id=1, source_target_pairs={{0,96},{32,0},{64,32},{96,64},{1,97},{33,1},{65,33},{97,65},{2,98}... | collective-permute-start | bytes 1572872 | tf_op jit(solution)/shard_map/ppermute | solution.py:31
  67.4 16.8 %collective-permute-start.1 = (bf16[256,1024]{1,0:T(8,128)(2,1)}, bf16[256,1024]{1,0:T(8,128)(2,1)}, u32[]{:S(2)}, u32[]{:S(2)}) collective-permute-start(bf16[256,1024]{1,0:T(8,128)(2,1)} %collective-permute-done), channel_id=1, source_target_pairs={{0,32},{32,64},{64,96},{96,0},{1,33},{33,65},{65,97},{97,1},{2,34}... | collective-permute-start | bytes 1572872 | tf_op jit(solution)/shard_map/ppermute | solution.py:28
  94.7 24.5 %all-to-all-start = ((bf16[4,64,1024]{2,1,0:T(8,128)(2,1)}), bf16[4,64,1024]{2,1,0:T(8,128)(2,1)}, u32[]{:S(2)}, u32[]{:S(2)}) async-start(bf16[4,64,1024]{2,1,0:T(8,128)(2,1)} %bitcast.70), calls=%async_computation | async-start | bytes 1048576 | tf_op jit(solution)/shard_map/all_to_all | solution.py:93
  123.0 12.8 %collective-permute-start.3 = (bf16[1024,256]{1,0:T(8,128)(2,1)}, bf16[1024,256]{1,0:T(8,128)(2,1)S(1)}, u32[]{:S(2)}, u32[]{:S(2)}) collective-permute-start(bf16[1024,256]{1,0:T(8,128)(2,1)} %fusion.4), channel_id=1, source_target_pairs={{0,128},{128,0},{256,384},{384,256},{1,129},{129,1},{257,385},{385... | collective-permute-start | bytes 1572872 | tf_op jit(solution)/shard_map/ppermute | solution.py:11
  129.1 6.7 %copy-start.1 = (f32[1024,256]{1,0:T(8,128)S(1)}, f32[1024,256]{1,0:T(8,128)}, u32[]{:S(2)}) copy-start(f32[1024,256]{1,0:T(8,128)} %get-tuple-element.12) | copy-start | bytes 3145732
Sparse Core Ops, SparseCore 0:
  9.5 78.4 all-gather.4

commit v18 on v15

--- a/solution.py
+++ b/solution.py
@@ -39,6 +39,12 @@
     return stacked[(index - sources) % n]
 
 
+def inverse_order(target):
+    slots = jnp.arange(target.shape[0], dtype=jnp.int32)
+    hit = target[None, :] == slots[:, None]
+    return jnp.sum(jnp.where(hit, slots[None, :], 0), axis=1, dtype=jnp.int32)
+
+
 def local(inverse_factor, panel, trailing, extend_map):
     nrow = lax.axis_size("row")
     nz = lax.axis_size("z")
@@ -76,13 +82,13 @@
     depth_row = slots_row % per_class
     source_row = (depth_row * ncol + class_row) * nrow + row_index
     target_row = class_row * per_class + block_map[source_row] // group
-    gather_row = jnp.argsort(target_row)
+    gather_row = inverse_order(target_row)
     slots_col = jnp.arange(nrow * per_class, dtype=jnp.int32)
     class_col = slots_col // per_class
     depth_col = slots_col % per_class
     source_col = (depth_col * ncol + col_index) * nrow + class_col
     target_col = class_col * per_class + block_map[source_col] // group
-    gather_col = jnp.argsort(target_col)
+    gather_col = inverse_order(target_col)
 
     own_blocks = (
         lax.dynamic_slice_in_dim(gather_col, row_index * per_class, per_class, 0)
@@ -91,9 +97,11 @@
     copies = jnp.tile(own_blocks, nrow)
     piece = piece.reshape(per_class, width, order)[copies].reshape(nrow, share, order)
     col_side = lax.all_to_all(piece, "row", 0, 0, tiled=True).reshape(cols_here, order)
-    lane = jnp.arange(cols_here, dtype=jnp.int32)
-    picked = gather_col[lane // width] * width + lane % width
-    select_cols = (lane[:, None] == picked[None, :]).astype(jnp.float32)
+    blocks_col = slots_col[:, None] == gather_col[None, :]
+    same = jnp.arange(width)[:, None] == jnp.arange(width)[None, :]
+    select_cols = (blocks_col[:, None, :, None] & same[None, :, None, :]).reshape(
+        cols_here, cols_here
+    ).astype(jnp.float32)
 
     solved = solve(columns)
     member = lax.axis_index("front") % 2

time: 135 us -> 134 us (level)
  waiting for transfers between devices: 18.9 us -> 31.5 us
  other arithmetic: 16.8 us -> 4.83 us
  local copies, waits for them, and re-layouts: 13.3 us -> 11.9 us
    ppermute x2, waiting for transfers between devices: 0.01 us -> 9.23 us  [ring_gather(): forward = lax.ppermute(forward, axis, ahead)]
    add x1 -> x0, other arithmetic: 5.55 us -> none  [local(): picked = gather_col[lane // width] * width + lane % width]
    gather x6 -> x0, other arithmetic: 4.59 us -> none  [local(): picked = gather_col[lane // width] * width + lane % width]
    sort x2 -> x0, other arithmetic: 3.78 us -> none  [the longest x1 2.54 us: local(): gather_row = jnp.argsort(target_row)]
    all_gather x1, waiting for transfers between devices: 6.78 us -> 9.98 us  [local(): columns = lax.all_gather(panel[0], ('z', 'core'), axis=1, tiled=True)]
    dynamic_slice x1, local copies, waits for them, and re-layouts: 3.04 us -> 1.52 us  [half_update(): rows = lax.dynamic_slice_in_dim(local_trailing, which * half, half, 0)]
    another operation x1, other arithmetic: 1.59 us -> 2.97 us  [ring_gather(): stacked = jnp.stack(by_offset)]
  transfers between devices with their start and end apart: 6 -> 6, of which waited for: 3 -> 5; matrix products, arithmetic and copies ran while one was open for 26% -> 16% of each run, Pallas kernels for 0% -> 0%
where the time goes in v18:
time: 134 us; the launch traced here: 133 us
  blocking collectives  40.4 us (30%)
  waiting for transfers between devices  31.5 us (24%)
  starting transfers between devices  17.3 us (13%)
  between operations  13.7 us (10%)
  matrix products  13.1 us (10%)
  local copies, waits for them, and re-layouts  11.9 us (9%)
  other arithmetic  4.83 us (4%)
    all_gather x1, blocking collectives, local(): inverse = lax.all_gather(inverse, 'z', axis=0, tiled=True)  38.4 us
    ppermute x1, waiting for transfers between devices, from_partner(): return lax.ppermute(value, axis, pairs)  10.5 us
    all_gather x1, waiting for transfers between devices, local(): columns = lax.all_gather(panel[0], ('z', 'core'), axis=1, tiled=True)  9.98 us
    ppermute x2, waiting for transfers between devices, ring_gather(): forward = lax.ppermute(forward, axis, ahead)  9.23 us
    dot_general x2, matrix products, solve(): jnp.dot(rows, inverse, preferred_element_type=jnp.float32)  8.61 us
    ppermute x2, starting transfers between devices, ring_gather(): forward = lax.ppermute(forward, axis, ahead)  6.7 us
    all_to_all x1, starting transfers between devices, local(): lax.all_to_all(piece, 'row', 0, 0, tiled=True).reshape(cols_here, order)  4.37 us
    ppermute x1, starting transfers between devices, ring_gather(): backward = lax.ppermute(backward, axis, behind)  3.65 us
  transfers between devices with their start and end apart: 6, of which 5 were waited for; matrix products, arithmetic and copies ran while one was open for 16% of the time, Pallas kernels for 0%

profile of v18, /device:TPU:24, one launch (start us, length us, event | category | flops | bytes accessed | tf_op | source)
XLA Modules:
  0.0 132.7 jit_solution(17239717450245742176)
XLA Ops:
  7.3 2.0 %all-gather = bf16[1,16,1024]{2,1,0:T(8,128)(2,1)S(1)} all-gather(bf16[1,8,1024]{2,1,0:T(8,128)(2,1)} %param.4), channel_id=2, replica_groups=mesh['front'=4,'row'=4,'z'=16,'core'=2] {'core'}, dimensions={1}, use_global_device_ids=true | all-gather | bytes 49152 | tf_op jit(solution)/shard_map/all_gather | solution.py:57
  9.3 38.4 %all-gather.1 = bf16[1,256,1024]{2,1,0:T(8,128)(2,1)S(1)} all-gather(bf16[1,16,1024]{2,1,0:T(8,128)(2,1)S(1)} %all-gather), channel_id=3, replica_groups=mesh['front'=4,'row'=4,'z'=16,'core'=2] {'z'}, dimensions={1}, use_global_device_ids=true | all-gather | bytes 557056 | tf_op jit(solution)/shard_map/all_gather | solution.py:58
  47.7 3.4 %collective-permute-start = (bf16[256,1024]{1,0:T(8,128)(2,1)S(1)}, bf16[256,1024]{1,0:T(8,128)(2,1)}, u32[]{:S(2)}, u32[]{:S(2)}) collective-permute-start(bf16[256,1024]{1,0:T(8,128)(2,1)S(1)} %bitcast.60), channel_id=1, source_target_pairs={{0,32},{32,64},{64,96},{96,0},{1,33},{33,65},{65,97},{97,1},{2,34}... | collective-permute-start | bytes 1572872 | tf_op jit(solution)/shard_map/ppermute | solution.py:28
  51.1 3.7 %collective-permute-start.2 = (bf16[256,1024]{1,0:T(8,128)(2,1)S(1)}, bf16[256,1024]{1,0:T(8,128)(2,1)}, u32[]{:S(2)}, u32[]{:S(2)}) collective-permute-start(bf16[256,1024]{1,0:T(8,128)(2,1)S(1)} %bitcast.61), channel_id=1, source_target_pairs={{0,96},{32,0},{64,32},{96,64},{1,97},{33,1},{65,33},{97,65},{2,98}... | collective-permute-start | bytes 1572872 | tf_op jit(solution)/shard_map/ppermute | solution.py:31
  54.8 1.3 gather_fusion.3
  57.6 2.5 %collective-permute-done = bf16[256,1024]{1,0:T(8,128)(2,1)} collective-permute-done((bf16[256,1024]{1,0:T(8,128)(2,1)S(1)}, bf16[256,1024]{1,0:T(8,128)(2,1)}, u32[]{:S(2)}, u32[]{:S(2)}) %collective-permute-start) | collective-permute-done | bytes 524320 | tf_op jit(solution)/shard_map/ppermute | solution.py:28
  60.0 3.3 %collective-permute-start.1 = (bf16[256,1024]{1,0:T(8,128)(2,1)}, bf16[256,1024]{1,0:T(8,128)(2,1)}, u32[]{:S(2)}, u32[]{:S(2)}) collective-permute-start(bf16[256,1024]{1,0:T(8,128)(2,1)} %collective-permute-done), channel_id=1, source_target_pairs={{0,32},{32,64},{64,96},{96,0},{1,33},{33,65},{65,97},{97,1},{2,34}... | collective-permute-start | bytes 1572872 | tf_op jit(solution)/shard_map/ppermute | solution.py:28
  63.4 0.9 and.163
  64.4 1.5 %dynamic-slice_bitcast_fusion.2 = (f32[1024,256]{1,0:T(8,128)}, f32[1024,256]{1,0:T(8,128)}) fusion(f32[1,2048,256]{2,1,0:T(8,128)S(1)} %copy-done.3, s32[]{:T(128)S(6)} %select_n.191, s32[]{:T(128)S(6)} %select_n.171), kind=kLoop, calls=%fused_computation.16 | loop fusion | bytes 4194312 | tf_op jit(solution)/shard_map/dynamic_slice | solution.py:112
  65.9 6.7 %collective-permute-done.1 = bf16[256,1024]{1,0:T(8,128)(2,1)} collective-permute-done((bf16[256,1024]{1,0:T(8,128)(2,1)}, bf16[256,1024]{1,0:T(8,128)(2,1)}, u32[]{:S(2)}, u32[]{:S(2)}) %collective-permute-start.1) | collective-permute-done | bytes 524320 | tf_op jit(solution)/shard_map/ppermute | solution.py:28
  72.6 3.0 %pad_maximum_fusion = bf16[4,256,1024]{2,1,0:T(8,128)(2,1)} fusion(bf16[1,256,1024]{2,1,0:T(8,128)(2,1)} %bitcast.4, bf16[1,256,1024]{2,1,0:T(8,128)(2,1)} %bitcast.3, bf16[1,256,1024]{2,1,0:T(8,128)(2,1)} %bitcast.2, bf16[1,256,1024]{2,1,0:T(8,128)(2,1)S(1)} %all-gather.1), kind=kLoop, calls=%fused_computation.9 | loop fusion | flops 3145728 | bytes 4194304 | tf_op jit(solution)/shard_map/stack | solution.py:37
  75.6 2.3 %gather_fusion = bf16[4,256,1024]{2,1,0:T(8,128)(2,1)S(1)} fusion(bf16[4,256,1024]{2,1,0:T(8,128)(2,1)} %pad_maximum_fusion, s32[1024]{0:T(1024)S(1)} %pad_clamp_fusion.5), kind=kCustom, calls=%fused_computation | custom fusion | bytes 4194320 | tf_op jit(solution)/shard_map/gather | solution.py:39
  77.9 10.0 %all-gather.5.cloned.1.call-done = bf16[1,2048,1024]{1,2,0:T(8,128)(2,1)} async-done(((bf16[1,2048,32]{1,2,0:T(8,128)(2,1)}), bf16[1,2048,1024]{1,2,0:T(8,128)(2,1)}) %all-gather.5.cloned.1.call-update) | async-done | bytes 4194320 | tf_op jit(solution)/shard_map/all_gather | solution.py:63
  87.9 1.6 %convolution_convert_fusion = bf16[64,1024]{1,0:T(8,128)(2,1)S(1)} fusion(bf16[1024,1024]{1,0:T(8,128)(2,1)S(1)} %bitcast.53, bf16[1,2048,1024]{1,2,0:T(8,128)(2,1)} %all-gather.5.cloned.1.call-done, s32[]{:T(128)S(6)} %select_n.180), kind=kOutput, calls=%fused_computation.14 | convolution fusion | flops 134283264 | bytes 2490372 | tf_op jit(solution)/shard_map/dot_general | solution.py:66
  89.4 1.4 %gather_fusion.2 = bf16[16,16,1024]{2,1,0:T(8,128)(2,1)} fusion(bf16[4,16,1024]{2,1,0:T(8,128)(2,1)S(1)} %bitcast.58, s32[1024]{0:T(1024)S(1)} %pad_clamp_fusion.3), kind=kCustom, calls=%fused_computation.2 | custom fusion | bytes 1048640 | tf_op jit(solution)/shard_map/gather | solution.py:98
  90.8 4.4 %all-to-all-start = ((bf16[4,64,1024]{2,1,0:T(8,128)(2,1)}), bf16[4,64,1024]{2,1,0:T(8,128)(2,1)S(1)}, u32[]{:S(2)}, u32[]{:S(2)}) async-start(bf16[4,64,1024]{2,1,0:T(8,128)(2,1)} %bitcast.14), calls=%async_computation | async-start | bytes 1048576 | tf_op jit(solution)/shard_map/all_to_all | solution.py:99
  95.2 7.0 %fusion.2 = bf16[1024,2048]{1,0:T(8,128)(2,1)S(1)} fusion(bf16[1024,1024]{1,0:T(8,128)(2,1)S(1)} %bitcast.54, bf16[1,2048,1024]{1,2,0:T(8,128)(2,1)} %all-gather.5.cloned.1.call-done), kind=kOutput, calls=%fused_computation.8 | convolution fusion | flops 4297064448 | bytes 10485760 | tf_op jit(solution)/shard_map/dot_general | solution.py:66
  102.2 1.8 %dynamic-slice_bitcast_fusion = (bf16[1024,1024]{0,1:T(8,128)(2,1)}, bf16[1024,1024]{0,1:T(8,128)(2,1)S(1)}) fusion(bf16[1024,2048]{1,0:T(8,128)(2,1)S(1)} %fusion.2, s32[]{:T(128)S(6)} %select_n.191, s32[]{:T(128)S(6)} %select_n.171), kind=kLoop, calls=%fused_computation.10 | loop fusion | bytes 8388616 | tf_op jit(solution)/shard_map/dynamic_slice | solution.py:113
  104.0 1.1 all-to-all-done
  105.1 2.5 %fusion.26 = f32[1024,256]{1,0:T(8,128)S(1)} fusion(bf16[1024,1024]{0,1:T(8,128)(2,1)} %get-tuple-element.12, bf16[256,1024]{1,0:T(8,128)(2,1)S(1)} %bitcast.55), kind=kOutput, calls=%fused_computation.87 | convolution fusion | flops 536870912 | bytes 3670016 | tf_op jit(solution)/shard_map/dot_general | solution.py:15
  108.2 1.4 %gather_fusion.5 = bf16[64,16,256]{2,1,0:T(8,128)(2,1)} fusion(bf16[64,16,256]{2,1,0:T(8,128)(2,1)S(1)} %bitcast.59, s32[1024]{0:T(1024)S(1)} %pad_clamp_fusion), kind=kCustom, calls=%fused_computation.5 | custom fusion | bytes 1048832 | tf_op jit(solution)/shard_map/gather | solution.py:126
  109.6 2.6 %collective-permute-start.3 = (bf16[1024,256]{1,0:T(8,128)(2,1)}, bf16[1024,256]{1,0:T(8,128)(2,1)S(1)}, u32[]{:S(2)}, u32[]{:S(2)}) collective-permute-start(bf16[1024,256]{1,0:T(8,128)(2,1)} %bitcast.62), channel_id=1, source_target_pairs={{0,128},{128,0},{256,384},{384,256},{1,129},{129,1},{257,385},{385... | collective-permute-start | bytes 1572872 | tf_op jit(solution)/shard_map/ppermute | solution.py:11
  114.3 10.5 %collective-permute-done.3 = bf16[1024,256]{1,0:T(8,128)(2,1)S(1)} collective-permute-done((bf16[1024,256]{1,0:T(8,128)(2,1)}, bf16[1024,256]{1,0:T(8,128)(2,1)S(1)}, u32[]{:S(2)}, u32[]{:S(2)}) %collective-permute-start.3) | collective-permute-done | bytes 524320 | tf_op jit(solution)/shard_map/ppermute | solution.py:11
  124.8 1.1 bitcast_add_fusion
  (36 shorter events, 5.0 us)
Async XLA Ops:
  6.5 48.2 %copy-start = (s32[1,512]{1,0:T(1,128)S(1)}, s32[1,512]{1,0:T(1,128)}, u32[]{:S(2)}) copy-start(s32[1,512]{1,0:T(1,128)} %param.7) | copy-start | bytes 6148
  6.5 57.8 %copy-start.3 = (f32[1,2048,256]{2,1,0:T(8,128)S(1)}, f32[1,2048,256]{2,1,0:T(8,128)}, u32[]{:S(2)}) copy-start(f32[1,2048,256]{2,1,0:T(8,128)} %param.6) | copy-start | bytes 6291460
  6.5 81.3 %all-gather.5.cloned.1.call-start = ((), (), s32[]{:S(2)}) async-start(), calls=%async_computation.1 | async-start | bytes 4325376 | tf_op jit(solution)/shard_map/all_gather | solution.py:63
  47.7 12.4 %collective-permute-start = (bf16[256,1024]{1,0:T(8,128)(2,1)S(1)}, bf16[256,1024]{1,0:T(8,128)(2,1)}, u32[]{:S(2)}, u32[]{:S(2)}) collective-permute-start(bf16[256,1024]{1,0:T(8,128)(2,1)S(1)} %bitcast.60), channel_id=1, source_target_pairs={{0,32},{32,64},{64,96},{96,0},{1,33},{33,65},{65,97},{97,1},{2,34}... | collective-permute-start | bytes 1572872 | tf_op jit(solution)/shard_map/ppermute | solution.py:28
  51.1 14.8 %collective-permute-start.2 = (bf16[256,1024]{1,0:T(8,128)(2,1)S(1)}, bf16[256,1024]{1,0:T(8,128)(2,1)}, u32[]{:S(2)}, u32[]{:S(2)}) collective-permute-start(bf16[256,1024]{1,0:T(8,128)(2,1)S(1)} %bitcast.61), channel_id=1, source_target_pairs={{0,96},{32,0},{64,32},{96,64},{1,97},{33,1},{65,33},{97,65},{2,98}... | collective-permute-start | bytes 1572872 | tf_op jit(solution)/shard_map/ppermute | solution.py:31
  60.0 12.6 %collective-permute-start.1 = (bf16[256,1024]{1,0:T(8,128)(2,1)}, bf16[256,1024]{1,0:T(8,128)(2,1)}, u32[]{:S(2)}, u32[]{:S(2)}) collective-permute-start(bf16[256,1024]{1,0:T(8,128)(2,1)} %collective-permute-done), channel_id=1, source_target_pairs={{0,32},{32,64},{64,96},{96,0},{1,33},{33,65},{65,97},{97,1},{2,34}... | collective-permute-start | bytes 1572872 | tf_op jit(solution)/shard_map/ppermute | solution.py:28
  90.8 14.3 %all-to-all-start = ((bf16[4,64,1024]{2,1,0:T(8,128)(2,1)}), bf16[4,64,1024]{2,1,0:T(8,128)(2,1)S(1)}, u32[]{:S(2)}, u32[]{:S(2)}) async-start(bf16[4,64,1024]{2,1,0:T(8,128)(2,1)} %bitcast.14), calls=%async_computation | async-start | bytes 1048576 | tf_op jit(solution)/shard_map/all_to_all | solution.py:99
  105.1 2.5 %copy-start.2 = (f32[1024,256]{1,0:T(8,128)S(1)}, f32[1024,256]{1,0:T(8,128)}, u32[]{:S(2)}) copy-start(f32[1024,256]{1,0:T(8,128)} %get-tuple-element.11) | copy-start | bytes 3145732
  109.6 3.4 %copy-start.1 = (f32[1024,256]{1,0:T(8,128)S(1)}, f32[1024,256]{1,0:T(8,128)}, u32[]{:S(2)}) copy-start(f32[1024,256]{1,0:T(8,128)} %get-tuple-element.9) | copy-start | bytes 3145732
  109.6 15.2 %collective-permute-start.3 = (bf16[1024,256]{1,0:T(8,128)(2,1)}, bf16[1024,256]{1,0:T(8,128)(2,1)S(1)}, u32[]{:S(2)}, u32[]{:S(2)}) collective-permute-start(bf16[1024,256]{1,0:T(8,128)(2,1)} %bitcast.62), channel_id=1, source_target_pairs={{0,128},{128,0},{256,384},{384,256},{1,129},{129,1},{257,385},{385... | collective-permute-start | bytes 1572872 | tf_op jit(solution)/shard_map/ppermute | solution.py:11
Sparse Core Ops, SparseCore 0:
  9.5 78.3 all-gather.4

commit v19 on v18

--- a/solution.py
+++ b/solution.py
@@ -17,24 +17,12 @@
     )
 
 
-def ring_gather(value, axis, index, n):
-    ahead = [(source, (source + 1) % n) for source in range(n)]
-    behind = [(source, (source - 1) % n) for source in range(n)]
+def direct_gather(value, axis, index, n):
     held = [value]
-    forward = value
-    backward = value
-    for step in range(1, n):
-        if step % 2:
-            forward = lax.ppermute(forward, axis, ahead)
-            held.append(forward)
-        else:
-            backward = lax.ppermute(backward, axis, behind)
-            held.append(backward)
-    offsets = [0] + [(step + 1) // 2 if step % 2 else -(step // 2) for step in range(1, n)]
-    by_offset = [None] * n
-    for offset, block in zip(offsets, held):
-        by_offset[offset % n] = block
-    stacked = jnp.stack(by_offset)
+    for offset in range(1, n):
+        pairs = [(source, (source + offset) % n) for source in range(n)]
+        held.append(lax.ppermute(value, axis, pairs))
+    stacked = jnp.stack(held)
     sources = jnp.arange(n, dtype=jnp.int32)
     return stacked[(index - sources) % n]
 
@@ -56,7 +44,7 @@
 
     inverse = lax.all_gather(inverse_factor[0], "core", axis=0, tiled=True)
     inverse = lax.all_gather(inverse, "z", axis=0, tiled=True)
-    inverse = ring_gather(inverse, "row", row_index, nrow)
+    inverse = direct_gather(inverse, "row", row_index, nrow)
     order = inverse.shape[-1]
     inverse = inverse.reshape(order, order)
 

time: 134 us -> 134 us (level)
  starting transfers between devices: 17.3 us -> 19 us
  waiting for transfers between devices: 31.5 us -> 29.8 us
    ppermute x3, waiting for transfers between devices: 9.23 us -> 6.27 us  [direct_gather(): held.append(lax.ppermute(value, axis, pairs))]
    ppermute x3, starting transfers between devices: 10.4 us -> 11.9 us  [direct_gather(): held.append(lax.ppermute(value, axis, pairs))]
    all_gather x1, waiting for transfers between devices: 9.98 us -> 11.5 us  [local(): columns = lax.all_gather(panel[0], ('z', 'core'), axis=1, tiled=True)]
  transfers between devices with their start and end apart: 6 -> 6, of which waited for: 5 -> 6; matrix products, arithmetic and copies ran while one was open for 16% -> 16% of each run, Pallas kernels for 0% -> 0%
where the time goes in v19:
time: 134 us; the launch traced here: 133 us
  blocking collectives  40.4 us (30%)
  waiting for transfers between devices  29.8 us (22%)
  starting transfers between devices  19 us (14%)
  between operations  13.7 us (10%)
  matrix products  13.1 us (10%)
  local copies, waits for them, and re-layouts  11.9 us (9%)
  other arithmetic  4.81 us (4%)
    all_gather x1, blocking collectives, local(): inverse = lax.all_gather(inverse, 'z', axis=0, tiled=True)  38.4 us
    ppermute x3, starting transfers between devices, direct_gather(): held.append(lax.ppermute(value, axis, pairs))  11.9 us
    all_gather x1, waiting for transfers between devices, local(): columns = lax.all_gather(panel[0], ('z', 'core'), axis=1, tiled=True)  11.5 us
    ppermute x1, waiting for transfers between devices, from_partner(): return lax.ppermute(value, axis, pairs)  10.2 us
    dot_general x2, matrix products, solve(): jnp.dot(rows, inverse, preferred_element_type=jnp.float32)  8.6 us
    ppermute x3, waiting for transfers between devices, direct_gather(): held.append(lax.ppermute(value, axis, pairs))  6.27 us
    all_to_all x1, starting transfers between devices, local(): lax.all_to_all(piece, 'row', 0, 0, tiled=True).reshape(cols_here, order)  4.32 us
    dot_general x2, matrix products, outer_rows(): lax.dot_general(left, right, (((1,), (1,)), ((), ())), preferred_element_...  3.23 us
  transfers between devices with their start and end apart: 6, of which 6 were waited for; matrix products, arithmetic and copies ran while one was open for 16% of the time, Pallas kernels for 0%

profile of v19, /device:TPU:24, one launch (start us, length us, event | category | flops | bytes accessed | tf_op | source)
XLA Modules:
  0.0 132.7 jit_solution(8455642040778946989)
XLA Ops:
  7.3 2.0 %all-gather = bf16[1,16,1024]{2,1,0:T(8,128)(2,1)S(1)} all-gather(bf16[1,8,1024]{2,1,0:T(8,128)(2,1)} %param.4), channel_id=2, replica_groups=mesh['front'=4,'row'=4,'z'=16,'core'=2] {'core'}, dimensions={1}, use_global_device_ids=true | all-gather | bytes 49152 | tf_op jit(solution)/shard_map/all_gather | solution.py:45
  9.3 38.4 %all-gather.1 = bf16[1,256,1024]{2,1,0:T(8,128)(2,1)S(1)} all-gather(bf16[1,16,1024]{2,1,0:T(8,128)(2,1)S(1)} %all-gather), channel_id=3, replica_groups=mesh['front'=4,'row'=4,'z'=16,'core'=2] {'z'}, dimensions={1}, use_global_device_ids=true | all-gather | bytes 557056 | tf_op jit(solution)/shard_map/all_gather | solution.py:46
  47.7 4.8 %collective-permute-start.1 = (bf16[256,1024]{1,0:T(8,128)(2,1)S(1)}, bf16[256,1024]{1,0:T(8,128)(2,1)}, u32[]{:S(2)}, u32[]{:S(2)}) collective-permute-start(bf16[256,1024]{1,0:T(8,128)(2,1)S(1)} %bitcast.60), channel_id=1, source_target_pairs={{0,64},{32,96},{64,0},{96,32},{1,65},{33,97},{65,1},{97,33},{2,66}... | collective-permute-start | bytes 1572872 | tf_op jit(solution)/shard_map/ppermute | solution.py:24
  52.5 2.6 %collective-permute-start = (bf16[256,1024]{1,0:T(8,128)(2,1)S(1)}, bf16[256,1024]{1,0:T(8,128)(2,1)}, u32[]{:S(2)}, u32[]{:S(2)}) collective-permute-start(bf16[256,1024]{1,0:T(8,128)(2,1)S(1)} %bitcast.61), channel_id=1, source_target_pairs={{0,32},{32,64},{64,96},{96,0},{1,33},{33,65},{65,97},{97,1},{2,34}... | collective-permute-start | bytes 1572872 | tf_op jit(solution)/shard_map/ppermute | solution.py:24
  55.0 4.5 %collective-permute-start.2 = (bf16[256,1024]{1,0:T(8,128)(2,1)S(1)}, bf16[256,1024]{1,0:T(8,128)(2,1)}, u32[]{:S(2)}, u32[]{:S(2)}) collective-permute-start(bf16[256,1024]{1,0:T(8,128)(2,1)S(1)} %bitcast.62), channel_id=1, source_target_pairs={{0,96},{32,0},{64,32},{96,64},{1,97},{33,1},{65,33},{97,65},{2,98}... | collective-permute-start | bytes 1572872 | tf_op jit(solution)/shard_map/ppermute | solution.py:24
  59.6 1.3 gather_fusion.3
  62.5 0.9 and.163
  63.4 1.5 %dynamic-slice_bitcast_fusion.2 = (f32[1024,256]{1,0:T(8,128)}, f32[1024,256]{1,0:T(8,128)}) fusion(f32[1,2048,256]{2,1,0:T(8,128)S(1)} %copy-done.3, s32[]{:T(128)S(6)} %select_n.191, s32[]{:T(128)S(6)} %select_n.171), kind=kLoop, calls=%fused_computation.16 | loop fusion | bytes 4194312 | tf_op jit(solution)/shard_map/dynamic_slice | solution.py:100
  65.5 5.6 %collective-permute-done = bf16[256,1024]{1,0:T(8,128)(2,1)} collective-permute-done((bf16[256,1024]{1,0:T(8,128)(2,1)S(1)}, bf16[256,1024]{1,0:T(8,128)(2,1)}, u32[]{:S(2)}, u32[]{:S(2)}) %collective-permute-start) | collective-permute-done | bytes 524320 | tf_op jit(solution)/shard_map/ppermute | solution.py:24
  71.2 2.9 %pad_maximum_fusion = bf16[4,256,1024]{2,1,0:T(8,128)(2,1)} fusion(bf16[1,256,1024]{2,1,0:T(8,128)(2,1)} %bitcast.4, bf16[1,256,1024]{2,1,0:T(8,128)(2,1)} %bitcast.3, bf16[1,256,1024]{2,1,0:T(8,128)(2,1)} %bitcast.2, bf16[1,256,1024]{2,1,0:T(8,128)(2,1)S(1)} %all-gather.1), kind=kLoop, calls=%fused_computation.9 | loop fusion | flops 3145728 | bytes 4194304 | tf_op jit(solution)/shard_map/stack | solution.py:25
  74.1 2.3 %gather_fusion = bf16[4,256,1024]{2,1,0:T(8,128)(2,1)S(1)} fusion(bf16[4,256,1024]{2,1,0:T(8,128)(2,1)} %pad_maximum_fusion, s32[1024]{0:T(1024)S(1)} %pad_clamp_fusion.5), kind=kCustom, calls=%fused_computation | custom fusion | bytes 4194320 | tf_op jit(solution)/shard_map/gather | solution.py:27
  76.4 11.5 %all-gather.5.cloned.1.call-done = bf16[1,2048,1024]{1,2,0:T(8,128)(2,1)} async-done(((bf16[1,2048,32]{1,2,0:T(8,128)(2,1)}), bf16[1,2048,1024]{1,2,0:T(8,128)(2,1)}) %all-gather.5.cloned.1.call-update) | async-done | bytes 4194320 | tf_op jit(solution)/shard_map/all_gather | solution.py:51
  87.9 1.6 %convolution_convert_fusion = bf16[64,1024]{1,0:T(8,128)(2,1)S(1)} fusion(bf16[1024,1024]{1,0:T(8,128)(2,1)S(1)} %bitcast.53, bf16[1,2048,1024]{1,2,0:T(8,128)(2,1)} %all-gather.5.cloned.1.call-done, s32[]{:T(128)S(6)} %select_n.180), kind=kOutput, calls=%fused_computation.14 | convolution fusion | flops 134283264 | bytes 2490372 | tf_op jit(solution)/shard_map/dot_general | solution.py:54
  89.5 1.4 %gather_fusion.2 = bf16[16,16,1024]{2,1,0:T(8,128)(2,1)} fusion(bf16[4,16,1024]{2,1,0:T(8,128)(2,1)S(1)} %bitcast.58, s32[1024]{0:T(1024)S(1)} %pad_clamp_fusion.3), kind=kCustom, calls=%fused_computation.2 | custom fusion | bytes 1048640 | tf_op jit(solution)/shard_map/gather | solution.py:86
  90.8 4.3 %all-to-all-start = ((bf16[4,64,1024]{2,1,0:T(8,128)(2,1)}), bf16[4,64,1024]{2,1,0:T(8,128)(2,1)S(1)}, u32[]{:S(2)}, u32[]{:S(2)}) async-start(bf16[4,64,1024]{2,1,0:T(8,128)(2,1)} %bitcast.14), calls=%async_computation | async-start | bytes 1048576 | tf_op jit(solution)/shard_map/all_to_all | solution.py:87
  95.2 7.0 %fusion.2 = bf16[1024,2048]{1,0:T(8,128)(2,1)S(1)} fusion(bf16[1024,1024]{1,0:T(8,128)(2,1)S(1)} %bitcast.54, bf16[1,2048,1024]{1,2,0:T(8,128)(2,1)} %all-gather.5.cloned.1.call-done), kind=kOutput, calls=%fused_computation.8 | convolution fusion | flops 4297064448 | bytes 10485760 | tf_op jit(solution)/shard_map/dot_general | solution.py:54
  102.2 1.8 %dynamic-slice_bitcast_fusion = (bf16[1024,1024]{0,1:T(8,128)(2,1)}, bf16[1024,1024]{0,1:T(8,128)(2,1)S(1)}) fusion(bf16[1024,2048]{1,0:T(8,128)(2,1)S(1)} %fusion.2, s32[]{:T(128)S(6)} %select_n.191, s32[]{:T(128)S(6)} %select_n.171), kind=kLoop, calls=%fused_computation.10 | loop fusion | bytes 8388616 | tf_op jit(solution)/shard_map/dynamic_slice | solution.py:101
  104.0 1.1 all-to-all-done
  105.1 2.5 %fusion.26 = f32[1024,256]{1,0:T(8,128)S(1)} fusion(bf16[1024,1024]{0,1:T(8,128)(2,1)} %get-tuple-element.12, bf16[256,1024]{1,0:T(8,128)(2,1)S(1)} %bitcast.55), kind=kOutput, calls=%fused_computation.87 | convolution fusion | flops 536870912 | bytes 3670016 | tf_op jit(solution)/shard_map/dot_general | solution.py:15
  108.2 1.4 %gather_fusion.5 = bf16[64,16,256]{2,1,0:T(8,128)(2,1)} fusion(bf16[64,16,256]{2,1,0:T(8,128)(2,1)S(1)} %bitcast.59, s32[1024]{0:T(1024)S(1)} %pad_clamp_fusion), kind=kCustom, calls=%fused_computation.5 | custom fusion | bytes 1048832 | tf_op jit(solution)/shard_map/gather | solution.py:114
  109.6 2.8 %collective-permute-start.3 = (bf16[1024,256]{1,0:T(8,128)(2,1)}, bf16[1024,256]{1,0:T(8,128)(2,1)S(1)}, u32[]{:S(2)}, u32[]{:S(2)}) collective-permute-start(bf16[1024,256]{1,0:T(8,128)(2,1)} %bitcast.63), channel_id=1, source_target_pairs={{0,128},{128,0},{256,384},{384,256},{1,129},{129,1},{257,385},{385... | collective-permute-start | bytes 1572872 | tf_op jit(solution)/shard_map/ppermute | solution.py:11
  112.5 0.8 fusion.25
  114.5 10.2 %collective-permute-done.3 = bf16[1024,256]{1,0:T(8,128)(2,1)S(1)} collective-permute-done((bf16[1024,256]{1,0:T(8,128)(2,1)}, bf16[1024,256]{1,0:T(8,128)(2,1)S(1)}, u32[]{:S(2)}, u32[]{:S(2)}) %collective-permute-start.3) | collective-permute-done | bytes 524320 | tf_op jit(solution)/shard_map/ppermute | solution.py:11
  124.8 1.1 bitcast_add_fusion
  (36 shorter events, 4.9 us)
Async XLA Ops:
  6.5 53.1 %copy-start = (s32[1,512]{1,0:T(1,128)S(1)}, s32[1,512]{1,0:T(1,128)}, u32[]{:S(2)}) copy-start(s32[1,512]{1,0:T(1,128)} %param.7) | copy-start | bytes 6148
  6.5 56.8 %copy-start.3 = (f32[1,2048,256]{2,1,0:T(8,128)S(1)}, f32[1,2048,256]{2,1,0:T(8,128)}, u32[]{:S(2)}) copy-start(f32[1,2048,256]{2,1,0:T(8,128)} %param.6) | copy-start | bytes 6291460
  6.5 81.3 %all-gather.5.cloned.1.call-start = ((), (), s32[]{:S(2)}) async-start(), calls=%async_computation.1 | async-start | bytes 4325376 | tf_op jit(solution)/shard_map/all_gather | solution.py:51
  47.7 17.9 %collective-permute-start.1 = (bf16[256,1024]{1,0:T(8,128)(2,1)S(1)}, bf16[256,1024]{1,0:T(8,128)(2,1)}, u32[]{:S(2)}, u32[]{:S(2)}) collective-permute-start(bf16[256,1024]{1,0:T(8,128)(2,1)S(1)} %bitcast.60), channel_id=1, source_target_pairs={{0,64},{32,96},{64,0},{96,32},{1,65},{33,97},{65,1},{97,33},{2,66}... | collective-permute-start | bytes 1572872 | tf_op jit(solution)/shard_map/ppermute | solution.py:24
  52.5 18.6 %collective-permute-start = (bf16[256,1024]{1,0:T(8,128)(2,1)S(1)}, bf16[256,1024]{1,0:T(8,128)(2,1)}, u32[]{:S(2)}, u32[]{:S(2)}) collective-permute-start(bf16[256,1024]{1,0:T(8,128)(2,1)S(1)} %bitcast.61), channel_id=1, source_target_pairs={{0,32},{32,64},{64,96},{96,0},{1,33},{33,65},{65,97},{97,1},{2,34}... | collective-permute-start | bytes 1572872 | tf_op jit(solution)/shard_map/ppermute | solution.py:24
  55.0 16.1 %collective-permute-start.2 = (bf16[256,1024]{1,0:T(8,128)(2,1)S(1)}, bf16[256,1024]{1,0:T(8,128)(2,1)}, u32[]{:S(2)}, u32[]{:S(2)}) collective-permute-start(bf16[256,1024]{1,0:T(8,128)(2,1)S(1)} %bitcast.62), channel_id=1, source_target_pairs={{0,96},{32,0},{64,32},{96,64},{1,97},{33,1},{65,33},{97,65},{2,98}... | collective-permute-start | bytes 1572872 | tf_op jit(solution)/shard_map/ppermute | solution.py:24
  90.8 14.2 %all-to-all-start = ((bf16[4,64,1024]{2,1,0:T(8,128)(2,1)}), bf16[4,64,1024]{2,1,0:T(8,128)(2,1)S(1)}, u32[]{:S(2)}, u32[]{:S(2)}) async-start(bf16[4,64,1024]{2,1,0:T(8,128)(2,1)} %bitcast.14), calls=%async_computation | async-start | bytes 1048576 | tf_op jit(solution)/shard_map/all_to_all | solution.py:87
  105.1 2.5 %copy-start.2 = (f32[1024,256]{1,0:T(8,128)S(1)}, f32[1024,256]{1,0:T(8,128)}, u32[]{:S(2)}) copy-start(f32[1024,256]{1,0:T(8,128)} %get-tuple-element.11) | copy-start | bytes 3145732
  109.6 3.6 %copy-start.1 = (f32[1024,256]{1,0:T(8,128)S(1)}, f32[1024,256]{1,0:T(8,128)}, u32[]{:S(2)}) copy-start(f32[1024,256]{1,0:T(8,128)} %get-tuple-element.9) | copy-start | bytes 3145732
  109.6 15.2 %collective-permute-start.3 = (bf16[1024,256]{1,0:T(8,128)(2,1)}, bf16[1024,256]{1,0:T(8,128)(2,1)S(1)}, u32[]{:S(2)}, u32[]{:S(2)}) collective-permute-start(bf16[1024,256]{1,0:T(8,128)(2,1)} %bitcast.63), channel_id=1, source_target_pairs={{0,128},{128,0},{256,384},{384,256},{1,129},{129,1},{257,385},{385... | collective-permute-start | bytes 1572872 | tf_op jit(solution)/shard_map/ppermute | solution.py:11
Sparse Core Ops, SparseCore 0:
  9.5 78.3 all-gather.4
